TPU v7x, 32 devices: a whole 2x2x4 slice. The times are simulated.
32 devices in a mesh: circ: 4 (over z), normal: 2 (over y), span: 4 (over x, core).
Axes of the slice: x: 2, y: 2, z: 4, core: 2. Of those that a mesh axis runs over, the one named last changes fastest.
Arguments:
- adjoint: float32 [5, 16, 32, 512], P(None, 'span', 'normal', 'circ'), may hold values from -6 to 6
- objective_grad: float32 [5, 16, 32, 512], P(None, 'span', 'normal', 'circ'), may hold values from -6 to 6
- face_weights: float32 [3, 16, 32, 512], P(None, 'span', 'normal', 'circ'), may hold values from 0.2 to 2
- owner_jac: float32 [3, 5, 5], replicated, may hold values from -2.5 to 2.5
- neighbor_jac: float32 [3, 5, 5], replicated, may hold values from -2.5 to 2.5
- coupling: float32 [3, 5], replicated, may hold values from -2.5 to 2.5
- stiffness: float32 [16, 32, 512], P('span', 'normal', 'circ'), may hold values from 0.3 to 3
- wall_kernel: float32 [16, 32, 512], P('span', 'normal', 'circ'), may hold values from -0.25 to 0.25
- panel_owner: int32 [16, 512], P('span', 'circ'), may hold values from 0 to 511, as said below
Outputs:
- adjoint_residual: float32 [5, 16, 32, 512], P(None, 'span', 'normal', 'circ')
- mesh_adjoint: float32 [3, 16, 32, 512], P(None, 'span', 'normal', 'circ')
- panel_sens: float32 [3, 512], P(None, 'span')
Inputs may be any that keep to these rules, and one draw needn't show every extreme that they name: `panel_owner`: the panel of a wall face at station k is owned by span index k // 4 or the one beside it; panels hold ragged numbers of faces.
All inputs are finite; a program needn't handle non-finite values.
Results may differ from a plain program's by a relative error of at most 0.00011.
Values sent between devices are 32-bit elements; how exact they have to be, the bound alone decides.
No kernel may reach another device: no remote copies, remote signals or barrier semaphores. Data moves between devices by JAX's collectives and lax.ppermute only.
A program may use at most 64 MiB of HBM per device.

v0:
```python
import jax
import jax.numpy as jnp
from jax import lax
from jax.sharding import PartitionSpec as P

PANEL_DEV = 128
SWEEPS = 4


def padded_2(array, sides, width, wrap):
    for axis, dim in sides:
        peers, length = (lax.axis_size(axis), array.shape[dim])
        up = [(i, (i + 1) % peers) for i in range(peers if wrap else peers - 1)]
        down = [(j, i) for i, j in up]
        last = lax.slice_in_dim(array, length - width, length, axis=dim)
        initial = lax.slice_in_dim(array, 0, width, axis=dim)
        before = lax.ppermute(last, axis, up)
        after = lax.ppermute(initial, axis, down)
        array = jnp.concatenate([before, array, after], axis=dim)
    return array


def neighbor_sum(padded):
    total = padded[:, 2:, 1:-1, 1:-1] + padded[:, :-2, 1:-1, 1:-1]
    total = total + padded[:, 1:-1, 2:, 1:-1] + padded[:, 1:-1, :-2, 1:-1]
    return total + padded[:, 1:-1, 1:-1, 2:] + padded[:, 1:-1, 1:-1, :-2]


def inner(field):
    return field[:, 1:-1, 1:-1, 1:-1]


def flux_transpose(padded, owner_jac, neighbor_jac):
    psi = padded[:5]
    weights = padded[5:]
    center = inner(psi)
    total = jnp.zeros_like(center)
    for direction in range(3):
        lower = [slice(None), slice(1, -1), slice(1, -1), slice(1, -1)]
        upper = [slice(None), slice(1, -1), slice(1, -1), slice(1, -1)]
        lower[direction + 1] = slice(0, -2)
        upper[direction + 1] = slice(2, None)
        w_here = weights[direction, 1:-1, 1:-1, 1:-1]
        w_lower = weights[direction][tuple(lower[1:])]
        up_term = w_here[None] * (center - psi[tuple(upper)])
        down_term = w_lower[None] * (psi[tuple(lower)] - center)
        total = total + jnp.einsum(
            "uv,ukji->vkji", owner_jac[direction], up_term, precision=lax.Precision.HIGHEST
        )
        total = total + jnp.einsum(
            "uv,ukji->vkji", neighbor_jac[direction], down_term, precision=lax.Precision.HIGHEST
        )
    return total


def relax(mesh_pad, stiff_pad, force_pad):
    weighted = stiff_pad[None] * mesh_pad
    stiff_in = stiff_pad[1:-1, 1:-1, 1:-1]
    diag_term = 6.0 * stiff_in + 1.0
    mesh_in = inner(mesh_pad)
    return (
        mesh_in
        + 0.8
        * (inner(force_pad) - diag_term[None] * mesh_in + neighbor_sum(weighted))
        / diag_term[None]
    )


def run_sweeps(stiff_pad, force_pad):
    mesh_pad = 0.8 * force_pad / (6.0 * stiff_pad[None] + 1.0)
    for sweep in range(1, SWEEPS):
        mesh_pad = relax(mesh_pad, stiff_pad, force_pad)
        stiff_pad = stiff_pad[1:-1, 1:-1, 1:-1]
        force_pad = inner(force_pad)
    return mesh_pad


def on_device(
    adjoint,
    objective_grad,
    face_weights,
    owner_jac,
    neighbor_jac,
    coupling,
    stiffness,
    wall_kernel,
    panel_owner,
):
    stacked = jnp.concatenate([adjoint, face_weights], axis=0)
    beside_all = padded_2(stacked, (("circ", 3),), 1, True)
    padded = padded_2(beside_all, (("normal", 2), ("span", 1)), 1, False)
    residual = flux_transpose(padded, owner_jac, neighbor_jac) + adjoint - objective_grad
    forcing = jnp.einsum("mv,vkji->mkji", coupling, residual, precision=lax.Precision.HIGHEST)
    margin = SWEEPS - 1
    joined = jnp.concatenate([stiffness[None], forcing], axis=0)
    cycle_pad = padded_2(joined, (("circ", 3),), margin, True)
    full_pad = padded_2(cycle_pad, (("normal", 2), ("span", 1)), margin, False)
    mesh = run_sweeps(full_pad[0], full_pad[1:])
    wall_sens = jnp.sum(wall_kernel[None] * mesh, axis=2)
    panel_count = PANEL_DEV * lax.axis_size("span")
    onehot = (
        panel_owner[:, :, None] == jnp.arange(panel_count, dtype=jnp.int32)[None, None, :]
    ).astype(jnp.float32)
    terms = jnp.einsum("mki,kip->mp", wall_sens, onehot, precision=lax.Precision.HIGHEST)
    total = lax.psum(terms, ("circ", "normal", "span"))
    panels = lax.dynamic_slice_in_dim(total, lax.axis_index("span") * PANEL_DEV, PANEL_DEV, 1)
    return (residual, mesh, panels)


def solution(mesh):
    placed = (
        P(None, "span", "normal", "circ"),
        P(None, "span", "normal", "circ"),
        P(None, "span", "normal", "circ"),
        P(),
        P(),
        P(),
        P("span", "normal", "circ"),
        P("span", "normal", "circ"),
        P("span", "circ"),
    )
    return jax.shard_map(
        on_device,
        mesh=mesh,
        in_specs=placed,
        out_specs=(
            P(None, "span", "normal", "circ"),
            P(None, "span", "normal", "circ"),
            P(None, "span"),
        ),
        check_vma=False,
    )
```

profile of v0, /device:TPU:0, one launch (start us, length us, event | category | flops | bytes accessed | tf_op | source)
XLA Modules:
  0.0 114.6 jit_solution(1528439476088058492)
XLA Ops:
  0.7 1.0 constant_dynamic-update-slice_fusion.1
  1.8 3.1 %collective-permute-start = (f32[8,4,16,1]{3,2,1,0:T(8,128)S(1)}, f32[8,4,16,1]{3,2,1,0:T(8,128)S(1)}, u32[]{:S(2)}, u32[]{:S(2)}) collective-permute-start(f32[8,4,16,1]{3,2,1,0:T(8,128)S(1)} %get-tuple-element.32), channel_id=1, source_target_pairs={{0,8},{8,16},{16,24},{24,0},{1,9},{9,17},{17,25},{25,1},{2,10},{10... | collective-permute-start | bytes 6152 | tf_op jit(solution)/shard_map/ppermute | solution.py:17
  4.9 2.1 %collective-permute-start.1 = (f32[8,4,16,1]{3,2,1,0:T(8,128)S(1)}, f32[8,4,16,1]{3,2,1,0:T(8,128)S(1)}, u32[]{:S(2)}, u32[]{:S(2)}) collective-permute-start(f32[8,4,16,1]{3,2,1,0:T(8,128)S(1)} %get-tuple-element.33), channel_id=1, source_target_pairs={{8,0},{16,8},{24,16},{0,24},{9,1},{17,9},{25,17},{1,25},{10,2},{18... | collective-permute-start | bytes 6152 | tf_op jit(solution)/shard_map/ppermute | solution.py:18
  7.0 7.1 %collective-permute-done = f32[8,4,16,1]{3,2,1,0:T(8,128)S(1)} collective-permute-done((f32[8,4,16,1]{3,2,1,0:T(8,128)S(1)}, f32[8,4,16,1]{3,2,1,0:T(8,128)S(1)}, u32[]{:S(2)}, u32[]{:S(2)}) %collective-permute-start) | collective-permute-done | bytes 2080 | tf_op jit(solution)/shard_map/ppermute | solution.py:17
  14.1 4.2 %collective-permute-done.1 = f32[8,4,16,1]{3,2,1,0:T(8,128)S(1)} collective-permute-done((f32[8,4,16,1]{3,2,1,0:T(8,128)S(1)}, f32[8,4,16,1]{3,2,1,0:T(8,128)S(1)}, u32[]{:S(2)}, u32[]{:S(2)}) %collective-permute-start.1) | collective-permute-done | bytes 2080 | tf_op jit(solution)/shard_map/ppermute | solution.py:18
  18.2 0.3 pad_maximum_fusion.38
  18.5 3.4 %collective-permute-start.2 = (f32[8,4,1,130]{3,2,1,0:T(1,128)S(1)}, f32[8,4,1,130]{3,2,1,0:T(1,128)S(1)}, u32[]{:S(2)}, u32[]{:S(2)}) collective-permute-start(f32[8,4,1,130]{3,2,1,0:T(1,128)S(1)} %get-tuple-element.24), channel_id=1, source_target_pairs={{0,4},{1,5},{2,6},{3,7},{8,12},{9,13},{10,14},{11,15},{16,20},{17,... | collective-permute-start | bytes 49928 | tf_op jit(solution)/shard_map/ppermute | solution.py:17
  22.0 1.3 %collective-permute-start.3 = (f32[8,4,1,130]{3,2,1,0:T(1,128)S(1)}, f32[8,4,1,130]{3,2,1,0:T(1,128)S(1)}, u32[]{:S(2)}, u32[]{:S(2)}) collective-permute-start(f32[8,4,1,130]{3,2,1,0:T(1,128)S(1)} %get-tuple-element.25), channel_id=1, source_target_pairs={{4,0},{5,1},{6,2},{7,3},{12,8},{13,9},{14,10},{15,11},{20,16},{21,... | collective-permute-start | bytes 49928 | tf_op jit(solution)/shard_map/ppermute | solution.py:18
  23.3 0.2 collective-permute-done.2
  23.5 4.2 %collective-permute-done.3 = f32[8,4,1,130]{3,2,1,0:T(1,128)S(1)} collective-permute-done((f32[8,4,1,130]{3,2,1,0:T(1,128)S(1)}, f32[8,4,1,130]{3,2,1,0:T(1,128)S(1)}, u32[]{:S(2)}, u32[]{:S(2)}) %collective-permute-start.3) | collective-permute-done | bytes 16672 | tf_op jit(solution)/shard_map/ppermute | solution.py:18
  27.8 0.2 pad_maximum_fusion.2
  28.0 1.3 %collective-permute-start.5 = (f32[8,1,18,130]{3,2,1,0:T(8,128)S(1)}, f32[8,1,18,130]{3,2,1,0:T(8,128)S(1)}, u32[]{:S(2)}, u32[]{:S(2)}) collective-permute-start(f32[8,1,18,130]{3,2,1,0:T(8,128)S(1)} %get-tuple-element.22), channel_id=1, source_target_pairs={{0,1},{1,2},{2,3},{4,5},{5,6},{6,7},{8,9},{9,10},{10,11},{12,13},{... | collective-permute-start | bytes 224648 | tf_op jit(solution)/shard_map/ppermute | solution.py:17
  29.3 1.3 %collective-permute-start.4 = (f32[8,1,18,130]{3,2,1,0:T(8,128)S(1)}, f32[8,1,18,130]{3,2,1,0:T(8,128)S(1)}, u32[]{:S(2)}, u32[]{:S(2)}) collective-permute-start(f32[8,1,18,130]{3,2,1,0:T(8,128)S(1)} %get-tuple-element.23), channel_id=1, source_target_pairs={{1,0},{2,1},{3,2},{5,4},{6,5},{7,6},{9,8},{10,9},{11,10},{13,12},{... | collective-permute-start | bytes 224648 | tf_op jit(solution)/shard_map/ppermute | solution.py:18
  30.6 3.7 %collective-permute-done.4 = f32[8,1,18,130]{3,2,1,0:T(8,128)S(1)} collective-permute-done((f32[8,1,18,130]{3,2,1,0:T(8,128)S(1)}, f32[8,1,18,130]{3,2,1,0:T(8,128)S(1)}, u32[]{:S(2)}, u32[]{:S(2)}) %collective-permute-start.4) | collective-permute-done | bytes 74912 | tf_op jit(solution)/shard_map/ppermute | solution.py:18
  34.8 0.7 copy-done.1
  35.6 0.5 fusion.14
  36.1 0.5 convolution_add_fusion.4
  36.6 0.3 fusion.21
  36.9 0.5 convolution_add_fusion.3
  37.4 0.5 convolution_add_fusion.2
  37.8 0.5 convolution_add_fusion.1
  38.3 0.4 copy-done.3
  38.7 0.6 fusion.2
  39.4 0.3 convolution_bitcast_fusion
  39.7 0.4 copy-done.2
  40.3 1.2 %collective-permute-start.6 = (f32[4,4,16,3]{3,0,2,1:T(4,128)S(1)}, f32[4,4,16,3]{3,0,2,1:T(4,128)S(1)}, u32[]{:S(2)}, u32[]{:S(2)}) collective-permute-start(f32[4,4,16,3]{3,0,2,1:T(4,128)S(1)} %get-tuple-element.38), channel_id=1, source_target_pairs={{0,8},{8,16},{16,24},{24,0},{1,9},{9,17},{17,25},{25,1},{2,10},{10... | collective-permute-start | bytes 9224 | tf_op jit(solution)/shard_map/ppermute | solution.py:17
  41.5 2.7 %collective-permute-start.7 = (f32[4,4,16,3]{3,0,2,1:T(4,128)S(1)}, f32[4,4,16,3]{3,0,2,1:T(4,128)S(1)}, u32[]{:S(2)}, u32[]{:S(2)}) collective-permute-start(f32[4,4,16,3]{3,0,2,1:T(4,128)S(1)} %get-tuple-element.39), channel_id=1, source_target_pairs={{8,0},{16,8},{24,16},{0,24},{9,1},{17,9},{25,17},{1,25},{10,2},{18... | collective-permute-start | bytes 9224 | tf_op jit(solution)/shard_map/ppermute | solution.py:18
  44.2 3.1 %collective-permute-done.6 = f32[4,4,16,3]{3,0,2,1:T(4,128)S(1)} collective-permute-done((f32[4,4,16,3]{3,0,2,1:T(4,128)S(1)}, f32[4,4,16,3]{3,0,2,1:T(4,128)S(1)}, u32[]{:S(2)}, u32[]{:S(2)}) %collective-permute-start.6) | collective-permute-done | bytes 3104 | tf_op jit(solution)/shard_map/ppermute | solution.py:17
  47.3 0.6 collective-permute-done.7
  48.1 1.6 %collective-permute-start.8 = (f32[4,4,3,134]{3,0,2,1:T(4,128)S(1)}, f32[4,4,3,134]{3,0,2,1:T(4,128)S(1)}, u32[]{:S(2)}, u32[]{:S(2)}) collective-permute-start(f32[4,4,3,134]{3,0,2,1:T(4,128)S(1)} %get-tuple-element.28), channel_id=1, source_target_pairs={{0,4},{1,5},{2,6},{3,7},{8,12},{9,13},{10,14},{11,15},{16,20},{17,... | collective-permute-start | bytes 77192 | tf_op jit(solution)/shard_map/ppermute | solution.py:17
  49.7 1.3 %collective-permute-start.9 = (f32[4,4,3,134]{3,0,2,1:T(4,128)S(1)}, f32[4,4,3,134]{3,0,2,1:T(4,128)S(1)}, u32[]{:S(2)}, u32[]{:S(2)}) collective-permute-start(f32[4,4,3,134]{3,0,2,1:T(4,128)S(1)} %get-tuple-element.29), channel_id=1, source_target_pairs={{4,0},{5,1},{6,2},{7,3},{12,8},{13,9},{14,10},{15,11},{20,16},{21,... | collective-permute-start | bytes 77192 | tf_op jit(solution)/shard_map/ppermute | solution.py:18
  51.0 0.4 collective-permute-done.8
  51.4 4.3 %collective-permute-done.9 = f32[4,4,3,134]{3,0,2,1:T(4,128)S(1)} collective-permute-done((f32[4,4,3,134]{3,0,2,1:T(4,128)S(1)}, f32[4,4,3,134]{3,0,2,1:T(4,128)S(1)}, u32[]{:S(2)}, u32[]{:S(2)}) %collective-permute-start.9) | collective-permute-done | bytes 25760 | tf_op jit(solution)/shard_map/ppermute | solution.py:18
  55.7 0.4 pad_maximum_fusion.1
  56.2 3.2 %collective-permute-start.10 = (f32[4,3,22,134]{3,0,2,1:T(4,128)S(1)}, f32[4,3,22,134]{3,0,2,1:T(4,128)S(1)}, u32[]{:S(2)}, u32[]{:S(2)}) collective-permute-start(f32[4,3,22,134]{3,0,2,1:T(4,128)S(1)} %get-tuple-element.30), channel_id=1, source_target_pairs={{0,1},{1,2},{2,3},{4,5},{5,6},{6,7},{8,9},{9,10},{10,11},{12,13},{... | collective-permute-start | bytes 424520 | tf_op jit(solution)/shard_map/ppermute | solution.py:17
  59.4 1.5 %collective-permute-start.11 = (f32[4,3,22,134]{3,0,2,1:T(4,128)S(1)}, f32[4,3,22,134]{3,0,2,1:T(4,128)S(1)}, u32[]{:S(2)}, u32[]{:S(2)}) collective-permute-start(f32[4,3,22,134]{3,0,2,1:T(4,128)S(1)} %get-tuple-element.31), channel_id=1, source_target_pairs={{1,0},{2,1},{3,2},{5,4},{6,5},{7,6},{9,8},{10,9},{11,10},{13,12},{... | collective-permute-start | bytes 424520 | tf_op jit(solution)/shard_map/ppermute | solution.py:18
  60.9 0.7 copy.32
  61.6 3.4 %collective-permute-done.11 = f32[4,3,22,134]{3,0,2,1:T(4,128)S(1)} collective-permute-done((f32[4,3,22,134]{3,0,2,1:T(4,128)S(1)}, f32[4,3,22,134]{3,0,2,1:T(4,128)S(1)}, u32[]{:S(2)}, u32[]{:S(2)}) %collective-permute-start.11) | collective-permute-done | bytes 141536 | tf_op jit(solution)/shard_map/ppermute | solution.py:18
  65.0 0.5 pad_maximum_fusion
  65.5 0.3 multiply_add_fusion
  66.2 0.5 broadcast_multiply_fusion
  66.8 2.4 %broadcast_multiply_fusion.1 = (f32[3,8,20,132]{3,0,2,1:T(4,128)S(1)}, f32[3,8,20,132]{3,0,2,1:T(4,128)S(1)}) fusion(f32[8,20,132]{2,1,0:T(8,128)S(1)} %get-tuple-element.37, f32[3,10,22,134]{3,0,2,1:T(4,128)S(1)} %get-tuple-element.12, f32[8,20,132]{2,1,0:T(8,128)S(1)} %get-tuple-element.36, f32[4,10,22,134]{3,0,2,1:T(4,128)S(1)} %pad_maximum_fusion, ...), kind=kLoop, calls=%fused_computation.35 | loop fusion | flops 760320 | bytes 2703360 | tf_op jit(solution)/shard_map/mul | solution.py:57
  69.2 1.7 %broadcast_multiply_fusion.2 = (f32[3,6,18,130]{3,0,2,1:T(4,128)S(1)}, f32[3,6,18,130]{3,0,2,1:T(4,128)S(1)}) fusion(f32[6,18,130]{2,1,0:T(8,128)S(1)} %get-tuple-element.35, f32[3,8,20,132]{3,0,2,1:T(4,128)S(1)} %get-tuple-element.10, f32[6,18,130]{2,1,0:T(8,128)S(1)} %get-tuple-element.34, f32[4,10,22,134]{3,0,2,1:T(4,128)S(1)} %pad_maximum_fusion, ...), kind=kLoop, calls=%fused_computation.46 | loop fusion | flops 505440 | bytes 1797120 | tf_op jit(solution)/shard_map/mul | solution.py:57
  70.9 0.5 multiply_reduce_fusion
  71.6 0.5 convolution_bitcast_fusion.1
  72.1 41.3 %psum.7 = f32[3,512]{1,0:T(4,128)S(1)} all-reduce(f32[3,512]{1,0:T(4,128)S(1)} %convolution_bitcast_fusion.1), channel_id=1, replica_groups=mesh['circ'=4,'normal'=2,'span'=4] {'circ','normal','span'}, use_global_device_ids=true, to_apply=%region_1.0 | all-reduce | flops 1536 | bytes 12288 | tf_op jit(solution)/shard_map/psum | solution.py:105
  113.4 0.6 copy.33
  114.0 0.6 constant_dynamic-slice_fusion
  (35 shorter events, 1.8 us)
Async XLA Ops:
  0.6 38.7 %copy-start = (f32[3,5]{1,0:T(4,128)S(1)}, f32[3,5]{1,0:T(4,128)}, u32[]{:S(2)}) copy-start(f32[3,5]{1,0:T(4,128)} %param.14) | copy-start | bytes 184
  0.6 1.0 copy-start.4
  1.8 12.3 %collective-permute-start = (f32[8,4,16,1]{3,2,1,0:T(8,128)S(1)}, f32[8,4,16,1]{3,2,1,0:T(8,128)S(1)}, u32[]{:S(2)}, u32[]{:S(2)}) collective-permute-start(f32[8,4,16,1]{3,2,1,0:T(8,128)S(1)} %get-tuple-element.32), channel_id=1, source_target_pairs={{0,8},{8,16},{16,24},{24,0},{1,9},{9,17},{17,25},{25,1},{2,10},{10... | collective-permute-start | bytes 6152 | tf_op jit(solution)/shard_map/ppermute | solution.py:17
  4.9 13.4 %collective-permute-start.1 = (f32[8,4,16,1]{3,2,1,0:T(8,128)S(1)}, f32[8,4,16,1]{3,2,1,0:T(8,128)S(1)}, u32[]{:S(2)}, u32[]{:S(2)}) collective-permute-start(f32[8,4,16,1]{3,2,1,0:T(8,128)S(1)} %get-tuple-element.33), channel_id=1, source_target_pairs={{8,0},{16,8},{24,16},{0,24},{9,1},{17,9},{25,17},{1,25},{10,2},{18... | collective-permute-start | bytes 6152 | tf_op jit(solution)/shard_map/ppermute | solution.py:18
  7.0 16.3 %copy-start.6 = (f32[3,5,5]{2,0,1:T(4,128)S(1)}, f32[3,5,5]{2,0,1:T(4,128)}, u32[]{:S(2)}) copy-start(f32[3,5,5]{2,0,1:T(4,128)} %param.12) | copy-start | bytes 904
  18.5 5.0 %collective-permute-start.2 = (f32[8,4,1,130]{3,2,1,0:T(1,128)S(1)}, f32[8,4,1,130]{3,2,1,0:T(1,128)S(1)}, u32[]{:S(2)}, u32[]{:S(2)}) collective-permute-start(f32[8,4,1,130]{3,2,1,0:T(1,128)S(1)} %get-tuple-element.24), channel_id=1, source_target_pairs={{0,4},{1,5},{2,6},{3,7},{8,12},{9,13},{10,14},{11,15},{16,20},{17,... | collective-permute-start | bytes 49928 | tf_op jit(solution)/shard_map/ppermute | solution.py:17
  22.0 5.8 %collective-permute-start.3 = (f32[8,4,1,130]{3,2,1,0:T(1,128)S(1)}, f32[8,4,1,130]{3,2,1,0:T(1,128)S(1)}, u32[]{:S(2)}, u32[]{:S(2)}) collective-permute-start(f32[8,4,1,130]{3,2,1,0:T(1,128)S(1)} %get-tuple-element.25), channel_id=1, source_target_pairs={{4,0},{5,1},{6,2},{7,3},{12,8},{13,9},{14,10},{15,11},{20,16},{21,... | collective-permute-start | bytes 49928 | tf_op jit(solution)/shard_map/ppermute | solution.py:18
  23.3 7.3 %copy-start.7 = (f32[3,5,5]{2,0,1:T(4,128)S(1)}, f32[3,5,5]{2,0,1:T(4,128)}, u32[]{:S(2)}) copy-start(f32[3,5,5]{2,0,1:T(4,128)} %param.13) | copy-start | bytes 904
  28.0 2.6 %collective-permute-start.5 = (f32[8,1,18,130]{3,2,1,0:T(8,128)S(1)}, f32[8,1,18,130]{3,2,1,0:T(8,128)S(1)}, u32[]{:S(2)}, u32[]{:S(2)}) collective-permute-start(f32[8,1,18,130]{3,2,1,0:T(8,128)S(1)} %get-tuple-element.22), channel_id=1, source_target_pairs={{0,1},{1,2},{2,3},{4,5},{5,6},{6,7},{8,9},{9,10},{10,11},{12,13},{... | collective-permute-start | bytes 224648 | tf_op jit(solution)/shard_map/ppermute | solution.py:17
  29.3 5.1 %collective-permute-start.4 = (f32[8,1,18,130]{3,2,1,0:T(8,128)S(1)}, f32[8,1,18,130]{3,2,1,0:T(8,128)S(1)}, u32[]{:S(2)}, u32[]{:S(2)}) collective-permute-start(f32[8,1,18,130]{3,2,1,0:T(8,128)S(1)} %get-tuple-element.23), channel_id=1, source_target_pairs={{1,0},{2,1},{3,2},{5,4},{6,5},{7,6},{9,8},{10,9},{11,10},{13,12},{... | collective-permute-start | bytes 224648 | tf_op jit(solution)/shard_map/ppermute | solution.py:18
  34.5 0.9 copy-start.1
  37.8 0.9 copy-start.3
  39.4 0.8 copy-start.2
  40.3 7.0 %collective-permute-start.6 = (f32[4,4,16,3]{3,0,2,1:T(4,128)S(1)}, f32[4,4,16,3]{3,0,2,1:T(4,128)S(1)}, u32[]{:S(2)}, u32[]{:S(2)}) collective-permute-start(f32[4,4,16,3]{3,0,2,1:T(4,128)S(1)} %get-tuple-element.38), channel_id=1, source_target_pairs={{0,8},{8,16},{16,24},{24,0},{1,9},{9,17},{17,25},{25,1},{2,10},{10... | collective-permute-start | bytes 9224 | tf_op jit(solution)/shard_map/ppermute | solution.py:17
  41.5 6.4 %collective-permute-start.7 = (f32[4,4,16,3]{3,0,2,1:T(4,128)S(1)}, f32[4,4,16,3]{3,0,2,1:T(4,128)S(1)}, u32[]{:S(2)}, u32[]{:S(2)}) collective-permute-start(f32[4,4,16,3]{3,0,2,1:T(4,128)S(1)} %get-tuple-element.39), channel_id=1, source_target_pairs={{8,0},{16,8},{24,16},{0,24},{9,1},{17,9},{25,17},{1,25},{10,2},{18... | collective-permute-start | bytes 9224 | tf_op jit(solution)/shard_map/ppermute | solution.py:18
  48.1 3.4 %collective-permute-start.8 = (f32[4,4,3,134]{3,0,2,1:T(4,128)S(1)}, f32[4,4,3,134]{3,0,2,1:T(4,128)S(1)}, u32[]{:S(2)}, u32[]{:S(2)}) collective-permute-start(f32[4,4,3,134]{3,0,2,1:T(4,128)S(1)} %get-tuple-element.28), channel_id=1, source_target_pairs={{0,4},{1,5},{2,6},{3,7},{8,12},{9,13},{10,14},{11,15},{16,20},{17,... | collective-permute-start | bytes 77192 | tf_op jit(solution)/shard_map/ppermute | solution.py:17
  49.7 6.0 %collective-permute-start.9 = (f32[4,4,3,134]{3,0,2,1:T(4,128)S(1)}, f32[4,4,3,134]{3,0,2,1:T(4,128)S(1)}, u32[]{:S(2)}, u32[]{:S(2)}) collective-permute-start(f32[4,4,3,134]{3,0,2,1:T(4,128)S(1)} %get-tuple-element.29), channel_id=1, source_target_pairs={{4,0},{5,1},{6,2},{7,3},{12,8},{13,9},{14,10},{15,11},{20,16},{21,... | collective-permute-start | bytes 77192 | tf_op jit(solution)/shard_map/ppermute | solution.py:18
  56.2 5.4 %collective-permute-start.10 = (f32[4,3,22,134]{3,0,2,1:T(4,128)S(1)}, f32[4,3,22,134]{3,0,2,1:T(4,128)S(1)}, u32[]{:S(2)}, u32[]{:S(2)}) collective-permute-start(f32[4,3,22,134]{3,0,2,1:T(4,128)S(1)} %get-tuple-element.30), channel_id=1, source_target_pairs={{0,1},{1,2},{2,3},{4,5},{5,6},{6,7},{8,9},{9,10},{10,11},{12,13},{... | collective-permute-start | bytes 424520 | tf_op jit(solution)/shard_map/ppermute | solution.py:17
  59.4 5.6 %collective-permute-start.11 = (f32[4,3,22,134]{3,0,2,1:T(4,128)S(1)}, f32[4,3,22,134]{3,0,2,1:T(4,128)S(1)}, u32[]{:S(2)}, u32[]{:S(2)}) collective-permute-start(f32[4,3,22,134]{3,0,2,1:T(4,128)S(1)} %get-tuple-element.31), channel_id=1, source_target_pairs={{1,0},{2,1},{3,2},{5,4},{6,5},{7,6},{9,8},{10,9},{11,10},{13,12},{... | collective-permute-start | bytes 424520 | tf_op jit(solution)/shard_map/ppermute | solution.py:18
  69.2 1.7 %copy-start.5 = (f32[4,16,128]{2,1,0:T(8,128)S(1)}, f32[4,16,128]{2,1,0:T(8,128)}, u32[]{:S(2)}) copy-start(f32[4,16,128]{2,1,0:T(8,128)} %param.16) | copy-start | bytes 98308
  70.9 0.7 copy-start.8
where the time goes:
time: 115 us
  blocking collectives  41.3 us (36%)
  waiting for transfers between devices  31.3 us (27%)
  starting transfers between devices  23.9 us (21%)
  other arithmetic  8.29 us (7%)
  local copies, waits for them, and re-layouts  5.05 us (4%)
  matrix products  3.7 us (3%)
    psum x1, blocking collectives, on_device(): total = lax.psum(terms, ('circ', 'normal', 'span'))  41.3 us
    ppermute x6, waiting for transfers between devices, padded_2(): after = lax.ppermute(initial, axis, down)  20.4 us
    ppermute x6, starting transfers between devices, padded_2(): before = lax.ppermute(last, axis, up)  13.8 us
    ppermute x6, waiting for transfers between devices, padded_2(): before = lax.ppermute(last, axis, up)  10.9 us
    ppermute x6, starting transfers between devices, padded_2(): after = lax.ppermute(initial, axis, down)  10.1 us
    mul x3, other arithmetic, relax(): weighted = stiff_pad[None] * mesh_pad  4.64 us
    unnamed x22, local copies, waits for them, and re-layouts  4.09 us
  transfers between devices with their start and end apart: 12, of which 10 were waited for; matrix products, arithmetic and copies ran while one was open for 1% of the time, Pallas kernels for 0%

commit v1 on v0

--- a/solution.py
+++ b/solution.py
@@ -75,6 +75,38 @@
     return mesh_pad
 
 
+def face_halos(array, axis, dim, wrap):
+    peers, length = (lax.axis_size(axis), array.shape[dim])
+    up = [(i, (i + 1) % peers) for i in range(peers if wrap else peers - 1)]
+    down = [(j, i) for i, j in up]
+    before = lax.ppermute(lax.slice_in_dim(array, length - 1, length, axis=dim), axis, up)
+    after = lax.ppermute(lax.slice_in_dim(array, 0, 1, axis=dim), axis, down)
+    return before, after
+
+
+def flux_faces(stacked, halos, owner_jac, neighbor_jac):
+    center = stacked[:5]
+    total = jnp.zeros_like(center)
+    for direction in range(3):
+        dim = direction + 1
+        before, after = halos[direction]
+        line = jnp.concatenate([before, stacked, after], axis=dim)
+        length = line.shape[dim]
+        upper = lax.slice_in_dim(line[:5], 2, length, axis=dim)
+        lower = lax.slice_in_dim(line[:5], 0, length - 2, axis=dim)
+        w_here = stacked[5 + direction]
+        w_lower = lax.slice_in_dim(line[5 + direction], 0, length - 2, axis=direction)
+        up_term = w_here[None] * (center - upper)
+        down_term = w_lower[None] * (lower - center)
+        total = total + jnp.einsum(
+            "uv,ukji->vkji", owner_jac[direction], up_term, precision=lax.Precision.HIGHEST
+        )
+        total = total + jnp.einsum(
+            "uv,ukji->vkji", neighbor_jac[direction], down_term, precision=lax.Precision.HIGHEST
+        )
+    return total
+
+
 def on_device(
     adjoint,
     objective_grad,
@@ -87,9 +119,12 @@
     panel_owner,
 ):
     stacked = jnp.concatenate([adjoint, face_weights], axis=0)
-    beside_all = padded_2(stacked, (("circ", 3),), 1, True)
-    padded = padded_2(beside_all, (("normal", 2), ("span", 1)), 1, False)
-    residual = flux_transpose(padded, owner_jac, neighbor_jac) + adjoint - objective_grad
+    halos = [
+        face_halos(stacked, "span", 1, False),
+        face_halos(stacked, "normal", 2, False),
+        face_halos(stacked, "circ", 3, True),
+    ]
+    residual = flux_faces(stacked, halos, owner_jac, neighbor_jac) + adjoint - objective_grad
     forcing = jnp.einsum("mv,vkji->mkji", coupling, residual, precision=lax.Precision.HIGHEST)
     margin = SWEEPS - 1
     joined = jnp.concatenate([stiffness[None], forcing], axis=0)
@@ -97,13 +132,20 @@
     full_pad = padded_2(cycle_pad, (("normal", 2), ("span", 1)), margin, False)
     mesh = run_sweeps(full_pad[0], full_pad[1:])
     wall_sens = jnp.sum(wall_kernel[None] * mesh, axis=2)
-    panel_count = PANEL_DEV * lax.axis_size("span")
+    span = lax.axis_index("span")
+    first = (span - 1) * PANEL_DEV
+    local = panel_owner - first
     onehot = (
-        panel_owner[:, :, None] == jnp.arange(panel_count, dtype=jnp.int32)[None, None, :]
+        local[:, :, None] == jnp.arange(3 * PANEL_DEV, dtype=jnp.int32)[None, None, :]
     ).astype(jnp.float32)
     terms = jnp.einsum("mki,kip->mp", wall_sens, onehot, precision=lax.Precision.HIGHEST)
-    total = lax.psum(terms, ("circ", "normal", "span"))
-    panels = lax.dynamic_slice_in_dim(total, lax.axis_index("span") * PANEL_DEV, PANEL_DEV, 1)
+    terms = lax.psum(terms, ("circ", "normal"))
+    peers = lax.axis_size("span")
+    up = [(i, i + 1) for i in range(peers - 1)]
+    down = [(j, i) for i, j in up]
+    from_below = lax.ppermute(terms[:, 2 * PANEL_DEV :], "span", up)
+    from_above = lax.ppermute(terms[:, :PANEL_DEV], "span", down)
+    panels = terms[:, PANEL_DEV : 2 * PANEL_DEV] + from_below + from_above
     return (residual, mesh, panels)
 
 

time: 115 us -> 97.3 us (0.85)
  the two profiles are of different devices: /device:TPU:0 before, /device:TPU:1 now
where the time goes in v1:
time: 97.3 us; the launch traced here: 96.7 us
  starting transfers between devices  37.8 us (39%)
  waiting for transfers between devices  24.3 us (25%)
  blocking collectives  15.7 us (16%)
  other arithmetic  7.93 us (8%)
  local copies, waits for them, and re-layouts  6.33 us (7%)
  matrix products  3.63 us (4%)
  between operations  1.09 us (1%)
    psum x1, blocking collectives, on_device(): terms = lax.psum(terms, ('circ', 'normal'))  15.7 us
    ppermute x3, waiting for transfers between devices, padded_2(): after = lax.ppermute(initial, axis, down)  9.35 us
    ppermute x3, starting transfers between devices, face_halos(): lax.ppermute(lax.slice_in_dim(array, length - 1, length, axis=dim), axis,...  9.28 us
    ppermute x3, starting transfers between devices, padded_2(): before = lax.ppermute(last, axis, up)  8.22 us
    ppermute x3, starting transfers between devices, padded_2(): after = lax.ppermute(initial, axis, down)  7.59 us
    unnamed x26, local copies, waits for them, and re-layouts  6.03 us
    ppermute x3, waiting for transfers between devices, face_halos(): lax.ppermute(lax.slice_in_dim(array, length - 1, length, axis=dim), axis,...  5.83 us
    ppermute x1, starting transfers between devices, on_device(): from_below = lax.ppermute(terms[:, 2 * PANEL_DEV:], 'span', up)  5.51 us
  transfers between devices with their start and end apart: 14, of which 8 were waited for; matrix products, arithmetic and copies ran while one was open for 2% of the time, Pallas kernels for 0%

profile of v1, /device:TPU:1, one launch (start us, length us, event | category | flops | bytes accessed | tf_op | source)
XLA Modules:
  0.0 96.7 jit_solution(18193311845943295380)
XLA Ops:
  0.7 1.0 constant_dynamic-update-slice_fusion.1
  1.7 4.0 %collective-permute-start.3 = (f32[8,4,1,128]{3,2,1,0:T(1,128)S(1)}, f32[8,4,1,128]{3,2,1,0:T(1,128)S(1)}, u32[]{:S(2)}, u32[]{:S(2)}) collective-permute-start(f32[8,4,1,128]{3,2,1,0:T(1,128)S(1)} %get-tuple-element.28), channel_id=1, source_target_pairs={{0,4},{1,5},{2,6},{3,7},{8,12},{9,13},{10,14},{11,15},{16,20},{17,... | collective-permute-start | bytes 49160 | tf_op jit(solution)/shard_map/ppermute | solution.py:82
  5.7 1.3 %collective-permute-start.2 = (f32[8,4,1,128]{3,2,1,0:T(1,128)S(1)}, f32[8,4,1,128]{3,2,1,0:T(1,128)S(1)}, u32[]{:S(2)}, u32[]{:S(2)}) collective-permute-start(f32[8,4,1,128]{3,2,1,0:T(1,128)S(1)} %get-tuple-element.29), channel_id=1, source_target_pairs={{4,0},{5,1},{6,2},{7,3},{12,8},{13,9},{14,10},{15,11},{20,16},{21,... | collective-permute-start | bytes 49160 | tf_op jit(solution)/shard_map/ppermute | solution.py:83
  7.0 4.0 %collective-permute-start.1 = (f32[8,1,16,128]{3,2,1,0:T(8,128)S(1)}, f32[8,1,16,128]{3,2,1,0:T(8,128)S(1)}, u32[]{:S(2)}, u32[]{:S(2)}) collective-permute-start(f32[8,1,16,128]{3,2,1,0:T(8,128)S(1)} %get-tuple-element.30), channel_id=1, source_target_pairs={{0,1},{1,2},{2,3},{4,5},{5,6},{6,7},{8,9},{9,10},{10,11},{12,13},{... | collective-permute-start | bytes 196616 | tf_op jit(solution)/shard_map/ppermute | solution.py:82
  11.1 1.3 %collective-permute-start.5 = (f32[8,4,16,1]{3,2,1,0:T(8,128)S(1)}, f32[8,4,16,1]{3,2,1,0:T(8,128)S(1)}, u32[]{:S(2)}, u32[]{:S(2)}) collective-permute-start(f32[8,4,16,1]{3,2,1,0:T(8,128)S(1)} %get-tuple-element.26), channel_id=1, source_target_pairs={{0,8},{8,16},{16,24},{24,0},{1,9},{9,17},{17,25},{25,1},{2,10},{10... | collective-permute-start | bytes 6152 | tf_op jit(solution)/shard_map/ppermute | solution.py:82
  12.4 2.1 %collective-permute-start.4 = (f32[8,4,16,1]{3,2,1,0:T(8,128)S(1)}, f32[8,4,16,1]{3,2,1,0:T(8,128)S(1)}, u32[]{:S(2)}, u32[]{:S(2)}) collective-permute-start(f32[8,4,16,1]{3,2,1,0:T(8,128)S(1)} %get-tuple-element.27), channel_id=1, source_target_pairs={{8,0},{16,8},{24,16},{0,24},{9,1},{17,9},{25,17},{1,25},{10,2},{18... | collective-permute-start | bytes 6152 | tf_op jit(solution)/shard_map/ppermute | solution.py:83
  14.6 0.7 copy-done.9
  15.3 5.8 %collective-permute-done.5 = f32[8,4,16,1]{3,2,1,0:T(8,128)S(1)} collective-permute-done((f32[8,4,16,1]{3,2,1,0:T(8,128)S(1)}, f32[8,4,16,1]{3,2,1,0:T(8,128)S(1)}, u32[]{:S(2)}, u32[]{:S(2)}) %collective-permute-start.5) | collective-permute-done | bytes 2080 | tf_op jit(solution)/shard_map/ppermute | solution.py:82
  21.1 1.9 %collective-permute-start = (f32[8,1,16,128]{3,2,1,0:T(8,128)S(1)}, f32[8,1,16,128]{3,2,1,0:T(8,128)S(1)}, u32[]{:S(2)}, u32[]{:S(2)}) collective-permute-start(f32[8,1,16,128]{3,2,1,0:T(8,128)S(1)} %get-tuple-element.31), channel_id=1, source_target_pairs={{1,0},{2,1},{3,2},{5,4},{6,5},{7,6},{9,8},{10,9},{11,10},{13,12},{... | collective-permute-start | bytes 196616 | tf_op jit(solution)/shard_map/ppermute | solution.py:83
  23.0 2.3 %collective-permute-done.4 = f32[8,4,16,1]{3,2,1,0:T(8,128)S(1)} collective-permute-done((f32[8,4,16,1]{3,2,1,0:T(8,128)S(1)}, f32[8,4,16,1]{3,2,1,0:T(8,128)S(1)}, u32[]{:S(2)}, u32[]{:S(2)}) %collective-permute-start.4) | collective-permute-done | bytes 2080 | tf_op jit(solution)/shard_map/ppermute | solution.py:83
  25.4 0.6 copy-done.5
  26.1 0.6 copy-done.6
  26.7 0.9 copy-done.1
  27.8 0.5 fusion.14
  28.3 0.5 convolution_add_fusion.4
  28.7 0.5 convolution_add_fusion.3
  29.2 0.5 convolution_add_fusion.2
  29.7 0.5 convolution_add_fusion.1
  30.1 0.4 copy-done.3
  30.6 0.6 fusion.2
  31.2 0.3 convolution_bitcast_fusion
  31.6 0.4 copy-done.2
  32.2 0.8 collective-permute-start.6
  32.9 4.4 %collective-permute-start.7 = (f32[4,4,16,3]{3,0,2,1:T(4,128)S(1)}, f32[4,4,16,3]{3,0,2,1:T(4,128)S(1)}, u32[]{:S(2)}, u32[]{:S(2)}) collective-permute-start(f32[4,4,16,3]{3,0,2,1:T(4,128)S(1)} %get-tuple-element.37), channel_id=1, source_target_pairs={{8,0},{16,8},{24,16},{0,24},{9,1},{17,9},{25,17},{1,25},{10,2},{18... | collective-permute-start | bytes 9224 | tf_op jit(solution)/shard_map/ppermute | solution.py:18
  37.3 3.7 %collective-permute-done.6 = f32[4,4,16,3]{3,0,2,1:T(4,128)S(1)} collective-permute-done((f32[4,4,16,3]{3,0,2,1:T(4,128)S(1)}, f32[4,4,16,3]{3,0,2,1:T(4,128)S(1)}, u32[]{:S(2)}, u32[]{:S(2)}) %collective-permute-start.6) | collective-permute-done | bytes 3104 | tf_op jit(solution)/shard_map/ppermute | solution.py:17
  41.0 1.1 %collective-permute-done.7 = f32[4,4,16,3]{3,0,2,1:T(4,128)S(1)} collective-permute-done((f32[4,4,16,3]{3,0,2,1:T(4,128)S(1)}, f32[4,4,16,3]{3,0,2,1:T(4,128)S(1)}, u32[]{:S(2)}, u32[]{:S(2)}) %collective-permute-start.7) | collective-permute-done | bytes 3104 | tf_op jit(solution)/shard_map/ppermute | solution.py:18
  42.3 4.1 %collective-permute-start.8 = (f32[4,4,3,134]{3,0,2,1:T(4,128)S(1)}, f32[4,4,3,134]{3,0,2,1:T(4,128)S(1)}, u32[]{:S(2)}, u32[]{:S(2)}) collective-permute-start(f32[4,4,3,134]{3,0,2,1:T(4,128)S(1)} %get-tuple-element.16), channel_id=1, source_target_pairs={{0,4},{1,5},{2,6},{3,7},{8,12},{9,13},{10,14},{11,15},{16,20},{17,... | collective-permute-start | bytes 77192 | tf_op jit(solution)/shard_map/ppermute | solution.py:17
  46.4 1.3 %collective-permute-start.9 = (f32[4,4,3,134]{3,0,2,1:T(4,128)S(1)}, f32[4,4,3,134]{3,0,2,1:T(4,128)S(1)}, u32[]{:S(2)}, u32[]{:S(2)}) collective-permute-start(f32[4,4,3,134]{3,0,2,1:T(4,128)S(1)} %get-tuple-element.17), channel_id=1, source_target_pairs={{4,0},{5,1},{6,2},{7,3},{12,8},{13,9},{14,10},{15,11},{20,16},{21,... | collective-permute-start | bytes 77192 | tf_op jit(solution)/shard_map/ppermute | solution.py:18
  47.7 3.9 %collective-permute-done.9 = f32[4,4,3,134]{3,0,2,1:T(4,128)S(1)} collective-permute-done((f32[4,4,3,134]{3,0,2,1:T(4,128)S(1)}, f32[4,4,3,134]{3,0,2,1:T(4,128)S(1)}, u32[]{:S(2)}, u32[]{:S(2)}) %collective-permute-start.9) | collective-permute-done | bytes 25760 | tf_op jit(solution)/shard_map/ppermute | solution.py:18
  51.6 0.4 pad_maximum_fusion.1
  52.1 3.4 %collective-permute-start.10 = (f32[4,3,22,134]{3,0,2,1:T(4,128)S(1)}, f32[4,3,22,134]{3,0,2,1:T(4,128)S(1)}, u32[]{:S(2)}, u32[]{:S(2)}) collective-permute-start(f32[4,3,22,134]{3,0,2,1:T(4,128)S(1)} %get-tuple-element.24), channel_id=1, source_target_pairs={{0,1},{1,2},{2,3},{4,5},{5,6},{6,7},{8,9},{9,10},{10,11},{12,13},{... | collective-permute-start | bytes 424520 | tf_op jit(solution)/shard_map/ppermute | solution.py:17
  55.5 1.9 %collective-permute-start.11 = (f32[4,3,22,134]{3,0,2,1:T(4,128)S(1)}, f32[4,3,22,134]{3,0,2,1:T(4,128)S(1)}, u32[]{:S(2)}, u32[]{:S(2)}) collective-permute-start(f32[4,3,22,134]{3,0,2,1:T(4,128)S(1)} %get-tuple-element.25), channel_id=1, source_target_pairs={{1,0},{2,1},{3,2},{5,4},{6,5},{7,6},{9,8},{10,9},{11,10},{13,12},{... | collective-permute-start | bytes 424520 | tf_op jit(solution)/shard_map/ppermute | solution.py:18
  57.4 1.4 %collective-permute-done.10 = f32[4,3,22,134]{3,0,2,1:T(4,128)S(1)} collective-permute-done((f32[4,3,22,134]{3,0,2,1:T(4,128)S(1)}, f32[4,3,22,134]{3,0,2,1:T(4,128)S(1)}, u32[]{:S(2)}, u32[]{:S(2)}) %collective-permute-start.10) | collective-permute-done | bytes 141536 | tf_op jit(solution)/shard_map/ppermute | solution.py:17
  58.9 4.4 %collective-permute-done.11 = f32[4,3,22,134]{3,0,2,1:T(4,128)S(1)} collective-permute-done((f32[4,3,22,134]{3,0,2,1:T(4,128)S(1)}, f32[4,3,22,134]{3,0,2,1:T(4,128)S(1)}, u32[]{:S(2)}, u32[]{:S(2)}) %collective-permute-start.11) | collective-permute-done | bytes 141536 | tf_op jit(solution)/shard_map/ppermute | solution.py:18
  63.3 0.5 pad_maximum_fusion
  63.7 0.3 multiply_add_fusion
  64.4 0.5 broadcast_multiply_fusion
  65.0 2.4 %broadcast_multiply_fusion.1 = (f32[3,8,20,132]{3,0,2,1:T(4,128)S(1)}, f32[3,8,20,132]{3,0,2,1:T(4,128)S(1)}) fusion(f32[8,20,132]{2,1,0:T(8,128)S(1)} %get-tuple-element.35, f32[3,10,22,134]{3,0,2,1:T(4,128)S(1)} %get-tuple-element.12, f32[8,20,132]{2,1,0:T(8,128)S(1)} %get-tuple-element.34, f32[4,10,22,134]{3,0,2,1:T(4,128)S(1)} %pad_maximum_fusion, ...), kind=kLoop, calls=%fused_computation.35 | loop fusion | flops 760320 | bytes 2703360 | tf_op jit(solution)/shard_map/mul | solution.py:57
  67.5 1.7 %broadcast_multiply_fusion.2 = (f32[3,6,18,130]{3,0,2,1:T(4,128)S(1)}, f32[3,6,18,130]{3,0,2,1:T(4,128)S(1)}) fusion(f32[6,18,130]{2,1,0:T(8,128)S(1)} %get-tuple-element.33, f32[3,8,20,132]{3,0,2,1:T(4,128)S(1)} %get-tuple-element.10, f32[6,18,130]{2,1,0:T(8,128)S(1)} %get-tuple-element.32, f32[4,10,22,134]{3,0,2,1:T(4,128)S(1)} %pad_maximum_fusion, ...), kind=kLoop, calls=%fused_computation.46 | loop fusion | flops 505440 | bytes 1797120 | tf_op jit(solution)/shard_map/mul | solution.py:57
  69.1 0.5 multiply_reduce_fusion
  69.6 0.4 convolution_bitcast_fusion.1
  70.0 15.7 %psum.7 = f32[3,384]{1,0:T(4,128)S(1)} all-reduce(f32[3,384]{1,0:T(4,128)S(1)} %convolution_bitcast_fusion.1), channel_id=1, replica_groups=mesh['circ'=4,'normal'=2,'span'=4] {'circ','normal'}, use_global_device_ids=true, to_apply=%region_1.0 | all-reduce | flops 1152 | bytes 9216 | tf_op jit(solution)/shard_map/psum | solution.py:142
  85.7 5.5 %collective-permute-start.12 = (f32[3,128]{1,0:T(4,128)S(1)}, f32[3,128]{1,0:T(4,128)S(1)}, u32[]{:S(2)}, u32[]{:S(2)}) collective-permute-start(f32[3,128]{1,0:T(4,128)S(1)} %get-tuple-element.47), channel_id=1, source_target_pairs={{0,1},{1,2},{2,3},{4,5},{5,6},{6,7},{8,9},{9,10},{10,11},{12,13},{... | collective-permute-start | bytes 4616 | tf_op jit(solution)/shard_map/ppermute | solution.py:146
  91.2 1.9 %collective-permute-start.13 = (f32[3,128]{1,0:T(4,128)S(1)}, f32[3,128]{1,0:T(4,128)S(1)}, u32[]{:S(2)}, u32[]{:S(2)}) collective-permute-start(f32[3,128]{1,0:T(4,128)S(1)} %get-tuple-element.48), channel_id=1, source_target_pairs={{1,0},{2,1},{3,2},{5,4},{6,5},{7,6},{9,8},{10,9},{11,10},{13,12},{... | collective-permute-start | bytes 4616 | tf_op jit(solution)/shard_map/ppermute | solution.py:147
  93.2 0.7 copy.32
  93.9 0.6 copy.33
  94.5 1.6 %collective-permute-done.13 = f32[3,128]{1,0:T(4,128)S(1)} collective-permute-done((f32[3,128]{1,0:T(4,128)S(1)}, f32[3,128]{1,0:T(4,128)S(1)}, u32[]{:S(2)}, u32[]{:S(2)}) %collective-permute-start.13) | collective-permute-done | bytes 1568 | tf_op jit(solution)/shard_map/ppermute | solution.py:147
  96.1 0.6 fusion.33
  (46 shorter events, 1.4 us)
Async XLA Ops:
  0.6 30.6 %copy-start = (f32[3,5]{1,0:T(4,128)S(1)}, f32[3,5]{1,0:T(4,128)}, u32[]{:S(2)}) copy-start(f32[3,5]{1,0:T(4,128)} %param.14) | copy-start | bytes 184
  0.6 1.0 %copy-start.4 = (f32[3,4,16,128]{3,2,1,0:T(8,128)S(1)}, f32[3,4,16,128]{3,2,1,0:T(8,128)}, u32[]{:S(2)}) copy-start(f32[3,4,16,128]{3,2,1,0:T(8,128)} %param.11) | copy-start | bytes 294916
  1.7 24.3 %collective-permute-start.3 = (f32[8,4,1,128]{3,2,1,0:T(1,128)S(1)}, f32[8,4,1,128]{3,2,1,0:T(1,128)S(1)}, u32[]{:S(2)}, u32[]{:S(2)}) collective-permute-start(f32[8,4,1,128]{3,2,1,0:T(1,128)S(1)} %get-tuple-element.28), channel_id=1, source_target_pairs={{0,4},{1,5},{2,6},{3,7},{8,12},{9,13},{10,14},{11,15},{16,20},{17,... | collective-permute-start | bytes 49160 | tf_op jit(solution)/shard_map/ppermute | solution.py:82
  5.7 20.4 %collective-permute-start.2 = (f32[8,4,1,128]{3,2,1,0:T(1,128)S(1)}, f32[8,4,1,128]{3,2,1,0:T(1,128)S(1)}, u32[]{:S(2)}, u32[]{:S(2)}) collective-permute-start(f32[8,4,1,128]{3,2,1,0:T(1,128)S(1)} %get-tuple-element.29), channel_id=1, source_target_pairs={{4,0},{5,1},{6,2},{7,3},{12,8},{13,9},{14,10},{15,11},{20,16},{21,... | collective-permute-start | bytes 49160 | tf_op jit(solution)/shard_map/ppermute | solution.py:83
  7.0 19.7 %collective-permute-start.1 = (f32[8,1,16,128]{3,2,1,0:T(8,128)S(1)}, f32[8,1,16,128]{3,2,1,0:T(8,128)S(1)}, u32[]{:S(2)}, u32[]{:S(2)}) collective-permute-start(f32[8,1,16,128]{3,2,1,0:T(8,128)S(1)} %get-tuple-element.30), channel_id=1, source_target_pairs={{0,1},{1,2},{2,3},{4,5},{5,6},{6,7},{8,9},{9,10},{10,11},{12,13},{... | collective-permute-start | bytes 196616 | tf_op jit(solution)/shard_map/ppermute | solution.py:82
  11.1 10.0 %collective-permute-start.5 = (f32[8,4,16,1]{3,2,1,0:T(8,128)S(1)}, f32[8,4,16,1]{3,2,1,0:T(8,128)S(1)}, u32[]{:S(2)}, u32[]{:S(2)}) collective-permute-start(f32[8,4,16,1]{3,2,1,0:T(8,128)S(1)} %get-tuple-element.26), channel_id=1, source_target_pairs={{0,8},{8,16},{16,24},{24,0},{1,9},{9,17},{17,25},{25,1},{2,10},{10... | collective-permute-start | bytes 6152 | tf_op jit(solution)/shard_map/ppermute | solution.py:82
  12.4 2.1 %copy-start.8 = (f32[3,5,5]{2,0,1:T(4,128)S(1)}, f32[3,5,5]{2,0,1:T(4,128)}, u32[]{:S(2)}) copy-start(f32[3,5,5]{2,0,1:T(4,128)} %param.12) | copy-start | bytes 904
  12.4 12.8 %collective-permute-start.4 = (f32[8,4,16,1]{3,2,1,0:T(8,128)S(1)}, f32[8,4,16,1]{3,2,1,0:T(8,128)S(1)}, u32[]{:S(2)}, u32[]{:S(2)}) collective-permute-start(f32[8,4,16,1]{3,2,1,0:T(8,128)S(1)} %get-tuple-element.27), channel_id=1, source_target_pairs={{8,0},{16,8},{24,16},{0,24},{9,1},{17,9},{25,17},{1,25},{10,2},{18... | collective-permute-start | bytes 6152 | tf_op jit(solution)/shard_map/ppermute | solution.py:83
  14.6 0.7 copy-start.9
  21.1 5.6 %collective-permute-start = (f32[8,1,16,128]{3,2,1,0:T(8,128)S(1)}, f32[8,1,16,128]{3,2,1,0:T(8,128)S(1)}, u32[]{:S(2)}, u32[]{:S(2)}) collective-permute-start(f32[8,1,16,128]{3,2,1,0:T(8,128)S(1)} %get-tuple-element.31), channel_id=1, source_target_pairs={{1,0},{2,1},{3,2},{5,4},{6,5},{7,6},{9,8},{10,9},{11,10},{13,12},{... | collective-permute-start | bytes 196616 | tf_op jit(solution)/shard_map/ppermute | solution.py:83
  25.4 0.6 copy-start.5
  26.0 0.6 copy-start.6
  26.7 0.9 copy-start.1
  26.7 0.9 slice-start
  26.7 0.9 slice-start.1
  29.7 0.9 copy-start.3
  31.2 0.8 copy-start.2
  32.2 8.9 %collective-permute-start.6 = (f32[4,4,16,3]{3,0,2,1:T(4,128)S(1)}, f32[4,4,16,3]{3,0,2,1:T(4,128)S(1)}, u32[]{:S(2)}, u32[]{:S(2)}) collective-permute-start(f32[4,4,16,3]{3,0,2,1:T(4,128)S(1)} %get-tuple-element.36), channel_id=1, source_target_pairs={{0,8},{8,16},{16,24},{24,0},{1,9},{9,17},{17,25},{25,1},{2,10},{10... | collective-permute-start | bytes 9224 | tf_op jit(solution)/shard_map/ppermute | solution.py:17
  32.9 9.2 %collective-permute-start.7 = (f32[4,4,16,3]{3,0,2,1:T(4,128)S(1)}, f32[4,4,16,3]{3,0,2,1:T(4,128)S(1)}, u32[]{:S(2)}, u32[]{:S(2)}) collective-permute-start(f32[4,4,16,3]{3,0,2,1:T(4,128)S(1)} %get-tuple-element.37), channel_id=1, source_target_pairs={{8,0},{16,8},{24,16},{0,24},{9,1},{17,9},{25,17},{1,25},{10,2},{18... | collective-permute-start | bytes 9224 | tf_op jit(solution)/shard_map/ppermute | solution.py:18
  42.3 5.4 %collective-permute-start.8 = (f32[4,4,3,134]{3,0,2,1:T(4,128)S(1)}, f32[4,4,3,134]{3,0,2,1:T(4,128)S(1)}, u32[]{:S(2)}, u32[]{:S(2)}) collective-permute-start(f32[4,4,3,134]{3,0,2,1:T(4,128)S(1)} %get-tuple-element.16), channel_id=1, source_target_pairs={{0,4},{1,5},{2,6},{3,7},{8,12},{9,13},{10,14},{11,15},{16,20},{17,... | collective-permute-start | bytes 77192 | tf_op jit(solution)/shard_map/ppermute | solution.py:17
  46.4 5.2 %collective-permute-start.9 = (f32[4,4,3,134]{3,0,2,1:T(4,128)S(1)}, f32[4,4,3,134]{3,0,2,1:T(4,128)S(1)}, u32[]{:S(2)}, u32[]{:S(2)}) collective-permute-start(f32[4,4,3,134]{3,0,2,1:T(4,128)S(1)} %get-tuple-element.17), channel_id=1, source_target_pairs={{4,0},{5,1},{6,2},{7,3},{12,8},{13,9},{14,10},{15,11},{20,16},{21,... | collective-permute-start | bytes 77192 | tf_op jit(solution)/shard_map/ppermute | solution.py:18
  52.1 5.3 %copy-start.10 = (s32[4,128]{1,0:T(4,128)S(1)}, s32[4,128]{1,0:T(4,128)}, u32[]{:S(2)}) copy-start(s32[4,128]{1,0:T(4,128)} %param.17) | copy-start | bytes 6148
  52.1 6.8 %collective-permute-start.10 = (f32[4,3,22,134]{3,0,2,1:T(4,128)S(1)}, f32[4,3,22,134]{3,0,2,1:T(4,128)S(1)}, u32[]{:S(2)}, u32[]{:S(2)}) collective-permute-start(f32[4,3,22,134]{3,0,2,1:T(4,128)S(1)} %get-tuple-element.24), channel_id=1, source_target_pairs={{0,1},{1,2},{2,3},{4,5},{5,6},{6,7},{8,9},{9,10},{10,11},{12,13},{... | collective-permute-start | bytes 424520 | tf_op jit(solution)/shard_map/ppermute | solution.py:17
  55.5 7.8 %collective-permute-start.11 = (f32[4,3,22,134]{3,0,2,1:T(4,128)S(1)}, f32[4,3,22,134]{3,0,2,1:T(4,128)S(1)}, u32[]{:S(2)}, u32[]{:S(2)}) collective-permute-start(f32[4,3,22,134]{3,0,2,1:T(4,128)S(1)} %get-tuple-element.25), channel_id=1, source_target_pairs={{1,0},{2,1},{3,2},{5,4},{6,5},{7,6},{9,8},{10,9},{11,10},{13,12},{... | collective-permute-start | bytes 424520 | tf_op jit(solution)/shard_map/ppermute | solution.py:18
  67.4 1.7 %copy-start.7 = (f32[4,16,128]{2,1,0:T(8,128)S(1)}, f32[4,16,128]{2,1,0:T(8,128)}, u32[]{:S(2)}) copy-start(f32[4,16,128]{2,1,0:T(8,128)} %param.16) | copy-start | bytes 98308
  85.7 8.8 %collective-permute-start.12 = (f32[3,128]{1,0:T(4,128)S(1)}, f32[3,128]{1,0:T(4,128)S(1)}, u32[]{:S(2)}, u32[]{:S(2)}) collective-permute-start(f32[3,128]{1,0:T(4,128)S(1)} %get-tuple-element.47), channel_id=1, source_target_pairs={{0,1},{1,2},{2,3},{4,5},{5,6},{6,7},{8,9},{9,10},{10,11},{12,13},{... | collective-permute-start | bytes 4616 | tf_op jit(solution)/shard_map/ppermute | solution.py:146
  91.2 4.9 %collective-permute-start.13 = (f32[3,128]{1,0:T(4,128)S(1)}, f32[3,128]{1,0:T(4,128)S(1)}, u32[]{:S(2)}, u32[]{:S(2)}) collective-permute-start(f32[3,128]{1,0:T(4,128)S(1)} %get-tuple-element.48), channel_id=1, source_target_pairs={{1,0},{2,1},{3,2},{5,4},{6,5},{7,6},{9,8},{10,9},{11,10},{13,12},{... | collective-permute-start | bytes 4616 | tf_op jit(solution)/shard_map/ppermute | solution.py:147

commit v2 on v1

--- a/solution.py
+++ b/solution.py
@@ -1,3 +1,6 @@
+import itertools
+import math
+
 import jax
 import jax.numpy as jnp
 from jax import lax
@@ -75,13 +78,81 @@
     return mesh_pad
 
 
+ORDER = ("circ", "normal", "span")
+WRAP = {"circ": True, "normal": False, "span": False}
+
+
+def edge(array, dim, side, width):
+    length = array.shape[dim]
+    start = length - width if side < 0 else 0
+    return lax.slice_in_dim(array, start, start + width, axis=dim)
+
+
+def pairs_for(offsets):
+    axes = [a for a in ORDER if a in offsets]
+    sizes = [lax.axis_size(a) for a in axes]
+    pairs = []
+    for source in itertools.product(*[range(n) for n in sizes]):
+        target, inside = [], True
+        for axis, q, n in zip(axes, source, sizes):
+            t = q + offsets[axis]
+            if WRAP[axis]:
+                t %= n
+            elif not 0 <= t < n:
+                inside = False
+            target.append(t)
+        if inside:
+            lin = lambda v: sum(x * math.prod(sizes[i + 1 :]) for i, x in enumerate(v))
+            pairs.append((lin(source), lin(target)))
+    return tuple(axes), pairs
+
+
+def take(array, rel, dims, width):
+    for axis, r in rel.items():
+        if r:
+            array = edge(array, dims[axis], r, width)
+    return array
+
+
+def receive(array, rel, dims, width):
+    rel = {a: r for a, r in rel.items() if r}
+    axes, pairs = pairs_for({a: -r for a, r in rel.items()})
+    return lax.ppermute(take(array, rel, dims, width), axes, pairs)
+
+
+def receive_pair(array, rel, axis, dims, width):
+    low = dict(rel, **{axis: -1})
+    high = dict(rel, **{axis: 1})
+    if lax.axis_size(axis) != 2 or WRAP[axis]:
+        return receive(array, low, dims, width), receive(array, high, dims, width)
+    me = lax.axis_index(axis)
+    sent = jnp.where(me == 0, take(array, low, dims, width), take(array, high, dims, width))
+    low_nz = {a: r for a, r in low.items() if r}
+    axes, pairs = pairs_for({a: -r for a, r in low_nz.items()})
+    _, back = pairs_for({a: -r for a, r in dict(low_nz, **{axis: 1}).items()})
+    got = lax.ppermute(sent, axes, pairs + back)
+    zero = jnp.zeros_like(got)
+    return jnp.where(me == 1, got, zero), jnp.where(me == 0, got, zero)
+
+
 def face_halos(array, axis, dim, wrap):
-    peers, length = (lax.axis_size(axis), array.shape[dim])
-    up = [(i, (i + 1) % peers) for i in range(peers if wrap else peers - 1)]
-    down = [(j, i) for i, j in up]
-    before = lax.ppermute(lax.slice_in_dim(array, length - 1, length, axis=dim), axis, up)
-    after = lax.ppermute(lax.slice_in_dim(array, 0, 1, axis=dim), axis, down)
-    return before, after
+    return receive_pair(array, {}, axis, {axis: dim}, 1)
+
+
+def padded_sweeps(joined, width):
+    dims = {"span": 1, "normal": 2, "circ": 3}
+    before_c = receive(joined, {"circ": -1}, dims, width)
+    after_c = receive(joined, {"circ": 1}, dims, width)
+    low_n, high_n = receive_pair(joined, {}, "normal", dims, width)
+    low_lc, high_lc = receive_pair(joined, {"circ": -1}, "normal", dims, width)
+    low_hc, high_hc = receive_pair(joined, {"circ": 1}, "normal", dims, width)
+    top = jnp.concatenate([low_lc, low_n, low_hc], axis=3)
+    middle = jnp.concatenate([before_c, joined, after_c], axis=3)
+    bottom = jnp.concatenate([high_lc, high_n, high_hc], axis=3)
+    plane = jnp.concatenate([top, middle, bottom], axis=2)
+    before_s = receive(plane, {"span": -1}, dims, width)
+    after_s = receive(plane, {"span": 1}, dims, width)
+    return jnp.concatenate([before_s, plane, after_s], axis=1)
 
 
 def flux_faces(stacked, halos, owner_jac, neighbor_jac):
@@ -128,8 +199,7 @@
     forcing = jnp.einsum("mv,vkji->mkji", coupling, residual, precision=lax.Precision.HIGHEST)
     margin = SWEEPS - 1
     joined = jnp.concatenate([stiffness[None], forcing], axis=0)
-    cycle_pad = padded_2(joined, (("circ", 3),), margin, True)
-    full_pad = padded_2(cycle_pad, (("normal", 2), ("span", 1)), margin, False)
+    full_pad = padded_sweeps(joined, margin)
     mesh = run_sweeps(full_pad[0], full_pad[1:])
     wall_sens = jnp.sum(wall_kernel[None] * mesh, axis=2)
     span = lax.axis_index("span")

time: 97.3 us -> 91.7 us (0.942)
  waiting for transfers between devices: 24.3 us -> 19.2 us
  starting transfers between devices: 37.8 us -> 34.9 us
  blocking collectives: 15.7 us -> 18 us
    ppermute x12, waiting for transfers between devices: 22.6 us -> 17.6 us  [the longest x8 17.6 us: receive(): return lax.ppermute(take(array, rel, dims, width), axes, pairs)]
    ppermute x12, starting transfers between devices: 30.4 us -> 27.5 us  [the longest x8 20.7 us: receive(): return lax.ppermute(take(array, rel, dims, width), axes, pairs)]
    psum x1, blocking collectives: 15.7 us -> 18 us  [on_device(): terms = lax.psum(terms, ('circ', 'normal'))]
  transfers between devices with their start and end apart: 14 -> 14, of which waited for: 8 -> 6; matrix products, arithmetic and copies ran while one was open for 2% -> 2% of each run, Pallas kernels for 0% -> 0%
where the time goes in v2:
time: 91.7 us; the launch traced here: 91.2 us
  starting transfers between devices  34.9 us (38%)
  waiting for transfers between devices  19.2 us (21%)
  blocking collectives  18 us (20%)
  other arithmetic  8.1 us (9%)
  local copies, waits for them, and re-layouts  6.3 us (7%)
  matrix products  3.63 us (4%)
  between operations  1.1 us (1%)
    ppermute x8, starting transfers between devices, receive(): return lax.ppermute(take(array, rel, dims, width), axes, pairs)  20.7 us
    psum x1, blocking collectives, on_device(): terms = lax.psum(terms, ('circ', 'normal'))  18 us
    ppermute x8, waiting for transfers between devices, receive(): return lax.ppermute(take(array, rel, dims, width), axes, pairs)  17.6 us
    ppermute x4, starting transfers between devices, receive_pair(): got = lax.ppermute(sent, axes, pairs + back)  6.74 us
    unnamed x26, local copies, waits for them, and re-layouts  6.03 us
    ppermute x1, starting transfers between devices, on_device(): from_below = lax.ppermute(terms[:, 2 * PANEL_DEV:], 'span', up)  5.51 us
    mul x3, other arithmetic, relax(): weighted = stiff_pad[None] * mesh_pad  4.64 us
    ppermute x1, starting transfers between devices, on_device(): from_above = lax.ppermute(terms[:, :PANEL_DEV], 'span', down)  1.92 us
  transfers between devices with their start and end apart: 14, of which 6 were waited for; matrix products, arithmetic and copies ran while one was open for 2% of the time, Pallas kernels for 0%

profile of v2, /device:TPU:1, one launch (start us, length us, event | category | flops | bytes accessed | tf_op | source)
XLA Modules:
  0.0 91.2 jit_solution(10565960005895678062)
XLA Ops:
  0.7 1.0 %constant_dynamic-update-slice_fusion.1 = f32[8,4,16,128]{3,2,1,0:T(8,128)S(1)} fusion(f32[5,4,16,128]{3,2,1,0:T(8,128)} %param.9), kind=kLoop, calls=%fused_computation.122 | loop fusion | bytes 327680
  1.7 2.1 %collective-permute-start.2 = (f32[8,4,1,128]{3,2,1,0:T(1,128)S(1)}, f32[8,4,1,128]{3,2,1,0:T(1,128)S(1)}, u32[]{:S(2)}, u32[]{:S(2)}) collective-permute-start(f32[8,4,1,128]{3,2,1,0:T(1,128)S(1)} %broadcast_select_fusion.2), channel_id=1, source_target_pairs={{0,4},{4,0},{1,5},{5,1},{2,6},{6,2},{3,7},{7,3},{8,12},{12,8},{9,1... | collective-permute-start | bytes 49160 | tf_op jit(solution)/shard_map/ppermute | solution.py:133
  3.8 4.0 %collective-permute-start.1 = (f32[8,1,16,128]{3,2,1,0:T(8,128)S(1)}, f32[8,1,16,128]{3,2,1,0:T(8,128)S(1)}, u32[]{:S(2)}, u32[]{:S(2)}) collective-permute-start(f32[8,1,16,128]{3,2,1,0:T(8,128)S(1)} %get-tuple-element.26), channel_id=1, source_target_pairs={{0,1},{1,2},{2,3},{4,5},{5,6},{6,7},{8,9},{9,10},{10,11},{12,13},{... | collective-permute-start | bytes 196616 | tf_op jit(solution)/shard_map/ppermute | solution.py:120
  7.8 1.9 %collective-permute-start = (f32[8,1,16,128]{3,2,1,0:T(8,128)S(1)}, f32[8,1,16,128]{3,2,1,0:T(8,128)S(1)}, u32[]{:S(2)}, u32[]{:S(2)}) collective-permute-start(f32[8,1,16,128]{3,2,1,0:T(8,128)S(1)} %get-tuple-element.27), channel_id=1, source_target_pairs={{1,0},{2,1},{3,2},{5,4},{6,5},{7,6},{9,8},{10,9},{11,10},{13,12},{... | collective-permute-start | bytes 196616 | tf_op jit(solution)/shard_map/ppermute | solution.py:120
  9.7 0.1 fusion.47
  9.9 1.3 %collective-permute-start.4 = (f32[8,4,16,1]{3,2,1,0:T(8,128)S(1)}, f32[8,4,16,1]{3,2,1,0:T(8,128)S(1)}, u32[]{:S(2)}, u32[]{:S(2)}) collective-permute-start(f32[8,4,16,1]{3,2,1,0:T(8,128)S(1)} %get-tuple-element.24), channel_id=1, source_target_pairs={{0,8},{8,16},{16,24},{24,0},{1,9},{9,17},{17,25},{25,1},{2,10},{10... | collective-permute-start | bytes 6152 | tf_op jit(solution)/shard_map/ppermute | solution.py:120
  11.2 2.1 %collective-permute-start.3 = (f32[8,4,16,1]{3,2,1,0:T(8,128)S(1)}, f32[8,4,16,1]{3,2,1,0:T(8,128)S(1)}, u32[]{:S(2)}, u32[]{:S(2)}) collective-permute-start(f32[8,4,16,1]{3,2,1,0:T(8,128)S(1)} %get-tuple-element.25), channel_id=1, source_target_pairs={{0,24},{8,0},{16,8},{24,16},{1,25},{9,1},{17,9},{25,17},{2,26},{10... | collective-permute-start | bytes 6152 | tf_op jit(solution)/shard_map/ppermute | solution.py:120
  13.4 0.7 copy-done.9
  14.0 5.9 %collective-permute-done.4 = f32[8,4,16,1]{3,2,1,0:T(8,128)S(1)} collective-permute-done((f32[8,4,16,1]{3,2,1,0:T(8,128)S(1)}, f32[8,4,16,1]{3,2,1,0:T(8,128)S(1)}, u32[]{:S(2)}, u32[]{:S(2)}) %collective-permute-start.4) | collective-permute-done | bytes 2080 | tf_op jit(solution)/shard_map/ppermute | solution.py:120
  19.9 3.5 %collective-permute-done.3 = f32[8,4,16,1]{3,2,1,0:T(8,128)S(1)} collective-permute-done((f32[8,4,16,1]{3,2,1,0:T(8,128)S(1)}, f32[8,4,16,1]{3,2,1,0:T(8,128)S(1)}, u32[]{:S(2)}, u32[]{:S(2)}) %collective-permute-start.3) | collective-permute-done | bytes 2080 | tf_op jit(solution)/shard_map/ppermute | solution.py:120
  23.5 0.6 copy-done.5
  24.2 0.6 copy-done.6
  24.9 0.9 copy-done.1
  25.8 0.2 fusion.17
  26.0 0.5 fusion.14
  26.5 0.5 convolution_add_fusion.4
  26.9 0.5 convolution_add_fusion.3
  27.4 0.5 convolution_add_fusion.2
  27.9 0.5 convolution_add_fusion.1
  28.3 0.4 copy-done.3
  28.8 0.6 fusion.2
  29.4 0.3 convolution_bitcast_fusion
  29.8 0.4 copy-done.2
  30.3 0.2 fusion.28
  30.5 0.5 collective-permute-start.5
  31.0 1.5 %collective-permute-start.6 = (f32[4,4,3,128]{3,0,2,1:T(4,128)S(1)}, f32[4,4,3,128]{3,0,2,1:T(4,128)S(1)}, u32[]{:S(2)}, u32[]{:S(2)}) collective-permute-start(f32[4,4,3,128]{3,0,2,1:T(4,128)S(1)} %fusion.38), channel_id=1, source_target_pairs={{0,4},{4,0},{1,5},{5,1},{2,6},{6,2},{3,7},{7,3},{8,12},{12,8},{9,1... | collective-permute-start | bytes 73736 | tf_op jit(solution)/shard_map/ppermute | solution.py:133
  32.5 2.6 %collective-permute-start.7 = (f32[4,4,3,3]{3,0,2,1:T(4,128)S(1)}, f32[4,4,3,3]{3,0,2,1:T(4,128)S(1)}, u32[]{:S(2)}, u32[]{:S(2)}) collective-permute-start(f32[4,4,3,3]{3,0,2,1:T(4,128)S(1)} %get-tuple-element.35), channel_id=1, source_target_pairs={{0,28},{8,4},{16,12},{24,20},{4,24},{12,0},{20,8},{28,16},{1,29},{... | collective-permute-start | bytes 1736 | tf_op jit(solution)/shard_map/ppermute | solution.py:133
  35.1 3.3 %collective-permute-start.9 = (f32[4,4,16,3]{3,0,2,1:T(4,128)S(1)}, f32[4,4,16,3]{3,0,2,1:T(4,128)S(1)}, u32[]{:S(2)}, u32[]{:S(2)}) collective-permute-start(f32[4,4,16,3]{3,0,2,1:T(4,128)S(1)} %get-tuple-element.33), channel_id=1, source_target_pairs={{0,24},{8,0},{16,8},{24,16},{1,25},{9,1},{17,9},{25,17},{2,26},{10... | collective-permute-start | bytes 9224 | tf_op jit(solution)/shard_map/ppermute | solution.py:120
  38.5 2.4 %collective-permute-done.8 = f32[4,4,16,3]{3,0,2,1:T(4,128)S(1)} collective-permute-done((f32[4,4,16,3]{3,0,2,1:T(4,128)S(1)}, f32[4,4,16,3]{3,0,2,1:T(4,128)S(1)}, u32[]{:S(2)}, u32[]{:S(2)}) %collective-permute-start.8) | collective-permute-done | bytes 3104 | tf_op jit(solution)/shard_map/ppermute | solution.py:120
  40.8 0.5 maximum_maximum_fusion
  41.4 6.2 %collective-permute-start.10 = (f32[4,3,22,134]{3,0,2,1:T(4,128)S(1)}, f32[4,3,22,134]{3,0,2,1:T(4,128)S(1)}, u32[]{:S(2)}, u32[]{:S(2)}) collective-permute-start(f32[4,3,22,134]{3,0,2,1:T(4,128)S(1)} %get-tuple-element.22), channel_id=1, source_target_pairs={{0,1},{1,2},{2,3},{4,5},{5,6},{6,7},{8,9},{9,10},{10,11},{12,13},{... | collective-permute-start | bytes 424520 | tf_op jit(solution)/shard_map/ppermute | solution.py:120
  47.6 1.9 %collective-permute-start.11 = (f32[4,3,22,134]{3,0,2,1:T(4,128)S(1)}, f32[4,3,22,134]{3,0,2,1:T(4,128)S(1)}, u32[]{:S(2)}, u32[]{:S(2)}) collective-permute-start(f32[4,3,22,134]{3,0,2,1:T(4,128)S(1)} %get-tuple-element.23), channel_id=1, source_target_pairs={{1,0},{2,1},{3,2},{5,4},{6,5},{7,6},{9,8},{10,9},{11,10},{13,12},{... | collective-permute-start | bytes 424520 | tf_op jit(solution)/shard_map/ppermute | solution.py:120
  49.6 1.4 %collective-permute-done.10 = f32[4,3,22,134]{3,0,2,1:T(4,128)S(1)} collective-permute-done((f32[4,3,22,134]{3,0,2,1:T(4,128)S(1)}, f32[4,3,22,134]{3,0,2,1:T(4,128)S(1)}, u32[]{:S(2)}, u32[]{:S(2)}) %collective-permute-start.10) | collective-permute-done | bytes 141536 | tf_op jit(solution)/shard_map/ppermute | solution.py:120
  51.0 4.4 %collective-permute-done.11 = f32[4,3,22,134]{3,0,2,1:T(4,128)S(1)} collective-permute-done((f32[4,3,22,134]{3,0,2,1:T(4,128)S(1)}, f32[4,3,22,134]{3,0,2,1:T(4,128)S(1)}, u32[]{:S(2)}, u32[]{:S(2)}) %collective-permute-start.11) | collective-permute-done | bytes 141536 | tf_op jit(solution)/shard_map/ppermute | solution.py:120
  55.4 0.5 pad_maximum_fusion
  55.9 0.3 multiply_add_fusion
  56.6 0.5 broadcast_multiply_fusion
  57.2 2.4 %broadcast_multiply_fusion.1 = (f32[3,8,20,132]{3,0,2,1:T(4,128)S(1)}, f32[3,8,20,132]{3,0,2,1:T(4,128)S(1)}) fusion(f32[8,20,132]{2,1,0:T(8,128)S(1)} %get-tuple-element.31, f32[3,10,22,134]{3,0,2,1:T(4,128)S(1)} %get-tuple-element.12, f32[8,20,132]{2,1,0:T(8,128)S(1)} %get-tuple-element.30, f32[4,10,22,134]{3,0,2,1:T(4,128)S(1)} %pad_maximum_fusion, ...), kind=kLoop, calls=%fused_computation.42 | loop fusion | flops 760320 | bytes 2703360 | tf_op jit(solution)/shard_map/mul | solution.py:60
  59.6 1.7 %broadcast_multiply_fusion.2 = (f32[3,6,18,130]{3,0,2,1:T(4,128)S(1)}, f32[3,6,18,130]{3,0,2,1:T(4,128)S(1)}) fusion(f32[6,18,130]{2,1,0:T(8,128)S(1)} %get-tuple-element.29, f32[3,8,20,132]{3,0,2,1:T(4,128)S(1)} %get-tuple-element.10, f32[6,18,130]{2,1,0:T(8,128)S(1)} %get-tuple-element.28, f32[4,10,22,134]{3,0,2,1:T(4,128)S(1)} %pad_maximum_fusion, ...), kind=kLoop, calls=%fused_computation.53 | loop fusion | flops 505440 | bytes 1797120 | tf_op jit(solution)/shard_map/mul | solution.py:60
  61.3 0.5 multiply_reduce_fusion
  61.8 0.4 convolution_bitcast_fusion.1
  62.2 18.0 %psum.7 = f32[3,384]{1,0:T(4,128)S(1)} all-reduce(f32[3,384]{1,0:T(4,128)S(1)} %convolution_bitcast_fusion.1), channel_id=1, replica_groups=mesh['circ'=4,'normal'=2,'span'=4] {'circ','normal'}, use_global_device_ids=true, to_apply=%region_1.2 | all-reduce | flops 1152 | bytes 9216 | tf_op jit(solution)/shard_map/psum | solution.py:212
  80.2 5.5 %collective-permute-start.12 = (f32[3,128]{1,0:T(4,128)S(1)}, f32[3,128]{1,0:T(4,128)S(1)}, u32[]{:S(2)}, u32[]{:S(2)}) collective-permute-start(f32[3,128]{1,0:T(4,128)S(1)} %get-tuple-element.53), channel_id=1, source_target_pairs={{0,1},{1,2},{2,3},{4,5},{5,6},{6,7},{8,9},{9,10},{10,11},{12,13},{... | collective-permute-start | bytes 4616 | tf_op jit(solution)/shard_map/ppermute | solution.py:216
  85.8 1.9 %collective-permute-start.13 = (f32[3,128]{1,0:T(4,128)S(1)}, f32[3,128]{1,0:T(4,128)S(1)}, u32[]{:S(2)}, u32[]{:S(2)}) collective-permute-start(f32[3,128]{1,0:T(4,128)S(1)} %get-tuple-element.54), channel_id=1, source_target_pairs={{1,0},{2,1},{3,2},{5,4},{6,5},{7,6},{9,8},{10,9},{11,10},{13,12},{... | collective-permute-start | bytes 4616 | tf_op jit(solution)/shard_map/ppermute | solution.py:217
  87.7 0.7 copy.32
  88.4 0.6 copy.33
  89.0 1.6 %collective-permute-done.13 = f32[3,128]{1,0:T(4,128)S(1)} collective-permute-done((f32[3,128]{1,0:T(4,128)S(1)}, f32[3,128]{1,0:T(4,128)S(1)}, u32[]{:S(2)}, u32[]{:S(2)}) %collective-permute-start.13) | collective-permute-done | bytes 1568 | tf_op jit(solution)/shard_map/ppermute | solution.py:217
  90.7 0.6 fusion.43
  (51 shorter events, 0.9 us)
Async XLA Ops:
  0.6 28.8 %copy-start = (f32[3,5]{1,0:T(4,128)S(1)}, f32[3,5]{1,0:T(4,128)}, u32[]{:S(2)}) copy-start(f32[3,5]{1,0:T(4,128)} %param.14) | copy-start | bytes 184
  0.7 1.0 %copy-start.4 = (f32[3,4,16,128]{3,2,1,0:T(8,128)S(1)}, f32[3,4,16,128]{3,2,1,0:T(8,128)}, u32[]{:S(2)}) copy-start(f32[3,4,16,128]{3,2,1,0:T(8,128)} %param.11) | copy-start | bytes 294916
  1.7 22.5 %collective-permute-start.2 = (f32[8,4,1,128]{3,2,1,0:T(1,128)S(1)}, f32[8,4,1,128]{3,2,1,0:T(1,128)S(1)}, u32[]{:S(2)}, u32[]{:S(2)}) collective-permute-start(f32[8,4,1,128]{3,2,1,0:T(1,128)S(1)} %broadcast_select_fusion.2), channel_id=1, source_target_pairs={{0,4},{4,0},{1,5},{5,1},{2,6},{6,2},{3,7},{7,3},{8,12},{12,8},{9,1... | collective-permute-start | bytes 49160 | tf_op jit(solution)/shard_map/ppermute | solution.py:133
  3.8 21.0 %collective-permute-start.1 = (f32[8,1,16,128]{3,2,1,0:T(8,128)S(1)}, f32[8,1,16,128]{3,2,1,0:T(8,128)S(1)}, u32[]{:S(2)}, u32[]{:S(2)}) collective-permute-start(f32[8,1,16,128]{3,2,1,0:T(8,128)S(1)} %get-tuple-element.26), channel_id=1, source_target_pairs={{0,1},{1,2},{2,3},{4,5},{5,6},{6,7},{8,9},{9,10},{10,11},{12,13},{... | collective-permute-start | bytes 196616 | tf_op jit(solution)/shard_map/ppermute | solution.py:120
  7.8 17.1 %collective-permute-start = (f32[8,1,16,128]{3,2,1,0:T(8,128)S(1)}, f32[8,1,16,128]{3,2,1,0:T(8,128)S(1)}, u32[]{:S(2)}, u32[]{:S(2)}) collective-permute-start(f32[8,1,16,128]{3,2,1,0:T(8,128)S(1)} %get-tuple-element.27), channel_id=1, source_target_pairs={{1,0},{2,1},{3,2},{5,4},{6,5},{7,6},{9,8},{10,9},{11,10},{13,12},{... | collective-permute-start | bytes 196616 | tf_op jit(solution)/shard_map/ppermute | solution.py:120
  9.9 10.1 %collective-permute-start.4 = (f32[8,4,16,1]{3,2,1,0:T(8,128)S(1)}, f32[8,4,16,1]{3,2,1,0:T(8,128)S(1)}, u32[]{:S(2)}, u32[]{:S(2)}) collective-permute-start(f32[8,4,16,1]{3,2,1,0:T(8,128)S(1)} %get-tuple-element.24), channel_id=1, source_target_pairs={{0,8},{8,16},{16,24},{24,0},{1,9},{9,17},{17,25},{25,1},{2,10},{10... | collective-permute-start | bytes 6152 | tf_op jit(solution)/shard_map/ppermute | solution.py:120
  11.2 2.1 %copy-start.8 = (f32[3,5,5]{2,0,1:T(4,128)S(1)}, f32[3,5,5]{2,0,1:T(4,128)}, u32[]{:S(2)}) copy-start(f32[3,5,5]{2,0,1:T(4,128)} %param.12) | copy-start | bytes 904
  11.2 12.2 %collective-permute-start.3 = (f32[8,4,16,1]{3,2,1,0:T(8,128)S(1)}, f32[8,4,16,1]{3,2,1,0:T(8,128)S(1)}, u32[]{:S(2)}, u32[]{:S(2)}) collective-permute-start(f32[8,4,16,1]{3,2,1,0:T(8,128)S(1)} %get-tuple-element.25), channel_id=1, source_target_pairs={{0,24},{8,0},{16,8},{24,16},{1,25},{9,1},{17,9},{25,17},{2,26},{10... | collective-permute-start | bytes 6152 | tf_op jit(solution)/shard_map/ppermute | solution.py:120
  13.3 0.7 copy-start.9
  23.5 0.6 copy-start.5
  24.2 0.6 copy-start.6
  24.8 0.9 %copy-start.1 = (f32[5,4,16,128]{3,2,1,0:T(8,128)S(1)}, f32[5,4,16,128]{3,2,1,0:T(8,128)}, u32[]{:S(2)}) copy-start(f32[5,4,16,128]{3,2,1,0:T(8,128)} %param.9) | copy-start | bytes 491524
  24.8 0.9 %slice-start = ((f32[4,16,130]{2,1,0:T(8,128)}), f32[4,16,128]{2,1,0:T(8,128)S(1)}, s32[]{:S(2)}) async-start(f32[4,16,130]{2,1,0:T(8,128)} %copy-done.5), calls=%async_computation | async-start | bytes 65536 | tf_op jit(solution)/shard_map/slice | solution.py:169
  24.8 0.9 %slice-start.1 = ((f32[4,18,128]{2,1,0:T(8,128)}), f32[4,16,128]{2,1,0:T(8,128)S(1)}, s32[]{:S(2)}) async-start(f32[4,18,128]{2,1,0:T(8,128)} %copy-done.6), calls=%async_computation.1 | async-start | bytes 65536 | tf_op jit(solution)/shard_map/slice | solution.py:169
  27.9 0.9 %copy-start.3 = (f32[5,4,16,128]{3,2,1,0:T(8,128)S(1)}, f32[5,4,16,128]{3,2,1,0:T(8,128)}, u32[]{:S(2)}) copy-start(f32[5,4,16,128]{3,2,1,0:T(8,128)} %param.10) | copy-start | bytes 491524
  29.4 0.8 copy-start.2
  30.5 7.9 %collective-permute-start.5 = (f32[4,4,3,3]{3,0,2,1:T(4,128)S(1)}, f32[4,4,3,3]{3,0,2,1:T(4,128)S(1)}, u32[]{:S(2)}, u32[]{:S(2)}) collective-permute-start(f32[4,4,3,3]{3,0,2,1:T(4,128)S(1)} %get-tuple-element.34), channel_id=1, source_target_pairs={{0,12},{8,20},{16,28},{24,4},{4,8},{12,16},{20,24},{28,0},{1,13},{... | collective-permute-start | bytes 1736 | tf_op jit(solution)/shard_map/ppermute | solution.py:133
  31.0 7.4 %collective-permute-start.6 = (f32[4,4,3,128]{3,0,2,1:T(4,128)S(1)}, f32[4,4,3,128]{3,0,2,1:T(4,128)S(1)}, u32[]{:S(2)}, u32[]{:S(2)}) collective-permute-start(f32[4,4,3,128]{3,0,2,1:T(4,128)S(1)} %fusion.38), channel_id=1, source_target_pairs={{0,4},{4,0},{1,5},{5,1},{2,6},{6,2},{3,7},{7,3},{8,12},{12,8},{9,1... | collective-permute-start | bytes 73736 | tf_op jit(solution)/shard_map/ppermute | solution.py:133
  32.5 5.9 %collective-permute-start.7 = (f32[4,4,3,3]{3,0,2,1:T(4,128)S(1)}, f32[4,4,3,3]{3,0,2,1:T(4,128)S(1)}, u32[]{:S(2)}, u32[]{:S(2)}) collective-permute-start(f32[4,4,3,3]{3,0,2,1:T(4,128)S(1)} %get-tuple-element.35), channel_id=1, source_target_pairs={{0,28},{8,4},{16,12},{24,20},{4,24},{12,0},{20,8},{28,16},{1,29},{... | collective-permute-start | bytes 1736 | tf_op jit(solution)/shard_map/ppermute | solution.py:133
  35.1 5.7 %collective-permute-start.8 = (f32[4,4,16,3]{3,0,2,1:T(4,128)S(1)}, f32[4,4,16,3]{3,0,2,1:T(4,128)S(1)}, u32[]{:S(2)}, u32[]{:S(2)}) collective-permute-start(f32[4,4,16,3]{3,0,2,1:T(4,128)S(1)} %get-tuple-element.32), channel_id=1, source_target_pairs={{0,8},{8,16},{16,24},{24,0},{1,9},{9,17},{17,25},{25,1},{2,10},{10... | collective-permute-start | bytes 9224 | tf_op jit(solution)/shard_map/ppermute | solution.py:120
  35.1 5.7 %collective-permute-start.9 = (f32[4,4,16,3]{3,0,2,1:T(4,128)S(1)}, f32[4,4,16,3]{3,0,2,1:T(4,128)S(1)}, u32[]{:S(2)}, u32[]{:S(2)}) collective-permute-start(f32[4,4,16,3]{3,0,2,1:T(4,128)S(1)} %get-tuple-element.33), channel_id=1, source_target_pairs={{0,24},{8,0},{16,8},{24,16},{1,25},{9,1},{17,9},{25,17},{2,26},{10... | collective-permute-start | bytes 9224 | tf_op jit(solution)/shard_map/ppermute | solution.py:120
  41.4 8.1 %copy-start.10 = (s32[4,128]{1,0:T(4,128)S(1)}, s32[4,128]{1,0:T(4,128)}, u32[]{:S(2)}) copy-start(s32[4,128]{1,0:T(4,128)} %param.17) | copy-start | bytes 6148
  41.4 9.6 %collective-permute-start.10 = (f32[4,3,22,134]{3,0,2,1:T(4,128)S(1)}, f32[4,3,22,134]{3,0,2,1:T(4,128)S(1)}, u32[]{:S(2)}, u32[]{:S(2)}) collective-permute-start(f32[4,3,22,134]{3,0,2,1:T(4,128)S(1)} %get-tuple-element.22), channel_id=1, source_target_pairs={{0,1},{1,2},{2,3},{4,5},{5,6},{6,7},{8,9},{9,10},{10,11},{12,13},{... | collective-permute-start | bytes 424520 | tf_op jit(solution)/shard_map/ppermute | solution.py:120
  47.6 7.8 %collective-permute-start.11 = (f32[4,3,22,134]{3,0,2,1:T(4,128)S(1)}, f32[4,3,22,134]{3,0,2,1:T(4,128)S(1)}, u32[]{:S(2)}, u32[]{:S(2)}) collective-permute-start(f32[4,3,22,134]{3,0,2,1:T(4,128)S(1)} %get-tuple-element.23), channel_id=1, source_target_pairs={{1,0},{2,1},{3,2},{5,4},{6,5},{7,6},{9,8},{10,9},{11,10},{13,12},{... | collective-permute-start | bytes 424520 | tf_op jit(solution)/shard_map/ppermute | solution.py:120
  59.6 1.7 %copy-start.7 = (f32[4,16,128]{2,1,0:T(8,128)S(1)}, f32[4,16,128]{2,1,0:T(8,128)}, u32[]{:S(2)}) copy-start(f32[4,16,128]{2,1,0:T(8,128)} %param.16) | copy-start | bytes 98308
  80.2 8.8 %collective-permute-start.12 = (f32[3,128]{1,0:T(4,128)S(1)}, f32[3,128]{1,0:T(4,128)S(1)}, u32[]{:S(2)}, u32[]{:S(2)}) collective-permute-start(f32[3,128]{1,0:T(4,128)S(1)} %get-tuple-element.53), channel_id=1, source_target_pairs={{0,1},{1,2},{2,3},{4,5},{5,6},{6,7},{8,9},{9,10},{10,11},{12,13},{... | collective-permute-start | bytes 4616 | tf_op jit(solution)/shard_map/ppermute | solution.py:216
  85.8 4.9 %collective-permute-start.13 = (f32[3,128]{1,0:T(4,128)S(1)}, f32[3,128]{1,0:T(4,128)S(1)}, u32[]{:S(2)}, u32[]{:S(2)}) collective-permute-start(f32[3,128]{1,0:T(4,128)S(1)} %get-tuple-element.54), channel_id=1, source_target_pairs={{1,0},{2,1},{3,2},{5,4},{6,5},{7,6},{9,8},{10,9},{11,10},{13,12},{... | collective-permute-start | bytes 4616 | tf_op jit(solution)/shard_map/ppermute | solution.py:217

commit v3 on v2

--- a/solution.py
+++ b/solution.py
@@ -88,7 +88,7 @@
     return lax.slice_in_dim(array, start, start + width, axis=dim)
 
 
-def pairs_for(offsets):
+def pairs_for(offsets, wrap=()):
     axes = [a for a in ORDER if a in offsets]
     sizes = [lax.axis_size(a) for a in axes]
     pairs = []
@@ -96,7 +96,7 @@
         target, inside = [], True
         for axis, q, n in zip(axes, source, sizes):
             t = q + offsets[axis]
-            if WRAP[axis]:
+            if WRAP[axis] or axis in wrap:
                 t %= n
             elif not 0 <= t < n:
                 inside = False
@@ -176,6 +176,26 @@
             "uv,ukji->vkji", neighbor_jac[direction], down_term, precision=lax.Precision.HIGHEST
         )
     return total
+
+
+def shifted(array, offsets):
+    axes, pairs = pairs_for(offsets, ("normal",))
+    return lax.ppermute(array, axes, pairs)
+
+
+def reduce_panels(terms):
+    below, own, above = (terms[:, i * PANEL_DEV : (i + 1) * PANEL_DEV] for i in range(3))
+    if lax.axis_size("normal") != 2 or lax.axis_size("circ") > 4:
+        own = lax.psum(own + shifted(above, {"span": 1}) + shifted(below, {"span": -1}), ("circ", "normal"))
+        return own
+    partner = {"normal": 1}
+    total = own + shifted(above, {"span": 1}) + shifted(below, {"span": -1})
+    total = total + shifted(own, partner)
+    total = total + shifted(above, dict(partner, span=1)) + shifted(below, dict(partner, span=-1))
+    summed = total
+    for step in range(1, lax.axis_size("circ")):
+        summed = summed + shifted(total, {"circ": step})
+    return summed
 
 
 def on_device(
@@ -209,13 +229,7 @@
         local[:, :, None] == jnp.arange(3 * PANEL_DEV, dtype=jnp.int32)[None, None, :]
     ).astype(jnp.float32)
     terms = jnp.einsum("mki,kip->mp", wall_sens, onehot, precision=lax.Precision.HIGHEST)
-    terms = lax.psum(terms, ("circ", "normal"))
-    peers = lax.axis_size("span")
-    up = [(i, i + 1) for i in range(peers - 1)]
-    down = [(j, i) for i, j in up]
-    from_below = lax.ppermute(terms[:, 2 * PANEL_DEV :], "span", up)
-    from_above = lax.ppermute(terms[:, :PANEL_DEV], "span", down)
-    panels = terms[:, PANEL_DEV : 2 * PANEL_DEV] + from_below + from_above
+    panels = reduce_panels(terms)
     return (residual, mesh, panels)
 
 

time: 91.7 us -> 85 us (0.927)
  the two profiles are of different devices: /device:TPU:1 before, /device:TPU:0 now
where the time goes in v3:
time: 85 us; the launch traced here: 84.5 us
  starting transfers between devices  42.2 us (50%)
  waiting for transfers between devices  23.1 us (27%)
  other arithmetic  8.11 us (10%)
  local copies, waits for them, and re-layouts  6.3 us (7%)
  matrix products  3.64 us (4%)
  between operations  1.14 us (1%)
    ppermute x8, starting transfers between devices, shifted(): return lax.ppermute(array, axes, pairs)  20.5 us
    ppermute x8, waiting for transfers between devices, receive(): return lax.ppermute(take(array, rel, dims, width), axes, pairs)  18.9 us
    ppermute x8, starting transfers between devices, receive(): return lax.ppermute(take(array, rel, dims, width), axes, pairs)  13.2 us
    ppermute x4, starting transfers between devices, receive_pair(): got = lax.ppermute(sent, axes, pairs + back)  8.51 us
    unnamed x26, local copies, waits for them, and re-layouts  6.03 us
    mul x3, other arithmetic, relax(): weighted = stiff_pad[None] * mesh_pad  4.64 us
    ppermute x8, waiting for transfers between devices, shifted(): return lax.ppermute(array, axes, pairs)  4.18 us
  transfers between devices with their start and end apart: 20, of which 7 were waited for; matrix products, arithmetic and copies ran while one was open for 2% of the time, Pallas kernels for 0%

profile of v3, /device:TPU:0, one launch (start us, length us, event | category | flops | bytes accessed | tf_op | source)
XLA Modules:
  0.0 84.5 jit_solution(17784645287693975205)
XLA Ops:
  0.7 1.0 %constant_dynamic-update-slice_fusion.1 = f32[8,4,16,128]{3,2,1,0:T(8,128)S(1)} fusion(f32[5,4,16,128]{3,2,1,0:T(8,128)} %param.9), kind=kLoop, calls=%fused_computation.122 | loop fusion | bytes 327680
  1.7 3.0 %collective-permute-start.2 = (f32[8,4,1,128]{3,2,1,0:T(1,128)S(1)}, f32[8,4,1,128]{3,2,1,0:T(1,128)S(1)}, u32[]{:S(2)}, u32[]{:S(2)}) collective-permute-start(f32[8,4,1,128]{3,2,1,0:T(1,128)S(1)} %broadcast_select_fusion.2), channel_id=1, source_target_pairs={{0,4},{4,0},{1,5},{5,1},{2,6},{6,2},{3,7},{7,3},{8,12},{12,8},{9,1... | collective-permute-start | bytes 49160 | tf_op jit(solution)/shard_map/ppermute | solution.py:133
  4.7 1.5 %collective-permute-start.1 = (f32[8,1,16,128]{3,2,1,0:T(8,128)S(1)}, f32[8,1,16,128]{3,2,1,0:T(8,128)S(1)}, u32[]{:S(2)}, u32[]{:S(2)}) collective-permute-start(f32[8,1,16,128]{3,2,1,0:T(8,128)S(1)} %get-tuple-element.26), channel_id=1, source_target_pairs={{0,1},{1,2},{2,3},{4,5},{5,6},{6,7},{8,9},{9,10},{10,11},{12,13},{... | collective-permute-start | bytes 196616 | tf_op jit(solution)/shard_map/ppermute | solution.py:120
  6.2 1.3 %collective-permute-start = (f32[8,1,16,128]{3,2,1,0:T(8,128)S(1)}, f32[8,1,16,128]{3,2,1,0:T(8,128)S(1)}, u32[]{:S(2)}, u32[]{:S(2)}) collective-permute-start(f32[8,1,16,128]{3,2,1,0:T(8,128)S(1)} %get-tuple-element.27), channel_id=1, source_target_pairs={{1,0},{2,1},{3,2},{5,4},{6,5},{7,6},{9,8},{10,9},{11,10},{13,12},{... | collective-permute-start | bytes 196616 | tf_op jit(solution)/shard_map/ppermute | solution.py:120
  7.6 1.6 %collective-permute-start.4 = (f32[8,4,16,1]{3,2,1,0:T(8,128)S(1)}, f32[8,4,16,1]{3,2,1,0:T(8,128)S(1)}, u32[]{:S(2)}, u32[]{:S(2)}) collective-permute-start(f32[8,4,16,1]{3,2,1,0:T(8,128)S(1)} %get-tuple-element.24), channel_id=1, source_target_pairs={{0,8},{8,16},{16,24},{24,0},{1,9},{9,17},{17,25},{25,1},{2,10},{10... | collective-permute-start | bytes 6152 | tf_op jit(solution)/shard_map/ppermute | solution.py:120
  9.3 2.2 %collective-permute-start.3 = (f32[8,4,16,1]{3,2,1,0:T(8,128)S(1)}, f32[8,4,16,1]{3,2,1,0:T(8,128)S(1)}, u32[]{:S(2)}, u32[]{:S(2)}) collective-permute-start(f32[8,4,16,1]{3,2,1,0:T(8,128)S(1)} %get-tuple-element.25), channel_id=1, source_target_pairs={{0,24},{8,0},{16,8},{24,16},{1,25},{9,1},{17,9},{25,17},{2,26},{10... | collective-permute-start | bytes 6152 | tf_op jit(solution)/shard_map/ppermute | solution.py:120
  11.6 0.7 copy-done.9
  12.2 4.7 %collective-permute-done.4 = f32[8,4,16,1]{3,2,1,0:T(8,128)S(1)} collective-permute-done((f32[8,4,16,1]{3,2,1,0:T(8,128)S(1)}, f32[8,4,16,1]{3,2,1,0:T(8,128)S(1)}, u32[]{:S(2)}, u32[]{:S(2)}) %collective-permute-start.4) | collective-permute-done | bytes 2080 | tf_op jit(solution)/shard_map/ppermute | solution.py:120
  17.0 6.8 %collective-permute-done.3 = f32[8,4,16,1]{3,2,1,0:T(8,128)S(1)} collective-permute-done((f32[8,4,16,1]{3,2,1,0:T(8,128)S(1)}, f32[8,4,16,1]{3,2,1,0:T(8,128)S(1)}, u32[]{:S(2)}, u32[]{:S(2)}) %collective-permute-start.3) | collective-permute-done | bytes 2080 | tf_op jit(solution)/shard_map/ppermute | solution.py:120
  23.9 0.6 copy-done.5
  24.5 0.6 copy-done.6
  25.2 0.9 %copy-done.1 = f32[5,4,16,128]{3,2,1,0:T(8,128)S(1)} copy-done((f32[5,4,16,128]{3,2,1,0:T(8,128)S(1)}, f32[5,4,16,128]{3,2,1,0:T(8,128)}, u32[]{:S(2)}) %copy-start.1) | copy-done | bytes 163864
  26.3 0.5 fusion.14
  26.8 0.5 convolution_add_fusion.4
  27.2 0.5 convolution_add_fusion.3
  27.7 0.5 convolution_add_fusion.2
  28.2 0.5 convolution_add_fusion.1
  28.6 0.4 copy-done.3
  29.1 0.6 fusion.2
  30.1 0.4 copy-done.2
  30.8 0.8 collective-permute-start.5
  31.6 1.8 %collective-permute-start.6 = (f32[4,4,3,128]{3,0,2,1:T(4,128)S(1)}, f32[4,4,3,128]{3,0,2,1:T(4,128)S(1)}, u32[]{:S(2)}, u32[]{:S(2)}) collective-permute-start(f32[4,4,3,128]{3,0,2,1:T(4,128)S(1)} %fusion.38), channel_id=1, source_target_pairs={{0,4},{4,0},{1,5},{5,1},{2,6},{6,2},{3,7},{7,3},{8,12},{12,8},{9,1... | collective-permute-start | bytes 73736 | tf_op jit(solution)/shard_map/ppermute | solution.py:133
  33.4 2.9 %collective-permute-start.7 = (f32[4,4,3,3]{3,0,2,1:T(4,128)S(1)}, f32[4,4,3,3]{3,0,2,1:T(4,128)S(1)}, u32[]{:S(2)}, u32[]{:S(2)}) collective-permute-start(f32[4,4,3,3]{3,0,2,1:T(4,128)S(1)} %get-tuple-element.35), channel_id=1, source_target_pairs={{0,28},{8,4},{16,12},{24,20},{4,24},{12,0},{20,8},{28,16},{1,29},{... | collective-permute-start | bytes 1736 | tf_op jit(solution)/shard_map/ppermute | solution.py:133
  36.3 3.8 %collective-permute-start.9 = (f32[4,4,16,3]{3,0,2,1:T(4,128)S(1)}, f32[4,4,16,3]{3,0,2,1:T(4,128)S(1)}, u32[]{:S(2)}, u32[]{:S(2)}) collective-permute-start(f32[4,4,16,3]{3,0,2,1:T(4,128)S(1)} %get-tuple-element.33), channel_id=1, source_target_pairs={{0,24},{8,0},{16,8},{24,16},{1,25},{9,1},{17,9},{25,17},{2,26},{10... | collective-permute-start | bytes 9224 | tf_op jit(solution)/shard_map/ppermute | solution.py:120
  40.2 4.0 %collective-permute-done.8 = f32[4,4,16,3]{3,0,2,1:T(4,128)S(1)} collective-permute-done((f32[4,4,16,3]{3,0,2,1:T(4,128)S(1)}, f32[4,4,16,3]{3,0,2,1:T(4,128)S(1)}, u32[]{:S(2)}, u32[]{:S(2)}) %collective-permute-start.8) | collective-permute-done | bytes 3104 | tf_op jit(solution)/shard_map/ppermute | solution.py:120
  44.2 0.5 maximum_maximum_fusion
  44.7 1.3 %collective-permute-start.10 = (f32[4,3,22,134]{3,0,2,1:T(4,128)S(1)}, f32[4,3,22,134]{3,0,2,1:T(4,128)S(1)}, u32[]{:S(2)}, u32[]{:S(2)}) collective-permute-start(f32[4,3,22,134]{3,0,2,1:T(4,128)S(1)} %get-tuple-element.22), channel_id=1, source_target_pairs={{0,1},{1,2},{2,3},{4,5},{5,6},{6,7},{8,9},{9,10},{10,11},{12,13},{... | collective-permute-start | bytes 424520 | tf_op jit(solution)/shard_map/ppermute | solution.py:120
  46.1 1.5 %collective-permute-start.11 = (f32[4,3,22,134]{3,0,2,1:T(4,128)S(1)}, f32[4,3,22,134]{3,0,2,1:T(4,128)S(1)}, u32[]{:S(2)}, u32[]{:S(2)}) collective-permute-start(f32[4,3,22,134]{3,0,2,1:T(4,128)S(1)} %get-tuple-element.23), channel_id=1, source_target_pairs={{1,0},{2,1},{3,2},{5,4},{6,5},{7,6},{9,8},{10,9},{11,10},{13,12},{... | collective-permute-start | bytes 424520 | tf_op jit(solution)/shard_map/ppermute | solution.py:120
  47.6 3.4 %collective-permute-done.11 = f32[4,3,22,134]{3,0,2,1:T(4,128)S(1)} collective-permute-done((f32[4,3,22,134]{3,0,2,1:T(4,128)S(1)}, f32[4,3,22,134]{3,0,2,1:T(4,128)S(1)}, u32[]{:S(2)}, u32[]{:S(2)}) %collective-permute-start.11) | collective-permute-done | bytes 141536 | tf_op jit(solution)/shard_map/ppermute | solution.py:120
  51.0 0.5 pad_maximum_fusion
  52.3 0.5 broadcast_multiply_fusion
  52.8 2.4 %broadcast_multiply_fusion.1 = (f32[3,8,20,132]{3,0,2,1:T(4,128)S(1)}, f32[3,8,20,132]{3,0,2,1:T(4,128)S(1)}) fusion(f32[8,20,132]{2,1,0:T(8,128)S(1)} %get-tuple-element.31, f32[3,10,22,134]{3,0,2,1:T(4,128)S(1)} %get-tuple-element.12, f32[8,20,132]{2,1,0:T(8,128)S(1)} %get-tuple-element.30, f32[4,10,22,134]{3,0,2,1:T(4,128)S(1)} %pad_maximum_fusion, ...), kind=kLoop, calls=%fused_computation.42 | loop fusion | flops 760320 | bytes 2703360 | tf_op jit(solution)/shard_map/mul | solution.py:60
  55.3 1.7 %broadcast_multiply_fusion.2 = (f32[3,6,18,130]{3,0,2,1:T(4,128)S(1)}, f32[3,6,18,130]{3,0,2,1:T(4,128)S(1)}) fusion(f32[6,18,130]{2,1,0:T(8,128)S(1)} %get-tuple-element.29, f32[3,8,20,132]{3,0,2,1:T(4,128)S(1)} %get-tuple-element.10, f32[6,18,130]{2,1,0:T(8,128)S(1)} %get-tuple-element.28, f32[4,10,22,134]{3,0,2,1:T(4,128)S(1)} %pad_maximum_fusion, ...), kind=kLoop, calls=%fused_computation.53 | loop fusion | flops 505440 | bytes 1797120 | tf_op jit(solution)/shard_map/mul | solution.py:60
  56.9 0.5 multiply_reduce_fusion
  57.4 0.4 convolution_bitcast_fusion.1
  57.9 1.6 %collective-permute-start.14 = (f32[3,128]{1,0:T(4,128)S(1)}, f32[3,128]{1,0:T(4,128)S(1)}, u32[]{:S(2)}, u32[]{:S(2)}) collective-permute-start(f32[3,128]{1,0:T(4,128)S(1)} %get-tuple-element.53), channel_id=1, source_target_pairs={{0,4},{4,0},{1,5},{5,1},{2,6},{6,2},{3,7},{7,3},{8,12},{12,8},{9,1... | collective-permute-start | bytes 4616 | tf_op jit(solution)/shard_map/ppermute | solution.py:183
  59.4 1.3 %collective-permute-start.16 = (f32[3,128]{1,0:T(4,128)S(1)}, f32[3,128]{1,0:T(4,128)S(1)}, u32[]{:S(2)}, u32[]{:S(2)}) collective-permute-start(f32[3,128]{1,0:T(4,128)S(1)} %get-tuple-element.54), channel_id=1, source_target_pairs={{1,4},{2,5},{3,6},{5,0},{6,1},{7,2},{9,12},{10,13},{11,14},{13,8},... | collective-permute-start | bytes 4616 | tf_op jit(solution)/shard_map/ppermute | solution.py:183
  60.7 1.3 %collective-permute-start.13 = (f32[3,128]{1,0:T(4,128)S(1)}, f32[3,128]{1,0:T(4,128)S(1)}, u32[]{:S(2)}, u32[]{:S(2)}) collective-permute-start(f32[3,128]{1,0:T(4,128)S(1)} %get-tuple-element.54), channel_id=1, source_target_pairs={{1,0},{2,1},{3,2},{5,4},{6,5},{7,6},{9,8},{10,9},{11,10},{13,12},{... | collective-permute-start | bytes 4616 | tf_op jit(solution)/shard_map/ppermute | solution.py:183
  62.0 7.8 %collective-permute-start.15 = (f32[3,128]{1,0:T(4,128)S(1)}, f32[3,128]{1,0:T(4,128)S(1)}, u32[]{:S(2)}, u32[]{:S(2)}) collective-permute-start(f32[3,128]{1,0:T(4,128)S(1)} %get-tuple-element.55), channel_id=1, source_target_pairs={{0,5},{1,6},{2,7},{4,1},{5,2},{6,3},{8,13},{9,14},{10,15},{12,9},{... | collective-permute-start | bytes 4616 | tf_op jit(solution)/shard_map/ppermute | solution.py:183
  69.9 4.4 %collective-permute-start.12 = (f32[3,128]{1,0:T(4,128)S(1)}, f32[3,128]{1,0:T(4,128)S(1)}, u32[]{:S(2)}, u32[]{:S(2)}) collective-permute-start(f32[3,128]{1,0:T(4,128)S(1)} %get-tuple-element.55), channel_id=1, source_target_pairs={{0,1},{1,2},{2,3},{4,5},{5,6},{6,7},{8,9},{9,10},{10,11},{12,13},{... | collective-permute-start | bytes 4616 | tf_op jit(solution)/shard_map/ppermute | solution.py:183
  74.3 0.8 collective-permute-done.12
  75.1 3.4 %collective-permute-start.19 = (f32[3,128]{1,0:T(4,128)S(1)}, f32[3,128]{1,0:T(4,128)S(1)}, u32[]{:S(2)}, u32[]{:S(2)}) collective-permute-start(f32[3,128]{1,0:T(4,128)S(1)} %add_add_fusion.1), channel_id=1, source_target_pairs={{0,24},{8,0},{16,8},{24,16},{1,25},{9,1},{17,9},{25,17},{2,26},{10... | collective-permute-start | bytes 4616 | tf_op jit(solution)/shard_map/ppermute | solution.py:183
  78.5 0.6 collective-permute-start.17
  79.2 0.7 copy.32
  79.9 0.6 copy.33
  80.5 2.5 %collective-permute-done.18 = f32[3,128]{1,0:T(4,128)S(1)} collective-permute-done((f32[3,128]{1,0:T(4,128)S(1)}, f32[3,128]{1,0:T(4,128)S(1)}, u32[]{:S(2)}, u32[]{:S(2)}) %collective-permute-start.18) | collective-permute-done | bytes 1568 | tf_op jit(solution)/shard_map/ppermute | solution.py:183
  83.0 0.9 %collective-permute-done.17 = f32[3,128]{1,0:T(4,128)S(1)} collective-permute-done((f32[3,128]{1,0:T(4,128)S(1)}, f32[3,128]{1,0:T(4,128)S(1)}, u32[]{:S(2)}, u32[]{:S(2)}) %collective-permute-start.17) | collective-permute-done | bytes 1568 | tf_op jit(solution)/shard_map/ppermute | solution.py:183
  83.9 0.6 add_add_fusion
  (63 shorter events, 2.1 us)
Async XLA Ops:
  0.6 29.1 %copy-start = (f32[3,5]{1,0:T(4,128)S(1)}, f32[3,5]{1,0:T(4,128)}, u32[]{:S(2)}) copy-start(f32[3,5]{1,0:T(4,128)} %param.14) | copy-start | bytes 184
  0.7 1.0 %copy-start.4 = (f32[3,4,16,128]{3,2,1,0:T(8,128)S(1)}, f32[3,4,16,128]{3,2,1,0:T(8,128)}, u32[]{:S(2)}) copy-start(f32[3,4,16,128]{3,2,1,0:T(8,128)} %param.11) | copy-start | bytes 294916
  1.7 22.8 %collective-permute-start.2 = (f32[8,4,1,128]{3,2,1,0:T(1,128)S(1)}, f32[8,4,1,128]{3,2,1,0:T(1,128)S(1)}, u32[]{:S(2)}, u32[]{:S(2)}) collective-permute-start(f32[8,4,1,128]{3,2,1,0:T(1,128)S(1)} %broadcast_select_fusion.2), channel_id=1, source_target_pairs={{0,4},{4,0},{1,5},{5,1},{2,6},{6,2},{3,7},{7,3},{8,12},{12,8},{9,1... | collective-permute-start | bytes 49160 | tf_op jit(solution)/shard_map/ppermute | solution.py:133
  4.7 20.4 %collective-permute-start.1 = (f32[8,1,16,128]{3,2,1,0:T(8,128)S(1)}, f32[8,1,16,128]{3,2,1,0:T(8,128)S(1)}, u32[]{:S(2)}, u32[]{:S(2)}) collective-permute-start(f32[8,1,16,128]{3,2,1,0:T(8,128)S(1)} %get-tuple-element.26), channel_id=1, source_target_pairs={{0,1},{1,2},{2,3},{4,5},{5,6},{6,7},{8,9},{9,10},{10,11},{12,13},{... | collective-permute-start | bytes 196616 | tf_op jit(solution)/shard_map/ppermute | solution.py:120
  6.2 19.0 %collective-permute-start = (f32[8,1,16,128]{3,2,1,0:T(8,128)S(1)}, f32[8,1,16,128]{3,2,1,0:T(8,128)S(1)}, u32[]{:S(2)}, u32[]{:S(2)}) collective-permute-start(f32[8,1,16,128]{3,2,1,0:T(8,128)S(1)} %get-tuple-element.27), channel_id=1, source_target_pairs={{1,0},{2,1},{3,2},{5,4},{6,5},{7,6},{9,8},{10,9},{11,10},{13,12},{... | collective-permute-start | bytes 196616 | tf_op jit(solution)/shard_map/ppermute | solution.py:120
  7.6 9.3 %collective-permute-start.4 = (f32[8,4,16,1]{3,2,1,0:T(8,128)S(1)}, f32[8,4,16,1]{3,2,1,0:T(8,128)S(1)}, u32[]{:S(2)}, u32[]{:S(2)}) collective-permute-start(f32[8,4,16,1]{3,2,1,0:T(8,128)S(1)} %get-tuple-element.24), channel_id=1, source_target_pairs={{0,8},{8,16},{16,24},{24,0},{1,9},{9,17},{17,25},{25,1},{2,10},{10... | collective-permute-start | bytes 6152 | tf_op jit(solution)/shard_map/ppermute | solution.py:120
  9.3 2.3 %copy-start.8 = (f32[3,5,5]{2,0,1:T(4,128)S(1)}, f32[3,5,5]{2,0,1:T(4,128)}, u32[]{:S(2)}) copy-start(f32[3,5,5]{2,0,1:T(4,128)} %param.12) | copy-start | bytes 904
  9.3 14.5 %collective-permute-start.3 = (f32[8,4,16,1]{3,2,1,0:T(8,128)S(1)}, f32[8,4,16,1]{3,2,1,0:T(8,128)S(1)}, u32[]{:S(2)}, u32[]{:S(2)}) collective-permute-start(f32[8,4,16,1]{3,2,1,0:T(8,128)S(1)} %get-tuple-element.25), channel_id=1, source_target_pairs={{0,24},{8,0},{16,8},{24,16},{1,25},{9,1},{17,9},{25,17},{2,26},{10... | collective-permute-start | bytes 6152 | tf_op jit(solution)/shard_map/ppermute | solution.py:120
  11.5 0.7 copy-start.9
  23.8 0.6 copy-start.5
  24.5 0.6 copy-start.6
  25.2 0.9 %copy-start.1 = (f32[5,4,16,128]{3,2,1,0:T(8,128)S(1)}, f32[5,4,16,128]{3,2,1,0:T(8,128)}, u32[]{:S(2)}) copy-start(f32[5,4,16,128]{3,2,1,0:T(8,128)} %param.9) | copy-start | bytes 491524
  25.2 0.9 %slice-start = ((f32[4,16,130]{2,1,0:T(8,128)}), f32[4,16,128]{2,1,0:T(8,128)S(1)}, s32[]{:S(2)}) async-start(f32[4,16,130]{2,1,0:T(8,128)} %copy-done.5), calls=%async_computation | async-start | bytes 65536 | tf_op jit(solution)/shard_map/slice | solution.py:169
  25.2 0.9 %slice-start.1 = ((f32[4,18,128]{2,1,0:T(8,128)}), f32[4,16,128]{2,1,0:T(8,128)S(1)}, s32[]{:S(2)}) async-start(f32[4,18,128]{2,1,0:T(8,128)} %copy-done.6), calls=%async_computation.1 | async-start | bytes 65536 | tf_op jit(solution)/shard_map/slice | solution.py:169
  28.2 0.9 %copy-start.3 = (f32[5,4,16,128]{3,2,1,0:T(8,128)S(1)}, f32[5,4,16,128]{3,2,1,0:T(8,128)}, u32[]{:S(2)}) copy-start(f32[5,4,16,128]{3,2,1,0:T(8,128)} %param.10) | copy-start | bytes 491524
  29.7 0.8 copy-start.2
  30.8 9.3 %collective-permute-start.5 = (f32[4,4,3,3]{3,0,2,1:T(4,128)S(1)}, f32[4,4,3,3]{3,0,2,1:T(4,128)S(1)}, u32[]{:S(2)}, u32[]{:S(2)}) collective-permute-start(f32[4,4,3,3]{3,0,2,1:T(4,128)S(1)} %get-tuple-element.34), channel_id=1, source_target_pairs={{0,12},{8,20},{16,28},{24,4},{4,8},{12,16},{20,24},{28,0},{1,13},{... | collective-permute-start | bytes 1736 | tf_op jit(solution)/shard_map/ppermute | solution.py:133
  31.6 8.5 %collective-permute-start.6 = (f32[4,4,3,128]{3,0,2,1:T(4,128)S(1)}, f32[4,4,3,128]{3,0,2,1:T(4,128)S(1)}, u32[]{:S(2)}, u32[]{:S(2)}) collective-permute-start(f32[4,4,3,128]{3,0,2,1:T(4,128)S(1)} %fusion.38), channel_id=1, source_target_pairs={{0,4},{4,0},{1,5},{5,1},{2,6},{6,2},{3,7},{7,3},{8,12},{12,8},{9,1... | collective-permute-start | bytes 73736 | tf_op jit(solution)/shard_map/ppermute | solution.py:133
  33.4 6.7 %collective-permute-start.7 = (f32[4,4,3,3]{3,0,2,1:T(4,128)S(1)}, f32[4,4,3,3]{3,0,2,1:T(4,128)S(1)}, u32[]{:S(2)}, u32[]{:S(2)}) collective-permute-start(f32[4,4,3,3]{3,0,2,1:T(4,128)S(1)} %get-tuple-element.35), channel_id=1, source_target_pairs={{0,28},{8,4},{16,12},{24,20},{4,24},{12,0},{20,8},{28,16},{1,29},{... | collective-permute-start | bytes 1736 | tf_op jit(solution)/shard_map/ppermute | solution.py:133
  36.3 7.9 %collective-permute-start.8 = (f32[4,4,16,3]{3,0,2,1:T(4,128)S(1)}, f32[4,4,16,3]{3,0,2,1:T(4,128)S(1)}, u32[]{:S(2)}, u32[]{:S(2)}) collective-permute-start(f32[4,4,16,3]{3,0,2,1:T(4,128)S(1)} %get-tuple-element.32), channel_id=1, source_target_pairs={{0,8},{8,16},{16,24},{24,0},{1,9},{9,17},{17,25},{25,1},{2,10},{10... | collective-permute-start | bytes 9224 | tf_op jit(solution)/shard_map/ppermute | solution.py:120
  36.3 7.9 %collective-permute-start.9 = (f32[4,4,16,3]{3,0,2,1:T(4,128)S(1)}, f32[4,4,16,3]{3,0,2,1:T(4,128)S(1)}, u32[]{:S(2)}, u32[]{:S(2)}) collective-permute-start(f32[4,4,16,3]{3,0,2,1:T(4,128)S(1)} %get-tuple-element.33), channel_id=1, source_target_pairs={{0,24},{8,0},{16,8},{24,16},{1,25},{9,1},{17,9},{25,17},{2,26},{10... | collective-permute-start | bytes 9224 | tf_op jit(solution)/shard_map/ppermute | solution.py:120
  44.7 2.8 %copy-start.10 = (s32[4,128]{1,0:T(4,128)S(1)}, s32[4,128]{1,0:T(4,128)}, u32[]{:S(2)}) copy-start(s32[4,128]{1,0:T(4,128)} %param.17) | copy-start | bytes 6148
  44.7 2.8 %collective-permute-start.10 = (f32[4,3,22,134]{3,0,2,1:T(4,128)S(1)}, f32[4,3,22,134]{3,0,2,1:T(4,128)S(1)}, u32[]{:S(2)}, u32[]{:S(2)}) collective-permute-start(f32[4,3,22,134]{3,0,2,1:T(4,128)S(1)} %get-tuple-element.22), channel_id=1, source_target_pairs={{0,1},{1,2},{2,3},{4,5},{5,6},{6,7},{8,9},{9,10},{10,11},{12,13},{... | collective-permute-start | bytes 424520 | tf_op jit(solution)/shard_map/ppermute | solution.py:120
  46.1 5.0 %collective-permute-start.11 = (f32[4,3,22,134]{3,0,2,1:T(4,128)S(1)}, f32[4,3,22,134]{3,0,2,1:T(4,128)S(1)}, u32[]{:S(2)}, u32[]{:S(2)}) collective-permute-start(f32[4,3,22,134]{3,0,2,1:T(4,128)S(1)} %get-tuple-element.23), channel_id=1, source_target_pairs={{1,0},{2,1},{3,2},{5,4},{6,5},{7,6},{9,8},{10,9},{11,10},{13,12},{... | collective-permute-start | bytes 424520 | tf_op jit(solution)/shard_map/ppermute | solution.py:120
  55.3 1.7 %copy-start.7 = (f32[4,16,128]{2,1,0:T(8,128)S(1)}, f32[4,16,128]{2,1,0:T(8,128)}, u32[]{:S(2)}) copy-start(f32[4,16,128]{2,1,0:T(8,128)} %param.16) | copy-start | bytes 98308
  57.9 16.4 %collective-permute-start.14 = (f32[3,128]{1,0:T(4,128)S(1)}, f32[3,128]{1,0:T(4,128)S(1)}, u32[]{:S(2)}, u32[]{:S(2)}) collective-permute-start(f32[3,128]{1,0:T(4,128)S(1)} %get-tuple-element.53), channel_id=1, source_target_pairs={{0,4},{4,0},{1,5},{5,1},{2,6},{6,2},{3,7},{7,3},{8,12},{12,8},{9,1... | collective-permute-start | bytes 4616 | tf_op jit(solution)/shard_map/ppermute | solution.py:183
  59.4 14.9 %collective-permute-start.16 = (f32[3,128]{1,0:T(4,128)S(1)}, f32[3,128]{1,0:T(4,128)S(1)}, u32[]{:S(2)}, u32[]{:S(2)}) collective-permute-start(f32[3,128]{1,0:T(4,128)S(1)} %get-tuple-element.54), channel_id=1, source_target_pairs={{1,4},{2,5},{3,6},{5,0},{6,1},{7,2},{9,12},{10,13},{11,14},{13,8},... | collective-permute-start | bytes 4616 | tf_op jit(solution)/shard_map/ppermute | solution.py:183
  60.7 13.6 %collective-permute-start.13 = (f32[3,128]{1,0:T(4,128)S(1)}, f32[3,128]{1,0:T(4,128)S(1)}, u32[]{:S(2)}, u32[]{:S(2)}) collective-permute-start(f32[3,128]{1,0:T(4,128)S(1)} %get-tuple-element.54), channel_id=1, source_target_pairs={{1,0},{2,1},{3,2},{5,4},{6,5},{7,6},{9,8},{10,9},{11,10},{13,12},{... | collective-permute-start | bytes 4616 | tf_op jit(solution)/shard_map/ppermute | solution.py:183
  62.0 12.3 %collective-permute-start.15 = (f32[3,128]{1,0:T(4,128)S(1)}, f32[3,128]{1,0:T(4,128)S(1)}, u32[]{:S(2)}, u32[]{:S(2)}) collective-permute-start(f32[3,128]{1,0:T(4,128)S(1)} %get-tuple-element.55), channel_id=1, source_target_pairs={{0,5},{1,6},{2,7},{4,1},{5,2},{6,3},{8,13},{9,14},{10,15},{12,9},{... | collective-permute-start | bytes 4616 | tf_op jit(solution)/shard_map/ppermute | solution.py:183
  69.9 5.2 %collective-permute-start.12 = (f32[3,128]{1,0:T(4,128)S(1)}, f32[3,128]{1,0:T(4,128)S(1)}, u32[]{:S(2)}, u32[]{:S(2)}) collective-permute-start(f32[3,128]{1,0:T(4,128)S(1)} %get-tuple-element.55), channel_id=1, source_target_pairs={{0,1},{1,2},{2,3},{4,5},{5,6},{6,7},{8,9},{9,10},{10,11},{12,13},{... | collective-permute-start | bytes 4616 | tf_op jit(solution)/shard_map/ppermute | solution.py:183
  75.1 5.4 %collective-permute-start.19 = (f32[3,128]{1,0:T(4,128)S(1)}, f32[3,128]{1,0:T(4,128)S(1)}, u32[]{:S(2)}, u32[]{:S(2)}) collective-permute-start(f32[3,128]{1,0:T(4,128)S(1)} %add_add_fusion.1), channel_id=1, source_target_pairs={{0,24},{8,0},{16,8},{24,16},{1,25},{9,1},{17,9},{25,17},{2,26},{10... | collective-permute-start | bytes 4616 | tf_op jit(solution)/shard_map/ppermute | solution.py:183
  78.5 4.5 %collective-permute-start.18 = (f32[3,128]{1,0:T(4,128)S(1)}, f32[3,128]{1,0:T(4,128)S(1)}, u32[]{:S(2)}, u32[]{:S(2)}) collective-permute-start(f32[3,128]{1,0:T(4,128)S(1)} %add_add_fusion.1), channel_id=1, source_target_pairs={{0,16},{8,24},{16,0},{24,8},{1,17},{9,25},{17,1},{25,9},{2,18},{10... | collective-permute-start | bytes 4616 | tf_op jit(solution)/shard_map/ppermute | solution.py:183
  78.5 5.4 %collective-permute-start.17 = (f32[3,128]{1,0:T(4,128)S(1)}, f32[3,128]{1,0:T(4,128)S(1)}, u32[]{:S(2)}, u32[]{:S(2)}) collective-permute-start(f32[3,128]{1,0:T(4,128)S(1)} %add_add_fusion.1), channel_id=1, source_target_pairs={{0,8},{8,16},{16,24},{24,0},{1,9},{9,17},{17,25},{25,1},{2,10},{10... | collective-permute-start | bytes 4616 | tf_op jit(solution)/shard_map/ppermute | solution.py:183

commit v4 on v3

--- a/solution.py
+++ b/solution.py
@@ -155,26 +155,37 @@
     return jnp.concatenate([before_s, plane, after_s], axis=1)
 
 
+def jac_apply(jac, term):
+    return jnp.einsum("uv,ukji->vkji", jac, term, precision=lax.Precision.HIGHEST)
+
+
 def flux_faces(stacked, halos, owner_jac, neighbor_jac):
-    center = stacked[:5]
-    total = jnp.zeros_like(center)
+    psi = stacked[:5]
+    inner_terms = []
     for direction in range(3):
         dim = direction + 1
+        length = stacked.shape[dim]
+        low = lax.slice_in_dim(psi, 0, length - 1, axis=dim)
+        high = lax.slice_in_dim(psi, 1, length, axis=dim)
+        w_low = lax.slice_in_dim(stacked[5 + direction], 0, length - 1, axis=direction)
+        between = w_low[None] * (low - high)
+        inner_terms.append((jac_apply(owner_jac[direction], between), jac_apply(neighbor_jac[direction], between)))
+    inner_terms = lax.optimization_barrier(inner_terms)
+    total = jnp.zeros_like(psi)
+    for direction in range(3):
+        dim = direction + 1
+        length = stacked.shape[dim]
         before, after = halos[direction]
-        line = jnp.concatenate([before, stacked, after], axis=dim)
-        length = line.shape[dim]
-        upper = lax.slice_in_dim(line[:5], 2, length, axis=dim)
-        lower = lax.slice_in_dim(line[:5], 0, length - 2, axis=dim)
-        w_here = stacked[5 + direction]
-        w_lower = lax.slice_in_dim(line[5 + direction], 0, length - 2, axis=direction)
-        up_term = w_here[None] * (center - upper)
-        down_term = w_lower[None] * (lower - center)
-        total = total + jnp.einsum(
-            "uv,ukji->vkji", owner_jac[direction], up_term, precision=lax.Precision.HIGHEST
-        )
-        total = total + jnp.einsum(
-            "uv,ukji->vkji", neighbor_jac[direction], down_term, precision=lax.Precision.HIGHEST
-        )
+        last = lax.slice_in_dim(psi, length - 1, length, axis=dim)
+        first = lax.slice_in_dim(psi, 0, 1, axis=dim)
+        w_last = lax.slice_in_dim(stacked[5 + direction], length - 1, length, axis=direction)
+        up_edge = w_last[None] * (last - after[:5])
+        down_edge = before[5 + direction][None] * (before[:5] - first)
+        up_inner, down_inner = inner_terms[direction]
+        up = jnp.concatenate([up_inner, jac_apply(owner_jac[direction], up_edge)], axis=dim)
+        down = jnp.concatenate([jac_apply(neighbor_jac[direction], down_edge), down_inner], axis=dim)
+        total = total + up
+        total = total + down
     return total
 
 

time: 85 us -> 82.6 us (0.972)
  waiting for transfers between devices: 23.1 us -> 19.4 us
  matrix products: 3.64 us -> 4.57 us
    ppermute x8, waiting for transfers between devices: 18.9 us -> 15.2 us  [receive(): return lax.ppermute(take(array, rel, dims, width), axes, pairs)]
    unnamed x26 -> x22, local copies, waits for them, and re-layouts: 6.03 us -> 4.56 us
    dot_general x6 -> x12, matrix products: 2.88 us -> 3.82 us  [jac_apply(): jnp.einsum('uv,ukji->vkji', jac, term, precision=lax.Precision.HIGHEST)]
  transfers between devices with their start and end apart: 20 -> 20, of which waited for: 7 -> 7; matrix products, arithmetic and copies ran while one was open for 2% -> 8% of each run, Pallas kernels for 0% -> 0%
where the time goes in v4:
time: 82.6 us; the launch traced here: 82.1 us
  starting transfers between devices  42.2 us (51%)
  waiting for transfers between devices  19.4 us (23%)
  other arithmetic  8.51 us (10%)
  local copies, waits for them, and re-layouts  6.12 us (7%)
  matrix products  4.57 us (6%)
  between operations  1.2 us (1%)
    ppermute x8, starting transfers between devices, shifted(): return lax.ppermute(array, axes, pairs)  20.5 us
    ppermute x8, waiting for transfers between devices, receive(): return lax.ppermute(take(array, rel, dims, width), axes, pairs)  15.2 us
    ppermute x8, starting transfers between devices, receive(): return lax.ppermute(take(array, rel, dims, width), axes, pairs)  13.2 us
    ppermute x4, starting transfers between devices, receive_pair(): got = lax.ppermute(sent, axes, pairs + back)  8.52 us
    mul x3, other arithmetic, relax(): weighted = stiff_pad[None] * mesh_pad  4.64 us
    unnamed x22, local copies, waits for them, and re-layouts  4.56 us
    ppermute x8, waiting for transfers between devices, shifted(): return lax.ppermute(array, axes, pairs)  4.18 us
    dot_general x12, matrix products, jac_apply(): jnp.einsum('uv,ukji->vkji', jac, term, precision=lax.Precision.HIGHEST)  3.82 us
  transfers between devices with their start and end apart: 20, of which 7 were waited for; matrix products, arithmetic and copies ran while one was open for 8% of the time, Pallas kernels for 0%

profile of v4, /device:TPU:0, one launch (start us, length us, event | category | flops | bytes accessed | tf_op | source)
XLA Modules:
  0.0 82.1 jit_solution(1433582908059021176)
XLA Ops:
  0.7 1.0 %constant_dynamic-update-slice_fusion.1 = f32[8,4,16,128]{3,2,1,0:T(8,128)S(1)} fusion(f32[5,4,16,128]{3,2,1,0:T(8,128)} %param.9), kind=kLoop, calls=%fused_computation.134 | loop fusion | bytes 327680
  1.7 3.0 %collective-permute-start.2 = (f32[8,4,1,128]{3,2,1,0:T(1,128)S(1)}, f32[8,4,1,128]{3,2,1,0:T(1,128)S(1)}, u32[]{:S(2)}, u32[]{:S(2)}) collective-permute-start(f32[8,4,1,128]{3,2,1,0:T(1,128)S(1)} %broadcast_select_fusion.1), channel_id=1, source_target_pairs={{0,4},{4,0},{1,5},{5,1},{2,6},{6,2},{3,7},{7,3},{8,12},{12,8},{9,1... | collective-permute-start | bytes 49160 | tf_op jit(solution)/shard_map/ppermute | solution.py:133
  4.7 1.5 %collective-permute-start.1 = (f32[8,1,16,128]{3,2,1,0:T(8,128)S(1)}, f32[8,1,16,128]{3,2,1,0:T(8,128)S(1)}, u32[]{:S(2)}, u32[]{:S(2)}) collective-permute-start(f32[8,1,16,128]{3,2,1,0:T(8,128)S(1)} %get-tuple-element.35), channel_id=1, source_target_pairs={{0,1},{1,2},{2,3},{4,5},{5,6},{6,7},{8,9},{9,10},{10,11},{12,13},{... | collective-permute-start | bytes 196616 | tf_op jit(solution)/shard_map/ppermute | solution.py:120
  6.2 1.3 %collective-permute-start = (f32[8,1,16,128]{3,2,1,0:T(8,128)S(1)}, f32[8,1,16,128]{3,2,1,0:T(8,128)S(1)}, u32[]{:S(2)}, u32[]{:S(2)}) collective-permute-start(f32[8,1,16,128]{3,2,1,0:T(8,128)S(1)} %get-tuple-element.36), channel_id=1, source_target_pairs={{1,0},{2,1},{3,2},{5,4},{6,5},{7,6},{9,8},{10,9},{11,10},{13,12},{... | collective-permute-start | bytes 196616 | tf_op jit(solution)/shard_map/ppermute | solution.py:120
  7.7 1.6 %collective-permute-start.4 = (f32[8,4,16,1]{3,2,1,0:T(8,128)S(1)}, f32[8,4,16,1]{3,2,1,0:T(8,128)S(1)}, u32[]{:S(2)}, u32[]{:S(2)}) collective-permute-start(f32[8,4,16,1]{3,2,1,0:T(8,128)S(1)} %get-tuple-element.33), channel_id=1, source_target_pairs={{0,8},{8,16},{16,24},{24,0},{1,9},{9,17},{17,25},{25,1},{2,10},{10... | collective-permute-start | bytes 6152 | tf_op jit(solution)/shard_map/ppermute | solution.py:120
  9.3 2.2 %collective-permute-start.3 = (f32[8,4,16,1]{3,2,1,0:T(8,128)S(1)}, f32[8,4,16,1]{3,2,1,0:T(8,128)S(1)}, u32[]{:S(2)}, u32[]{:S(2)}) collective-permute-start(f32[8,4,16,1]{3,2,1,0:T(8,128)S(1)} %get-tuple-element.34), channel_id=1, source_target_pairs={{0,24},{8,0},{16,8},{24,16},{1,25},{9,1},{17,9},{25,17},{2,26},{10... | collective-permute-start | bytes 6152 | tf_op jit(solution)/shard_map/ppermute | solution.py:120
  11.5 0.7 copy-done.6
  12.3 0.7 copy-done.7
  13.1 0.4 convolution_bitcast_fusion.4
  13.5 0.4 convolution_bitcast_fusion.5
  13.9 0.4 convolution_bitcast_fusion.2
  14.3 0.4 convolution_bitcast_fusion.3
  14.8 0.4 convolution_bitcast_fusion
  15.2 0.4 convolution_bitcast_fusion.1
  15.8 1.1 %collective-permute-done.4 = f32[8,4,16,1]{3,2,1,0:T(8,128)S(1)} collective-permute-done((f32[8,4,16,1]{3,2,1,0:T(8,128)S(1)}, f32[8,4,16,1]{3,2,1,0:T(8,128)S(1)}, u32[]{:S(2)}, u32[]{:S(2)}) %collective-permute-start.4) | collective-permute-done | bytes 2080 | tf_op jit(solution)/shard_map/ppermute | solution.py:120
  17.1 6.7 %collective-permute-done.3 = f32[8,4,16,1]{3,2,1,0:T(8,128)S(1)} collective-permute-done((f32[8,4,16,1]{3,2,1,0:T(8,128)S(1)}, f32[8,4,16,1]{3,2,1,0:T(8,128)S(1)}, u32[]{:S(2)}, u32[]{:S(2)}) %collective-permute-start.3) | collective-permute-done | bytes 2080 | tf_op jit(solution)/shard_map/ppermute | solution.py:120
  26.4 0.4 copy-done.4
  26.8 0.4 fusion.15
  27.2 0.3 convolution_bitcast_fusion.6
  27.6 0.4 copy-done.2
  28.3 0.8 %collective-permute-start.5 = (f32[4,4,3,3]{3,0,2,1:T(4,128)S(1)}, f32[4,4,3,3]{3,0,2,1:T(4,128)S(1)}, u32[]{:S(2)}, u32[]{:S(2)}) collective-permute-start(f32[4,4,3,3]{3,0,2,1:T(4,128)S(1)} %get-tuple-element.43), channel_id=1, source_target_pairs={{0,12},{8,20},{16,28},{24,4},{4,8},{12,16},{20,24},{28,0},{1,13},{... | collective-permute-start | bytes 1736 | tf_op jit(solution)/shard_map/ppermute | solution.py:133
  29.2 1.8 %collective-permute-start.6 = (f32[4,4,3,128]{3,0,2,1:T(4,128)S(1)}, f32[4,4,3,128]{3,0,2,1:T(4,128)S(1)}, u32[]{:S(2)}, u32[]{:S(2)}) collective-permute-start(f32[4,4,3,128]{3,0,2,1:T(4,128)S(1)} %fusion.34), channel_id=1, source_target_pairs={{0,4},{4,0},{1,5},{5,1},{2,6},{6,2},{3,7},{7,3},{8,12},{12,8},{9,1... | collective-permute-start | bytes 73736 | tf_op jit(solution)/shard_map/ppermute | solution.py:133
  31.0 2.9 %collective-permute-start.7 = (f32[4,4,3,3]{3,0,2,1:T(4,128)S(1)}, f32[4,4,3,3]{3,0,2,1:T(4,128)S(1)}, u32[]{:S(2)}, u32[]{:S(2)}) collective-permute-start(f32[4,4,3,3]{3,0,2,1:T(4,128)S(1)} %get-tuple-element.44), channel_id=1, source_target_pairs={{0,28},{8,4},{16,12},{24,20},{4,24},{12,0},{20,8},{28,16},{1,29},{... | collective-permute-start | bytes 1736 | tf_op jit(solution)/shard_map/ppermute | solution.py:133
  33.8 3.8 %collective-permute-start.9 = (f32[4,4,16,3]{3,0,2,1:T(4,128)S(1)}, f32[4,4,16,3]{3,0,2,1:T(4,128)S(1)}, u32[]{:S(2)}, u32[]{:S(2)}) collective-permute-start(f32[4,4,16,3]{3,0,2,1:T(4,128)S(1)} %get-tuple-element.42), channel_id=1, source_target_pairs={{0,24},{8,0},{16,8},{24,16},{1,25},{9,1},{17,9},{25,17},{2,26},{10... | collective-permute-start | bytes 9224 | tf_op jit(solution)/shard_map/ppermute | solution.py:120
  37.7 4.0 %collective-permute-done.8 = f32[4,4,16,3]{3,0,2,1:T(4,128)S(1)} collective-permute-done((f32[4,4,16,3]{3,0,2,1:T(4,128)S(1)}, f32[4,4,16,3]{3,0,2,1:T(4,128)S(1)}, u32[]{:S(2)}, u32[]{:S(2)}) %collective-permute-start.8) | collective-permute-done | bytes 3104 | tf_op jit(solution)/shard_map/ppermute | solution.py:120
  41.7 0.5 maximum_maximum_fusion
  42.3 1.3 %collective-permute-start.10 = (f32[4,3,22,134]{3,0,2,1:T(4,128)S(1)}, f32[4,3,22,134]{3,0,2,1:T(4,128)S(1)}, u32[]{:S(2)}, u32[]{:S(2)}) collective-permute-start(f32[4,3,22,134]{3,0,2,1:T(4,128)S(1)} %get-tuple-element.31), channel_id=1, source_target_pairs={{0,1},{1,2},{2,3},{4,5},{5,6},{6,7},{8,9},{9,10},{10,11},{12,13},{... | collective-permute-start | bytes 424520 | tf_op jit(solution)/shard_map/ppermute | solution.py:120
  43.6 1.5 %collective-permute-start.11 = (f32[4,3,22,134]{3,0,2,1:T(4,128)S(1)}, f32[4,3,22,134]{3,0,2,1:T(4,128)S(1)}, u32[]{:S(2)}, u32[]{:S(2)}) collective-permute-start(f32[4,3,22,134]{3,0,2,1:T(4,128)S(1)} %get-tuple-element.32), channel_id=1, source_target_pairs={{1,0},{2,1},{3,2},{5,4},{6,5},{7,6},{9,8},{10,9},{11,10},{13,12},{... | collective-permute-start | bytes 424520 | tf_op jit(solution)/shard_map/ppermute | solution.py:120
  45.1 3.4 %collective-permute-done.11 = f32[4,3,22,134]{3,0,2,1:T(4,128)S(1)} collective-permute-done((f32[4,3,22,134]{3,0,2,1:T(4,128)S(1)}, f32[4,3,22,134]{3,0,2,1:T(4,128)S(1)}, u32[]{:S(2)}, u32[]{:S(2)}) %collective-permute-start.11) | collective-permute-done | bytes 141536 | tf_op jit(solution)/shard_map/ppermute | solution.py:120
  48.5 0.5 pad_maximum_fusion
  49.8 0.5 broadcast_multiply_fusion
  50.3 2.4 %broadcast_multiply_fusion.1 = (f32[3,8,20,132]{3,0,2,1:T(4,128)S(1)}, f32[3,8,20,132]{3,0,2,1:T(4,128)S(1)}) fusion(f32[8,20,132]{2,1,0:T(8,128)S(1)} %get-tuple-element.40, f32[3,10,22,134]{3,0,2,1:T(4,128)S(1)} %get-tuple-element.27, f32[8,20,132]{2,1,0:T(8,128)S(1)} %get-tuple-element.39, f32[4,10,22,134]{3,0,2,1:T(4,128)S(1)} %pad_maximum_fusion, ...), kind=kLoop, calls=%fused_computation.46 | loop fusion | flops 760320 | bytes 2703360 | tf_op jit(solution)/shard_map/mul | solution.py:60
  52.8 1.7 %broadcast_multiply_fusion.2 = (f32[3,6,18,130]{3,0,2,1:T(4,128)S(1)}, f32[3,6,18,130]{3,0,2,1:T(4,128)S(1)}) fusion(f32[6,18,130]{2,1,0:T(8,128)S(1)} %get-tuple-element.38, f32[3,8,20,132]{3,0,2,1:T(4,128)S(1)} %get-tuple-element.25, f32[6,18,130]{2,1,0:T(8,128)S(1)} %get-tuple-element.37, f32[4,10,22,134]{3,0,2,1:T(4,128)S(1)} %pad_maximum_fusion, ...), kind=kLoop, calls=%fused_computation.63 | loop fusion | flops 505440 | bytes 1797120 | tf_op jit(solution)/shard_map/mul | solution.py:60
  54.5 0.5 multiply_reduce_fusion
  55.0 0.4 convolution_bitcast_fusion.13
  55.4 1.6 %collective-permute-start.14 = (f32[3,128]{1,0:T(4,128)S(1)}, f32[3,128]{1,0:T(4,128)S(1)}, u32[]{:S(2)}, u32[]{:S(2)}) collective-permute-start(f32[3,128]{1,0:T(4,128)S(1)} %get-tuple-element.65), channel_id=1, source_target_pairs={{0,4},{4,0},{1,5},{5,1},{2,6},{6,2},{3,7},{7,3},{8,12},{12,8},{9,1... | collective-permute-start | bytes 4616 | tf_op jit(solution)/shard_map/ppermute | solution.py:194
  57.0 1.3 %collective-permute-start.16 = (f32[3,128]{1,0:T(4,128)S(1)}, f32[3,128]{1,0:T(4,128)S(1)}, u32[]{:S(2)}, u32[]{:S(2)}) collective-permute-start(f32[3,128]{1,0:T(4,128)S(1)} %get-tuple-element.66), channel_id=1, source_target_pairs={{1,4},{2,5},{3,6},{5,0},{6,1},{7,2},{9,12},{10,13},{11,14},{13,8},... | collective-permute-start | bytes 4616 | tf_op jit(solution)/shard_map/ppermute | solution.py:194
  58.3 1.3 %collective-permute-start.13 = (f32[3,128]{1,0:T(4,128)S(1)}, f32[3,128]{1,0:T(4,128)S(1)}, u32[]{:S(2)}, u32[]{:S(2)}) collective-permute-start(f32[3,128]{1,0:T(4,128)S(1)} %get-tuple-element.66), channel_id=1, source_target_pairs={{1,0},{2,1},{3,2},{5,4},{6,5},{7,6},{9,8},{10,9},{11,10},{13,12},{... | collective-permute-start | bytes 4616 | tf_op jit(solution)/shard_map/ppermute | solution.py:194
  59.6 7.8 %collective-permute-start.15 = (f32[3,128]{1,0:T(4,128)S(1)}, f32[3,128]{1,0:T(4,128)S(1)}, u32[]{:S(2)}, u32[]{:S(2)}) collective-permute-start(f32[3,128]{1,0:T(4,128)S(1)} %get-tuple-element.67), channel_id=1, source_target_pairs={{0,5},{1,6},{2,7},{4,1},{5,2},{6,3},{8,13},{9,14},{10,15},{12,9},{... | collective-permute-start | bytes 4616 | tf_op jit(solution)/shard_map/ppermute | solution.py:194
  67.4 4.4 %collective-permute-start.12 = (f32[3,128]{1,0:T(4,128)S(1)}, f32[3,128]{1,0:T(4,128)S(1)}, u32[]{:S(2)}, u32[]{:S(2)}) collective-permute-start(f32[3,128]{1,0:T(4,128)S(1)} %get-tuple-element.67), channel_id=1, source_target_pairs={{0,1},{1,2},{2,3},{4,5},{5,6},{6,7},{8,9},{9,10},{10,11},{12,13},{... | collective-permute-start | bytes 4616 | tf_op jit(solution)/shard_map/ppermute | solution.py:194
  71.9 0.8 collective-permute-done.12
  72.6 3.4 %collective-permute-start.19 = (f32[3,128]{1,0:T(4,128)S(1)}, f32[3,128]{1,0:T(4,128)S(1)}, u32[]{:S(2)}, u32[]{:S(2)}) collective-permute-start(f32[3,128]{1,0:T(4,128)S(1)} %add_add_fusion.1), channel_id=1, source_target_pairs={{0,24},{8,0},{16,8},{24,16},{1,25},{9,1},{17,9},{25,17},{2,26},{10... | collective-permute-start | bytes 4616 | tf_op jit(solution)/shard_map/ppermute | solution.py:194
  76.1 0.6 collective-permute-start.17
  76.7 0.7 copy.84
  77.4 0.6 copy.85
  78.1 2.5 %collective-permute-done.18 = f32[3,128]{1,0:T(4,128)S(1)} collective-permute-done((f32[3,128]{1,0:T(4,128)S(1)}, f32[3,128]{1,0:T(4,128)S(1)}, u32[]{:S(2)}, u32[]{:S(2)}) %collective-permute-start.18) | collective-permute-done | bytes 1568 | tf_op jit(solution)/shard_map/ppermute | solution.py:194
  80.6 0.9 %collective-permute-done.17 = f32[3,128]{1,0:T(4,128)S(1)} collective-permute-done((f32[3,128]{1,0:T(4,128)S(1)}, f32[3,128]{1,0:T(4,128)S(1)}, u32[]{:S(2)}, u32[]{:S(2)}) %collective-permute-start.17) | collective-permute-done | bytes 1568 | tf_op jit(solution)/shard_map/ppermute | solution.py:194
  81.5 0.6 add_add_fusion
  (75 shorter events, 4.4 us)
Async XLA Ops:
  0.6 26.6 %copy-start = (f32[3,5]{1,0:T(4,128)S(1)}, f32[3,5]{1,0:T(4,128)}, u32[]{:S(2)}) copy-start(f32[3,5]{1,0:T(4,128)} %param.14) | copy-start | bytes 184
  0.7 1.0 %copy-start.3 = (f32[3,4,16,128]{3,2,1,0:T(8,128)S(1)}, f32[3,4,16,128]{3,2,1,0:T(8,128)}, u32[]{:S(2)}) copy-start(f32[3,4,16,128]{3,2,1,0:T(8,128)} %param.11) | copy-start | bytes 294916
  1.7 23.7 %collective-permute-start.2 = (f32[8,4,1,128]{3,2,1,0:T(1,128)S(1)}, f32[8,4,1,128]{3,2,1,0:T(1,128)S(1)}, u32[]{:S(2)}, u32[]{:S(2)}) collective-permute-start(f32[8,4,1,128]{3,2,1,0:T(1,128)S(1)} %broadcast_select_fusion.1), channel_id=1, source_target_pairs={{0,4},{4,0},{1,5},{5,1},{2,6},{6,2},{3,7},{7,3},{8,12},{12,8},{9,1... | collective-permute-start | bytes 49160 | tf_op jit(solution)/shard_map/ppermute | solution.py:133
  4.7 21.1 %collective-permute-start.1 = (f32[8,1,16,128]{3,2,1,0:T(8,128)S(1)}, f32[8,1,16,128]{3,2,1,0:T(8,128)S(1)}, u32[]{:S(2)}, u32[]{:S(2)}) collective-permute-start(f32[8,1,16,128]{3,2,1,0:T(8,128)S(1)} %get-tuple-element.35), channel_id=1, source_target_pairs={{0,1},{1,2},{2,3},{4,5},{5,6},{6,7},{8,9},{9,10},{10,11},{12,13},{... | collective-permute-start | bytes 196616 | tf_op jit(solution)/shard_map/ppermute | solution.py:120
  6.2 19.7 %collective-permute-start = (f32[8,1,16,128]{3,2,1,0:T(8,128)S(1)}, f32[8,1,16,128]{3,2,1,0:T(8,128)S(1)}, u32[]{:S(2)}, u32[]{:S(2)}) collective-permute-start(f32[8,1,16,128]{3,2,1,0:T(8,128)S(1)} %get-tuple-element.36), channel_id=1, source_target_pairs={{1,0},{2,1},{3,2},{5,4},{6,5},{7,6},{9,8},{10,9},{11,10},{13,12},{... | collective-permute-start | bytes 196616 | tf_op jit(solution)/shard_map/ppermute | solution.py:120
  7.6 5.3 %copy-start.1 = (f32[5,4,16,128]{3,2,1,0:T(8,128)S(1)}, f32[5,4,16,128]{3,2,1,0:T(8,128)}, u32[]{:S(2)}) copy-start(f32[5,4,16,128]{3,2,1,0:T(8,128)} %param.9) | copy-start | bytes 491524
  7.7 9.3 %collective-permute-start.4 = (f32[8,4,16,1]{3,2,1,0:T(8,128)S(1)}, f32[8,4,16,1]{3,2,1,0:T(8,128)S(1)}, u32[]{:S(2)}, u32[]{:S(2)}) collective-permute-start(f32[8,4,16,1]{3,2,1,0:T(8,128)S(1)} %get-tuple-element.33), channel_id=1, source_target_pairs={{0,8},{8,16},{16,24},{24,0},{1,9},{9,17},{17,25},{25,1},{2,10},{10... | collective-permute-start | bytes 6152 | tf_op jit(solution)/shard_map/ppermute | solution.py:120
  9.3 14.5 %collective-permute-start.3 = (f32[8,4,16,1]{3,2,1,0:T(8,128)S(1)}, f32[8,4,16,1]{3,2,1,0:T(8,128)S(1)}, u32[]{:S(2)}, u32[]{:S(2)}) collective-permute-start(f32[8,4,16,1]{3,2,1,0:T(8,128)S(1)} %get-tuple-element.34), channel_id=1, source_target_pairs={{0,24},{8,0},{16,8},{24,16},{1,25},{9,1},{17,9},{25,17},{2,26},{10... | collective-permute-start | bytes 6152 | tf_op jit(solution)/shard_map/ppermute | solution.py:120
  11.5 0.7 copy-start.6
  12.2 0.7 copy-start.7
  25.9 0.9 %copy-start.4 = (f32[5,4,16,128]{3,2,1,0:T(8,128)S(1)}, f32[5,4,16,128]{3,2,1,0:T(8,128)}, u32[]{:S(2)}) copy-start(f32[5,4,16,128]{3,2,1,0:T(8,128)} %param.10) | copy-start | bytes 491524
  27.2 0.8 copy-start.2
  28.3 9.3 %collective-permute-start.5 = (f32[4,4,3,3]{3,0,2,1:T(4,128)S(1)}, f32[4,4,3,3]{3,0,2,1:T(4,128)S(1)}, u32[]{:S(2)}, u32[]{:S(2)}) collective-permute-start(f32[4,4,3,3]{3,0,2,1:T(4,128)S(1)} %get-tuple-element.43), channel_id=1, source_target_pairs={{0,12},{8,20},{16,28},{24,4},{4,8},{12,16},{20,24},{28,0},{1,13},{... | collective-permute-start | bytes 1736 | tf_op jit(solution)/shard_map/ppermute | solution.py:133
  29.2 8.5 %collective-permute-start.6 = (f32[4,4,3,128]{3,0,2,1:T(4,128)S(1)}, f32[4,4,3,128]{3,0,2,1:T(4,128)S(1)}, u32[]{:S(2)}, u32[]{:S(2)}) collective-permute-start(f32[4,4,3,128]{3,0,2,1:T(4,128)S(1)} %fusion.34), channel_id=1, source_target_pairs={{0,4},{4,0},{1,5},{5,1},{2,6},{6,2},{3,7},{7,3},{8,12},{12,8},{9,1... | collective-permute-start | bytes 73736 | tf_op jit(solution)/shard_map/ppermute | solution.py:133
  31.0 6.7 %collective-permute-start.7 = (f32[4,4,3,3]{3,0,2,1:T(4,128)S(1)}, f32[4,4,3,3]{3,0,2,1:T(4,128)S(1)}, u32[]{:S(2)}, u32[]{:S(2)}) collective-permute-start(f32[4,4,3,3]{3,0,2,1:T(4,128)S(1)} %get-tuple-element.44), channel_id=1, source_target_pairs={{0,28},{8,4},{16,12},{24,20},{4,24},{12,0},{20,8},{28,16},{1,29},{... | collective-permute-start | bytes 1736 | tf_op jit(solution)/shard_map/ppermute | solution.py:133
  33.8 7.9 %collective-permute-start.8 = (f32[4,4,16,3]{3,0,2,1:T(4,128)S(1)}, f32[4,4,16,3]{3,0,2,1:T(4,128)S(1)}, u32[]{:S(2)}, u32[]{:S(2)}) collective-permute-start(f32[4,4,16,3]{3,0,2,1:T(4,128)S(1)} %get-tuple-element.41), channel_id=1, source_target_pairs={{0,8},{8,16},{16,24},{24,0},{1,9},{9,17},{17,25},{25,1},{2,10},{10... | collective-permute-start | bytes 9224 | tf_op jit(solution)/shard_map/ppermute | solution.py:120
  33.8 7.9 %collective-permute-start.9 = (f32[4,4,16,3]{3,0,2,1:T(4,128)S(1)}, f32[4,4,16,3]{3,0,2,1:T(4,128)S(1)}, u32[]{:S(2)}, u32[]{:S(2)}) collective-permute-start(f32[4,4,16,3]{3,0,2,1:T(4,128)S(1)} %get-tuple-element.42), channel_id=1, source_target_pairs={{0,24},{8,0},{16,8},{24,16},{1,25},{9,1},{17,9},{25,17},{2,26},{10... | collective-permute-start | bytes 9224 | tf_op jit(solution)/shard_map/ppermute | solution.py:120
  42.3 2.8 %copy-start.8 = (s32[4,128]{1,0:T(4,128)S(1)}, s32[4,128]{1,0:T(4,128)}, u32[]{:S(2)}) copy-start(s32[4,128]{1,0:T(4,128)} %param.17) | copy-start | bytes 6148
  42.3 2.8 %collective-permute-start.10 = (f32[4,3,22,134]{3,0,2,1:T(4,128)S(1)}, f32[4,3,22,134]{3,0,2,1:T(4,128)S(1)}, u32[]{:S(2)}, u32[]{:S(2)}) collective-permute-start(f32[4,3,22,134]{3,0,2,1:T(4,128)S(1)} %get-tuple-element.31), channel_id=1, source_target_pairs={{0,1},{1,2},{2,3},{4,5},{5,6},{6,7},{8,9},{9,10},{10,11},{12,13},{... | collective-permute-start | bytes 424520 | tf_op jit(solution)/shard_map/ppermute | solution.py:120
  43.6 4.9 %collective-permute-start.11 = (f32[4,3,22,134]{3,0,2,1:T(4,128)S(1)}, f32[4,3,22,134]{3,0,2,1:T(4,128)S(1)}, u32[]{:S(2)}, u32[]{:S(2)}) collective-permute-start(f32[4,3,22,134]{3,0,2,1:T(4,128)S(1)} %get-tuple-element.32), channel_id=1, source_target_pairs={{1,0},{2,1},{3,2},{5,4},{6,5},{7,6},{9,8},{10,9},{11,10},{13,12},{... | collective-permute-start | bytes 424520 | tf_op jit(solution)/shard_map/ppermute | solution.py:120
  52.8 1.7 %copy-start.5 = (f32[4,16,128]{2,1,0:T(8,128)S(1)}, f32[4,16,128]{2,1,0:T(8,128)}, u32[]{:S(2)}) copy-start(f32[4,16,128]{2,1,0:T(8,128)} %param.16) | copy-start | bytes 98308
  55.4 16.4 %collective-permute-start.14 = (f32[3,128]{1,0:T(4,128)S(1)}, f32[3,128]{1,0:T(4,128)S(1)}, u32[]{:S(2)}, u32[]{:S(2)}) collective-permute-start(f32[3,128]{1,0:T(4,128)S(1)} %get-tuple-element.65), channel_id=1, source_target_pairs={{0,4},{4,0},{1,5},{5,1},{2,6},{6,2},{3,7},{7,3},{8,12},{12,8},{9,1... | collective-permute-start | bytes 4616 | tf_op jit(solution)/shard_map/ppermute | solution.py:194
  57.0 14.9 %collective-permute-start.16 = (f32[3,128]{1,0:T(4,128)S(1)}, f32[3,128]{1,0:T(4,128)S(1)}, u32[]{:S(2)}, u32[]{:S(2)}) collective-permute-start(f32[3,128]{1,0:T(4,128)S(1)} %get-tuple-element.66), channel_id=1, source_target_pairs={{1,4},{2,5},{3,6},{5,0},{6,1},{7,2},{9,12},{10,13},{11,14},{13,8},... | collective-permute-start | bytes 4616 | tf_op jit(solution)/shard_map/ppermute | solution.py:194
  58.3 13.6 %collective-permute-start.13 = (f32[3,128]{1,0:T(4,128)S(1)}, f32[3,128]{1,0:T(4,128)S(1)}, u32[]{:S(2)}, u32[]{:S(2)}) collective-permute-start(f32[3,128]{1,0:T(4,128)S(1)} %get-tuple-element.66), channel_id=1, source_target_pairs={{1,0},{2,1},{3,2},{5,4},{6,5},{7,6},{9,8},{10,9},{11,10},{13,12},{... | collective-permute-start | bytes 4616 | tf_op jit(solution)/shard_map/ppermute | solution.py:194
  59.6 12.3 %collective-permute-start.15 = (f32[3,128]{1,0:T(4,128)S(1)}, f32[3,128]{1,0:T(4,128)S(1)}, u32[]{:S(2)}, u32[]{:S(2)}) collective-permute-start(f32[3,128]{1,0:T(4,128)S(1)} %get-tuple-element.67), channel_id=1, source_target_pairs={{0,5},{1,6},{2,7},{4,1},{5,2},{6,3},{8,13},{9,14},{10,15},{12,9},{... | collective-permute-start | bytes 4616 | tf_op jit(solution)/shard_map/ppermute | solution.py:194
  67.4 5.2 %collective-permute-start.12 = (f32[3,128]{1,0:T(4,128)S(1)}, f32[3,128]{1,0:T(4,128)S(1)}, u32[]{:S(2)}, u32[]{:S(2)}) collective-permute-start(f32[3,128]{1,0:T(4,128)S(1)} %get-tuple-element.67), channel_id=1, source_target_pairs={{0,1},{1,2},{2,3},{4,5},{5,6},{6,7},{8,9},{9,10},{10,11},{12,13},{... | collective-permute-start | bytes 4616 | tf_op jit(solution)/shard_map/ppermute | solution.py:194
  72.6 5.4 %collective-permute-start.19 = (f32[3,128]{1,0:T(4,128)S(1)}, f32[3,128]{1,0:T(4,128)S(1)}, u32[]{:S(2)}, u32[]{:S(2)}) collective-permute-start(f32[3,128]{1,0:T(4,128)S(1)} %add_add_fusion.1), channel_id=1, source_target_pairs={{0,24},{8,0},{16,8},{24,16},{1,25},{9,1},{17,9},{25,17},{2,26},{10... | collective-permute-start | bytes 4616 | tf_op jit(solution)/shard_map/ppermute | solution.py:194
  76.1 4.5 %collective-permute-start.18 = (f32[3,128]{1,0:T(4,128)S(1)}, f32[3,128]{1,0:T(4,128)S(1)}, u32[]{:S(2)}, u32[]{:S(2)}) collective-permute-start(f32[3,128]{1,0:T(4,128)S(1)} %add_add_fusion.1), channel_id=1, source_target_pairs={{0,16},{8,24},{16,0},{24,8},{1,17},{9,25},{17,1},{25,9},{2,18},{10... | collective-permute-start | bytes 4616 | tf_op jit(solution)/shard_map/ppermute | solution.py:194
  76.1 5.4 %collective-permute-start.17 = (f32[3,128]{1,0:T(4,128)S(1)}, f32[3,128]{1,0:T(4,128)S(1)}, u32[]{:S(2)}, u32[]{:S(2)}) collective-permute-start(f32[3,128]{1,0:T(4,128)S(1)} %add_add_fusion.1), channel_id=1, source_target_pairs={{0,8},{8,16},{16,24},{24,0},{1,9},{9,17},{17,25},{25,1},{2,10},{10... | collective-permute-start | bytes 4616 | tf_op jit(solution)/shard_map/ppermute | solution.py:194

commit v5 on v4

--- a/solution.py
+++ b/solution.py
@@ -156,7 +156,13 @@
 
 
 def jac_apply(jac, term):
-    return jnp.einsum("uv,ukji->vkji", jac, term, precision=lax.Precision.HIGHEST)
+    rows = []
+    for v in range(jac.shape[1]):
+        acc = jac[0, v] * term[0]
+        for u in range(1, jac.shape[0]):
+            acc = acc + jac[u, v] * term[u]
+        rows.append(acc)
+    return jnp.stack(rows)
 
 
 def flux_faces(stacked, halos, owner_jac, neighbor_jac):
@@ -227,7 +233,7 @@
         face_halos(stacked, "circ", 3, True),
     ]
     residual = flux_faces(stacked, halos, owner_jac, neighbor_jac) + adjoint - objective_grad
-    forcing = jnp.einsum("mv,vkji->mkji", coupling, residual, precision=lax.Precision.HIGHEST)
+    forcing = jac_apply(coupling.T, residual)
     margin = SWEEPS - 1
     joined = jnp.concatenate([stiffness[None], forcing], axis=0)
     full_pad = padded_sweeps(joined, margin)

time: 82.6 us -> 272 us (3.29); the launches traced: 82.1 us -> 268 us
  other arithmetic: 8.51 us -> 202 us
  local copies, waits for them, and re-layouts: 6.12 us -> 10.4 us
  matrix products: 4.57 us -> 0.41 us
  starting transfers between devices: 42.2 us -> 38.1 us
  waiting for transfers between devices: 19.4 us -> 15.8 us
    unnamed x0 -> x48, other arithmetic: none -> 149 us
    another operation x1 -> x12, other arithmetic: 0.02 us -> 38.2 us  [jac_apply(): return jnp.stack(rows)]
    ppermute x8, waiting for transfers between devices: 15.2 us -> 4.2 us  [receive(): return lax.ppermute(take(array, rel, dims, width), axes, pairs)]
    add x1 -> x3, other arithmetic: 0.31 us -> 9.38 us  [jac_apply(): acc = acc + jac[u, v] * term[u]]
    slice x0 -> x13, local copies, waits for them, and re-layouts: none -> 8.75 us  [jac_apply(): acc = jac[0, v] * term[0]]
    ppermute x4, waiting for transfers between devices: 0.01 us -> 5.21 us  [receive_pair(): got = lax.ppermute(sent, axes, pairs + back)]
    dot_general x13 -> x0, matrix products: 4.16 us -> none  [the longest x12 3.82 us: jac_apply(): jnp.einsum('uv,ukji->vkji', jac, term, precision=lax.Precision.HIGHEST)]
    unnamed x22 -> x23, local copies, waits for them, and re-layouts: 4.56 us -> 1.03 us
  transfers between devices with their start and end apart: 20 -> 20, of which waited for: 7 -> 6; matrix products, arithmetic and copies ran while one was open for 8% -> 62% of each run, Pallas kernels for 0% -> 0%
where the time goes in v5:
time: 272 us; the launch traced here: 268 us
  other arithmetic  202 us (74%)
  starting transfers between devices  38.1 us (14%)
  waiting for transfers between devices  15.8 us (6%)
  local copies, waits for them, and re-layouts  10.4 us (4%)
    unnamed x48, other arithmetic  149 us
    another operation x12, other arithmetic, jac_apply(): return jnp.stack(rows)  38.2 us
    ppermute x8, starting transfers between devices, shifted(): return lax.ppermute(array, axes, pairs)  17.9 us
    ppermute x8, starting transfers between devices, receive(): return lax.ppermute(take(array, rel, dims, width), axes, pairs)  15.2 us
    add x3, other arithmetic, jac_apply(): acc = acc + jac[u, v] * term[u]  9.38 us
    slice x13, local copies, waits for them, and re-layouts, jac_apply(): acc = jac[0, v] * term[0]  8.75 us
    ppermute x8, waiting for transfers between devices, shifted(): return lax.ppermute(array, axes, pairs)  6.39 us
  transfers between devices with their start and end apart: 20, of which 6 were waited for; matrix products, arithmetic and copies ran while one was open for 62% of the time, Pallas kernels for 0%

profile of v5, /device:TPU:0, one launch (start us, length us, event | category | flops | bytes accessed | tf_op | source)
XLA Modules:
  0.0 268.3 jit_solution(16768364984357934669)
XLA Ops:
  1.8 3.1 %collective-permute-start.4 = (f32[8,4,16,1]{3,2,1,0:T(8,128)S(1)}, f32[8,4,16,1]{3,2,1,0:T(8,128)S(1)}, u32[]{:S(2)}, u32[]{:S(2)}) collective-permute-start(f32[8,4,16,1]{3,2,1,0:T(8,128)S(1)} %get-tuple-element.27), channel_id=1, source_target_pairs={{0,8},{8,16},{16,24},{24,0},{1,9},{9,17},{17,25},{25,1},{2,10},{10... | collective-permute-start | bytes 6152 | tf_op jit(solution)/shard_map/ppermute | solution.py:120
  26.0 3.2 %constant_dynamic-update-slice_fusion.24 = f32[5,4,16,127]{3,2,1,0:T(8,128)S(1)} fusion(f32[]{:T(128)} %bitcast.112, f32[]{:T(128)} %bitcast.111, f32[]{:T(128)} %bitcast.110, f32[]{:T(128)} %bitcast.109, f32[]{:T(128)} %bitcast.107, f32[5,4,16,127]{3,2,1,0:T(8,128)S(1)} %subtract_multiply_fusion), kind=kLoop, calls=%fused_computation.72 | loop fusion | flops 73151 | bytes 195348
  29.2 3.1 %constant_dynamic-update-slice_fusion.29 = f32[5,4,16,127]{3,2,1,0:T(8,128)S(1)} fusion(f32[]{:T(128)} %bitcast.138, f32[]{:T(128)} %bitcast.137, f32[]{:T(128)} %bitcast.136, f32[]{:T(128)} %bitcast.135, f32[]{:T(128)} %bitcast.134, f32[5,4,16,127]{3,2,1,0:T(8,128)S(1)} %subtract_multiply_fusion), kind=kLoop, calls=%fused_computation.77 | loop fusion | flops 73151 | bytes 195348
  32.4 3.2 %constant_dynamic-update-slice_fusion.4 = f32[5,3,16,128]{3,2,1,0:T(8,128)S(1)} fusion(f32[]{:T(128)} %bitcast.6, f32[]{:T(128)} %bitcast.5, f32[]{:T(128)} %bitcast.4, f32[]{:T(128)} %bitcast.3, f32[]{:T(128)} %bitcast.1, f32[5,3,16,128]{3,2,1,0:T(8,128)S(1)} %subtract_multiply_fusion.2), kind=kLoop, calls=%fused_computation.52 | loop fusion | flops 55295 | bytes 147476
  35.5 3.1 %constant_dynamic-update-slice_fusion.9 = f32[5,3,16,128]{3,2,1,0:T(8,128)S(1)} fusion(f32[]{:T(128)} %bitcast.32, f32[]{:T(128)} %bitcast.31, f32[]{:T(128)} %bitcast.30, f32[]{:T(128)} %bitcast.29, f32[]{:T(128)} %bitcast.28, f32[5,3,16,128]{3,2,1,0:T(8,128)S(1)} %subtract_multiply_fusion.2), kind=kLoop, calls=%fused_computation.57 | loop fusion | flops 55295 | bytes 147476
  38.6 3.2 %constant_dynamic-update-slice_fusion.13 = f32[5,4,15,128]{3,2,1,0:T(8,128)S(1)} fusion(f32[5,4,15,128]{3,2,1,0:T(8,128)S(1)} %constant_dynamic-update-slice_fusion.14, f32[]{:T(128)} %bitcast.64, f32[]{:T(128)} %bitcast.63, f32[]{:T(128)} %bitcast.62, f32[]{:T(128)} %bitcast.61, f32[]{:T(128)} %bitcast.60, f32[5,4,15,128]{3,2,1,0:T(8,128)S(1)} %subtract_multiply_fusion.1), kind=kLoop, calls=%fused_computation.61 | loop fusion | flops 69120 | bytes 196628
  41.8 3.1 %constant_dynamic-update-slice_fusion.12 = f32[5,4,15,128]{3,2,1,0:T(8,128)S(1)} fusion(f32[5,4,15,128]{3,2,1,0:T(8,128)S(1)} %constant_dynamic-update-slice_fusion.13, f32[]{:T(128)} %bitcast.69, f32[]{:T(128)} %bitcast.68, f32[]{:T(128)} %bitcast.67, f32[]{:T(128)} %bitcast.66, f32[]{:T(128)} %bitcast.65, f32[5,4,15,128]{3,2,1,0:T(8,128)S(1)} %subtract_multiply_fusion.1), kind=kLoop, calls=%fused_computation.60 | loop fusion | flops 69120 | bytes 196628
  48.0 3.2 %constant_dynamic-update-slice_fusion.10 = f32[5,4,15,128]{3,2,1,0:T(8,128)S(1)} fusion(f32[5,4,15,128]{3,2,1,0:T(8,128)S(1)} %constant_dynamic-update-slice_fusion.11, f32[]{:T(128)} %bitcast.79, f32[]{:T(128)} %bitcast.78, f32[]{:T(128)} %bitcast.77, f32[]{:T(128)} %bitcast.76, f32[]{:T(128)} %bitcast.75, f32[5,4,15,128]{3,2,1,0:T(8,128)S(1)} %subtract_multiply_fusion.1), kind=kLoop, calls=%fused_computation.58 | loop fusion | flops 69120 | bytes 196628 | tf_op jit(solution)/shard_map/stack | solution.py:165
  51.2 3.1 %constant_dynamic-update-slice_fusion.18 = f32[5,4,15,128]{3,2,1,0:T(8,128)S(1)} fusion(f32[5,4,15,128]{3,2,1,0:T(8,128)S(1)} %constant_dynamic-update-slice_fusion.19, f32[]{:T(128)} %bitcast.90, f32[]{:T(128)} %bitcast.89, f32[]{:T(128)} %bitcast.88, f32[]{:T(128)} %bitcast.87, f32[]{:T(128)} %bitcast.86, f32[5,4,15,128]{3,2,1,0:T(8,128)S(1)} %subtract_multiply_fusion.1), kind=kLoop, calls=%fused_computation.66 | loop fusion | flops 69120 | bytes 196628
  54.3 3.2 %constant_dynamic-update-slice_fusion.17 = f32[5,4,15,128]{3,2,1,0:T(8,128)S(1)} fusion(f32[5,4,15,128]{3,2,1,0:T(8,128)S(1)} %constant_dynamic-update-slice_fusion.18, f32[]{:T(128)} %bitcast.95, f32[]{:T(128)} %bitcast.94, f32[]{:T(128)} %bitcast.93, f32[]{:T(128)} %bitcast.92, f32[]{:T(128)} %bitcast.91, f32[5,4,15,128]{3,2,1,0:T(8,128)S(1)} %subtract_multiply_fusion.1), kind=kLoop, calls=%fused_computation.65 | loop fusion | flops 69120 | bytes 196628
  60.5 3.3 %constant_dynamic-update-slice_fusion.15 = f32[5,4,15,128]{3,2,1,0:T(8,128)S(1)} fusion(f32[5,4,15,128]{3,2,1,0:T(8,128)S(1)} %constant_dynamic-update-slice_fusion.16, f32[]{:T(128)} %bitcast.105, f32[]{:T(128)} %bitcast.104, f32[]{:T(128)} %bitcast.103, f32[]{:T(128)} %bitcast.102, f32[]{:T(128)} %bitcast.101, f32[5,4,15,128]{3,2,1,0:T(8,128)S(1)} %subtract_multiply_fusion.1), kind=kLoop, calls=%fused_computation.63 | loop fusion | flops 69120 | bytes 196628 | tf_op jit(solution)/shard_map/stack | solution.py:165
  63.8 3.1 %constant_dynamic-update-slice_fusion.23 = f32[5,4,16,127]{3,2,1,0:T(8,128)S(1)} fusion(f32[5,4,16,127]{3,2,1,0:T(8,128)S(1)} %constant_dynamic-update-slice_fusion.24, f32[]{:T(128)} %bitcast.117, f32[]{:T(128)} %bitcast.116, f32[]{:T(128)} %bitcast.115, f32[]{:T(128)} %bitcast.114, f32[]{:T(128)} %bitcast.113, f32[5,4,16,127]{3,2,1,0:T(8,128)S(1)} %subtract_multiply_fusion), kind=kLoop, calls=%fused_computation.71 | loop fusion | flops 73152 | bytes 196628
  70.0 3.1 %constant_dynamic-update-slice_fusion.21 = f32[5,4,16,127]{3,2,1,0:T(8,128)S(1)} fusion(f32[5,4,16,127]{3,2,1,0:T(8,128)S(1)} %constant_dynamic-update-slice_fusion.22, f32[]{:T(128)} %bitcast.127, f32[]{:T(128)} %bitcast.126, f32[]{:T(128)} %bitcast.125, f32[]{:T(128)} %bitcast.124, f32[]{:T(128)} %bitcast.123, f32[5,4,16,127]{3,2,1,0:T(8,128)S(1)} %subtract_multiply_fusion), kind=kLoop, calls=%fused_computation.69 | loop fusion | flops 73152 | bytes 196628
  73.1 3.2 %constant_dynamic-update-slice_fusion.20 = f32[5,4,16,127]{3,2,1,0:T(8,128)S(1)} fusion(f32[5,4,16,127]{3,2,1,0:T(8,128)S(1)} %constant_dynamic-update-slice_fusion.21, f32[]{:T(128)} %bitcast.132, f32[]{:T(128)} %bitcast.131, f32[]{:T(128)} %bitcast.130, f32[]{:T(128)} %bitcast.129, f32[]{:T(128)} %bitcast.128, f32[5,4,16,127]{3,2,1,0:T(8,128)S(1)} %subtract_multiply_fusion), kind=kLoop, calls=%fused_computation.68 | loop fusion | flops 73152 | bytes 196628 | tf_op jit(solution)/shard_map/stack | solution.py:165
  82.3 3.2 %constant_dynamic-update-slice_fusion.26 = f32[5,4,16,127]{3,2,1,0:T(8,128)S(1)} fusion(f32[5,4,16,127]{3,2,1,0:T(8,128)S(1)} %constant_dynamic-update-slice_fusion.27, f32[]{:T(128)} %bitcast.153, f32[]{:T(128)} %bitcast.152, f32[]{:T(128)} %bitcast.151, f32[]{:T(128)} %bitcast.150, f32[]{:T(128)} %bitcast.149, f32[5,4,16,127]{3,2,1,0:T(8,128)S(1)} %subtract_multiply_fusion), kind=kLoop, calls=%fused_computation.74 | loop fusion | flops 73152 | bytes 196628
  85.5 3.3 %constant_dynamic-update-slice_fusion.25 = f32[5,4,16,127]{3,2,1,0:T(8,128)S(1)} fusion(f32[5,4,16,127]{3,2,1,0:T(8,128)S(1)} %constant_dynamic-update-slice_fusion.26, f32[]{:T(128)} %bitcast.158, f32[]{:T(128)} %bitcast.157, f32[]{:T(128)} %bitcast.156, f32[]{:T(128)} %bitcast.155, f32[]{:T(128)} %bitcast.154, f32[5,4,16,127]{3,2,1,0:T(8,128)S(1)} %subtract_multiply_fusion), kind=kLoop, calls=%fused_computation.73 | loop fusion | flops 73152 | bytes 196628 | tf_op jit(solution)/shard_map/stack | solution.py:165
  88.8 3.2 %constant_dynamic-update-slice_fusion.3 = f32[5,3,16,128]{3,2,1,0:T(8,128)S(1)} fusion(f32[5,3,16,128]{3,2,1,0:T(8,128)S(1)} %constant_dynamic-update-slice_fusion.4, f32[]{:T(128)} %bitcast.11, f32[]{:T(128)} %bitcast.10, f32[]{:T(128)} %bitcast.9, f32[]{:T(128)} %bitcast.8, f32[]{:T(128)} %bitcast.7, f32[5,3,16,128]{3,2,1,0:T(8,128)S(1)} %subtract_multiply_fusion.2), kind=kLoop, calls=%fused_computation.51 | loop fusion | flops 55296 | bytes 147476
  95.1 3.1 %constant_dynamic-update-slice_fusion.1 = f32[5,3,16,128]{3,2,1,0:T(8,128)S(1)} fusion(f32[5,3,16,128]{3,2,1,0:T(8,128)S(1)} %constant_dynamic-update-slice_fusion.2, f32[]{:T(128)} %bitcast.21, f32[]{:T(128)} %bitcast.20, f32[]{:T(128)} %bitcast.19, f32[]{:T(128)} %bitcast.18, f32[]{:T(128)} %bitcast.17, f32[5,3,16,128]{3,2,1,0:T(8,128)S(1)} %subtract_multiply_fusion.2), kind=kLoop, calls=%fused_computation.49 | loop fusion | flops 55296 | bytes 147476
  98.2 3.1 %constant_dynamic-update-slice_fusion = f32[5,3,16,128]{3,2,1,0:T(8,128)S(1)} fusion(f32[5,3,16,128]{3,2,1,0:T(8,128)S(1)} %constant_dynamic-update-slice_fusion.1, f32[]{:T(128)} %bitcast.26, f32[]{:T(128)} %bitcast.25, f32[]{:T(128)} %bitcast.24, f32[]{:T(128)} %bitcast.23, f32[]{:T(128)} %bitcast.22, f32[5,3,16,128]{3,2,1,0:T(8,128)S(1)} %subtract_multiply_fusion.2), kind=kLoop, calls=%fused_computation.48 | loop fusion | flops 55296 | bytes 147476 | tf_op jit(solution)/shard_map/stack | solution.py:165
  104.3 3.1 %constant_dynamic-update-slice_fusion.7 = f32[5,3,16,128]{3,2,1,0:T(8,128)S(1)} fusion(f32[5,3,16,128]{3,2,1,0:T(8,128)S(1)} %constant_dynamic-update-slice_fusion.8, f32[]{:T(128)} %bitcast.42, f32[]{:T(128)} %bitcast.41, f32[]{:T(128)} %bitcast.40, f32[]{:T(128)} %bitcast.39, f32[]{:T(128)} %bitcast.38, f32[5,3,16,128]{3,2,1,0:T(8,128)S(1)} %subtract_multiply_fusion.2), kind=kLoop, calls=%fused_computation.55 | loop fusion | flops 55296 | bytes 147476
  107.4 3.2 %constant_dynamic-update-slice_fusion.6 = f32[5,3,16,128]{3,2,1,0:T(8,128)S(1)} fusion(f32[5,3,16,128]{3,2,1,0:T(8,128)S(1)} %constant_dynamic-update-slice_fusion.7, f32[]{:T(128)} %bitcast.47, f32[]{:T(128)} %bitcast.46, f32[]{:T(128)} %bitcast.45, f32[]{:T(128)} %bitcast.44, f32[]{:T(128)} %bitcast.43, f32[5,3,16,128]{3,2,1,0:T(8,128)S(1)} %subtract_multiply_fusion.2), kind=kLoop, calls=%fused_computation.54 | loop fusion | flops 55296 | bytes 147476
  110.6 3.1 %constant_dynamic-update-slice_fusion.5 = f32[5,3,16,128]{3,2,1,0:T(8,128)S(1)} fusion(f32[5,3,16,128]{3,2,1,0:T(8,128)S(1)} %constant_dynamic-update-slice_fusion.6, f32[]{:T(128)} %bitcast.52, f32[]{:T(128)} %bitcast.51, f32[]{:T(128)} %bitcast.50, f32[]{:T(128)} %bitcast.49, f32[]{:T(128)} %bitcast.48, f32[5,3,16,128]{3,2,1,0:T(8,128)S(1)} %subtract_multiply_fusion.2), kind=kLoop, calls=%fused_computation.53 | loop fusion | flops 55296 | bytes 147476 | tf_op jit(solution)/shard_map/stack | solution.py:165
  114.7 3.1 %constant_dynamic-update-slice_fusion.61 = f32[5,4,16,1]{3,2,1,0:T(8,128)S(1)} fusion(f32[5,4,16,1]{3,2,1,0:T(8,128)S(1)} %get-tuple-element.35, f32[]{:T(128)} %bitcast.138, f32[]{:T(128)} %bitcast.137, f32[]{:T(128)} %bitcast.136, f32[]{:T(128)} %bitcast.135, f32[]{:T(128)} %bitcast.134), kind=kLoop, calls=%fused_computation.109 | loop fusion | flops 575 | bytes 34068
  123.9 3.2 %constant_dynamic-update-slice_fusion.58 = f32[5,4,16,1]{3,2,1,0:T(8,128)S(1)} fusion(f32[5,4,16,1]{3,2,1,0:T(8,128)S(1)} %constant_dynamic-update-slice_fusion.59, f32[5,4,16,1]{3,2,1,0:T(8,128)S(1)} %get-tuple-element.35, f32[]{:T(128)} %bitcast.153, f32[]{:T(128)} %bitcast.152, f32[]{:T(128)} %bitcast.151, f32[]{:T(128)} %bitcast.150, f32[]{:T(128)} %bitcast.149), kind=kLoop, calls=%fused_computation.106 | loop fusion | flops 576 | bytes 196628
  127.1 3.3 %constant_dynamic-update-slice_fusion.57 = f32[5,4,16,1]{3,2,1,0:T(8,128)S(1)} fusion(f32[5,4,16,1]{3,2,1,0:T(8,128)S(1)} %constant_dynamic-update-slice_fusion.58, f32[5,4,16,1]{3,2,1,0:T(8,128)S(1)} %get-tuple-element.35, f32[]{:T(128)} %bitcast.158, f32[]{:T(128)} %bitcast.157, f32[]{:T(128)} %bitcast.156, f32[]{:T(128)} %bitcast.155, f32[]{:T(128)} %bitcast.154), kind=kLoop, calls=%fused_computation.105 | loop fusion | flops 576 | bytes 196628 | tf_op jit(solution)/shard_map/stack | solution.py:165
  130.4 3.2 %constant_dynamic-update-slice_fusion.56 = f32[5,4,16,1]{3,2,1,0:T(8,128)S(1)} fusion(f32[5,4,16,1]{3,2,1,0:T(8,128)S(1)} %get-tuple-element.36, f32[]{:T(128)} %bitcast.112, f32[]{:T(128)} %bitcast.111, f32[]{:T(128)} %bitcast.110, f32[]{:T(128)} %bitcast.109, f32[]{:T(128)} %bitcast.107), kind=kLoop, calls=%fused_computation.104 | loop fusion | flops 575 | bytes 34068
  133.5 3.1 %constant_dynamic-update-slice_fusion.55 = f32[5,4,16,1]{3,2,1,0:T(8,128)S(1)} fusion(f32[5,4,16,1]{3,2,1,0:T(8,128)S(1)} %constant_dynamic-update-slice_fusion.56, f32[5,4,16,1]{3,2,1,0:T(8,128)S(1)} %get-tuple-element.36, f32[]{:T(128)} %bitcast.117, f32[]{:T(128)} %bitcast.116, f32[]{:T(128)} %bitcast.115, f32[]{:T(128)} %bitcast.114, f32[]{:T(128)} %bitcast.113), kind=kLoop, calls=%fused_computation.103 | loop fusion | flops 576 | bytes 196628
  139.7 3.1 %constant_dynamic-update-slice_fusion.53 = f32[5,4,16,1]{3,2,1,0:T(8,128)S(1)} fusion(f32[5,4,16,1]{3,2,1,0:T(8,128)S(1)} %constant_dynamic-update-slice_fusion.54, f32[5,4,16,1]{3,2,1,0:T(8,128)S(1)} %get-tuple-element.36, f32[]{:T(128)} %bitcast.127, f32[]{:T(128)} %bitcast.126, f32[]{:T(128)} %bitcast.125, f32[]{:T(128)} %bitcast.124, f32[]{:T(128)} %bitcast.123), kind=kLoop, calls=%fused_computation.101 | loop fusion | flops 576 | bytes 196628
  142.9 3.2 %constant_dynamic-update-slice_fusion.52 = f32[5,4,16,1]{3,2,1,0:T(8,128)S(1)} fusion(f32[5,4,16,1]{3,2,1,0:T(8,128)S(1)} %constant_dynamic-update-slice_fusion.53, f32[5,4,16,1]{3,2,1,0:T(8,128)S(1)} %get-tuple-element.36, f32[]{:T(128)} %bitcast.132, f32[]{:T(128)} %bitcast.131, f32[]{:T(128)} %bitcast.130, f32[]{:T(128)} %bitcast.129, f32[]{:T(128)} %bitcast.128), kind=kLoop, calls=%fused_computation.100 | loop fusion | flops 576 | bytes 196628 | tf_op jit(solution)/shard_map/stack | solution.py:165
  149.2 3.1 %constant_dynamic-update-slice_fusion.50 = f32[5,4,1,128]{3,2,1,0:T(1,128)S(1)} fusion(f32[5,4,1,128]{3,2,1,0:T(1,128)S(1)} %constant_dynamic-update-slice_fusion.51, f32[]{:T(128)} %bitcast.90, f32[]{:T(128)} %bitcast.89, f32[]{:T(128)} %bitcast.88, f32[]{:T(128)} %bitcast.87, f32[]{:T(128)} %bitcast.86, f32[5,4,1,128]{3,2,1,0:T(1,128)S(1)} %get-tuple-element.37), kind=kLoop, calls=%fused_computation.98 | loop fusion | flops 4608 | bytes 12308
  152.3 3.2 %constant_dynamic-update-slice_fusion.49 = f32[5,4,1,128]{3,2,1,0:T(1,128)S(1)} fusion(f32[5,4,1,128]{3,2,1,0:T(1,128)S(1)} %constant_dynamic-update-slice_fusion.50, f32[]{:T(128)} %bitcast.95, f32[]{:T(128)} %bitcast.94, f32[]{:T(128)} %bitcast.93, f32[]{:T(128)} %bitcast.92, f32[]{:T(128)} %bitcast.91, f32[5,4,1,128]{3,2,1,0:T(1,128)S(1)} %get-tuple-element.37), kind=kLoop, calls=%fused_computation.97 | loop fusion | flops 4608 | bytes 12308
  158.5 3.3 %constant_dynamic-update-slice_fusion.47 = f32[5,4,1,128]{3,2,1,0:T(1,128)S(1)} fusion(f32[5,4,1,128]{3,2,1,0:T(1,128)S(1)} %constant_dynamic-update-slice_fusion.48, f32[]{:T(128)} %bitcast.105, f32[]{:T(128)} %bitcast.104, f32[]{:T(128)} %bitcast.103, f32[]{:T(128)} %bitcast.102, f32[]{:T(128)} %bitcast.101, f32[5,4,1,128]{3,2,1,0:T(1,128)S(1)} %get-tuple-element.37), kind=kLoop, calls=%fused_computation.95 | loop fusion | flops 4608 | bytes 12308 | tf_op jit(solution)/shard_map/stack | solution.py:165
  164.8 3.2 %constant_dynamic-update-slice_fusion.45 = f32[5,4,1,128]{3,2,1,0:T(1,128)S(1)} fusion(f32[5,4,1,128]{3,2,1,0:T(1,128)S(1)} %constant_dynamic-update-slice_fusion.46, f32[]{:T(128)} %bitcast.64, f32[]{:T(128)} %bitcast.63, f32[]{:T(128)} %bitcast.62, f32[]{:T(128)} %bitcast.61, f32[]{:T(128)} %bitcast.60, f32[5,4,1,128]{3,2,1,0:T(1,128)S(1)} %get-tuple-element.38), kind=kLoop, calls=%fused_computation.93 | loop fusion | flops 4608 | bytes 12308
  168.0 3.1 %constant_dynamic-update-slice_fusion.44 = f32[5,4,1,128]{3,2,1,0:T(1,128)S(1)} fusion(f32[5,4,1,128]{3,2,1,0:T(1,128)S(1)} %constant_dynamic-update-slice_fusion.45, f32[]{:T(128)} %bitcast.69, f32[]{:T(128)} %bitcast.68, f32[]{:T(128)} %bitcast.67, f32[]{:T(128)} %bitcast.66, f32[]{:T(128)} %bitcast.65, f32[5,4,1,128]{3,2,1,0:T(1,128)S(1)} %get-tuple-element.38), kind=kLoop, calls=%fused_computation.92 | loop fusion | flops 4608 | bytes 12308
  174.2 3.2 %constant_dynamic-update-slice_fusion.42 = f32[5,4,1,128]{3,2,1,0:T(1,128)S(1)} fusion(f32[5,4,1,128]{3,2,1,0:T(1,128)S(1)} %constant_dynamic-update-slice_fusion.43, f32[]{:T(128)} %bitcast.79, f32[]{:T(128)} %bitcast.78, f32[]{:T(128)} %bitcast.77, f32[]{:T(128)} %bitcast.76, f32[]{:T(128)} %bitcast.75, f32[5,4,1,128]{3,2,1,0:T(1,128)S(1)} %get-tuple-element.38), kind=kLoop, calls=%fused_computation.90 | loop fusion | flops 4608 | bytes 12308 | tf_op jit(solution)/shard_map/stack | solution.py:165
  177.4 3.1 %constant_dynamic-update-slice_fusion.41 = f32[5,1,16,128]{3,2,1,0:T(8,128)S(1)} fusion(f32[5,1,16,128]{3,2,1,0:T(8,128)S(1)} %get-tuple-element.39, f32[]{:T(128)} %bitcast.32, f32[]{:T(128)} %bitcast.31, f32[]{:T(128)} %bitcast.30, f32[]{:T(128)} %bitcast.29, f32[]{:T(128)} %bitcast.28), kind=kLoop, calls=%fused_computation.89 | loop fusion | flops 18431 | bytes 49172
  186.5 3.2 %constant_dynamic-update-slice_fusion.38 = f32[5,1,16,128]{3,2,1,0:T(8,128)S(1)} fusion(f32[5,1,16,128]{3,2,1,0:T(8,128)S(1)} %constant_dynamic-update-slice_fusion.39, f32[5,1,16,128]{3,2,1,0:T(8,128)S(1)} %get-tuple-element.39, f32[]{:T(128)} %bitcast.47, f32[]{:T(128)} %bitcast.46, f32[]{:T(128)} %bitcast.45, f32[]{:T(128)} %bitcast.44, f32[]{:T(128)} %bitcast.43), kind=kLoop, calls=%fused_computation.86 | loop fusion | flops 18432 | bytes 49172
  189.7 3.1 %constant_dynamic-update-slice_fusion.37 = f32[5,1,16,128]{3,2,1,0:T(8,128)S(1)} fusion(f32[5,1,16,128]{3,2,1,0:T(8,128)S(1)} %constant_dynamic-update-slice_fusion.38, f32[5,1,16,128]{3,2,1,0:T(8,128)S(1)} %get-tuple-element.39, f32[]{:T(128)} %bitcast.52, f32[]{:T(128)} %bitcast.51, f32[]{:T(128)} %bitcast.50, f32[]{:T(128)} %bitcast.49, f32[]{:T(128)} %bitcast.48), kind=kLoop, calls=%fused_computation.85 | loop fusion | flops 18432 | bytes 49172 | tf_op jit(solution)/shard_map/stack | solution.py:165
  192.9 3.2 %constant_dynamic-update-slice_fusion.36 = f32[5,1,16,128]{3,2,1,0:T(8,128)S(1)} fusion(f32[5,1,16,128]{3,2,1,0:T(8,128)S(1)} %get-tuple-element.40, f32[]{:T(128)} %bitcast.6, f32[]{:T(128)} %bitcast.5, f32[]{:T(128)} %bitcast.4, f32[]{:T(128)} %bitcast.3, f32[]{:T(128)} %bitcast.1), kind=kLoop, calls=%fused_computation.84 | loop fusion | flops 18431 | bytes 49172
  196.0 3.2 %constant_dynamic-update-slice_fusion.35 = f32[5,1,16,128]{3,2,1,0:T(8,128)S(1)} fusion(f32[5,1,16,128]{3,2,1,0:T(8,128)S(1)} %constant_dynamic-update-slice_fusion.36, f32[5,1,16,128]{3,2,1,0:T(8,128)S(1)} %get-tuple-element.40, f32[]{:T(128)} %bitcast.11, f32[]{:T(128)} %bitcast.10, f32[]{:T(128)} %bitcast.9, f32[]{:T(128)} %bitcast.8, f32[]{:T(128)} %bitcast.7), kind=kLoop, calls=%fused_computation.83 | loop fusion | flops 18432 | bytes 49172
  202.3 3.1 %constant_dynamic-update-slice_fusion.33 = f32[5,1,16,128]{3,2,1,0:T(8,128)S(1)} fusion(f32[5,1,16,128]{3,2,1,0:T(8,128)S(1)} %constant_dynamic-update-slice_fusion.34, f32[5,1,16,128]{3,2,1,0:T(8,128)S(1)} %get-tuple-element.40, f32[]{:T(128)} %bitcast.21, f32[]{:T(128)} %bitcast.20, f32[]{:T(128)} %bitcast.19, f32[]{:T(128)} %bitcast.18, f32[]{:T(128)} %bitcast.17), kind=kLoop, calls=%fused_computation.81 | loop fusion | flops 18432 | bytes 49172
  205.5 3.1 %constant_dynamic-update-slice_fusion.32 = f32[5,1,16,128]{3,2,1,0:T(8,128)S(1)} fusion(f32[5,1,16,128]{3,2,1,0:T(8,128)S(1)} %constant_dynamic-update-slice_fusion.33, f32[5,1,16,128]{3,2,1,0:T(8,128)S(1)} %get-tuple-element.40, f32[]{:T(128)} %bitcast.26, f32[]{:T(128)} %bitcast.25, f32[]{:T(128)} %bitcast.24, f32[]{:T(128)} %bitcast.23, f32[]{:T(128)} %bitcast.22), kind=kLoop, calls=%fused_computation.80 | loop fusion | flops 18432 | bytes 49172 | tf_op jit(solution)/shard_map/stack | solution.py:165
  208.8 3.3 %multiply_add_fusion.3 = f32[1,4,16,128]{3,2,1,0:T(8,128)S(1)} fusion(f32[5,4,16,128]{3,2,1,0:T(8,128)S(1)} %fusion.17, f32[]{:T(128)} %bitcast.174, f32[]{:T(128)} %bitcast.173, f32[]{:T(128)} %bitcast.172, f32[]{:T(128)} %bitcast.171, f32[]{:T(128)} %bitcast.170), kind=kLoop, calls=%fused_computation.134 | loop fusion | flops 73728 | bytes 196628 | tf_op jit(solution)/shard_map/add | solution.py:163
  225.7 5.2 %collective-permute-done.7 = f32[4,4,3,3]{3,2,1,0:T(4,128)S(1)} collective-permute-done((f32[4,4,3,3]{3,2,1,0:T(4,128)S(1)}, f32[4,4,3,3]{3,2,1,0:T(4,128)S(1)}, u32[]{:S(2)}, u32[]{:S(2)}) %collective-permute-start.7) | collective-permute-done | bytes 608 | tf_op jit(solution)/shard_map/ppermute | solution.py:133
  235.0 4.2 %collective-permute-done.11 = f32[4,3,22,134]{3,2,1,0:T(8,128)S(1)} collective-permute-done((f32[4,3,22,134]{3,2,1,0:T(8,128)S(1)}, f32[4,3,22,134]{3,2,1,0:T(8,128)S(1)}, u32[]{:S(2)}, u32[]{:S(2)}) %collective-permute-start.11) | collective-permute-done | bytes 141536 | tf_op jit(solution)/shard_map/ppermute | solution.py:120
  243.4 7.0 %collective-permute-start.12 = (f32[3,128]{1,0:T(4,128)S(1)}, f32[3,128]{1,0:T(4,128)S(1)}, u32[]{:S(2)}, u32[]{:S(2)}) collective-permute-start(f32[3,128]{1,0:T(4,128)S(1)} %get-tuple-element.61), channel_id=1, source_target_pairs={{0,1},{1,2},{2,3},{4,5},{5,6},{6,7},{8,9},{9,10},{10,11},{12,13},{... | collective-permute-start | bytes 4616 | tf_op jit(solution)/shard_map/ppermute | solution.py:200
  252.2 3.9 %collective-permute-start.15 = (f32[3,128]{1,0:T(4,128)S(1)}, f32[3,128]{1,0:T(4,128)S(1)}, u32[]{:S(2)}, u32[]{:S(2)}) collective-permute-start(f32[3,128]{1,0:T(4,128)S(1)} %get-tuple-element.61), channel_id=1, source_target_pairs={{0,5},{1,6},{2,7},{4,1},{5,2},{6,3},{8,13},{9,14},{10,15},{12,9},{... | collective-permute-start | bytes 4616 | tf_op jit(solution)/shard_map/ppermute | solution.py:200
  257.5 3.6 %collective-permute-done.16 = f32[3,128]{1,0:T(4,128)S(1)} collective-permute-done((f32[3,128]{1,0:T(4,128)S(1)}, f32[3,128]{1,0:T(4,128)S(1)}, u32[]{:S(2)}, u32[]{:S(2)}) %collective-permute-start.16) | collective-permute-done | bytes 1568 | tf_op jit(solution)/shard_map/ppermute | solution.py:200
  (138 shorter events, 106.8 us)
Async XLA Ops:
  0.6 1.0 copy-start.2
  1.8 112.7 %collective-permute-start.4 = (f32[8,4,16,1]{3,2,1,0:T(8,128)S(1)}, f32[8,4,16,1]{3,2,1,0:T(8,128)S(1)}, u32[]{:S(2)}, u32[]{:S(2)}) collective-permute-start(f32[8,4,16,1]{3,2,1,0:T(8,128)S(1)} %get-tuple-element.27), channel_id=1, source_target_pairs={{0,8},{8,16},{16,24},{24,0},{1,9},{9,17},{17,25},{25,1},{2,10},{10... | collective-permute-start | bytes 6152 | tf_op jit(solution)/shard_map/ppermute | solution.py:120
  4.8 109.7 %collective-permute-start.3 = (f32[8,4,16,1]{3,2,1,0:T(8,128)S(1)}, f32[8,4,16,1]{3,2,1,0:T(8,128)S(1)}, u32[]{:S(2)}, u32[]{:S(2)}) collective-permute-start(f32[8,4,16,1]{3,2,1,0:T(8,128)S(1)} %get-tuple-element.28), channel_id=1, source_target_pairs={{0,24},{8,0},{16,8},{24,16},{1,25},{9,1},{17,9},{25,17},{2,26},{10... | collective-permute-start | bytes 6152 | tf_op jit(solution)/shard_map/ppermute | solution.py:120
  7.0 139.1 %collective-permute-start.2 = (f32[8,4,1,128]{3,2,1,0:T(1,128)S(1)}, f32[8,4,1,128]{3,2,1,0:T(1,128)S(1)}, u32[]{:S(2)}, u32[]{:S(2)}) collective-permute-start(f32[8,4,1,128]{3,2,1,0:T(1,128)S(1)} %broadcast_select_fusion.1), channel_id=1, source_target_pairs={{0,4},{4,0},{1,5},{5,1},{2,6},{6,2},{3,7},{7,3},{8,12},{12,8},{9,1... | collective-permute-start | bytes 49160 | tf_op jit(solution)/shard_map/ppermute | solution.py:133
  8.7 168.7 %collective-permute-start.1 = (f32[8,1,16,128]{3,2,1,0:T(8,128)S(1)}, f32[8,1,16,128]{3,2,1,0:T(8,128)S(1)}, u32[]{:S(2)}, u32[]{:S(2)}) collective-permute-start(f32[8,1,16,128]{3,2,1,0:T(8,128)S(1)} %get-tuple-element.29), channel_id=1, source_target_pairs={{0,1},{1,2},{2,3},{4,5},{5,6},{6,7},{8,9},{9,10},{10,11},{12,13},{... | collective-permute-start | bytes 196616 | tf_op jit(solution)/shard_map/ppermute | solution.py:120
  10.0 1.3 copy-start.7
  10.0 167.4 %collective-permute-start = (f32[8,1,16,128]{3,2,1,0:T(8,128)S(1)}, f32[8,1,16,128]{3,2,1,0:T(8,128)S(1)}, u32[]{:S(2)}, u32[]{:S(2)}) collective-permute-start(f32[8,1,16,128]{3,2,1,0:T(8,128)S(1)} %get-tuple-element.30), channel_id=1, source_target_pairs={{1,0},{2,1},{3,2},{5,4},{6,5},{7,6},{9,8},{10,9},{11,10},{13,12},{... | collective-permute-start | bytes 196616 | tf_op jit(solution)/shard_map/ppermute | solution.py:120
  11.4 1.4 copy-start.8
  11.4 8.3 %copy-start = (f32[5,4,16,128]{3,2,1,0:T(8,128)S(1)}, f32[5,4,16,128]{3,2,1,0:T(8,128)}, u32[]{:S(2)}) copy-start(f32[5,4,16,128]{3,2,1,0:T(8,128)} %param.9) | copy-start | bytes 491524
  110.6 3.1 %copy-start.6 = (f32[3,5]{1,0:T(4,128)S(1)}, f32[3,5]{1,0:T(4,128)}, u32[]{:S(2)}) copy-start(f32[3,5]{1,0:T(4,128)} %param.14) | copy-start | bytes 184
  189.7 18.9 %copy-start.4 = (f32[5,4,16,128]{3,2,1,0:T(8,128)S(1)}, f32[5,4,16,128]{3,2,1,0:T(8,128)}, u32[]{:S(2)}) copy-start(f32[5,4,16,128]{3,2,1,0:T(8,128)} %param.10) | copy-start | bytes 491524
  208.8 6.4 %copy-start.1 = (f32[5,4,16,128]{3,2,1,0:T(8,128)}, f32[5,4,16,128]{3,2,1,0:T(8,128)S(1)}, u32[]{:S(2)}) copy-start(f32[5,4,16,128]{3,2,1,0:T(8,128)S(1)} %fusion.17) | copy-start | bytes 491524
  215.2 3.0 %copy-start.3 = (f32[4,16,128]{2,1,0:T(8,128)S(1)}, f32[4,16,128]{2,1,0:T(8,128)}, u32[]{:S(2)}) copy-start(f32[4,16,128]{2,1,0:T(8,128)} %param.15) | copy-start | bytes 98308
  218.5 7.2 %collective-permute-start.5 = (f32[4,4,3,3]{3,2,1,0:T(4,128)S(1)}, f32[4,4,3,3]{3,2,1,0:T(4,128)S(1)}, u32[]{:S(2)}, u32[]{:S(2)}) collective-permute-start(f32[4,4,3,3]{3,2,1,0:T(4,128)S(1)} %get-tuple-element.43), channel_id=1, source_target_pairs={{0,12},{8,20},{16,28},{24,4},{4,8},{12,16},{20,24},{28,0},{1,13},{... | collective-permute-start | bytes 1736 | tf_op jit(solution)/shard_map/ppermute | solution.py:133
  218.6 12.4 %collective-permute-start.8 = (f32[4,4,16,3]{3,2,1,0:T(8,128)S(1)}, f32[4,4,16,3]{3,2,1,0:T(8,128)S(1)}, u32[]{:S(2)}, u32[]{:S(2)}) collective-permute-start(f32[4,4,16,3]{3,2,1,0:T(8,128)S(1)} %get-tuple-element.41), channel_id=1, source_target_pairs={{0,8},{8,16},{16,24},{24,0},{1,9},{9,17},{17,25},{25,1},{2,10},{10... | collective-permute-start | bytes 9224 | tf_op jit(solution)/shard_map/ppermute | solution.py:120
  219.9 11.1 %collective-permute-start.9 = (f32[4,4,16,3]{3,2,1,0:T(8,128)S(1)}, f32[4,4,16,3]{3,2,1,0:T(8,128)S(1)}, u32[]{:S(2)}, u32[]{:S(2)}) collective-permute-start(f32[4,4,16,3]{3,2,1,0:T(8,128)S(1)} %get-tuple-element.42), channel_id=1, source_target_pairs={{0,24},{8,0},{16,8},{24,16},{1,25},{9,1},{17,9},{25,17},{2,26},{10... | collective-permute-start | bytes 9224 | tf_op jit(solution)/shard_map/ppermute | solution.py:120
  222.4 8.5 %collective-permute-start.7 = (f32[4,4,3,3]{3,2,1,0:T(4,128)S(1)}, f32[4,4,3,3]{3,2,1,0:T(4,128)S(1)}, u32[]{:S(2)}, u32[]{:S(2)}) collective-permute-start(f32[4,4,3,3]{3,2,1,0:T(4,128)S(1)} %get-tuple-element.44), channel_id=1, source_target_pairs={{0,28},{8,4},{16,12},{24,20},{4,24},{12,0},{20,8},{28,16},{1,29},{... | collective-permute-start | bytes 1736 | tf_op jit(solution)/shard_map/ppermute | solution.py:133
  225.3 5.6 %collective-permute-start.6 = (f32[4,4,3,128]{3,2,1,0:T(4,128)S(1)}, f32[4,4,3,128]{3,2,1,0:T(4,128)S(1)}, u32[]{:S(2)}, u32[]{:S(2)}) collective-permute-start(f32[4,4,3,128]{3,2,1,0:T(4,128)S(1)} %slice_select_fusion.1), channel_id=1, source_target_pairs={{0,4},{4,0},{1,5},{5,1},{2,6},{6,2},{3,7},{7,3},{8,12},{12,8},{9,1... | collective-permute-start | bytes 73736 | tf_op jit(solution)/shard_map/ppermute | solution.py:133
  231.4 3.6 %copy-start.9 = (s32[4,128]{1,0:T(4,128)S(1)}, s32[4,128]{1,0:T(4,128)}, u32[]{:S(2)}) copy-start(s32[4,128]{1,0:T(4,128)} %param.17) | copy-start | bytes 6148
  231.4 3.6 %collective-permute-start.10 = (f32[4,3,22,134]{3,2,1,0:T(8,128)S(1)}, f32[4,3,22,134]{3,2,1,0:T(8,128)S(1)}, u32[]{:S(2)}, u32[]{:S(2)}) collective-permute-start(f32[4,3,22,134]{3,2,1,0:T(8,128)S(1)} %get-tuple-element.25), channel_id=1, source_target_pairs={{0,1},{1,2},{2,3},{4,5},{5,6},{6,7},{8,9},{9,10},{10,11},{12,13},{... | collective-permute-start | bytes 424520 | tf_op jit(solution)/shard_map/ppermute | solution.py:120
  233.6 5.5 %collective-permute-start.11 = (f32[4,3,22,134]{3,2,1,0:T(8,128)S(1)}, f32[4,3,22,134]{3,2,1,0:T(8,128)S(1)}, u32[]{:S(2)}, u32[]{:S(2)}) collective-permute-start(f32[4,3,22,134]{3,2,1,0:T(8,128)S(1)} %get-tuple-element.26), channel_id=1, source_target_pairs={{1,0},{2,1},{3,2},{5,4},{6,5},{7,6},{9,8},{10,9},{11,10},{13,12},{... | collective-permute-start | bytes 424520 | tf_op jit(solution)/shard_map/ppermute | solution.py:120
  241.2 0.9 copy-start.5
  243.4 14.0 %collective-permute-start.12 = (f32[3,128]{1,0:T(4,128)S(1)}, f32[3,128]{1,0:T(4,128)S(1)}, u32[]{:S(2)}, u32[]{:S(2)}) collective-permute-start(f32[3,128]{1,0:T(4,128)S(1)} %get-tuple-element.61), channel_id=1, source_target_pairs={{0,1},{1,2},{2,3},{4,5},{5,6},{6,7},{8,9},{9,10},{10,11},{12,13},{... | collective-permute-start | bytes 4616 | tf_op jit(solution)/shard_map/ppermute | solution.py:200
  250.4 7.1 %collective-permute-start.13 = (f32[3,128]{1,0:T(4,128)S(1)}, f32[3,128]{1,0:T(4,128)S(1)}, u32[]{:S(2)}, u32[]{:S(2)}) collective-permute-start(f32[3,128]{1,0:T(4,128)S(1)} %get-tuple-element.60), channel_id=1, source_target_pairs={{1,0},{2,1},{3,2},{5,4},{6,5},{7,6},{9,8},{10,9},{11,10},{13,12},{... | collective-permute-start | bytes 4616 | tf_op jit(solution)/shard_map/ppermute | solution.py:200
  251.7 5.8 %collective-permute-start.14 = (f32[3,128]{1,0:T(4,128)S(1)}, f32[3,128]{1,0:T(4,128)S(1)}, u32[]{:S(2)}, u32[]{:S(2)}) collective-permute-start(f32[3,128]{1,0:T(4,128)S(1)} %get-tuple-element.59), channel_id=1, source_target_pairs={{0,4},{4,0},{1,5},{5,1},{2,6},{6,2},{3,7},{7,3},{8,12},{12,8},{9,1... | collective-permute-start | bytes 4616 | tf_op jit(solution)/shard_map/ppermute | solution.py:200
  252.2 5.2 %collective-permute-start.15 = (f32[3,128]{1,0:T(4,128)S(1)}, f32[3,128]{1,0:T(4,128)S(1)}, u32[]{:S(2)}, u32[]{:S(2)}) collective-permute-start(f32[3,128]{1,0:T(4,128)S(1)} %get-tuple-element.61), channel_id=1, source_target_pairs={{0,5},{1,6},{2,7},{4,1},{5,2},{6,3},{8,13},{9,14},{10,15},{12,9},{... | collective-permute-start | bytes 4616 | tf_op jit(solution)/shard_map/ppermute | solution.py:200
  256.1 4.9 %collective-permute-start.16 = (f32[3,128]{1,0:T(4,128)S(1)}, f32[3,128]{1,0:T(4,128)S(1)}, u32[]{:S(2)}, u32[]{:S(2)}) collective-permute-start(f32[3,128]{1,0:T(4,128)S(1)} %get-tuple-element.60), channel_id=1, source_target_pairs={{1,4},{2,5},{3,6},{5,0},{6,1},{7,2},{9,12},{10,13},{11,14},{13,8},... | collective-permute-start | bytes 4616 | tf_op jit(solution)/shard_map/ppermute | solution.py:200
  261.0 5.4 %collective-permute-start.17 = (f32[3,128]{1,0:T(4,128)S(1)}, f32[3,128]{1,0:T(4,128)S(1)}, u32[]{:S(2)}, u32[]{:S(2)}) collective-permute-start(f32[3,128]{1,0:T(4,128)S(1)} %add_add_fusion.1), channel_id=1, source_target_pairs={{0,8},{8,16},{16,24},{24,0},{1,9},{9,17},{17,25},{25,1},{2,10},{10... | collective-permute-start | bytes 4616 | tf_op jit(solution)/shard_map/ppermute | solution.py:200
  262.0 4.5 %collective-permute-start.18 = (f32[3,128]{1,0:T(4,128)S(1)}, f32[3,128]{1,0:T(4,128)S(1)}, u32[]{:S(2)}, u32[]{:S(2)}) collective-permute-start(f32[3,128]{1,0:T(4,128)S(1)} %add_add_fusion.1), channel_id=1, source_target_pairs={{0,16},{8,24},{16,0},{24,8},{1,17},{9,25},{17,1},{25,9},{2,18},{10... | collective-permute-start | bytes 4616 | tf_op jit(solution)/shard_map/ppermute | solution.py:200
  264.1 3.6 %collective-permute-start.19 = (f32[3,128]{1,0:T(4,128)S(1)}, f32[3,128]{1,0:T(4,128)S(1)}, u32[]{:S(2)}, u32[]{:S(2)}) collective-permute-start(f32[3,128]{1,0:T(4,128)S(1)} %add_add_fusion.1), channel_id=1, source_target_pairs={{0,24},{8,0},{16,8},{24,16},{1,25},{9,1},{17,9},{25,17},{2,26},{10... | collective-permute-start | bytes 4616 | tf_op jit(solution)/shard_map/ppermute | solution.py:200

commit v6 on v4

--- a/solution.py
+++ b/solution.py
@@ -156,7 +156,8 @@
 
 
 def jac_apply(jac, term):
-    return jnp.einsum("uv,ukji->vkji", jac, term, precision=lax.Precision.HIGHEST)
+    spread = (slice(None), slice(None)) + (None,) * (term.ndim - 1)
+    return jnp.sum(jac[spread] * term[:, None], axis=0)
 
 
 def flux_faces(stacked, halos, owner_jac, neighbor_jac):
@@ -227,7 +228,7 @@
         face_halos(stacked, "circ", 3, True),
     ]
     residual = flux_faces(stacked, halos, owner_jac, neighbor_jac) + adjoint - objective_grad
-    forcing = jnp.einsum("mv,vkji->mkji", coupling, residual, precision=lax.Precision.HIGHEST)
+    forcing = jac_apply(coupling.T, residual)
     margin = SWEEPS - 1
     joined = jnp.concatenate([stiffness[None], forcing], axis=0)
     full_pad = padded_sweeps(joined, margin)

time: 82.6 us -> 75.9 us (0.919)
  matrix products: 4.57 us -> 0.41 us
  starting transfers between devices: 42.2 us -> 38.6 us
  waiting for transfers between devices: 19.4 us -> 22.1 us
  other arithmetic: 8.51 us -> 7.07 us
    ppermute x4, waiting for transfers between devices: 0.01 us -> 4.37 us  [receive_pair(): got = lax.ppermute(sent, axes, pairs + back)]
    dot_general x13 -> x0, matrix products: 4.16 us -> none  [the longest x12 3.82 us: jac_apply(): jnp.einsum('uv,ukji->vkji', jac, term, precision=lax.Precision.HIGHEST)]
    mul x3, other arithmetic: 4.64 us -> 2.17 us  [relax(): weighted = stiff_pad[None] * mesh_pad]
    ppermute x8, waiting for transfers between devices: 15.2 us -> 12.8 us  [receive(): return lax.ppermute(take(array, rel, dims, width), axes, pairs)]
    ppermute x4, starting transfers between devices: 8.52 us -> 6.66 us  [receive_pair(): got = lax.ppermute(sent, axes, pairs + back)]
    ppermute x8, starting transfers between devices: 20.5 us -> 18.8 us  [shifted(): return lax.ppermute(array, axes, pairs)]
    reduce_sum x0 -> x9, other arithmetic: none -> 1.47 us  [jac_apply(): return jnp.sum(jac[spread] * term[:, None], axis=0)]
    unnamed x22 -> x23, local copies, waits for them, and re-layouts: 4.56 us -> 4.48 us
  transfers between devices with their start and end apart: 20 -> 20, of which waited for: 7 -> 7; matrix products, arithmetic and copies ran while one was open for 8% -> 4% of each run, Pallas kernels for 0% -> 0%
where the time goes in v6:
time: 75.9 us; the launch traced here: 74.9 us
  starting transfers between devices  38.6 us (51%)
  waiting for transfers between devices  22.1 us (29%)
  other arithmetic  7.07 us (9%)
  local copies, waits for them, and re-layouts  5.53 us (7%)
  between operations  1.24 us (2%)
    ppermute x8, starting transfers between devices, shifted(): return lax.ppermute(array, axes, pairs)  18.8 us
    ppermute x8, starting transfers between devices, receive(): return lax.ppermute(take(array, rel, dims, width), axes, pairs)  13.1 us
    ppermute x8, waiting for transfers between devices, receive(): return lax.ppermute(take(array, rel, dims, width), axes, pairs)  12.8 us
    ppermute x4, starting transfers between devices, receive_pair(): got = lax.ppermute(sent, axes, pairs + back)  6.66 us
    ppermute x8, waiting for transfers between devices, shifted(): return lax.ppermute(array, axes, pairs)  4.88 us
    unnamed x23, local copies, waits for them, and re-layouts  4.48 us
    ppermute x4, waiting for transfers between devices, receive_pair(): got = lax.ppermute(sent, axes, pairs + back)  4.37 us
    mul x3, other arithmetic, relax(): weighted = stiff_pad[None] * mesh_pad  2.17 us
  transfers between devices with their start and end apart: 20, of which 7 were waited for; matrix products, arithmetic and copies ran while one was open for 4% of the time, Pallas kernels for 0%

profile of v6, /device:TPU:0, one launch (start us, length us, event | category | flops | bytes accessed | tf_op | source)
XLA Modules:
  0.0 74.9 jit_solution(10996328793198828664)
XLA Ops:
  0.6 1.0 %constant_dynamic-update-slice_fusion.1 = f32[8,4,16,128]{3,2,1,0:T(8,128)S(1)} fusion(f32[5,4,16,128]{3,2,1,0:T(8,128)} %param.9), kind=kLoop, calls=%fused_computation.128 | loop fusion | bytes 327680
  1.7 3.0 %collective-permute-start.2 = (f32[8,4,1,128]{3,2,1,0:T(1,128)S(1)}, f32[8,4,1,128]{3,2,1,0:T(1,128)S(1)}, u32[]{:S(2)}, u32[]{:S(2)}) collective-permute-start(f32[8,4,1,128]{3,2,1,0:T(1,128)S(1)} %broadcast_select_fusion.1), channel_id=1, source_target_pairs={{0,4},{4,0},{1,5},{5,1},{2,6},{6,2},{3,7},{7,3},{8,12},{12,8},{9,1... | collective-permute-start | bytes 49160 | tf_op jit(solution)/shard_map/ppermute | solution.py:133
  4.7 1.5 %collective-permute-start.1 = (f32[8,1,16,128]{3,2,1,0:T(8,128)S(1)}, f32[8,1,16,128]{3,2,1,0:T(8,128)S(1)}, u32[]{:S(2)}, u32[]{:S(2)}) collective-permute-start(f32[8,1,16,128]{3,2,1,0:T(8,128)S(1)} %get-tuple-element.37), channel_id=1, source_target_pairs={{0,1},{1,2},{2,3},{4,5},{5,6},{6,7},{8,9},{9,10},{10,11},{12,13},{... | collective-permute-start | bytes 196616 | tf_op jit(solution)/shard_map/ppermute | solution.py:120
  6.2 1.3 %collective-permute-start = (f32[8,1,16,128]{3,2,1,0:T(8,128)S(1)}, f32[8,1,16,128]{3,2,1,0:T(8,128)S(1)}, u32[]{:S(2)}, u32[]{:S(2)}) collective-permute-start(f32[8,1,16,128]{3,2,1,0:T(8,128)S(1)} %get-tuple-element.38), channel_id=1, source_target_pairs={{1,0},{2,1},{3,2},{5,4},{6,5},{7,6},{9,8},{10,9},{11,10},{13,12},{... | collective-permute-start | bytes 196616 | tf_op jit(solution)/shard_map/ppermute | solution.py:120
  7.6 1.6 %collective-permute-start.4 = (f32[8,4,16,1]{3,2,1,0:T(8,128)S(1)}, f32[8,4,16,1]{3,2,1,0:T(8,128)S(1)}, u32[]{:S(2)}, u32[]{:S(2)}) collective-permute-start(f32[8,4,16,1]{3,2,1,0:T(8,128)S(1)} %get-tuple-element.36), channel_id=1, source_target_pairs={{0,8},{8,16},{16,24},{24,0},{1,9},{9,17},{17,25},{25,1},{2,10},{10... | collective-permute-start | bytes 6152 | tf_op jit(solution)/shard_map/ppermute | solution.py:120
  9.3 2.2 %collective-permute-start.3 = (f32[8,4,16,1]{3,2,1,0:T(8,128)S(1)}, f32[8,4,16,1]{3,2,1,0:T(8,128)S(1)}, u32[]{:S(2)}, u32[]{:S(2)}) collective-permute-start(f32[8,4,16,1]{3,2,1,0:T(8,128)S(1)} %get-tuple-element.35), channel_id=1, source_target_pairs={{0,24},{8,0},{16,8},{24,16},{1,25},{9,1},{17,9},{25,17},{2,26},{10... | collective-permute-start | bytes 6152 | tf_op jit(solution)/shard_map/ppermute | solution.py:120
  11.5 0.7 copy-done.6
  12.2 0.7 copy-done.7
  13.2 0.5 multiply_reduce_fusion.2
  13.7 0.2 multiply_reduce_fusion
  14.0 0.1 multiply_reduce_fusion.4
  14.1 0.2 slice_reduce_fusion.1
  14.3 0.7 copy-done.8
  15.1 1.9 %collective-permute-done.4 = f32[8,4,16,1]{3,2,1,0:T(8,128)S(1)} collective-permute-done((f32[8,4,16,1]{3,2,1,0:T(8,128)S(1)}, f32[8,4,16,1]{3,2,1,0:T(8,128)S(1)}, u32[]{:S(2)}, u32[]{:S(2)}) %collective-permute-start.4) | collective-permute-done | bytes 2080 | tf_op jit(solution)/shard_map/ppermute | solution.py:120
  17.1 6.7 %collective-permute-done.3 = f32[8,4,16,1]{3,2,1,0:T(8,128)S(1)} collective-permute-done((f32[8,4,16,1]{3,2,1,0:T(8,128)S(1)}, f32[8,4,16,1]{3,2,1,0:T(8,128)S(1)}, u32[]{:S(2)}, u32[]{:S(2)}) %collective-permute-start.3) | collective-permute-done | bytes 2080 | tf_op jit(solution)/shard_map/ppermute | solution.py:120
  23.7 0.3 fusion.11
  24.2 0.2 copy.47
  24.4 0.2 copy.48
  25.1 0.7 copy-done.4
  25.9 0.2 fusion.19
  26.2 0.7 copy-done.1
  27.1 0.8 %collective-permute-start.5 = (f32[4,4,3,3]{3,2,1,0:T(4,128)S(1)}, f32[4,4,3,3]{3,2,1,0:T(4,128)S(1)}, u32[]{:S(2)}, u32[]{:S(2)}) collective-permute-start(f32[4,4,3,3]{3,2,1,0:T(4,128)S(1)} %get-tuple-element.49), channel_id=1, source_target_pairs={{0,12},{8,20},{16,28},{24,4},{4,8},{12,16},{20,24},{28,0},{1,13},{... | collective-permute-start | bytes 1736 | tf_op jit(solution)/shard_map/ppermute | solution.py:133
  27.9 0.3 collective-permute-start.8
  28.2 3.6 %collective-permute-start.9 = (f32[4,4,16,3]{3,2,1,0:T(8,128)S(1)}, f32[4,4,16,3]{3,2,1,0:T(8,128)S(1)}, u32[]{:S(2)}, u32[]{:S(2)}) collective-permute-start(f32[4,4,16,3]{3,2,1,0:T(8,128)S(1)} %get-tuple-element.48), channel_id=1, source_target_pairs={{0,24},{8,0},{16,8},{24,16},{1,25},{9,1},{17,9},{25,17},{2,26},{10... | collective-permute-start | bytes 9224 | tf_op jit(solution)/shard_map/ppermute | solution.py:120
  31.8 2.2 %collective-permute-start.7 = (f32[4,4,3,3]{3,2,1,0:T(4,128)S(1)}, f32[4,4,3,3]{3,2,1,0:T(4,128)S(1)}, u32[]{:S(2)}, u32[]{:S(2)}) collective-permute-start(f32[4,4,3,3]{3,2,1,0:T(4,128)S(1)} %get-tuple-element.50), channel_id=1, source_target_pairs={{0,28},{8,4},{16,12},{24,20},{4,24},{12,0},{20,8},{28,16},{1,29},{... | collective-permute-start | bytes 1736 | tf_op jit(solution)/shard_map/ppermute | solution.py:133
  33.9 0.6 collective-permute-start.6
  34.6 4.4 %collective-permute-done.7 = f32[4,4,3,3]{3,2,1,0:T(4,128)S(1)} collective-permute-done((f32[4,4,3,3]{3,2,1,0:T(4,128)S(1)}, f32[4,4,3,3]{3,2,1,0:T(4,128)S(1)}, u32[]{:S(2)}, u32[]{:S(2)}) %collective-permute-start.7) | collective-permute-done | bytes 608 | tf_op jit(solution)/shard_map/ppermute | solution.py:133
  39.0 0.3 maximum_maximum_fusion
  39.4 1.3 %collective-permute-start.10 = (f32[4,3,22,134]{3,2,1,0:T(8,128)S(1)}, f32[4,3,22,134]{3,2,1,0:T(8,128)S(1)}, u32[]{:S(2)}, u32[]{:S(2)}) collective-permute-start(f32[4,3,22,134]{3,2,1,0:T(8,128)S(1)} %get-tuple-element.33), channel_id=1, source_target_pairs={{0,1},{1,2},{2,3},{4,5},{5,6},{6,7},{8,9},{9,10},{10,11},{12,13},{... | collective-permute-start | bytes 424520 | tf_op jit(solution)/shard_map/ppermute | solution.py:120
  40.7 1.3 %collective-permute-start.11 = (f32[4,3,22,134]{3,2,1,0:T(8,128)S(1)}, f32[4,3,22,134]{3,2,1,0:T(8,128)S(1)}, u32[]{:S(2)}, u32[]{:S(2)}) collective-permute-start(f32[4,3,22,134]{3,2,1,0:T(8,128)S(1)} %get-tuple-element.34), channel_id=1, source_target_pairs={{1,0},{2,1},{3,2},{5,4},{6,5},{7,6},{9,8},{10,9},{11,10},{13,12},{... | collective-permute-start | bytes 424520 | tf_op jit(solution)/shard_map/ppermute | solution.py:120
  42.1 4.3 %collective-permute-done.11 = f32[4,3,22,134]{3,2,1,0:T(8,128)S(1)} collective-permute-done((f32[4,3,22,134]{3,2,1,0:T(8,128)S(1)}, f32[4,3,22,134]{3,2,1,0:T(8,128)S(1)}, u32[]{:S(2)}, u32[]{:S(2)}) %collective-permute-start.11) | collective-permute-done | bytes 141536 | tf_op jit(solution)/shard_map/ppermute | solution.py:120
  46.3 0.3 pad_maximum_fusion
  47.2 1.2 %broadcast_multiply_fusion.1 = (f32[3,8,20,132]{3,2,1,0:T(8,128)S(1)}, f32[3,8,20,132]{3,2,1,0:T(8,128)S(1)}) fusion(f32[8,20,132]{2,1,0:T(8,128)S(1)} %get-tuple-element.42, f32[3,10,22,134]{3,2,1,0:T(8,128)S(1)} %get-tuple-element.29, f32[8,20,132]{2,1,0:T(8,128)S(1)} %get-tuple-element.41, f32[4,10,22,134]{3,2,1,0:T(8,128)S(1)} %pad_maximum_fusion, ...), kind=kLoop, calls=%fused_computation.42 | loop fusion | flops 760320 | bytes 2703360 | tf_op jit(solution)/shard_map/mul | solution.py:60
  48.4 0.9 %broadcast_multiply_fusion.2 = (f32[3,6,18,130]{3,2,1,0:T(8,128)S(1)}, f32[3,6,18,130]{3,2,1,0:T(8,128)S(1)}) fusion(f32[6,18,130]{2,1,0:T(8,128)S(1)} %get-tuple-element.40, f32[3,8,20,132]{3,2,1,0:T(8,128)S(1)} %get-tuple-element.27, f32[6,18,130]{2,1,0:T(8,128)S(1)} %get-tuple-element.39, f32[4,10,22,134]{3,2,1,0:T(8,128)S(1)} %pad_maximum_fusion, ...), kind=kLoop, calls=%fused_computation.45 | loop fusion | flops 505440 | bytes 1797120 | tf_op jit(solution)/shard_map/mul | solution.py:60
  49.3 0.9 %multiply_reduce_fusion.9 = (f32[3,4,128]{2,1,0:T(4,128)S(1)}, f32[3,4,16,128]{3,2,1,0:T(8,128)}) fusion(f32[4,16,128]{2,1,0:T(8,128)S(1)} %copy-done.5, f32[3,6,18,130]{3,2,1,0:T(8,128)S(1)} %get-tuple-element.25, f32[3,4,16,128]{3,2,1,0:T(8,128)S(1)} %multiply_reduce_fusion.6, f32[4,16,128]{2,1,0:T(8,128)S(1)} %fusion.38, ...), kind=kLoop, calls=%fused_computation.84 | loop fusion | flops 317952 | bytes 956416 | tf_op jit(solution)/shard_map/reduce_sum | solution.py:236
  50.1 0.4 convolution_bitcast_fusion
  50.6 7.0 %collective-permute-start.12 = (f32[3,128]{1,0:T(4,128)S(1)}, f32[3,128]{1,0:T(4,128)S(1)}, u32[]{:S(2)}, u32[]{:S(2)}) collective-permute-start(f32[3,128]{1,0:T(4,128)S(1)} %get-tuple-element.67), channel_id=1, source_target_pairs={{0,1},{1,2},{2,3},{4,5},{5,6},{6,7},{8,9},{9,10},{10,11},{12,13},{... | collective-permute-start | bytes 4616 | tf_op jit(solution)/shard_map/ppermute | solution.py:195
  57.5 1.3 %collective-permute-start.13 = (f32[3,128]{1,0:T(4,128)S(1)}, f32[3,128]{1,0:T(4,128)S(1)}, u32[]{:S(2)}, u32[]{:S(2)}) collective-permute-start(f32[3,128]{1,0:T(4,128)S(1)} %get-tuple-element.66), channel_id=1, source_target_pairs={{1,0},{2,1},{3,2},{5,4},{6,5},{7,6},{9,8},{10,9},{11,10},{13,12},{... | collective-permute-start | bytes 4616 | tf_op jit(solution)/shard_map/ppermute | solution.py:195
  58.8 0.6 collective-permute-start.14
  59.4 3.9 %collective-permute-start.15 = (f32[3,128]{1,0:T(4,128)S(1)}, f32[3,128]{1,0:T(4,128)S(1)}, u32[]{:S(2)}, u32[]{:S(2)}) collective-permute-start(f32[3,128]{1,0:T(4,128)S(1)} %get-tuple-element.67), channel_id=1, source_target_pairs={{0,5},{1,6},{2,7},{4,1},{5,2},{6,3},{8,13},{9,14},{10,15},{12,9},{... | collective-permute-start | bytes 4616 | tf_op jit(solution)/shard_map/ppermute | solution.py:195
  63.3 1.3 %collective-permute-start.16 = (f32[3,128]{1,0:T(4,128)S(1)}, f32[3,128]{1,0:T(4,128)S(1)}, u32[]{:S(2)}, u32[]{:S(2)}) collective-permute-start(f32[3,128]{1,0:T(4,128)S(1)} %get-tuple-element.66), channel_id=1, source_target_pairs={{1,4},{2,5},{3,6},{5,0},{6,1},{7,2},{9,12},{10,13},{11,14},{13,8},... | collective-permute-start | bytes 4616 | tf_op jit(solution)/shard_map/ppermute | solution.py:195
  64.6 3.6 %collective-permute-done.16 = f32[3,128]{1,0:T(4,128)S(1)} collective-permute-done((f32[3,128]{1,0:T(4,128)S(1)}, f32[3,128]{1,0:T(4,128)S(1)}, u32[]{:S(2)}, u32[]{:S(2)}) %collective-permute-start.16) | collective-permute-done | bytes 1568 | tf_op jit(solution)/shard_map/ppermute | solution.py:195
  68.2 0.6 collective-permute-start.17
  68.8 1.8 %collective-permute-start.18 = (f32[3,128]{1,0:T(4,128)S(1)}, f32[3,128]{1,0:T(4,128)S(1)}, u32[]{:S(2)}, u32[]{:S(2)}) collective-permute-start(f32[3,128]{1,0:T(4,128)S(1)} %add_add_fusion.1), channel_id=1, source_target_pairs={{0,16},{8,24},{16,0},{24,8},{1,17},{9,25},{17,1},{25,9},{2,18},{10... | collective-permute-start | bytes 4616 | tf_op jit(solution)/shard_map/ppermute | solution.py:195
  70.6 2.4 %collective-permute-start.19 = (f32[3,128]{1,0:T(4,128)S(1)}, f32[3,128]{1,0:T(4,128)S(1)}, u32[]{:S(2)}, u32[]{:S(2)}) collective-permute-start(f32[3,128]{1,0:T(4,128)S(1)} %add_add_fusion.1), channel_id=1, source_target_pairs={{0,24},{8,0},{16,8},{24,16},{1,25},{9,1},{17,9},{25,17},{2,26},{10... | collective-permute-start | bytes 4616 | tf_op jit(solution)/shard_map/ppermute | solution.py:195
  73.0 0.5 collective-permute-done.17
  73.6 0.8 %collective-permute-done.19 = f32[3,128]{1,0:T(4,128)S(1)} collective-permute-done((f32[3,128]{1,0:T(4,128)S(1)}, f32[3,128]{1,0:T(4,128)S(1)}, u32[]{:S(2)}, u32[]{:S(2)}) %collective-permute-start.19) | collective-permute-done | bytes 1568 | tf_op jit(solution)/shard_map/ppermute | solution.py:195
  74.3 0.6 add_add_fusion
  (76 shorter events, 2.2 us)
Async XLA Ops:
  0.6 1.0 %copy-start.3 = (f32[3,4,16,128]{3,2,1,0:T(8,128)S(1)}, f32[3,4,16,128]{3,2,1,0:T(8,128)}, u32[]{:S(2)}) copy-start(f32[3,4,16,128]{3,2,1,0:T(8,128)} %param.11) | copy-start | bytes 294916
  1.7 23.0 %collective-permute-start.2 = (f32[8,4,1,128]{3,2,1,0:T(1,128)S(1)}, f32[8,4,1,128]{3,2,1,0:T(1,128)S(1)}, u32[]{:S(2)}, u32[]{:S(2)}) collective-permute-start(f32[8,4,1,128]{3,2,1,0:T(1,128)S(1)} %broadcast_select_fusion.1), channel_id=1, source_target_pairs={{0,4},{4,0},{1,5},{5,1},{2,6},{6,2},{3,7},{7,3},{8,12},{12,8},{9,1... | collective-permute-start | bytes 49160 | tf_op jit(solution)/shard_map/ppermute | solution.py:133
  4.7 20.2 %collective-permute-start.1 = (f32[8,1,16,128]{3,2,1,0:T(8,128)S(1)}, f32[8,1,16,128]{3,2,1,0:T(8,128)S(1)}, u32[]{:S(2)}, u32[]{:S(2)}) collective-permute-start(f32[8,1,16,128]{3,2,1,0:T(8,128)S(1)} %get-tuple-element.37), channel_id=1, source_target_pairs={{0,1},{1,2},{2,3},{4,5},{5,6},{6,7},{8,9},{9,10},{10,11},{12,13},{... | collective-permute-start | bytes 196616 | tf_op jit(solution)/shard_map/ppermute | solution.py:120
  6.2 18.8 %collective-permute-start = (f32[8,1,16,128]{3,2,1,0:T(8,128)S(1)}, f32[8,1,16,128]{3,2,1,0:T(8,128)S(1)}, u32[]{:S(2)}, u32[]{:S(2)}) collective-permute-start(f32[8,1,16,128]{3,2,1,0:T(8,128)S(1)} %get-tuple-element.38), channel_id=1, source_target_pairs={{1,0},{2,1},{3,2},{5,4},{6,5},{7,6},{9,8},{10,9},{11,10},{13,12},{... | collective-permute-start | bytes 196616 | tf_op jit(solution)/shard_map/ppermute | solution.py:120
  7.6 5.3 %copy-start = (f32[5,4,16,128]{3,2,1,0:T(8,128)S(1)}, f32[5,4,16,128]{3,2,1,0:T(8,128)}, u32[]{:S(2)}) copy-start(f32[5,4,16,128]{3,2,1,0:T(8,128)} %param.9) | copy-start | bytes 491524
  7.6 9.3 %collective-permute-start.4 = (f32[8,4,16,1]{3,2,1,0:T(8,128)S(1)}, f32[8,4,16,1]{3,2,1,0:T(8,128)S(1)}, u32[]{:S(2)}, u32[]{:S(2)}) collective-permute-start(f32[8,4,16,1]{3,2,1,0:T(8,128)S(1)} %get-tuple-element.36), channel_id=1, source_target_pairs={{0,8},{8,16},{16,24},{24,0},{1,9},{9,17},{17,25},{25,1},{2,10},{10... | collective-permute-start | bytes 6152 | tf_op jit(solution)/shard_map/ppermute | solution.py:120
  9.3 14.5 %collective-permute-start.3 = (f32[8,4,16,1]{3,2,1,0:T(8,128)S(1)}, f32[8,4,16,1]{3,2,1,0:T(8,128)S(1)}, u32[]{:S(2)}, u32[]{:S(2)}) collective-permute-start(f32[8,4,16,1]{3,2,1,0:T(8,128)S(1)} %get-tuple-element.35), channel_id=1, source_target_pairs={{0,24},{8,0},{16,8},{24,16},{1,25},{9,1},{17,9},{25,17},{2,26},{10... | collective-permute-start | bytes 6152 | tf_op jit(solution)/shard_map/ppermute | solution.py:120
  11.5 0.7 copy-start.6
  12.2 0.7 copy-start.7
  14.3 0.7 copy-start.8
  24.9 0.9 %copy-start.4 = (f32[5,4,16,128]{3,2,1,0:T(8,128)S(1)}, f32[5,4,16,128]{3,2,1,0:T(8,128)}, u32[]{:S(2)}) copy-start(f32[5,4,16,128]{3,2,1,0:T(8,128)} %param.10) | copy-start | bytes 491524
  26.0 0.9 %copy-start.2 = (f32[5,4,16,128]{3,2,1,0:T(8,128)}, f32[5,4,16,128]{3,2,1,0:T(8,128)S(1)}, u32[]{:S(2)}) copy-start(f32[5,4,16,128]{3,2,1,0:T(8,128)S(1)} %fusion.19) | copy-start | bytes 491524
  26.0 0.8 %copy-start.1 = (f32[4,16,128]{2,1,0:T(8,128)S(1)}, f32[4,16,128]{2,1,0:T(8,128)}, u32[]{:S(2)}) copy-start(f32[4,16,128]{2,1,0:T(8,128)} %param.15) | copy-start | bytes 98308
  27.1 7.5 %collective-permute-start.5 = (f32[4,4,3,3]{3,2,1,0:T(4,128)S(1)}, f32[4,4,3,3]{3,2,1,0:T(4,128)S(1)}, u32[]{:S(2)}, u32[]{:S(2)}) collective-permute-start(f32[4,4,3,3]{3,2,1,0:T(4,128)S(1)} %get-tuple-element.49), channel_id=1, source_target_pairs={{0,12},{8,20},{16,28},{24,4},{4,8},{12,16},{20,24},{28,0},{1,13},{... | collective-permute-start | bytes 1736 | tf_op jit(solution)/shard_map/ppermute | solution.py:133
  27.9 11.1 %collective-permute-start.8 = (f32[4,4,16,3]{3,2,1,0:T(8,128)S(1)}, f32[4,4,16,3]{3,2,1,0:T(8,128)S(1)}, u32[]{:S(2)}, u32[]{:S(2)}) collective-permute-start(f32[4,4,16,3]{3,2,1,0:T(8,128)S(1)} %get-tuple-element.47), channel_id=1, source_target_pairs={{0,8},{8,16},{16,24},{24,0},{1,9},{9,17},{17,25},{25,1},{2,10},{10... | collective-permute-start | bytes 9224 | tf_op jit(solution)/shard_map/ppermute | solution.py:120
  28.2 10.8 %collective-permute-start.9 = (f32[4,4,16,3]{3,2,1,0:T(8,128)S(1)}, f32[4,4,16,3]{3,2,1,0:T(8,128)S(1)}, u32[]{:S(2)}, u32[]{:S(2)}) collective-permute-start(f32[4,4,16,3]{3,2,1,0:T(8,128)S(1)} %get-tuple-element.48), channel_id=1, source_target_pairs={{0,24},{8,0},{16,8},{24,16},{1,25},{9,1},{17,9},{25,17},{2,26},{10... | collective-permute-start | bytes 9224 | tf_op jit(solution)/shard_map/ppermute | solution.py:120
  31.8 7.2 %collective-permute-start.7 = (f32[4,4,3,3]{3,2,1,0:T(4,128)S(1)}, f32[4,4,3,3]{3,2,1,0:T(4,128)S(1)}, u32[]{:S(2)}, u32[]{:S(2)}) collective-permute-start(f32[4,4,3,3]{3,2,1,0:T(4,128)S(1)} %get-tuple-element.50), channel_id=1, source_target_pairs={{0,28},{8,4},{16,12},{24,20},{4,24},{12,0},{20,8},{28,16},{1,29},{... | collective-permute-start | bytes 1736 | tf_op jit(solution)/shard_map/ppermute | solution.py:133
  33.9 5.1 %collective-permute-start.6 = (f32[4,4,3,128]{3,2,1,0:T(4,128)S(1)}, f32[4,4,3,128]{3,2,1,0:T(4,128)S(1)}, u32[]{:S(2)}, u32[]{:S(2)}) collective-permute-start(f32[4,4,3,128]{3,2,1,0:T(4,128)S(1)} %fusion.33), channel_id=1, source_target_pairs={{0,4},{4,0},{1,5},{5,1},{2,6},{6,2},{3,7},{7,3},{8,12},{12,8},{9,1... | collective-permute-start | bytes 73736 | tf_op jit(solution)/shard_map/ppermute | solution.py:133
  39.4 2.6 %copy-start.9 = (s32[4,128]{1,0:T(4,128)S(1)}, s32[4,128]{1,0:T(4,128)}, u32[]{:S(2)}) copy-start(s32[4,128]{1,0:T(4,128)} %param.17) | copy-start | bytes 6148
  39.4 2.6 %collective-permute-start.10 = (f32[4,3,22,134]{3,2,1,0:T(8,128)S(1)}, f32[4,3,22,134]{3,2,1,0:T(8,128)S(1)}, u32[]{:S(2)}, u32[]{:S(2)}) collective-permute-start(f32[4,3,22,134]{3,2,1,0:T(8,128)S(1)} %get-tuple-element.33), channel_id=1, source_target_pairs={{0,1},{1,2},{2,3},{4,5},{5,6},{6,7},{8,9},{9,10},{10,11},{12,13},{... | collective-permute-start | bytes 424520 | tf_op jit(solution)/shard_map/ppermute | solution.py:120
  40.7 5.6 %collective-permute-start.11 = (f32[4,3,22,134]{3,2,1,0:T(8,128)S(1)}, f32[4,3,22,134]{3,2,1,0:T(8,128)S(1)}, u32[]{:S(2)}, u32[]{:S(2)}) collective-permute-start(f32[4,3,22,134]{3,2,1,0:T(8,128)S(1)} %get-tuple-element.34), channel_id=1, source_target_pairs={{1,0},{2,1},{3,2},{5,4},{6,5},{7,6},{9,8},{10,9},{11,10},{13,12},{... | collective-permute-start | bytes 424520 | tf_op jit(solution)/shard_map/ppermute | solution.py:120
  48.3 0.9 %copy-start.5 = (f32[4,16,128]{2,1,0:T(8,128)S(1)}, f32[4,16,128]{2,1,0:T(8,128)}, u32[]{:S(2)}) copy-start(f32[4,16,128]{2,1,0:T(8,128)} %param.16) | copy-start | bytes 98308
  50.6 14.0 %collective-permute-start.12 = (f32[3,128]{1,0:T(4,128)S(1)}, f32[3,128]{1,0:T(4,128)S(1)}, u32[]{:S(2)}, u32[]{:S(2)}) collective-permute-start(f32[3,128]{1,0:T(4,128)S(1)} %get-tuple-element.67), channel_id=1, source_target_pairs={{0,1},{1,2},{2,3},{4,5},{5,6},{6,7},{8,9},{9,10},{10,11},{12,13},{... | collective-permute-start | bytes 4616 | tf_op jit(solution)/shard_map/ppermute | solution.py:195
  57.5 7.1 %collective-permute-start.13 = (f32[3,128]{1,0:T(4,128)S(1)}, f32[3,128]{1,0:T(4,128)S(1)}, u32[]{:S(2)}, u32[]{:S(2)}) collective-permute-start(f32[3,128]{1,0:T(4,128)S(1)} %get-tuple-element.66), channel_id=1, source_target_pairs={{1,0},{2,1},{3,2},{5,4},{6,5},{7,6},{9,8},{10,9},{11,10},{13,12},{... | collective-permute-start | bytes 4616 | tf_op jit(solution)/shard_map/ppermute | solution.py:195
  58.8 5.8 %collective-permute-start.14 = (f32[3,128]{1,0:T(4,128)S(1)}, f32[3,128]{1,0:T(4,128)S(1)}, u32[]{:S(2)}, u32[]{:S(2)}) collective-permute-start(f32[3,128]{1,0:T(4,128)S(1)} %get-tuple-element.65), channel_id=1, source_target_pairs={{0,4},{4,0},{1,5},{5,1},{2,6},{6,2},{3,7},{7,3},{8,12},{12,8},{9,1... | collective-permute-start | bytes 4616 | tf_op jit(solution)/shard_map/ppermute | solution.py:195
  59.4 5.2 %collective-permute-start.15 = (f32[3,128]{1,0:T(4,128)S(1)}, f32[3,128]{1,0:T(4,128)S(1)}, u32[]{:S(2)}, u32[]{:S(2)}) collective-permute-start(f32[3,128]{1,0:T(4,128)S(1)} %get-tuple-element.67), channel_id=1, source_target_pairs={{0,5},{1,6},{2,7},{4,1},{5,2},{6,3},{8,13},{9,14},{10,15},{12,9},{... | collective-permute-start | bytes 4616 | tf_op jit(solution)/shard_map/ppermute | solution.py:195
  63.3 4.9 %collective-permute-start.16 = (f32[3,128]{1,0:T(4,128)S(1)}, f32[3,128]{1,0:T(4,128)S(1)}, u32[]{:S(2)}, u32[]{:S(2)}) collective-permute-start(f32[3,128]{1,0:T(4,128)S(1)} %get-tuple-element.66), channel_id=1, source_target_pairs={{1,4},{2,5},{3,6},{5,0},{6,1},{7,2},{9,12},{10,13},{11,14},{13,8},... | collective-permute-start | bytes 4616 | tf_op jit(solution)/shard_map/ppermute | solution.py:195
  68.2 5.4 %collective-permute-start.17 = (f32[3,128]{1,0:T(4,128)S(1)}, f32[3,128]{1,0:T(4,128)S(1)}, u32[]{:S(2)}, u32[]{:S(2)}) collective-permute-start(f32[3,128]{1,0:T(4,128)S(1)} %add_add_fusion.1), channel_id=1, source_target_pairs={{0,8},{8,16},{16,24},{24,0},{1,9},{9,17},{17,25},{25,1},{2,10},{10... | collective-permute-start | bytes 4616 | tf_op jit(solution)/shard_map/ppermute | solution.py:195
  68.8 4.8 %collective-permute-start.18 = (f32[3,128]{1,0:T(4,128)S(1)}, f32[3,128]{1,0:T(4,128)S(1)}, u32[]{:S(2)}, u32[]{:S(2)}) collective-permute-start(f32[3,128]{1,0:T(4,128)S(1)} %add_add_fusion.1), channel_id=1, source_target_pairs={{0,16},{8,24},{16,0},{24,8},{1,17},{9,25},{17,1},{25,9},{2,18},{10... | collective-permute-start | bytes 4616 | tf_op jit(solution)/shard_map/ppermute | solution.py:195
  70.6 3.7 %collective-permute-start.19 = (f32[3,128]{1,0:T(4,128)S(1)}, f32[3,128]{1,0:T(4,128)S(1)}, u32[]{:S(2)}, u32[]{:S(2)}) collective-permute-start(f32[3,128]{1,0:T(4,128)S(1)} %add_add_fusion.1), channel_id=1, source_target_pairs={{0,24},{8,0},{16,8},{24,16},{1,25},{9,1},{17,9},{25,17},{2,26},{10... | collective-permute-start | bytes 4616 | tf_op jit(solution)/shard_map/ppermute | solution.py:195

commit v7 on v6

--- a/solution.py
+++ b/solution.py
@@ -135,8 +135,11 @@
     return jnp.where(me == 1, got, zero), jnp.where(me == 0, got, zero)
 
 
-def face_halos(array, axis, dim, wrap):
-    return receive_pair(array, {}, axis, {axis: dim}, 1)
+def face_halos(fields, axis, dim, wrap):
+    thin = jnp.concatenate(
+        [jnp.concatenate([edge(f, dim, 1, 1), edge(f, dim, -1, 1)], axis=dim) for f in fields], axis=0
+    )
+    return receive_pair(thin, {}, axis, {axis: dim}, 1)
 
 
 def padded_sweeps(joined, width):
@@ -160,26 +163,25 @@
     return jnp.sum(jac[spread] * term[:, None], axis=0)
 
 
-def flux_faces(stacked, halos, owner_jac, neighbor_jac):
-    psi = stacked[:5]
+def flux_faces(psi, weights, halos, owner_jac, neighbor_jac):
     inner_terms = []
     for direction in range(3):
         dim = direction + 1
-        length = stacked.shape[dim]
+        length = psi.shape[dim]
         low = lax.slice_in_dim(psi, 0, length - 1, axis=dim)
         high = lax.slice_in_dim(psi, 1, length, axis=dim)
-        w_low = lax.slice_in_dim(stacked[5 + direction], 0, length - 1, axis=direction)
+        w_low = lax.slice_in_dim(weights[direction], 0, length - 1, axis=direction)
         between = w_low[None] * (low - high)
         inner_terms.append((jac_apply(owner_jac[direction], between), jac_apply(neighbor_jac[direction], between)))
     inner_terms = lax.optimization_barrier(inner_terms)
     total = jnp.zeros_like(psi)
     for direction in range(3):
         dim = direction + 1
-        length = stacked.shape[dim]
+        length = psi.shape[dim]
         before, after = halos[direction]
         last = lax.slice_in_dim(psi, length - 1, length, axis=dim)
         first = lax.slice_in_dim(psi, 0, 1, axis=dim)
-        w_last = lax.slice_in_dim(stacked[5 + direction], length - 1, length, axis=direction)
+        w_last = lax.slice_in_dim(weights[direction], length - 1, length, axis=direction)
         up_edge = w_last[None] * (last - after[:5])
         down_edge = before[5 + direction][None] * (before[:5] - first)
         up_inner, down_inner = inner_terms[direction]
@@ -221,13 +223,13 @@
     wall_kernel,
     panel_owner,
 ):
-    stacked = jnp.concatenate([adjoint, face_weights], axis=0)
+    fields = (adjoint, face_weights)
     halos = [
-        face_halos(stacked, "span", 1, False),
-        face_halos(stacked, "normal", 2, False),
-        face_halos(stacked, "circ", 3, True),
+        face_halos(fields, "span", 1, False),
+        face_halos(fields, "normal", 2, False),
+        face_halos(fields, "circ", 3, True),
     ]
-    residual = flux_faces(stacked, halos, owner_jac, neighbor_jac) + adjoint - objective_grad
+    residual = flux_faces(adjoint, face_weights, halos, owner_jac, neighbor_jac) + adjoint - objective_grad
     forcing = jac_apply(coupling.T, residual)
     margin = SWEEPS - 1
     joined = jnp.concatenate([stiffness[None], forcing], axis=0)

time: 75.9 us -> 70.3 us (0.926)
  waiting for transfers between devices: 22.1 us -> 15.1 us
  local copies, waits for them, and re-layouts: 5.53 us -> 7.17 us
    ppermute x8, waiting for transfers between devices: 12.8 us -> 4.03 us  [receive(): return lax.ppermute(take(array, rel, dims, width), axes, pairs)]
    slice x3 -> x9, local copies, waits for them, and re-layouts: 0.18 us -> 2.08 us  [edge(): return lax.slice_in_dim(array, start, start + width, axis=dim)]
    ppermute x8, waiting for transfers between devices: 4.88 us -> 6.45 us  [shifted(): return lax.ppermute(array, axes, pairs)]
    ppermute x8, starting transfers between devices: 13.1 us -> 14.2 us  [receive(): return lax.ppermute(take(array, rel, dims, width), axes, pairs)]
    ppermute x8, starting transfers between devices: 18.8 us -> 17.8 us  [shifted(): return lax.ppermute(array, axes, pairs)]
    unnamed x23 -> x34, local copies, waits for them, and re-layouts: 4.48 us -> 4.29 us
  transfers between devices with their start and end apart: 20 -> 20, of which waited for: 7 -> 5; matrix products, arithmetic and copies ran while one was open for 4% -> 5% of each run, Pallas kernels for 0% -> 0%
where the time goes in v7:
time: 70.3 us; the launch traced here: 69.7 us
  starting transfers between devices  38.8 us (55%)
  waiting for transfers between devices  15.1 us (21%)
  local copies, waits for them, and re-layouts  7.17 us (10%)
  other arithmetic  6.81 us (10%)
  between operations  1.38 us (2%)
    ppermute x8, starting transfers between devices, shifted(): return lax.ppermute(array, axes, pairs)  17.8 us
    ppermute x8, starting transfers between devices, receive(): return lax.ppermute(take(array, rel, dims, width), axes, pairs)  14.2 us
    ppermute x4, starting transfers between devices, receive_pair(): got = lax.ppermute(sent, axes, pairs + back)  6.77 us
    ppermute x8, waiting for transfers between devices, shifted(): return lax.ppermute(array, axes, pairs)  6.45 us
    ppermute x4, waiting for transfers between devices, receive_pair(): got = lax.ppermute(sent, axes, pairs + back)  4.61 us
    unnamed x34, local copies, waits for them, and re-layouts  4.29 us
    ppermute x8, waiting for transfers between devices, receive(): return lax.ppermute(take(array, rel, dims, width), axes, pairs)  4.03 us
    mul x3, other arithmetic, relax(): weighted = stiff_pad[None] * mesh_pad  2.17 us
  transfers between devices with their start and end apart: 20, of which 5 were waited for; matrix products, arithmetic and copies ran while one was open for 5% of the time, Pallas kernels for 0%

profile of v7, /device:TPU:0, one launch (start us, length us, event | category | flops | bytes accessed | tf_op | source)
XLA Modules:
  0.0 69.7 jit_solution(8099678702434374619)
XLA Ops:
  0.6 1.0 %fusion.49 = (f32[5,4,1,128]{3,2,1,0:T(1,128)S(1)}, f32[5,4,1,128]{3,2,1,0:T(1,128)S(1)}) fusion(f32[5,4,16,128]{3,2,1,0:T(8,128)} %param.9), kind=kLoop, calls=%fused_computation.143 | loop fusion | bytes 40960 | tf_op jit(solution)/shard_map/slice | solution.py:88
  1.7 0.8 %fusion.53 = (f32[3,4,1,128]{3,2,1,0:T(1,128)S(1)}, f32[3,4,1,128]{3,2,1,0:T(1,128)S(1)}) fusion(f32[3,4,16,128]{3,2,1,0:T(8,128)} %param.11), kind=kLoop, calls=%fused_computation.147 | loop fusion | bytes 24576 | tf_op jit(solution)/shard_map/slice | solution.py:88
  2.6 3.0 %collective-permute-start.2 = (f32[8,4,1,128]{3,0,2,1:T(8,128)S(1)}, f32[8,4,1,128]{3,0,2,1:T(8,128)S(1)}, u32[]{:S(2)}, u32[]{:S(2)}) collective-permute-start(f32[8,4,1,128]{3,0,2,1:T(8,128)S(1)} %slice_select_fusion.1), channel_id=1, source_target_pairs={{0,4},{4,0},{1,5},{5,1},{2,6},{6,2},{3,7},{7,3},{8,12},{12,8},{9,1... | collective-permute-start | bytes 49160 | tf_op jit(solution)/shard_map/ppermute | solution.py:133
  5.7 1.5 %collective-permute-start.1 = (f32[8,1,16,128]{3,2,1,0:T(8,128)S(1)}, f32[8,1,16,128]{3,2,1,0:T(8,128)S(1)}, u32[]{:S(2)}, u32[]{:S(2)}) collective-permute-start(f32[8,1,16,128]{3,2,1,0:T(8,128)S(1)} %get-tuple-element.49), channel_id=1, source_target_pairs={{0,1},{1,2},{2,3},{4,5},{5,6},{6,7},{8,9},{9,10},{10,11},{12,13},{... | collective-permute-start | bytes 196616 | tf_op jit(solution)/shard_map/ppermute | solution.py:120
  7.1 1.3 %collective-permute-start = (f32[8,1,16,128]{3,2,1,0:T(8,128)S(1)}, f32[8,1,16,128]{3,2,1,0:T(8,128)S(1)}, u32[]{:S(2)}, u32[]{:S(2)}) collective-permute-start(f32[8,1,16,128]{3,2,1,0:T(8,128)S(1)} %get-tuple-element.50), channel_id=1, source_target_pairs={{1,0},{2,1},{3,2},{5,4},{6,5},{7,6},{9,8},{10,9},{11,10},{13,12},{... | collective-permute-start | bytes 196616 | tf_op jit(solution)/shard_map/ppermute | solution.py:120
  9.0 0.2 copy.87
  9.2 0.3 copy.88
  9.5 1.6 %collective-permute-start.4 = (f32[8,4,16,1]{2,0,3,1:T(8,128)S(1)}, f32[8,4,16,1]{2,0,3,1:T(8,128)S(1)}, u32[]{:S(2)}, u32[]{:S(2)}) collective-permute-start(f32[8,4,16,1]{2,0,3,1:T(8,128)S(1)} %get-tuple-element.65), channel_id=1, source_target_pairs={{0,8},{8,16},{16,24},{24,0},{1,9},{9,17},{17,25},{25,1},{2,10},{10... | collective-permute-start | bytes 6152 | tf_op jit(solution)/shard_map/ppermute | solution.py:120
  11.1 2.2 %collective-permute-start.3 = (f32[8,4,16,1]{2,0,3,1:T(8,128)S(1)}, f32[8,4,16,1]{2,0,3,1:T(8,128)S(1)}, u32[]{:S(2)}, u32[]{:S(2)}) collective-permute-start(f32[8,4,16,1]{2,0,3,1:T(8,128)S(1)} %get-tuple-element.66), channel_id=1, source_target_pairs={{0,24},{8,0},{16,8},{24,16},{1,25},{9,1},{17,9},{25,17},{2,26},{10... | collective-permute-start | bytes 6152 | tf_op jit(solution)/shard_map/ppermute | solution.py:120
  13.4 0.7 copy-done.6
  14.1 0.7 copy-done.7
  15.1 0.5 multiply_reduce_fusion.2
  15.6 0.2 multiply_reduce_fusion
  15.8 0.1 multiply_reduce_fusion.4
  16.0 0.2 slice_reduce_fusion
  16.2 0.6 copy-done.8
  17.2 0.2 copy.74
  17.4 0.2 copy.72
  18.1 0.7 %copy-done.4 = f32[5,4,16,128]{3,2,1,0:T(8,128)S(1)} copy-done((f32[5,4,16,128]{3,2,1,0:T(8,128)S(1)}, f32[5,4,16,128]{3,2,1,0:T(8,128)}, u32[]{:S(2)}) %copy-start.4) | copy-done | bytes 163864
  18.8 0.2 fusion.15
  19.1 0.7 copy-done.2
  20.0 0.3 collective-permute-start.5
  20.4 1.6 %collective-permute-start.8 = (f32[4,4,16,3]{3,2,1,0:T(8,128)S(1)}, f32[4,4,16,3]{3,2,1,0:T(8,128)S(1)}, u32[]{:S(2)}, u32[]{:S(2)}) collective-permute-start(f32[4,4,16,3]{3,2,1,0:T(8,128)S(1)} %get-tuple-element.45), channel_id=1, source_target_pairs={{0,8},{8,16},{16,24},{24,0},{1,9},{9,17},{17,25},{25,1},{2,10},{10... | collective-permute-start | bytes 9224 | tf_op jit(solution)/shard_map/ppermute | solution.py:120
  22.0 2.5 %collective-permute-start.9 = (f32[4,4,16,3]{3,2,1,0:T(8,128)S(1)}, f32[4,4,16,3]{3,2,1,0:T(8,128)S(1)}, u32[]{:S(2)}, u32[]{:S(2)}) collective-permute-start(f32[4,4,16,3]{3,2,1,0:T(8,128)S(1)} %get-tuple-element.46), channel_id=1, source_target_pairs={{0,24},{8,0},{16,8},{24,16},{1,25},{9,1},{17,9},{25,17},{2,26},{10... | collective-permute-start | bytes 9224 | tf_op jit(solution)/shard_map/ppermute | solution.py:120
  24.5 2.4 %collective-permute-start.7 = (f32[4,4,3,3]{3,2,1,0:T(4,128)S(1)}, f32[4,4,3,3]{3,2,1,0:T(4,128)S(1)}, u32[]{:S(2)}, u32[]{:S(2)}) collective-permute-start(f32[4,4,3,3]{3,2,1,0:T(4,128)S(1)} %get-tuple-element.48), channel_id=1, source_target_pairs={{0,28},{8,4},{16,12},{24,20},{4,24},{12,0},{20,8},{28,16},{1,29},{... | collective-permute-start | bytes 1736 | tf_op jit(solution)/shard_map/ppermute | solution.py:133
  26.9 1.0 %collective-permute-start.6 = (f32[4,4,3,128]{3,2,1,0:T(4,128)S(1)}, f32[4,4,3,128]{3,2,1,0:T(4,128)S(1)}, u32[]{:S(2)}, u32[]{:S(2)}) collective-permute-start(f32[4,4,3,128]{3,2,1,0:T(4,128)S(1)} %fusion.29), channel_id=1, source_target_pairs={{0,4},{4,0},{1,5},{5,1},{2,6},{6,2},{3,7},{7,3},{8,12},{12,8},{9,1... | collective-permute-start | bytes 73736 | tf_op jit(solution)/shard_map/ppermute | solution.py:133
  28.0 4.6 %collective-permute-done.7 = f32[4,4,3,3]{3,2,1,0:T(4,128)S(1)} collective-permute-done((f32[4,4,3,3]{3,2,1,0:T(4,128)S(1)}, f32[4,4,3,3]{3,2,1,0:T(4,128)S(1)}, u32[]{:S(2)}, u32[]{:S(2)}) %collective-permute-start.7) | collective-permute-done | bytes 608 | tf_op jit(solution)/shard_map/ppermute | solution.py:133
  32.6 0.3 maximum_maximum_fusion
  33.0 2.2 %collective-permute-start.10 = (f32[4,3,22,134]{3,2,1,0:T(8,128)S(1)}, f32[4,3,22,134]{3,2,1,0:T(8,128)S(1)}, u32[]{:S(2)}, u32[]{:S(2)}) collective-permute-start(f32[4,3,22,134]{3,2,1,0:T(8,128)S(1)} %get-tuple-element.31), channel_id=1, source_target_pairs={{0,1},{1,2},{2,3},{4,5},{5,6},{6,7},{8,9},{9,10},{10,11},{12,13},{... | collective-permute-start | bytes 424520 | tf_op jit(solution)/shard_map/ppermute | solution.py:120
  35.2 1.3 %collective-permute-start.11 = (f32[4,3,22,134]{3,2,1,0:T(8,128)S(1)}, f32[4,3,22,134]{3,2,1,0:T(8,128)S(1)}, u32[]{:S(2)}, u32[]{:S(2)}) collective-permute-start(f32[4,3,22,134]{3,2,1,0:T(8,128)S(1)} %get-tuple-element.32), channel_id=1, source_target_pairs={{1,0},{2,1},{3,2},{5,4},{6,5},{7,6},{9,8},{10,9},{11,10},{13,12},{... | collective-permute-start | bytes 424520 | tf_op jit(solution)/shard_map/ppermute | solution.py:120
  36.5 4.0 %collective-permute-done.11 = f32[4,3,22,134]{3,2,1,0:T(8,128)S(1)} collective-permute-done((f32[4,3,22,134]{3,2,1,0:T(8,128)S(1)}, f32[4,3,22,134]{3,2,1,0:T(8,128)S(1)}, u32[]{:S(2)}, u32[]{:S(2)}) %collective-permute-start.11) | collective-permute-done | bytes 141536 | tf_op jit(solution)/shard_map/ppermute | solution.py:120
  40.6 0.3 pad_maximum_fusion
  41.4 1.2 %broadcast_multiply_fusion.1 = (f32[3,8,20,132]{3,2,1,0:T(8,128)S(1)}, f32[3,8,20,132]{3,2,1,0:T(8,128)S(1)}) fusion(f32[8,20,132]{2,1,0:T(8,128)S(1)} %get-tuple-element.36, f32[3,10,22,134]{3,2,1,0:T(8,128)S(1)} %get-tuple-element.27, f32[8,20,132]{2,1,0:T(8,128)S(1)} %get-tuple-element.35, f32[4,10,22,134]{3,2,1,0:T(8,128)S(1)} %pad_maximum_fusion, ...), kind=kLoop, calls=%fused_computation.42 | loop fusion | flops 760320 | bytes 2703360 | tf_op jit(solution)/shard_map/mul | solution.py:60
  42.6 0.9 %broadcast_multiply_fusion.2 = (f32[3,6,18,130]{3,2,1,0:T(8,128)S(1)}, f32[3,6,18,130]{3,2,1,0:T(8,128)S(1)}) fusion(f32[6,18,130]{2,1,0:T(8,128)S(1)} %get-tuple-element.34, f32[3,8,20,132]{3,2,1,0:T(8,128)S(1)} %get-tuple-element.25, f32[6,18,130]{2,1,0:T(8,128)S(1)} %get-tuple-element.33, f32[4,10,22,134]{3,2,1,0:T(8,128)S(1)} %pad_maximum_fusion, ...), kind=kLoop, calls=%fused_computation.45 | loop fusion | flops 505440 | bytes 1797120 | tf_op jit(solution)/shard_map/mul | solution.py:60
  43.5 0.9 %multiply_reduce_fusion.9 = (f32[3,4,128]{2,1,0:T(4,128)S(1)}, f32[3,4,16,128]{3,2,1,0:T(8,128)}) fusion(f32[4,16,128]{2,1,0:T(8,128)S(1)} %copy-done.5, f32[3,6,18,130]{3,2,1,0:T(8,128)S(1)} %get-tuple-element.23, f32[3,4,16,128]{3,2,1,0:T(8,128)S(1)} %multiply_reduce_fusion.6, f32[4,16,128]{2,1,0:T(8,128)S(1)} %fusion.34, ...), kind=kLoop, calls=%fused_computation.79 | loop fusion | flops 317952 | bytes 956416 | tf_op jit(solution)/shard_map/reduce_sum | solution.py:238
  44.4 0.4 convolution_bitcast_fusion
  44.8 7.0 %collective-permute-start.12 = (f32[3,128]{1,0:T(4,128)S(1)}, f32[3,128]{1,0:T(4,128)S(1)}, u32[]{:S(2)}, u32[]{:S(2)}) collective-permute-start(f32[3,128]{1,0:T(4,128)S(1)} %get-tuple-element.75), channel_id=1, source_target_pairs={{0,1},{1,2},{2,3},{4,5},{5,6},{6,7},{8,9},{9,10},{10,11},{12,13},{... | collective-permute-start | bytes 4616 | tf_op jit(solution)/shard_map/ppermute | solution.py:197
  51.8 1.3 %collective-permute-start.13 = (f32[3,128]{1,0:T(4,128)S(1)}, f32[3,128]{1,0:T(4,128)S(1)}, u32[]{:S(2)}, u32[]{:S(2)}) collective-permute-start(f32[3,128]{1,0:T(4,128)S(1)} %get-tuple-element.74), channel_id=1, source_target_pairs={{1,0},{2,1},{3,2},{5,4},{6,5},{7,6},{9,8},{10,9},{11,10},{13,12},{... | collective-permute-start | bytes 4616 | tf_op jit(solution)/shard_map/ppermute | solution.py:197
  53.1 0.8 %collective-permute-start.14 = (f32[3,128]{1,0:T(4,128)S(1)}, f32[3,128]{1,0:T(4,128)S(1)}, u32[]{:S(2)}, u32[]{:S(2)}) collective-permute-start(f32[3,128]{1,0:T(4,128)S(1)} %get-tuple-element.73), channel_id=1, source_target_pairs={{0,4},{4,0},{1,5},{5,1},{2,6},{6,2},{3,7},{7,3},{8,12},{12,8},{9,1... | collective-permute-start | bytes 4616 | tf_op jit(solution)/shard_map/ppermute | solution.py:197
  53.9 3.6 %collective-permute-start.15 = (f32[3,128]{1,0:T(4,128)S(1)}, f32[3,128]{1,0:T(4,128)S(1)}, u32[]{:S(2)}, u32[]{:S(2)}) collective-permute-start(f32[3,128]{1,0:T(4,128)S(1)} %get-tuple-element.75), channel_id=1, source_target_pairs={{0,5},{1,6},{2,7},{4,1},{5,2},{6,3},{8,13},{9,14},{10,15},{12,9},{... | collective-permute-start | bytes 4616 | tf_op jit(solution)/shard_map/ppermute | solution.py:197
  57.5 1.3 %collective-permute-start.16 = (f32[3,128]{1,0:T(4,128)S(1)}, f32[3,128]{1,0:T(4,128)S(1)}, u32[]{:S(2)}, u32[]{:S(2)}) collective-permute-start(f32[3,128]{1,0:T(4,128)S(1)} %get-tuple-element.74), channel_id=1, source_target_pairs={{1,4},{2,5},{3,6},{5,0},{6,1},{7,2},{9,12},{10,13},{11,14},{13,8},... | collective-permute-start | bytes 4616 | tf_op jit(solution)/shard_map/ppermute | solution.py:197
  58.8 3.6 %collective-permute-done.16 = f32[3,128]{1,0:T(4,128)S(1)} collective-permute-done((f32[3,128]{1,0:T(4,128)S(1)}, f32[3,128]{1,0:T(4,128)S(1)}, u32[]{:S(2)}, u32[]{:S(2)}) %collective-permute-start.16) | collective-permute-done | bytes 1568 | tf_op jit(solution)/shard_map/ppermute | solution.py:197
  62.4 0.5 collective-permute-start.17
  62.9 2.6 %collective-permute-start.18 = (f32[3,128]{1,0:T(4,128)S(1)}, f32[3,128]{1,0:T(4,128)S(1)}, u32[]{:S(2)}, u32[]{:S(2)}) collective-permute-start(f32[3,128]{1,0:T(4,128)S(1)} %add_add_fusion.1), channel_id=1, source_target_pairs={{0,16},{8,24},{16,0},{24,8},{1,17},{9,25},{17,1},{25,9},{2,18},{10... | collective-permute-start | bytes 4616 | tf_op jit(solution)/shard_map/ppermute | solution.py:197
  65.5 0.7 %collective-permute-start.19 = (f32[3,128]{1,0:T(4,128)S(1)}, f32[3,128]{1,0:T(4,128)S(1)}, u32[]{:S(2)}, u32[]{:S(2)}) collective-permute-start(f32[3,128]{1,0:T(4,128)S(1)} %add_add_fusion.1), channel_id=1, source_target_pairs={{0,24},{8,0},{16,8},{24,16},{1,25},{9,1},{17,9},{25,17},{2,26},{10... | collective-permute-start | bytes 4616 | tf_op jit(solution)/shard_map/ppermute | solution.py:197
  66.3 1.6 %collective-permute-done.17 = f32[3,128]{1,0:T(4,128)S(1)} collective-permute-done((f32[3,128]{1,0:T(4,128)S(1)}, f32[3,128]{1,0:T(4,128)S(1)}, u32[]{:S(2)}, u32[]{:S(2)}) %collective-permute-start.17) | collective-permute-done | bytes 1568 | tf_op jit(solution)/shard_map/ppermute | solution.py:197
  67.8 1.3 %collective-permute-done.19 = f32[3,128]{1,0:T(4,128)S(1)} collective-permute-done((f32[3,128]{1,0:T(4,128)S(1)}, f32[3,128]{1,0:T(4,128)S(1)}, u32[]{:S(2)}, u32[]{:S(2)}) %collective-permute-start.19) | collective-permute-done | bytes 1568 | tf_op jit(solution)/shard_map/ppermute | solution.py:197
  69.1 0.6 add_add_fusion
  (100 shorter events, 2.5 us)
Async XLA Ops:
  0.6 5.0 %copy-start = (f32[5,4,16,128]{3,2,1,0:T(8,128)S(1)}, f32[5,4,16,128]{3,2,1,0:T(8,128)}, u32[]{:S(2)}) copy-start(f32[5,4,16,128]{3,2,1,0:T(8,128)} %param.9) | copy-start | bytes 491524
  2.5 3.1 %copy-start.1 = (f32[3,4,16,128]{3,2,1,0:T(8,128)S(1)}, f32[3,4,16,128]{3,2,1,0:T(8,128)}, u32[]{:S(2)}) copy-start(f32[3,4,16,128]{3,2,1,0:T(8,128)} %param.11) | copy-start | bytes 294916
  2.6 15.1 %collective-permute-start.2 = (f32[8,4,1,128]{3,0,2,1:T(8,128)S(1)}, f32[8,4,1,128]{3,0,2,1:T(8,128)S(1)}, u32[]{:S(2)}, u32[]{:S(2)}) collective-permute-start(f32[8,4,1,128]{3,0,2,1:T(8,128)S(1)} %slice_select_fusion.1), channel_id=1, source_target_pairs={{0,4},{4,0},{1,5},{5,1},{2,6},{6,2},{3,7},{7,3},{8,12},{12,8},{9,1... | collective-permute-start | bytes 49160 | tf_op jit(solution)/shard_map/ppermute | solution.py:133
  5.7 12.2 %collective-permute-start.1 = (f32[8,1,16,128]{3,2,1,0:T(8,128)S(1)}, f32[8,1,16,128]{3,2,1,0:T(8,128)S(1)}, u32[]{:S(2)}, u32[]{:S(2)}) collective-permute-start(f32[8,1,16,128]{3,2,1,0:T(8,128)S(1)} %get-tuple-element.49), channel_id=1, source_target_pairs={{0,1},{1,2},{2,3},{4,5},{5,6},{6,7},{8,9},{9,10},{10,11},{12,13},{... | collective-permute-start | bytes 196616 | tf_op jit(solution)/shard_map/ppermute | solution.py:120
  7.1 10.8 %collective-permute-start = (f32[8,1,16,128]{3,2,1,0:T(8,128)S(1)}, f32[8,1,16,128]{3,2,1,0:T(8,128)S(1)}, u32[]{:S(2)}, u32[]{:S(2)}) collective-permute-start(f32[8,1,16,128]{3,2,1,0:T(8,128)S(1)} %get-tuple-element.50), channel_id=1, source_target_pairs={{1,0},{2,1},{3,2},{5,4},{6,5},{7,6},{9,8},{10,9},{11,10},{13,12},{... | collective-permute-start | bytes 196616 | tf_op jit(solution)/shard_map/ppermute | solution.py:120
  9.5 7.4 %collective-permute-start.4 = (f32[8,4,16,1]{2,0,3,1:T(8,128)S(1)}, f32[8,4,16,1]{2,0,3,1:T(8,128)S(1)}, u32[]{:S(2)}, u32[]{:S(2)}) collective-permute-start(f32[8,4,16,1]{2,0,3,1:T(8,128)S(1)} %get-tuple-element.65), channel_id=1, source_target_pairs={{0,8},{8,16},{16,24},{24,0},{1,9},{9,17},{17,25},{25,1},{2,10},{10... | collective-permute-start | bytes 6152 | tf_op jit(solution)/shard_map/ppermute | solution.py:120
  11.1 5.9 %collective-permute-start.3 = (f32[8,4,16,1]{2,0,3,1:T(8,128)S(1)}, f32[8,4,16,1]{2,0,3,1:T(8,128)S(1)}, u32[]{:S(2)}, u32[]{:S(2)}) collective-permute-start(f32[8,4,16,1]{2,0,3,1:T(8,128)S(1)} %get-tuple-element.66), channel_id=1, source_target_pairs={{0,24},{8,0},{16,8},{24,16},{1,25},{9,1},{17,9},{25,17},{2,26},{10... | collective-permute-start | bytes 6152 | tf_op jit(solution)/shard_map/ppermute | solution.py:120
  13.4 0.7 %copy-start.6 = (f32[3,5,5]{2,0,1:T(4,128)S(1)}, f32[3,5,5]{2,0,1:T(4,128)}, u32[]{:S(2)}) copy-start(f32[3,5,5]{2,0,1:T(4,128)} %param.12) | copy-start | bytes 904
  14.1 0.7 %copy-start.7 = (f32[3,5,5]{2,0,1:T(4,128)S(1)}, f32[3,5,5]{2,0,1:T(4,128)}, u32[]{:S(2)}) copy-start(f32[3,5,5]{2,0,1:T(4,128)} %param.13) | copy-start | bytes 904
  16.2 0.7 copy-start.8
  17.9 0.9 %copy-start.4 = (f32[5,4,16,128]{3,2,1,0:T(8,128)S(1)}, f32[5,4,16,128]{3,2,1,0:T(8,128)}, u32[]{:S(2)}) copy-start(f32[5,4,16,128]{3,2,1,0:T(8,128)} %param.10) | copy-start | bytes 491524
  19.0 0.9 %copy-start.3 = (f32[5,4,16,128]{3,2,1,0:T(8,128)}, f32[5,4,16,128]{3,2,1,0:T(8,128)S(1)}, u32[]{:S(2)}) copy-start(f32[5,4,16,128]{3,2,1,0:T(8,128)S(1)} %fusion.15) | copy-start | bytes 491524
  19.0 0.8 %copy-start.2 = (f32[4,16,128]{2,1,0:T(8,128)S(1)}, f32[4,16,128]{2,1,0:T(8,128)}, u32[]{:S(2)}) copy-start(f32[4,16,128]{2,1,0:T(8,128)} %param.15) | copy-start | bytes 98308
  20.0 7.9 %collective-permute-start.5 = (f32[4,4,3,3]{3,2,1,0:T(4,128)S(1)}, f32[4,4,3,3]{3,2,1,0:T(4,128)S(1)}, u32[]{:S(2)}, u32[]{:S(2)}) collective-permute-start(f32[4,4,3,3]{3,2,1,0:T(4,128)S(1)} %get-tuple-element.47), channel_id=1, source_target_pairs={{0,12},{8,20},{16,28},{24,4},{4,8},{12,16},{20,24},{28,0},{1,13},{... | collective-permute-start | bytes 1736 | tf_op jit(solution)/shard_map/ppermute | solution.py:133
  20.4 12.3 %collective-permute-start.8 = (f32[4,4,16,3]{3,2,1,0:T(8,128)S(1)}, f32[4,4,16,3]{3,2,1,0:T(8,128)S(1)}, u32[]{:S(2)}, u32[]{:S(2)}) collective-permute-start(f32[4,4,16,3]{3,2,1,0:T(8,128)S(1)} %get-tuple-element.45), channel_id=1, source_target_pairs={{0,8},{8,16},{16,24},{24,0},{1,9},{9,17},{17,25},{25,1},{2,10},{10... | collective-permute-start | bytes 9224 | tf_op jit(solution)/shard_map/ppermute | solution.py:120
  22.0 10.6 %collective-permute-start.9 = (f32[4,4,16,3]{3,2,1,0:T(8,128)S(1)}, f32[4,4,16,3]{3,2,1,0:T(8,128)S(1)}, u32[]{:S(2)}, u32[]{:S(2)}) collective-permute-start(f32[4,4,16,3]{3,2,1,0:T(8,128)S(1)} %get-tuple-element.46), channel_id=1, source_target_pairs={{0,24},{8,0},{16,8},{24,16},{1,25},{9,1},{17,9},{25,17},{2,26},{10... | collective-permute-start | bytes 9224 | tf_op jit(solution)/shard_map/ppermute | solution.py:120
  24.5 8.0 %collective-permute-start.7 = (f32[4,4,3,3]{3,2,1,0:T(4,128)S(1)}, f32[4,4,3,3]{3,2,1,0:T(4,128)S(1)}, u32[]{:S(2)}, u32[]{:S(2)}) collective-permute-start(f32[4,4,3,3]{3,2,1,0:T(4,128)S(1)} %get-tuple-element.48), channel_id=1, source_target_pairs={{0,28},{8,4},{16,12},{24,20},{4,24},{12,0},{20,8},{28,16},{1,29},{... | collective-permute-start | bytes 1736 | tf_op jit(solution)/shard_map/ppermute | solution.py:133
  26.9 5.7 %collective-permute-start.6 = (f32[4,4,3,128]{3,2,1,0:T(4,128)S(1)}, f32[4,4,3,128]{3,2,1,0:T(4,128)S(1)}, u32[]{:S(2)}, u32[]{:S(2)}) collective-permute-start(f32[4,4,3,128]{3,2,1,0:T(4,128)S(1)} %fusion.29), channel_id=1, source_target_pairs={{0,4},{4,0},{1,5},{5,1},{2,6},{6,2},{3,7},{7,3},{8,12},{12,8},{9,1... | collective-permute-start | bytes 73736 | tf_op jit(solution)/shard_map/ppermute | solution.py:133
  33.0 3.5 %copy-start.9 = (s32[4,128]{1,0:T(4,128)S(1)}, s32[4,128]{1,0:T(4,128)}, u32[]{:S(2)}) copy-start(s32[4,128]{1,0:T(4,128)} %param.17) | copy-start | bytes 6148
  33.0 3.5 %collective-permute-start.10 = (f32[4,3,22,134]{3,2,1,0:T(8,128)S(1)}, f32[4,3,22,134]{3,2,1,0:T(8,128)S(1)}, u32[]{:S(2)}, u32[]{:S(2)}) collective-permute-start(f32[4,3,22,134]{3,2,1,0:T(8,128)S(1)} %get-tuple-element.31), channel_id=1, source_target_pairs={{0,1},{1,2},{2,3},{4,5},{5,6},{6,7},{8,9},{9,10},{10,11},{12,13},{... | collective-permute-start | bytes 424520 | tf_op jit(solution)/shard_map/ppermute | solution.py:120
  35.2 5.4 %collective-permute-start.11 = (f32[4,3,22,134]{3,2,1,0:T(8,128)S(1)}, f32[4,3,22,134]{3,2,1,0:T(8,128)S(1)}, u32[]{:S(2)}, u32[]{:S(2)}) collective-permute-start(f32[4,3,22,134]{3,2,1,0:T(8,128)S(1)} %get-tuple-element.32), channel_id=1, source_target_pairs={{1,0},{2,1},{3,2},{5,4},{6,5},{7,6},{9,8},{10,9},{11,10},{13,12},{... | collective-permute-start | bytes 424520 | tf_op jit(solution)/shard_map/ppermute | solution.py:120
  42.6 0.9 %copy-start.5 = (f32[4,16,128]{2,1,0:T(8,128)S(1)}, f32[4,16,128]{2,1,0:T(8,128)}, u32[]{:S(2)}) copy-start(f32[4,16,128]{2,1,0:T(8,128)} %param.16) | copy-start | bytes 98308
  44.8 14.0 %collective-permute-start.12 = (f32[3,128]{1,0:T(4,128)S(1)}, f32[3,128]{1,0:T(4,128)S(1)}, u32[]{:S(2)}, u32[]{:S(2)}) collective-permute-start(f32[3,128]{1,0:T(4,128)S(1)} %get-tuple-element.75), channel_id=1, source_target_pairs={{0,1},{1,2},{2,3},{4,5},{5,6},{6,7},{8,9},{9,10},{10,11},{12,13},{... | collective-permute-start | bytes 4616 | tf_op jit(solution)/shard_map/ppermute | solution.py:197
  51.8 7.1 %collective-permute-start.13 = (f32[3,128]{1,0:T(4,128)S(1)}, f32[3,128]{1,0:T(4,128)S(1)}, u32[]{:S(2)}, u32[]{:S(2)}) collective-permute-start(f32[3,128]{1,0:T(4,128)S(1)} %get-tuple-element.74), channel_id=1, source_target_pairs={{1,0},{2,1},{3,2},{5,4},{6,5},{7,6},{9,8},{10,9},{11,10},{13,12},{... | collective-permute-start | bytes 4616 | tf_op jit(solution)/shard_map/ppermute | solution.py:197
  53.1 5.8 %collective-permute-start.14 = (f32[3,128]{1,0:T(4,128)S(1)}, f32[3,128]{1,0:T(4,128)S(1)}, u32[]{:S(2)}, u32[]{:S(2)}) collective-permute-start(f32[3,128]{1,0:T(4,128)S(1)} %get-tuple-element.73), channel_id=1, source_target_pairs={{0,4},{4,0},{1,5},{5,1},{2,6},{6,2},{3,7},{7,3},{8,12},{12,8},{9,1... | collective-permute-start | bytes 4616 | tf_op jit(solution)/shard_map/ppermute | solution.py:197
  53.9 4.9 %collective-permute-start.15 = (f32[3,128]{1,0:T(4,128)S(1)}, f32[3,128]{1,0:T(4,128)S(1)}, u32[]{:S(2)}, u32[]{:S(2)}) collective-permute-start(f32[3,128]{1,0:T(4,128)S(1)} %get-tuple-element.75), channel_id=1, source_target_pairs={{0,5},{1,6},{2,7},{4,1},{5,2},{6,3},{8,13},{9,14},{10,15},{12,9},{... | collective-permute-start | bytes 4616 | tf_op jit(solution)/shard_map/ppermute | solution.py:197
  57.5 4.9 %collective-permute-start.16 = (f32[3,128]{1,0:T(4,128)S(1)}, f32[3,128]{1,0:T(4,128)S(1)}, u32[]{:S(2)}, u32[]{:S(2)}) collective-permute-start(f32[3,128]{1,0:T(4,128)S(1)} %get-tuple-element.74), channel_id=1, source_target_pairs={{1,4},{2,5},{3,6},{5,0},{6,1},{7,2},{9,12},{10,13},{11,14},{13,8},... | collective-permute-start | bytes 4616 | tf_op jit(solution)/shard_map/ppermute | solution.py:197
  62.4 5.4 %collective-permute-start.17 = (f32[3,128]{1,0:T(4,128)S(1)}, f32[3,128]{1,0:T(4,128)S(1)}, u32[]{:S(2)}, u32[]{:S(2)}) collective-permute-start(f32[3,128]{1,0:T(4,128)S(1)} %add_add_fusion.1), channel_id=1, source_target_pairs={{0,8},{8,16},{16,24},{24,0},{1,9},{9,17},{17,25},{25,1},{2,10},{10... | collective-permute-start | bytes 4616 | tf_op jit(solution)/shard_map/ppermute | solution.py:197
  62.9 4.9 %collective-permute-start.18 = (f32[3,128]{1,0:T(4,128)S(1)}, f32[3,128]{1,0:T(4,128)S(1)}, u32[]{:S(2)}, u32[]{:S(2)}) collective-permute-start(f32[3,128]{1,0:T(4,128)S(1)} %add_add_fusion.1), channel_id=1, source_target_pairs={{0,16},{8,24},{16,0},{24,8},{1,17},{9,25},{17,1},{25,9},{2,18},{10... | collective-permute-start | bytes 4616 | tf_op jit(solution)/shard_map/ppermute | solution.py:197
  65.5 3.6 %collective-permute-start.19 = (f32[3,128]{1,0:T(4,128)S(1)}, f32[3,128]{1,0:T(4,128)S(1)}, u32[]{:S(2)}, u32[]{:S(2)}) collective-permute-start(f32[3,128]{1,0:T(4,128)S(1)} %add_add_fusion.1), channel_id=1, source_target_pairs={{0,24},{8,0},{16,8},{24,16},{1,25},{9,1},{17,9},{25,17},{2,26},{10... | collective-permute-start | bytes 4616 | tf_op jit(solution)/shard_map/ppermute | solution.py:197

commit v8 on v7

--- a/solution.py
+++ b/solution.py
@@ -114,23 +114,33 @@
     return array
 
 
-def receive(array, rel, dims, width):
+def permute(array, axes, pairs, pack):
+    if not pack:
+        return lax.ppermute(array, axes, pairs)
+    size = array.size
+    rows = -(-size // 1024) * 8
+    flat = jnp.pad(array.reshape(-1), (0, rows * 128 - size)).reshape(rows, 128)
+    got = lax.ppermute(flat, axes, pairs)
+    return got.reshape(-1)[:size].reshape(array.shape)
+
+
+def receive(array, rel, dims, width, pack=False):
     rel = {a: r for a, r in rel.items() if r}
     axes, pairs = pairs_for({a: -r for a, r in rel.items()})
-    return lax.ppermute(take(array, rel, dims, width), axes, pairs)
-
-
-def receive_pair(array, rel, axis, dims, width):
+    return permute(take(array, rel, dims, width), axes, pairs, pack)
+
+
+def receive_pair(array, rel, axis, dims, width, pack=False):
     low = dict(rel, **{axis: -1})
     high = dict(rel, **{axis: 1})
     if lax.axis_size(axis) != 2 or WRAP[axis]:
-        return receive(array, low, dims, width), receive(array, high, dims, width)
+        return receive(array, low, dims, width, pack), receive(array, high, dims, width, pack)
     me = lax.axis_index(axis)
     sent = jnp.where(me == 0, take(array, low, dims, width), take(array, high, dims, width))
     low_nz = {a: r for a, r in low.items() if r}
     axes, pairs = pairs_for({a: -r for a, r in low_nz.items()})
     _, back = pairs_for({a: -r for a, r in dict(low_nz, **{axis: 1}).items()})
-    got = lax.ppermute(sent, axes, pairs + back)
+    got = permute(sent, axes, pairs + back, pack)
     zero = jnp.zeros_like(got)
     return jnp.where(me == 1, got, zero), jnp.where(me == 0, got, zero)
 
@@ -144,17 +154,17 @@
 
 def padded_sweeps(joined, width):
     dims = {"span": 1, "normal": 2, "circ": 3}
-    before_c = receive(joined, {"circ": -1}, dims, width)
-    after_c = receive(joined, {"circ": 1}, dims, width)
-    low_n, high_n = receive_pair(joined, {}, "normal", dims, width)
-    low_lc, high_lc = receive_pair(joined, {"circ": -1}, "normal", dims, width)
-    low_hc, high_hc = receive_pair(joined, {"circ": 1}, "normal", dims, width)
+    before_c = receive(joined, {"circ": -1}, dims, width, True)
+    after_c = receive(joined, {"circ": 1}, dims, width, True)
+    low_n, high_n = receive_pair(joined, {}, "normal", dims, width, True)
+    low_lc, high_lc = receive_pair(joined, {"circ": -1}, "normal", dims, width, True)
+    low_hc, high_hc = receive_pair(joined, {"circ": 1}, "normal", dims, width, True)
     top = jnp.concatenate([low_lc, low_n, low_hc], axis=3)
     middle = jnp.concatenate([before_c, joined, after_c], axis=3)
     bottom = jnp.concatenate([high_lc, high_n, high_hc], axis=3)
     plane = jnp.concatenate([top, middle, bottom], axis=2)
-    before_s = receive(plane, {"span": -1}, dims, width)
-    after_s = receive(plane, {"span": 1}, dims, width)
+    before_s = receive(plane, {"span": -1}, dims, width, True)
+    after_s = receive(plane, {"span": 1}, dims, width, True)
     return jnp.concatenate([before_s, plane, after_s], axis=1)
 
 

time: 70.3 us -> 73.6 us (1.047)
  local copies, waits for them, and re-layouts: 7.17 us -> 9.71 us
  starting transfers between devices: 38.8 us -> 40.2 us
  waiting for transfers between devices: 15.1 us -> 14.3 us
    ppermute x12, waiting for transfers between devices: 8.65 us -> 6.63 us  [the longest x7 6.61 us: permute(): got = lax.ppermute(flat, axes, pairs)]
    reshape x0 -> x17, local copies, waits for them, and re-layouts: none -> 1.95 us  [the longest x13 1.11 us: permute(): flat = jnp.pad(array.reshape(-1), (0, rows * 128 - size)).reshape(rows, 128)]
    ppermute x12, starting transfers between devices: 21 us -> 22.8 us  [the longest x7 13.2 us: permute(): got = lax.ppermute(flat, axes, pairs)]
    ppermute x8, waiting for transfers between devices: 6.45 us -> 7.67 us  [shifted(): return lax.ppermute(array, axes, pairs)]
  transfers between devices with their start and end apart: 20 -> 20, of which waited for: 5 -> 6; matrix products, arithmetic and copies ran while one was open for 5% -> 7% of each run, Pallas kernels for 0% -> 0%
where the time goes in v8:
time: 73.6 us; the launch traced here: 72.9 us
  starting transfers between devices  40.2 us (55%)
  waiting for transfers between devices  14.3 us (19%)
  local copies, waits for them, and re-layouts  9.71 us (13%)
  other arithmetic  6.78 us (9%)
  between operations  1.53 us (2%)
    ppermute x8, starting transfers between devices, shifted(): return lax.ppermute(array, axes, pairs)  17.3 us
    ppermute x7, starting transfers between devices, permute(): got = lax.ppermute(flat, axes, pairs)  13.2 us
    ppermute x5, starting transfers between devices, permute(): return lax.ppermute(array, axes, pairs)  9.66 us
    ppermute x8, waiting for transfers between devices, shifted(): return lax.ppermute(array, axes, pairs)  7.67 us
    ppermute x7, waiting for transfers between devices, permute(): got = lax.ppermute(flat, axes, pairs)  6.61 us
    unnamed x34, local copies, waits for them, and re-layouts  4.29 us
    mul x3, other arithmetic, relax(): weighted = stiff_pad[None] * mesh_pad  2.17 us
    slice x9, local copies, waits for them, and re-layouts, edge(): return lax.slice_in_dim(array, start, start + width, axis=dim)  2.08 us
  transfers between devices with their start and end apart: 20, of which 6 were waited for; matrix products, arithmetic and copies ran while one was open for 7% of the time, Pallas kernels for 0%

profile of v8, /device:TPU:0, one launch (start us, length us, event | category | flops | bytes accessed | tf_op | source)
XLA Modules:
  0.0 72.9 jit_solution(12003906244630906500)
XLA Ops:
  0.6 1.0 %fusion.49 = (f32[5,4,1,128]{3,2,1,0:T(1,128)S(1)}, f32[5,4,1,128]{3,2,1,0:T(1,128)S(1)}) fusion(f32[5,4,16,128]{3,2,1,0:T(8,128)} %param.9), kind=kLoop, calls=%fused_computation.149 | loop fusion | bytes 40960 | tf_op jit(solution)/shard_map/slice | solution.py:88
  1.7 0.8 %fusion.53 = (f32[3,4,1,128]{3,2,1,0:T(1,128)S(1)}, f32[3,4,1,128]{3,2,1,0:T(1,128)S(1)}) fusion(f32[3,4,16,128]{3,2,1,0:T(8,128)} %param.11), kind=kLoop, calls=%fused_computation.153 | loop fusion | bytes 24576 | tf_op jit(solution)/shard_map/slice | solution.py:88
  2.6 3.0 %collective-permute-start.2 = (f32[8,4,1,128]{3,0,2,1:T(8,128)S(1)}, f32[8,4,1,128]{3,0,2,1:T(8,128)S(1)}, u32[]{:S(2)}, u32[]{:S(2)}) collective-permute-start(f32[8,4,1,128]{3,0,2,1:T(8,128)S(1)} %slice_select_fusion.1), channel_id=1, source_target_pairs={{0,4},{4,0},{1,5},{5,1},{2,6},{6,2},{3,7},{7,3},{8,12},{12,8},{9,1... | collective-permute-start | bytes 49160 | tf_op jit(solution)/shard_map/ppermute | solution.py:119
  5.7 1.5 %collective-permute-start.1 = (f32[8,1,16,128]{3,2,1,0:T(8,128)S(1)}, f32[8,1,16,128]{3,2,1,0:T(8,128)S(1)}, u32[]{:S(2)}, u32[]{:S(2)}) collective-permute-start(f32[8,1,16,128]{3,2,1,0:T(8,128)S(1)} %get-tuple-element.49), channel_id=1, source_target_pairs={{0,1},{1,2},{2,3},{4,5},{5,6},{6,7},{8,9},{9,10},{10,11},{12,13},{... | collective-permute-start | bytes 196616 | tf_op jit(solution)/shard_map/ppermute | solution.py:119
  7.1 1.3 %collective-permute-start = (f32[8,1,16,128]{3,2,1,0:T(8,128)S(1)}, f32[8,1,16,128]{3,2,1,0:T(8,128)S(1)}, u32[]{:S(2)}, u32[]{:S(2)}) collective-permute-start(f32[8,1,16,128]{3,2,1,0:T(8,128)S(1)} %get-tuple-element.50), channel_id=1, source_target_pairs={{1,0},{2,1},{3,2},{5,4},{6,5},{7,6},{9,8},{10,9},{11,10},{13,12},{... | collective-permute-start | bytes 196616 | tf_op jit(solution)/shard_map/ppermute | solution.py:119
  9.0 0.2 copy.113
  9.2 0.3 copy.114
  9.5 1.6 %collective-permute-start.4 = (f32[8,4,16,1]{2,0,3,1:T(8,128)S(1)}, f32[8,4,16,1]{2,0,3,1:T(8,128)S(1)}, u32[]{:S(2)}, u32[]{:S(2)}) collective-permute-start(f32[8,4,16,1]{2,0,3,1:T(8,128)S(1)} %get-tuple-element.59), channel_id=1, source_target_pairs={{0,8},{8,16},{16,24},{24,0},{1,9},{9,17},{17,25},{25,1},{2,10},{10... | collective-permute-start | bytes 6152 | tf_op jit(solution)/shard_map/ppermute | solution.py:119
  11.1 2.2 %collective-permute-start.3 = (f32[8,4,16,1]{2,0,3,1:T(8,128)S(1)}, f32[8,4,16,1]{2,0,3,1:T(8,128)S(1)}, u32[]{:S(2)}, u32[]{:S(2)}) collective-permute-start(f32[8,4,16,1]{2,0,3,1:T(8,128)S(1)} %get-tuple-element.60), channel_id=1, source_target_pairs={{0,24},{8,0},{16,8},{24,16},{1,25},{9,1},{17,9},{25,17},{2,26},{10... | collective-permute-start | bytes 6152 | tf_op jit(solution)/shard_map/ppermute | solution.py:119
  13.4 0.7 copy-done.6
  14.1 0.7 copy-done.7
  15.1 0.5 multiply_reduce_fusion.2
  15.6 0.2 multiply_reduce_fusion
  16.2 0.6 copy-done.8
  18.1 0.7 %copy-done.4 = f32[5,4,16,128]{3,2,1,0:T(8,128)S(1)} copy-done((f32[5,4,16,128]{3,2,1,0:T(8,128)S(1)}, f32[5,4,16,128]{3,2,1,0:T(8,128)}, u32[]{:S(2)}) %copy-start.4) | copy-done | bytes 163864
  19.1 0.7 copy-done.2
  20.1 0.2 reshape.208
  20.3 0.2 reshape.211
  20.5 3.9 %collective-permute-start.9 = (f32[8,128]{1,0:T(8,128)S(1)}, f32[8,128]{1,0:T(8,128)S(1)}, u32[]{:S(2)}, u32[]{:S(2)}) collective-permute-start(f32[8,128]{1,0:T(8,128)S(1)} %pad_bitcast_fusion.2), channel_id=1, source_target_pairs={{0,24},{8,0},{16,8},{24,16},{1,25},{9,1},{17,9},{25,17},{2,26},{10... | collective-permute-start | bytes 12296 | tf_op jit(solution)/shard_map/ppermute | solution.py:123
  24.4 1.1 %collective-permute-start.6 = (f32[48,128]{1,0:T(8,128)S(1)}, f32[48,128]{1,0:T(8,128)S(1)}, u32[]{:S(2)}, u32[]{:S(2)}) collective-permute-start(f32[48,128]{1,0:T(8,128)S(1)} %reshape.204), channel_id=1, source_target_pairs={{0,4},{4,0},{1,5},{5,1},{2,6},{6,2},{3,7},{7,3},{8,12},{12,8},{9,1... | collective-permute-start | bytes 73736 | tf_op jit(solution)/shard_map/ppermute | solution.py:123
  25.9 4.8 %collective-permute-start.7 = (f32[8,128]{1,0:T(8,128)S(1)}, f32[8,128]{1,0:T(8,128)S(1)}, u32[]{:S(2)}, u32[]{:S(2)}) collective-permute-start(f32[8,128]{1,0:T(8,128)S(1)} %pad_bitcast_fusion.4), channel_id=1, source_target_pairs={{0,28},{8,4},{16,12},{24,20},{4,24},{12,0},{20,8},{28,16},{1,29},{... | collective-permute-start | bytes 12296 | tf_op jit(solution)/shard_map/ppermute | solution.py:123
  30.6 1.4 %collective-permute-done.5 = f32[8,128]{1,0:T(8,128)S(1)} collective-permute-done((f32[8,128]{1,0:T(8,128)S(1)}, f32[8,128]{1,0:T(8,128)S(1)}, u32[]{:S(2)}, u32[]{:S(2)}) %collective-permute-start.5) | collective-permute-done | bytes 4128 | tf_op jit(solution)/shard_map/ppermute | solution.py:123
  32.1 0.2 reshape.210
  32.3 0.2 reshape.213
  33.1 0.3 maximum_maximum_fusion
  33.5 0.2 reshape.214
  33.7 2.0 %collective-permute-start.10 = (f32[280,128]{1,0:T(8,128)S(1)}, f32[280,128]{1,0:T(8,128)S(1)}, u32[]{:S(2)}, u32[]{:S(2)}) collective-permute-start(f32[280,128]{1,0:T(8,128)S(1)} %pad_bitcast_fusion.1), channel_id=1, source_target_pairs={{0,1},{1,2},{2,3},{4,5},{5,6},{6,7},{8,9},{9,10},{10,11},{12,13},{... | collective-permute-start | bytes 430088 | tf_op jit(solution)/shard_map/ppermute | solution.py:123
  35.8 0.2 reshape.218
  36.0 1.3 %collective-permute-start.11 = (f32[280,128]{1,0:T(8,128)S(1)}, f32[280,128]{1,0:T(8,128)S(1)}, u32[]{:S(2)}, u32[]{:S(2)}) collective-permute-start(f32[280,128]{1,0:T(8,128)S(1)} %pad_bitcast_fusion), channel_id=1, source_target_pairs={{1,0},{2,1},{3,2},{5,4},{6,5},{7,6},{9,8},{10,9},{11,10},{13,12},{... | collective-permute-start | bytes 430088 | tf_op jit(solution)/shard_map/ppermute | solution.py:123
  37.3 0.2 reshape.217
  37.6 5.2 %collective-permute-done.11 = f32[280,128]{1,0:T(8,128)S(1)} collective-permute-done((f32[280,128]{1,0:T(8,128)S(1)}, f32[280,128]{1,0:T(8,128)S(1)}, u32[]{:S(2)}, u32[]{:S(2)}) %collective-permute-start.11) | collective-permute-done | bytes 143392 | tf_op jit(solution)/shard_map/ppermute | solution.py:123
  42.8 0.2 reshape.221
  43.0 0.3 pad_maximum_fusion
  43.9 1.2 %broadcast_multiply_fusion.1 = (f32[3,8,20,132]{3,2,1,0:T(8,128)S(1)}, f32[3,8,20,132]{3,2,1,0:T(8,128)S(1)}) fusion(f32[8,20,132]{2,1,0:T(8,128)S(1)} %get-tuple-element.36, f32[3,10,22,134]{3,2,1,0:T(8,128)S(1)} %get-tuple-element.27, f32[8,20,132]{2,1,0:T(8,128)S(1)} %get-tuple-element.35, f32[4,10,22,134]{3,2,1,0:T(8,128)S(1)} %pad_maximum_fusion, ...), kind=kLoop, calls=%fused_computation.42 | loop fusion | flops 760320 | bytes 2703360 | tf_op jit(solution)/shard_map/mul | solution.py:60
  45.0 0.9 %broadcast_multiply_fusion.2 = (f32[3,6,18,130]{3,2,1,0:T(8,128)S(1)}, f32[3,6,18,130]{3,2,1,0:T(8,128)S(1)}) fusion(f32[6,18,130]{2,1,0:T(8,128)S(1)} %get-tuple-element.34, f32[3,8,20,132]{3,2,1,0:T(8,128)S(1)} %get-tuple-element.25, f32[6,18,130]{2,1,0:T(8,128)S(1)} %get-tuple-element.33, f32[4,10,22,134]{3,2,1,0:T(8,128)S(1)} %pad_maximum_fusion, ...), kind=kLoop, calls=%fused_computation.45 | loop fusion | flops 505440 | bytes 1797120 | tf_op jit(solution)/shard_map/mul | solution.py:60
  45.9 0.9 %multiply_reduce_fusion.9 = (f32[3,4,128]{2,1,0:T(4,128)S(1)}, f32[3,4,16,128]{3,2,1,0:T(8,128)}) fusion(f32[4,16,128]{2,1,0:T(8,128)S(1)} %copy-done.5, f32[3,6,18,130]{3,2,1,0:T(8,128)S(1)} %get-tuple-element.23, f32[3,4,16,128]{3,2,1,0:T(8,128)S(1)} %multiply_reduce_fusion.6, f32[4,16,128]{2,1,0:T(8,128)S(1)} %fusion.34, ...), kind=kLoop, calls=%fused_computation.81 | loop fusion | flops 317952 | bytes 956416 | tf_op jit(solution)/shard_map/reduce_sum | solution.py:248
  46.8 0.4 convolution_bitcast_fusion
  47.2 5.6 %collective-permute-start.12 = (f32[3,128]{1,0:T(4,128)S(1)}, f32[3,128]{1,0:T(4,128)S(1)}, u32[]{:S(2)}, u32[]{:S(2)}) collective-permute-start(f32[3,128]{1,0:T(4,128)S(1)} %get-tuple-element.71), channel_id=1, source_target_pairs={{0,1},{1,2},{2,3},{4,5},{5,6},{6,7},{8,9},{9,10},{10,11},{12,13},{... | collective-permute-start | bytes 4616 | tf_op jit(solution)/shard_map/ppermute | solution.py:207
  52.8 1.3 %collective-permute-start.13 = (f32[3,128]{1,0:T(4,128)S(1)}, f32[3,128]{1,0:T(4,128)S(1)}, u32[]{:S(2)}, u32[]{:S(2)}) collective-permute-start(f32[3,128]{1,0:T(4,128)S(1)} %get-tuple-element.70), channel_id=1, source_target_pairs={{1,0},{2,1},{3,2},{5,4},{6,5},{7,6},{9,8},{10,9},{11,10},{13,12},{... | collective-permute-start | bytes 4616 | tf_op jit(solution)/shard_map/ppermute | solution.py:207
  54.1 1.3 %collective-permute-start.14 = (f32[3,128]{1,0:T(4,128)S(1)}, f32[3,128]{1,0:T(4,128)S(1)}, u32[]{:S(2)}, u32[]{:S(2)}) collective-permute-start(f32[3,128]{1,0:T(4,128)S(1)} %get-tuple-element.69), channel_id=1, source_target_pairs={{0,4},{4,0},{1,5},{5,1},{2,6},{6,2},{3,7},{7,3},{8,12},{12,8},{9,1... | collective-permute-start | bytes 4616 | tf_op jit(solution)/shard_map/ppermute | solution.py:207
  55.4 3.1 %collective-permute-start.15 = (f32[3,128]{1,0:T(4,128)S(1)}, f32[3,128]{1,0:T(4,128)S(1)}, u32[]{:S(2)}, u32[]{:S(2)}) collective-permute-start(f32[3,128]{1,0:T(4,128)S(1)} %get-tuple-element.71), channel_id=1, source_target_pairs={{0,5},{1,6},{2,7},{4,1},{5,2},{6,3},{8,13},{9,14},{10,15},{12,9},{... | collective-permute-start | bytes 4616 | tf_op jit(solution)/shard_map/ppermute | solution.py:207
  58.5 1.3 %collective-permute-start.16 = (f32[3,128]{1,0:T(4,128)S(1)}, f32[3,128]{1,0:T(4,128)S(1)}, u32[]{:S(2)}, u32[]{:S(2)}) collective-permute-start(f32[3,128]{1,0:T(4,128)S(1)} %get-tuple-element.70), channel_id=1, source_target_pairs={{1,4},{2,5},{3,6},{5,0},{6,1},{7,2},{9,12},{10,13},{11,14},{13,8},... | collective-permute-start | bytes 4616 | tf_op jit(solution)/shard_map/ppermute | solution.py:207
  59.9 4.1 %collective-permute-done.16 = f32[3,128]{1,0:T(4,128)S(1)} collective-permute-done((f32[3,128]{1,0:T(4,128)S(1)}, f32[3,128]{1,0:T(4,128)S(1)}, u32[]{:S(2)}, u32[]{:S(2)}) %collective-permute-start.16) | collective-permute-done | bytes 1568 | tf_op jit(solution)/shard_map/ppermute | solution.py:207
  64.0 4.7 %collective-permute-start.18 = (f32[3,128]{1,0:T(4,128)S(1)}, f32[3,128]{1,0:T(4,128)S(1)}, u32[]{:S(2)}, u32[]{:S(2)}) collective-permute-start(f32[3,128]{1,0:T(4,128)S(1)} %add_add_fusion.1), channel_id=1, source_target_pairs={{0,16},{8,24},{16,0},{24,8},{1,17},{9,25},{17,1},{25,9},{2,18},{10... | collective-permute-start | bytes 4616 | tf_op jit(solution)/shard_map/ppermute | solution.py:207
  68.7 1.0 %collective-permute-done.17 = f32[3,128]{1,0:T(4,128)S(1)} collective-permute-done((f32[3,128]{1,0:T(4,128)S(1)}, f32[3,128]{1,0:T(4,128)S(1)}, u32[]{:S(2)}, u32[]{:S(2)}) %collective-permute-start.17) | collective-permute-done | bytes 1568 | tf_op jit(solution)/shard_map/ppermute | solution.py:207
  69.7 0.6 collective-permute-done.18
  70.3 2.0 %collective-permute-done.19 = f32[3,128]{1,0:T(4,128)S(1)} collective-permute-done((f32[3,128]{1,0:T(4,128)S(1)}, f32[3,128]{1,0:T(4,128)S(1)}, u32[]{:S(2)}, u32[]{:S(2)}) %collective-permute-start.19) | collective-permute-done | bytes 1568 | tf_op jit(solution)/shard_map/ppermute | solution.py:207
  72.3 0.6 add_add_fusion
  (123 shorter events, 4.4 us)
Async XLA Ops:
  0.6 5.0 %copy-start = (f32[5,4,16,128]{3,2,1,0:T(8,128)S(1)}, f32[5,4,16,128]{3,2,1,0:T(8,128)}, u32[]{:S(2)}) copy-start(f32[5,4,16,128]{3,2,1,0:T(8,128)} %param.9) | copy-start | bytes 491524
  2.5 3.1 %copy-start.1 = (f32[3,4,16,128]{3,2,1,0:T(8,128)S(1)}, f32[3,4,16,128]{3,2,1,0:T(8,128)}, u32[]{:S(2)}) copy-start(f32[3,4,16,128]{3,2,1,0:T(8,128)} %param.11) | copy-start | bytes 294916
  2.6 15.1 %collective-permute-start.2 = (f32[8,4,1,128]{3,0,2,1:T(8,128)S(1)}, f32[8,4,1,128]{3,0,2,1:T(8,128)S(1)}, u32[]{:S(2)}, u32[]{:S(2)}) collective-permute-start(f32[8,4,1,128]{3,0,2,1:T(8,128)S(1)} %slice_select_fusion.1), channel_id=1, source_target_pairs={{0,4},{4,0},{1,5},{5,1},{2,6},{6,2},{3,7},{7,3},{8,12},{12,8},{9,1... | collective-permute-start | bytes 49160 | tf_op jit(solution)/shard_map/ppermute | solution.py:119
  5.7 12.2 %collective-permute-start.1 = (f32[8,1,16,128]{3,2,1,0:T(8,128)S(1)}, f32[8,1,16,128]{3,2,1,0:T(8,128)S(1)}, u32[]{:S(2)}, u32[]{:S(2)}) collective-permute-start(f32[8,1,16,128]{3,2,1,0:T(8,128)S(1)} %get-tuple-element.49), channel_id=1, source_target_pairs={{0,1},{1,2},{2,3},{4,5},{5,6},{6,7},{8,9},{9,10},{10,11},{12,13},{... | collective-permute-start | bytes 196616 | tf_op jit(solution)/shard_map/ppermute | solution.py:119
  7.1 10.8 %collective-permute-start = (f32[8,1,16,128]{3,2,1,0:T(8,128)S(1)}, f32[8,1,16,128]{3,2,1,0:T(8,128)S(1)}, u32[]{:S(2)}, u32[]{:S(2)}) collective-permute-start(f32[8,1,16,128]{3,2,1,0:T(8,128)S(1)} %get-tuple-element.50), channel_id=1, source_target_pairs={{1,0},{2,1},{3,2},{5,4},{6,5},{7,6},{9,8},{10,9},{11,10},{13,12},{... | collective-permute-start | bytes 196616 | tf_op jit(solution)/shard_map/ppermute | solution.py:119
  9.5 7.4 %collective-permute-start.4 = (f32[8,4,16,1]{2,0,3,1:T(8,128)S(1)}, f32[8,4,16,1]{2,0,3,1:T(8,128)S(1)}, u32[]{:S(2)}, u32[]{:S(2)}) collective-permute-start(f32[8,4,16,1]{2,0,3,1:T(8,128)S(1)} %get-tuple-element.59), channel_id=1, source_target_pairs={{0,8},{8,16},{16,24},{24,0},{1,9},{9,17},{17,25},{25,1},{2,10},{10... | collective-permute-start | bytes 6152 | tf_op jit(solution)/shard_map/ppermute | solution.py:119
  11.1 5.9 %collective-permute-start.3 = (f32[8,4,16,1]{2,0,3,1:T(8,128)S(1)}, f32[8,4,16,1]{2,0,3,1:T(8,128)S(1)}, u32[]{:S(2)}, u32[]{:S(2)}) collective-permute-start(f32[8,4,16,1]{2,0,3,1:T(8,128)S(1)} %get-tuple-element.60), channel_id=1, source_target_pairs={{0,24},{8,0},{16,8},{24,16},{1,25},{9,1},{17,9},{25,17},{2,26},{10... | collective-permute-start | bytes 6152 | tf_op jit(solution)/shard_map/ppermute | solution.py:119
  13.4 0.7 copy-start.6
  14.1 0.7 copy-start.7
  16.2 0.7 copy-start.8
  17.9 0.9 %copy-start.4 = (f32[5,4,16,128]{3,2,1,0:T(8,128)S(1)}, f32[5,4,16,128]{3,2,1,0:T(8,128)}, u32[]{:S(2)}) copy-start(f32[5,4,16,128]{3,2,1,0:T(8,128)} %param.10) | copy-start | bytes 491524
  19.0 0.9 %copy-start.3 = (f32[5,4,16,128]{3,2,1,0:T(8,128)}, f32[5,4,16,128]{3,2,1,0:T(8,128)S(1)}, u32[]{:S(2)}) copy-start(f32[5,4,16,128]{3,2,1,0:T(8,128)S(1)} %fusion.15) | copy-start | bytes 491524
  19.0 0.8 %copy-start.2 = (f32[4,16,128]{2,1,0:T(8,128)S(1)}, f32[4,16,128]{2,1,0:T(8,128)}, u32[]{:S(2)}) copy-start(f32[4,16,128]{2,1,0:T(8,128)} %param.15) | copy-start | bytes 98308
  20.3 11.8 %collective-permute-start.8 = (f32[8,128]{1,0:T(8,128)S(1)}, f32[8,128]{1,0:T(8,128)S(1)}, u32[]{:S(2)}, u32[]{:S(2)}) collective-permute-start(f32[8,128]{1,0:T(8,128)S(1)} %pad_bitcast_fusion.3), channel_id=1, source_target_pairs={{0,8},{8,16},{16,24},{24,0},{1,9},{9,17},{17,25},{25,1},{2,10},{10... | collective-permute-start | bytes 12296 | tf_op jit(solution)/shard_map/ppermute | solution.py:123
  20.5 11.7 %collective-permute-start.9 = (f32[8,128]{1,0:T(8,128)S(1)}, f32[8,128]{1,0:T(8,128)S(1)}, u32[]{:S(2)}, u32[]{:S(2)}) collective-permute-start(f32[8,128]{1,0:T(8,128)S(1)} %pad_bitcast_fusion.2), channel_id=1, source_target_pairs={{0,24},{8,0},{16,8},{24,16},{1,25},{9,1},{17,9},{25,17},{2,26},{10... | collective-permute-start | bytes 12296 | tf_op jit(solution)/shard_map/ppermute | solution.py:123
  24.4 8.6 %collective-permute-start.6 = (f32[48,128]{1,0:T(8,128)S(1)}, f32[48,128]{1,0:T(8,128)S(1)}, u32[]{:S(2)}, u32[]{:S(2)}) collective-permute-start(f32[48,128]{1,0:T(8,128)S(1)} %reshape.204), channel_id=1, source_target_pairs={{0,4},{4,0},{1,5},{5,1},{2,6},{6,2},{3,7},{7,3},{8,12},{12,8},{9,1... | collective-permute-start | bytes 73736 | tf_op jit(solution)/shard_map/ppermute | solution.py:123
  25.7 6.4 %collective-permute-start.5 = (f32[8,128]{1,0:T(8,128)S(1)}, f32[8,128]{1,0:T(8,128)S(1)}, u32[]{:S(2)}, u32[]{:S(2)}) collective-permute-start(f32[8,128]{1,0:T(8,128)S(1)} %pad_bitcast_fusion.5), channel_id=1, source_target_pairs={{0,12},{8,20},{16,28},{24,4},{4,8},{12,16},{20,24},{28,0},{1,13},{... | collective-permute-start | bytes 12296 | tf_op jit(solution)/shard_map/ppermute | solution.py:123
  25.9 6.2 %collective-permute-start.7 = (f32[8,128]{1,0:T(8,128)S(1)}, f32[8,128]{1,0:T(8,128)S(1)}, u32[]{:S(2)}, u32[]{:S(2)}) collective-permute-start(f32[8,128]{1,0:T(8,128)S(1)} %pad_bitcast_fusion.4), channel_id=1, source_target_pairs={{0,28},{8,4},{16,12},{24,20},{4,24},{12,0},{20,8},{28,16},{1,29},{... | collective-permute-start | bytes 12296 | tf_op jit(solution)/shard_map/ppermute | solution.py:123
  33.7 3.6 %collective-permute-start.10 = (f32[280,128]{1,0:T(8,128)S(1)}, f32[280,128]{1,0:T(8,128)S(1)}, u32[]{:S(2)}, u32[]{:S(2)}) collective-permute-start(f32[280,128]{1,0:T(8,128)S(1)} %pad_bitcast_fusion.1), channel_id=1, source_target_pairs={{0,1},{1,2},{2,3},{4,5},{5,6},{6,7},{8,9},{9,10},{10,11},{12,13},{... | collective-permute-start | bytes 430088 | tf_op jit(solution)/shard_map/ppermute | solution.py:123
  36.0 1.3 %copy-start.9 = (s32[4,128]{1,0:T(4,128)S(1)}, s32[4,128]{1,0:T(4,128)}, u32[]{:S(2)}) copy-start(s32[4,128]{1,0:T(4,128)} %param.17) | copy-start | bytes 6148
  36.0 6.8 %collective-permute-start.11 = (f32[280,128]{1,0:T(8,128)S(1)}, f32[280,128]{1,0:T(8,128)S(1)}, u32[]{:S(2)}, u32[]{:S(2)}) collective-permute-start(f32[280,128]{1,0:T(8,128)S(1)} %pad_bitcast_fusion), channel_id=1, source_target_pairs={{1,0},{2,1},{3,2},{5,4},{6,5},{7,6},{9,8},{10,9},{11,10},{13,12},{... | collective-permute-start | bytes 430088 | tf_op jit(solution)/shard_map/ppermute | solution.py:123
  45.0 0.9 %copy-start.5 = (f32[4,16,128]{2,1,0:T(8,128)S(1)}, f32[4,16,128]{2,1,0:T(8,128)}, u32[]{:S(2)}) copy-start(f32[4,16,128]{2,1,0:T(8,128)} %param.16) | copy-start | bytes 98308
  47.2 12.6 %collective-permute-start.12 = (f32[3,128]{1,0:T(4,128)S(1)}, f32[3,128]{1,0:T(4,128)S(1)}, u32[]{:S(2)}, u32[]{:S(2)}) collective-permute-start(f32[3,128]{1,0:T(4,128)S(1)} %get-tuple-element.71), channel_id=1, source_target_pairs={{0,1},{1,2},{2,3},{4,5},{5,6},{6,7},{8,9},{9,10},{10,11},{12,13},{... | collective-permute-start | bytes 4616 | tf_op jit(solution)/shard_map/ppermute | solution.py:207
  52.8 7.1 %collective-permute-start.13 = (f32[3,128]{1,0:T(4,128)S(1)}, f32[3,128]{1,0:T(4,128)S(1)}, u32[]{:S(2)}, u32[]{:S(2)}) collective-permute-start(f32[3,128]{1,0:T(4,128)S(1)} %get-tuple-element.70), channel_id=1, source_target_pairs={{1,0},{2,1},{3,2},{5,4},{6,5},{7,6},{9,8},{10,9},{11,10},{13,12},{... | collective-permute-start | bytes 4616 | tf_op jit(solution)/shard_map/ppermute | solution.py:207
  54.1 5.8 %collective-permute-start.14 = (f32[3,128]{1,0:T(4,128)S(1)}, f32[3,128]{1,0:T(4,128)S(1)}, u32[]{:S(2)}, u32[]{:S(2)}) collective-permute-start(f32[3,128]{1,0:T(4,128)S(1)} %get-tuple-element.69), channel_id=1, source_target_pairs={{0,4},{4,0},{1,5},{5,1},{2,6},{6,2},{3,7},{7,3},{8,12},{12,8},{9,1... | collective-permute-start | bytes 4616 | tf_op jit(solution)/shard_map/ppermute | solution.py:207
  55.4 4.5 %collective-permute-start.15 = (f32[3,128]{1,0:T(4,128)S(1)}, f32[3,128]{1,0:T(4,128)S(1)}, u32[]{:S(2)}, u32[]{:S(2)}) collective-permute-start(f32[3,128]{1,0:T(4,128)S(1)} %get-tuple-element.71), channel_id=1, source_target_pairs={{0,5},{1,6},{2,7},{4,1},{5,2},{6,3},{8,13},{9,14},{10,15},{12,9},{... | collective-permute-start | bytes 4616 | tf_op jit(solution)/shard_map/ppermute | solution.py:207
  58.5 5.4 %collective-permute-start.16 = (f32[3,128]{1,0:T(4,128)S(1)}, f32[3,128]{1,0:T(4,128)S(1)}, u32[]{:S(2)}, u32[]{:S(2)}) collective-permute-start(f32[3,128]{1,0:T(4,128)S(1)} %get-tuple-element.70), channel_id=1, source_target_pairs={{1,4},{2,5},{3,6},{5,0},{6,1},{7,2},{9,12},{10,13},{11,14},{13,8},... | collective-permute-start | bytes 4616 | tf_op jit(solution)/shard_map/ppermute | solution.py:207
  64.0 5.8 %collective-permute-start.17 = (f32[3,128]{1,0:T(4,128)S(1)}, f32[3,128]{1,0:T(4,128)S(1)}, u32[]{:S(2)}, u32[]{:S(2)}) collective-permute-start(f32[3,128]{1,0:T(4,128)S(1)} %add_add_fusion.1), channel_id=1, source_target_pairs={{0,8},{8,16},{16,24},{24,0},{1,9},{9,17},{17,25},{25,1},{2,10},{10... | collective-permute-start | bytes 4616 | tf_op jit(solution)/shard_map/ppermute | solution.py:207
  64.0 6.3 %collective-permute-start.18 = (f32[3,128]{1,0:T(4,128)S(1)}, f32[3,128]{1,0:T(4,128)S(1)}, u32[]{:S(2)}, u32[]{:S(2)}) collective-permute-start(f32[3,128]{1,0:T(4,128)S(1)} %add_add_fusion.1), channel_id=1, source_target_pairs={{0,16},{8,24},{16,0},{24,8},{1,17},{9,25},{17,1},{25,9},{2,18},{10... | collective-permute-start | bytes 4616 | tf_op jit(solution)/shard_map/ppermute | solution.py:207
  68.7 3.6 %collective-permute-start.19 = (f32[3,128]{1,0:T(4,128)S(1)}, f32[3,128]{1,0:T(4,128)S(1)}, u32[]{:S(2)}, u32[]{:S(2)}) collective-permute-start(f32[3,128]{1,0:T(4,128)S(1)} %add_add_fusion.1), channel_id=1, source_target_pairs={{0,24},{8,0},{16,8},{24,16},{1,25},{9,1},{17,9},{25,17},{2,26},{10... | collective-permute-start | bytes 4616 | tf_op jit(solution)/shard_map/ppermute | solution.py:207

commit v9 on v7

--- a/solution.py
+++ b/solution.py
@@ -163,7 +163,7 @@
     return jnp.sum(jac[spread] * term[:, None], axis=0)
 
 
-def flux_faces(psi, weights, halos, owner_jac, neighbor_jac):
+def flux_faces(psi, weights, halos, owner_jac, neighbor_jac, base, stiffness):
     inner_terms = []
     for direction in range(3):
         dim = direction + 1
@@ -173,8 +173,7 @@
         w_low = lax.slice_in_dim(weights[direction], 0, length - 1, axis=direction)
         between = w_low[None] * (low - high)
         inner_terms.append((jac_apply(owner_jac[direction], between), jac_apply(neighbor_jac[direction], between)))
-    inner_terms = lax.optimization_barrier(inner_terms)
-    total = jnp.zeros_like(psi)
+    inner_terms, total, stiffness = lax.optimization_barrier((inner_terms, base, stiffness))
     for direction in range(3):
         dim = direction + 1
         length = psi.shape[dim]
@@ -189,7 +188,7 @@
         down = jnp.concatenate([jac_apply(neighbor_jac[direction], down_edge), down_inner], axis=dim)
         total = total + up
         total = total + down
-    return total
+    return total, stiffness
 
 
 def shifted(array, offsets):
@@ -229,7 +228,9 @@
         face_halos(fields, "normal", 2, False),
         face_halos(fields, "circ", 3, True),
     ]
-    residual = flux_faces(adjoint, face_weights, halos, owner_jac, neighbor_jac) + adjoint - objective_grad
+    residual, stiffness = flux_faces(
+        adjoint, face_weights, halos, owner_jac, neighbor_jac, adjoint - objective_grad, stiffness
+    )
     forcing = jac_apply(coupling.T, residual)
     margin = SWEEPS - 1
     joined = jnp.concatenate([stiffness[None], forcing], axis=0)

time: 70.3 us -> 71 us (level)
    ppermute x8, waiting for transfers between devices: 6.45 us -> 7.16 us  [shifted(): return lax.ppermute(array, axes, pairs)]
    unnamed x34 -> x32, local copies, waits for them, and re-layouts: 4.29 us -> 4.05 us
    reduce_sum x9 -> x10, other arithmetic: 1.46 us -> 1.53 us  [jac_apply(): return jnp.sum(jac[spread] * term[:, None], axis=0)]
  transfers between devices with their start and end apart: 20 -> 20, of which waited for: 5 -> 6; matrix products, arithmetic and copies ran while one was open for 5% -> 5% of each run, Pallas kernels for 0% -> 0%
where the time goes in v9:
time: 71 us; the launch traced here: 70.3 us
  starting transfers between devices  39.3 us (55%)
  waiting for transfers between devices  15.3 us (22%)
  local copies, waits for them, and re-layouts  6.93 us (10%)
  other arithmetic  6.9 us (10%)
  between operations  1.39 us (2%)
    ppermute x8, starting transfers between devices, shifted(): return lax.ppermute(array, axes, pairs)  18.3 us
    ppermute x8, starting transfers between devices, receive(): return lax.ppermute(take(array, rel, dims, width), axes, pairs)  14.2 us
    ppermute x8, waiting for transfers between devices, shifted(): return lax.ppermute(array, axes, pairs)  7.16 us
    ppermute x4, starting transfers between devices, receive_pair(): got = lax.ppermute(sent, axes, pairs + back)  6.77 us
    ppermute x4, waiting for transfers between devices, receive_pair(): got = lax.ppermute(sent, axes, pairs + back)  4.61 us
    unnamed x32, local copies, waits for them, and re-layouts  4.05 us
    ppermute x8, waiting for transfers between devices, receive(): return lax.ppermute(take(array, rel, dims, width), axes, pairs)  3.57 us
    mul x3, other arithmetic, relax(): weighted = stiff_pad[None] * mesh_pad  2.17 us
  transfers between devices with their start and end apart: 20, of which 6 were waited for; matrix products, arithmetic and copies ran while one was open for 5% of the time, Pallas kernels for 0%

profile of v9, /device:TPU:0, one launch (start us, length us, event | category | flops | bytes accessed | tf_op | source)
XLA Modules:
  0.0 70.3 jit_solution(11585068644068251844)
XLA Ops:
  0.6 1.0 %fusion.48 = (f32[5,4,1,128]{3,2,1,0:T(1,128)S(1)}, f32[5,4,1,128]{3,2,1,0:T(1,128)S(1)}) fusion(f32[5,4,16,128]{3,2,1,0:T(8,128)} %param.9), kind=kLoop, calls=%fused_computation.142 | loop fusion | bytes 40960 | tf_op jit(solution)/shard_map/slice | solution.py:88
  1.7 0.8 %fusion.52 = (f32[3,4,1,128]{3,2,1,0:T(1,128)S(1)}, f32[3,4,1,128]{3,2,1,0:T(1,128)S(1)}) fusion(f32[3,4,16,128]{3,2,1,0:T(8,128)} %param.11), kind=kLoop, calls=%fused_computation.146 | loop fusion | bytes 24576 | tf_op jit(solution)/shard_map/slice | solution.py:88
  2.6 3.0 %collective-permute-start.2 = (f32[8,4,1,128]{3,0,2,1:T(8,128)S(1)}, f32[8,4,1,128]{3,0,2,1:T(8,128)S(1)}, u32[]{:S(2)}, u32[]{:S(2)}) collective-permute-start(f32[8,4,1,128]{3,0,2,1:T(8,128)S(1)} %slice_select_fusion.1), channel_id=1, source_target_pairs={{0,4},{4,0},{1,5},{5,1},{2,6},{6,2},{3,7},{7,3},{8,12},{12,8},{9,1... | collective-permute-start | bytes 49160 | tf_op jit(solution)/shard_map/ppermute | solution.py:133
  5.7 1.5 %collective-permute-start.1 = (f32[8,1,16,128]{3,2,1,0:T(8,128)S(1)}, f32[8,1,16,128]{3,2,1,0:T(8,128)S(1)}, u32[]{:S(2)}, u32[]{:S(2)}) collective-permute-start(f32[8,1,16,128]{3,2,1,0:T(8,128)S(1)} %get-tuple-element.53), channel_id=1, source_target_pairs={{0,1},{1,2},{2,3},{4,5},{5,6},{6,7},{8,9},{9,10},{10,11},{12,13},{... | collective-permute-start | bytes 196616 | tf_op jit(solution)/shard_map/ppermute | solution.py:120
  7.1 1.3 %collective-permute-start = (f32[8,1,16,128]{3,2,1,0:T(8,128)S(1)}, f32[8,1,16,128]{3,2,1,0:T(8,128)S(1)}, u32[]{:S(2)}, u32[]{:S(2)}) collective-permute-start(f32[8,1,16,128]{3,2,1,0:T(8,128)S(1)} %get-tuple-element.54), channel_id=1, source_target_pairs={{1,0},{2,1},{3,2},{5,4},{6,5},{7,6},{9,8},{10,9},{11,10},{13,12},{... | collective-permute-start | bytes 196616 | tf_op jit(solution)/shard_map/ppermute | solution.py:120
  9.0 0.2 copy.87
  9.2 0.3 copy.88
  9.5 1.6 %collective-permute-start.4 = (f32[8,4,16,1]{2,0,3,1:T(8,128)S(1)}, f32[8,4,16,1]{2,0,3,1:T(8,128)S(1)}, u32[]{:S(2)}, u32[]{:S(2)}) collective-permute-start(f32[8,4,16,1]{2,0,3,1:T(8,128)S(1)} %get-tuple-element.69), channel_id=1, source_target_pairs={{0,8},{8,16},{16,24},{24,0},{1,9},{9,17},{17,25},{25,1},{2,10},{10... | collective-permute-start | bytes 6152 | tf_op jit(solution)/shard_map/ppermute | solution.py:120
  11.1 2.2 %collective-permute-start.3 = (f32[8,4,16,1]{2,0,3,1:T(8,128)S(1)}, f32[8,4,16,1]{2,0,3,1:T(8,128)S(1)}, u32[]{:S(2)}, u32[]{:S(2)}) collective-permute-start(f32[8,4,16,1]{2,0,3,1:T(8,128)S(1)} %get-tuple-element.70), channel_id=1, source_target_pairs={{0,24},{8,0},{16,8},{24,16},{1,25},{9,1},{17,9},{25,17},{2,26},{10... | collective-permute-start | bytes 6152 | tf_op jit(solution)/shard_map/ppermute | solution.py:120
  13.4 0.7 copy-done.6
  14.1 0.7 copy-done.7
  15.1 0.1 multiply_reduce_fusion.4
  15.3 0.5 multiply_reduce_fusion.2
  15.7 0.2 multiply_reduce_fusion
  16.0 0.2 slice_reduce_fusion
  16.1 0.5 copy-done.4
  16.7 0.6 copy-done.8
  17.8 0.2 copy.74
  18.0 0.2 copy.72
  18.7 0.2 fusion.14
  19.0 0.7 copy-done.2
  19.9 0.3 collective-permute-start.5
  20.2 1.6 %collective-permute-start.8 = (f32[4,4,16,3]{3,2,1,0:T(8,128)S(1)}, f32[4,4,16,3]{3,2,1,0:T(8,128)S(1)}, u32[]{:S(2)}, u32[]{:S(2)}) collective-permute-start(f32[4,4,16,3]{3,2,1,0:T(8,128)S(1)} %get-tuple-element.49), channel_id=1, source_target_pairs={{0,8},{8,16},{16,24},{24,0},{1,9},{9,17},{17,25},{25,1},{2,10},{10... | collective-permute-start | bytes 9224 | tf_op jit(solution)/shard_map/ppermute | solution.py:120
  21.8 2.5 %collective-permute-start.9 = (f32[4,4,16,3]{3,2,1,0:T(8,128)S(1)}, f32[4,4,16,3]{3,2,1,0:T(8,128)S(1)}, u32[]{:S(2)}, u32[]{:S(2)}) collective-permute-start(f32[4,4,16,3]{3,2,1,0:T(8,128)S(1)} %get-tuple-element.50), channel_id=1, source_target_pairs={{0,24},{8,0},{16,8},{24,16},{1,25},{9,1},{17,9},{25,17},{2,26},{10... | collective-permute-start | bytes 9224 | tf_op jit(solution)/shard_map/ppermute | solution.py:120
  24.4 1.0 %collective-permute-start.6 = (f32[4,4,3,128]{3,2,1,0:T(4,128)S(1)}, f32[4,4,3,128]{3,2,1,0:T(4,128)S(1)}, u32[]{:S(2)}, u32[]{:S(2)}) collective-permute-start(f32[4,4,3,128]{3,2,1,0:T(4,128)S(1)} %fusion.28), channel_id=1, source_target_pairs={{0,4},{4,0},{1,5},{5,1},{2,6},{6,2},{3,7},{7,3},{8,12},{12,8},{9,1... | collective-permute-start | bytes 73736 | tf_op jit(solution)/shard_map/ppermute | solution.py:133
  25.4 2.4 %collective-permute-start.7 = (f32[4,4,3,3]{3,2,1,0:T(4,128)S(1)}, f32[4,4,3,3]{3,2,1,0:T(4,128)S(1)}, u32[]{:S(2)}, u32[]{:S(2)}) collective-permute-start(f32[4,4,3,3]{3,2,1,0:T(4,128)S(1)} %get-tuple-element.52), channel_id=1, source_target_pairs={{0,28},{8,4},{16,12},{24,20},{4,24},{12,0},{20,8},{28,16},{1,29},{... | collective-permute-start | bytes 1736 | tf_op jit(solution)/shard_map/ppermute | solution.py:133
  27.8 4.6 %collective-permute-done.7 = f32[4,4,3,3]{3,2,1,0:T(4,128)S(1)} collective-permute-done((f32[4,4,3,3]{3,2,1,0:T(4,128)S(1)}, f32[4,4,3,3]{3,2,1,0:T(4,128)S(1)}, u32[]{:S(2)}, u32[]{:S(2)}) %collective-permute-start.7) | collective-permute-done | bytes 608 | tf_op jit(solution)/shard_map/ppermute | solution.py:133
  32.5 0.3 maximum_maximum_fusion
  32.9 2.2 %collective-permute-start.10 = (f32[4,3,22,134]{3,2,1,0:T(8,128)S(1)}, f32[4,3,22,134]{3,2,1,0:T(8,128)S(1)}, u32[]{:S(2)}, u32[]{:S(2)}) collective-permute-start(f32[4,3,22,134]{3,2,1,0:T(8,128)S(1)} %get-tuple-element.35), channel_id=1, source_target_pairs={{0,1},{1,2},{2,3},{4,5},{5,6},{6,7},{8,9},{9,10},{10,11},{12,13},{... | collective-permute-start | bytes 424520 | tf_op jit(solution)/shard_map/ppermute | solution.py:120
  35.1 1.3 %collective-permute-start.11 = (f32[4,3,22,134]{3,2,1,0:T(8,128)S(1)}, f32[4,3,22,134]{3,2,1,0:T(8,128)S(1)}, u32[]{:S(2)}, u32[]{:S(2)}) collective-permute-start(f32[4,3,22,134]{3,2,1,0:T(8,128)S(1)} %get-tuple-element.36), channel_id=1, source_target_pairs={{1,0},{2,1},{3,2},{5,4},{6,5},{7,6},{9,8},{10,9},{11,10},{13,12},{... | collective-permute-start | bytes 424520 | tf_op jit(solution)/shard_map/ppermute | solution.py:120
  36.4 3.6 %collective-permute-done.11 = f32[4,3,22,134]{3,2,1,0:T(8,128)S(1)} collective-permute-done((f32[4,3,22,134]{3,2,1,0:T(8,128)S(1)}, f32[4,3,22,134]{3,2,1,0:T(8,128)S(1)}, u32[]{:S(2)}, u32[]{:S(2)}) %collective-permute-start.11) | collective-permute-done | bytes 141536 | tf_op jit(solution)/shard_map/ppermute | solution.py:120
  40.0 0.3 pad_maximum_fusion
  40.8 1.2 %broadcast_multiply_fusion.1 = (f32[3,8,20,132]{3,2,1,0:T(8,128)S(1)}, f32[3,8,20,132]{3,2,1,0:T(8,128)S(1)}) fusion(f32[8,20,132]{2,1,0:T(8,128)S(1)} %get-tuple-element.40, f32[3,10,22,134]{3,2,1,0:T(8,128)S(1)} %get-tuple-element.31, f32[8,20,132]{2,1,0:T(8,128)S(1)} %get-tuple-element.39, f32[4,10,22,134]{3,2,1,0:T(8,128)S(1)} %pad_maximum_fusion, ...), kind=kLoop, calls=%fused_computation.42 | loop fusion | flops 760320 | bytes 2703360 | tf_op jit(solution)/shard_map/mul | solution.py:60
  42.0 0.9 %broadcast_multiply_fusion.2 = (f32[3,6,18,130]{3,2,1,0:T(8,128)S(1)}, f32[3,6,18,130]{3,2,1,0:T(8,128)S(1)}) fusion(f32[6,18,130]{2,1,0:T(8,128)S(1)} %get-tuple-element.38, f32[3,8,20,132]{3,2,1,0:T(8,128)S(1)} %get-tuple-element.29, f32[6,18,130]{2,1,0:T(8,128)S(1)} %get-tuple-element.37, f32[4,10,22,134]{3,2,1,0:T(8,128)S(1)} %pad_maximum_fusion, ...), kind=kLoop, calls=%fused_computation.45 | loop fusion | flops 505440 | bytes 1797120 | tf_op jit(solution)/shard_map/mul | solution.py:60
  42.9 0.9 %multiply_reduce_fusion.9 = (f32[3,4,128]{2,1,0:T(4,128)S(1)}, f32[3,4,16,128]{3,2,1,0:T(8,128)}) fusion(f32[4,16,128]{2,1,0:T(8,128)S(1)} %copy-done.5, f32[3,6,18,130]{3,2,1,0:T(8,128)S(1)} %get-tuple-element.27, f32[3,4,16,128]{3,2,1,0:T(8,128)S(1)} %multiply_reduce_fusion.6, f32[4,16,128]{2,1,0:T(8,128)S(1)} %fusion.33, ...), kind=kLoop, calls=%fused_computation.78 | loop fusion | flops 317952 | bytes 956416 | tf_op jit(solution)/shard_map/reduce_sum | solution.py:239
  43.8 0.4 convolution_bitcast_fusion
  44.2 7.0 %collective-permute-start.12 = (f32[3,128]{1,0:T(4,128)S(1)}, f32[3,128]{1,0:T(4,128)S(1)}, u32[]{:S(2)}, u32[]{:S(2)}) collective-permute-start(f32[3,128]{1,0:T(4,128)S(1)} %get-tuple-element.79), channel_id=1, source_target_pairs={{0,1},{1,2},{2,3},{4,5},{5,6},{6,7},{8,9},{9,10},{10,11},{12,13},{... | collective-permute-start | bytes 4616 | tf_op jit(solution)/shard_map/ppermute | solution.py:196
  51.2 1.3 %collective-permute-start.13 = (f32[3,128]{1,0:T(4,128)S(1)}, f32[3,128]{1,0:T(4,128)S(1)}, u32[]{:S(2)}, u32[]{:S(2)}) collective-permute-start(f32[3,128]{1,0:T(4,128)S(1)} %get-tuple-element.78), channel_id=1, source_target_pairs={{1,0},{2,1},{3,2},{5,4},{6,5},{7,6},{9,8},{10,9},{11,10},{13,12},{... | collective-permute-start | bytes 4616 | tf_op jit(solution)/shard_map/ppermute | solution.py:196
  52.5 0.8 %collective-permute-start.14 = (f32[3,128]{1,0:T(4,128)S(1)}, f32[3,128]{1,0:T(4,128)S(1)}, u32[]{:S(2)}, u32[]{:S(2)}) collective-permute-start(f32[3,128]{1,0:T(4,128)S(1)} %get-tuple-element.77), channel_id=1, source_target_pairs={{0,4},{4,0},{1,5},{5,1},{2,6},{6,2},{3,7},{7,3},{8,12},{12,8},{9,1... | collective-permute-start | bytes 4616 | tf_op jit(solution)/shard_map/ppermute | solution.py:196
  53.3 3.6 %collective-permute-start.15 = (f32[3,128]{1,0:T(4,128)S(1)}, f32[3,128]{1,0:T(4,128)S(1)}, u32[]{:S(2)}, u32[]{:S(2)}) collective-permute-start(f32[3,128]{1,0:T(4,128)S(1)} %get-tuple-element.79), channel_id=1, source_target_pairs={{0,5},{1,6},{2,7},{4,1},{5,2},{6,3},{8,13},{9,14},{10,15},{12,9},{... | collective-permute-start | bytes 4616 | tf_op jit(solution)/shard_map/ppermute | solution.py:196
  56.9 1.3 %collective-permute-start.16 = (f32[3,128]{1,0:T(4,128)S(1)}, f32[3,128]{1,0:T(4,128)S(1)}, u32[]{:S(2)}, u32[]{:S(2)}) collective-permute-start(f32[3,128]{1,0:T(4,128)S(1)} %get-tuple-element.78), channel_id=1, source_target_pairs={{1,4},{2,5},{3,6},{5,0},{6,1},{7,2},{9,12},{10,13},{11,14},{13,8},... | collective-permute-start | bytes 4616 | tf_op jit(solution)/shard_map/ppermute | solution.py:196
  58.2 3.6 %collective-permute-done.16 = f32[3,128]{1,0:T(4,128)S(1)} collective-permute-done((f32[3,128]{1,0:T(4,128)S(1)}, f32[3,128]{1,0:T(4,128)S(1)}, u32[]{:S(2)}, u32[]{:S(2)}) %collective-permute-start.16) | collective-permute-done | bytes 1568 | tf_op jit(solution)/shard_map/ppermute | solution.py:196
  61.8 1.0 %collective-permute-start.17 = (f32[3,128]{1,0:T(4,128)S(1)}, f32[3,128]{1,0:T(4,128)S(1)}, u32[]{:S(2)}, u32[]{:S(2)}) collective-permute-start(f32[3,128]{1,0:T(4,128)S(1)} %add_add_fusion.1), channel_id=1, source_target_pairs={{0,8},{8,16},{16,24},{24,0},{1,9},{9,17},{17,25},{25,1},{2,10},{10... | collective-permute-start | bytes 4616 | tf_op jit(solution)/shard_map/ppermute | solution.py:196
  62.8 3.3 %collective-permute-start.18 = (f32[3,128]{1,0:T(4,128)S(1)}, f32[3,128]{1,0:T(4,128)S(1)}, u32[]{:S(2)}, u32[]{:S(2)}) collective-permute-start(f32[3,128]{1,0:T(4,128)S(1)} %add_add_fusion.1), channel_id=1, source_target_pairs={{0,16},{8,24},{16,0},{24,8},{1,17},{9,25},{17,1},{25,9},{2,18},{10... | collective-permute-start | bytes 4616 | tf_op jit(solution)/shard_map/ppermute | solution.py:196
  66.1 1.1 %collective-permute-done.17 = f32[3,128]{1,0:T(4,128)S(1)} collective-permute-done((f32[3,128]{1,0:T(4,128)S(1)}, f32[3,128]{1,0:T(4,128)S(1)}, u32[]{:S(2)}, u32[]{:S(2)}) %collective-permute-start.17) | collective-permute-done | bytes 1568 | tf_op jit(solution)/shard_map/ppermute | solution.py:196
  67.2 0.5 collective-permute-done.18
  67.7 2.0 %collective-permute-done.19 = f32[3,128]{1,0:T(4,128)S(1)} collective-permute-done((f32[3,128]{1,0:T(4,128)S(1)}, f32[3,128]{1,0:T(4,128)S(1)}, u32[]{:S(2)}, u32[]{:S(2)}) %collective-permute-start.19) | collective-permute-done | bytes 1568 | tf_op jit(solution)/shard_map/ppermute | solution.py:196
  69.7 0.6 add_add_fusion
  (101 shorter events, 2.6 us)
Async XLA Ops:
  0.6 5.0 %copy-start = (f32[5,4,16,128]{3,2,1,0:T(8,128)S(1)}, f32[5,4,16,128]{3,2,1,0:T(8,128)}, u32[]{:S(2)}) copy-start(f32[5,4,16,128]{3,2,1,0:T(8,128)} %param.9) | copy-start | bytes 491524
  2.5 3.1 %copy-start.1 = (f32[3,4,16,128]{3,2,1,0:T(8,128)S(1)}, f32[3,4,16,128]{3,2,1,0:T(8,128)}, u32[]{:S(2)}) copy-start(f32[3,4,16,128]{3,2,1,0:T(8,128)} %param.11) | copy-start | bytes 294916
  2.6 15.6 %collective-permute-start.2 = (f32[8,4,1,128]{3,0,2,1:T(8,128)S(1)}, f32[8,4,1,128]{3,0,2,1:T(8,128)S(1)}, u32[]{:S(2)}, u32[]{:S(2)}) collective-permute-start(f32[8,4,1,128]{3,0,2,1:T(8,128)S(1)} %slice_select_fusion.1), channel_id=1, source_target_pairs={{0,4},{4,0},{1,5},{5,1},{2,6},{6,2},{3,7},{7,3},{8,12},{12,8},{9,1... | collective-permute-start | bytes 49160 | tf_op jit(solution)/shard_map/ppermute | solution.py:133
  5.7 12.8 %collective-permute-start.1 = (f32[8,1,16,128]{3,2,1,0:T(8,128)S(1)}, f32[8,1,16,128]{3,2,1,0:T(8,128)S(1)}, u32[]{:S(2)}, u32[]{:S(2)}) collective-permute-start(f32[8,1,16,128]{3,2,1,0:T(8,128)S(1)} %get-tuple-element.53), channel_id=1, source_target_pairs={{0,1},{1,2},{2,3},{4,5},{5,6},{6,7},{8,9},{9,10},{10,11},{12,13},{... | collective-permute-start | bytes 196616 | tf_op jit(solution)/shard_map/ppermute | solution.py:120
  7.1 11.3 %collective-permute-start = (f32[8,1,16,128]{3,2,1,0:T(8,128)S(1)}, f32[8,1,16,128]{3,2,1,0:T(8,128)S(1)}, u32[]{:S(2)}, u32[]{:S(2)}) collective-permute-start(f32[8,1,16,128]{3,2,1,0:T(8,128)S(1)} %get-tuple-element.54), channel_id=1, source_target_pairs={{1,0},{2,1},{3,2},{5,4},{6,5},{7,6},{9,8},{10,9},{11,10},{13,12},{... | collective-permute-start | bytes 196616 | tf_op jit(solution)/shard_map/ppermute | solution.py:120
  9.5 8.0 %collective-permute-start.4 = (f32[8,4,16,1]{2,0,3,1:T(8,128)S(1)}, f32[8,4,16,1]{2,0,3,1:T(8,128)S(1)}, u32[]{:S(2)}, u32[]{:S(2)}) collective-permute-start(f32[8,4,16,1]{2,0,3,1:T(8,128)S(1)} %get-tuple-element.69), channel_id=1, source_target_pairs={{0,8},{8,16},{16,24},{24,0},{1,9},{9,17},{17,25},{25,1},{2,10},{10... | collective-permute-start | bytes 6152 | tf_op jit(solution)/shard_map/ppermute | solution.py:120
  11.1 6.5 %collective-permute-start.3 = (f32[8,4,16,1]{2,0,3,1:T(8,128)S(1)}, f32[8,4,16,1]{2,0,3,1:T(8,128)S(1)}, u32[]{:S(2)}, u32[]{:S(2)}) collective-permute-start(f32[8,4,16,1]{2,0,3,1:T(8,128)S(1)} %get-tuple-element.70), channel_id=1, source_target_pairs={{0,24},{8,0},{16,8},{24,16},{1,25},{9,1},{17,9},{25,17},{2,26},{10... | collective-permute-start | bytes 6152 | tf_op jit(solution)/shard_map/ppermute | solution.py:120
  13.4 0.7 %copy-start.6 = (f32[3,5,5]{2,0,1:T(4,128)S(1)}, f32[3,5,5]{2,0,1:T(4,128)}, u32[]{:S(2)}) copy-start(f32[3,5,5]{2,0,1:T(4,128)} %param.12) | copy-start | bytes 904
  14.1 0.7 copy-start.7
  15.7 0.9 %copy-start.4 = (f32[5,4,16,128]{3,2,1,0:T(8,128)S(1)}, f32[5,4,16,128]{3,2,1,0:T(8,128)}, u32[]{:S(2)}) copy-start(f32[5,4,16,128]{3,2,1,0:T(8,128)} %param.10) | copy-start | bytes 491524
  16.7 0.7 copy-start.8
  18.9 0.9 %copy-start.3 = (f32[5,4,16,128]{3,2,1,0:T(8,128)}, f32[5,4,16,128]{3,2,1,0:T(8,128)S(1)}, u32[]{:S(2)}) copy-start(f32[5,4,16,128]{3,2,1,0:T(8,128)S(1)} %fusion.14) | copy-start | bytes 491524
  18.9 0.8 %copy-start.2 = (f32[4,16,128]{2,1,0:T(8,128)S(1)}, f32[4,16,128]{2,1,0:T(8,128)}, u32[]{:S(2)}) copy-start(f32[4,16,128]{2,1,0:T(8,128)} %param.15) | copy-start | bytes 98308
  19.9 7.9 %collective-permute-start.5 = (f32[4,4,3,3]{3,2,1,0:T(4,128)S(1)}, f32[4,4,3,3]{3,2,1,0:T(4,128)S(1)}, u32[]{:S(2)}, u32[]{:S(2)}) collective-permute-start(f32[4,4,3,3]{3,2,1,0:T(4,128)S(1)} %get-tuple-element.51), channel_id=1, source_target_pairs={{0,12},{8,20},{16,28},{24,4},{4,8},{12,16},{20,24},{28,0},{1,13},{... | collective-permute-start | bytes 1736 | tf_op jit(solution)/shard_map/ppermute | solution.py:133
  20.2 12.3 %collective-permute-start.8 = (f32[4,4,16,3]{3,2,1,0:T(8,128)S(1)}, f32[4,4,16,3]{3,2,1,0:T(8,128)S(1)}, u32[]{:S(2)}, u32[]{:S(2)}) collective-permute-start(f32[4,4,16,3]{3,2,1,0:T(8,128)S(1)} %get-tuple-element.49), channel_id=1, source_target_pairs={{0,8},{8,16},{16,24},{24,0},{1,9},{9,17},{17,25},{25,1},{2,10},{10... | collective-permute-start | bytes 9224 | tf_op jit(solution)/shard_map/ppermute | solution.py:120
  21.8 10.6 %collective-permute-start.9 = (f32[4,4,16,3]{3,2,1,0:T(8,128)S(1)}, f32[4,4,16,3]{3,2,1,0:T(8,128)S(1)}, u32[]{:S(2)}, u32[]{:S(2)}) collective-permute-start(f32[4,4,16,3]{3,2,1,0:T(8,128)S(1)} %get-tuple-element.50), channel_id=1, source_target_pairs={{0,24},{8,0},{16,8},{24,16},{1,25},{9,1},{17,9},{25,17},{2,26},{10... | collective-permute-start | bytes 9224 | tf_op jit(solution)/shard_map/ppermute | solution.py:120
  24.4 8.1 %collective-permute-start.6 = (f32[4,4,3,128]{3,2,1,0:T(4,128)S(1)}, f32[4,4,3,128]{3,2,1,0:T(4,128)S(1)}, u32[]{:S(2)}, u32[]{:S(2)}) collective-permute-start(f32[4,4,3,128]{3,2,1,0:T(4,128)S(1)} %fusion.28), channel_id=1, source_target_pairs={{0,4},{4,0},{1,5},{5,1},{2,6},{6,2},{3,7},{7,3},{8,12},{12,8},{9,1... | collective-permute-start | bytes 73736 | tf_op jit(solution)/shard_map/ppermute | solution.py:133
  25.4 7.1 %collective-permute-start.7 = (f32[4,4,3,3]{3,2,1,0:T(4,128)S(1)}, f32[4,4,3,3]{3,2,1,0:T(4,128)S(1)}, u32[]{:S(2)}, u32[]{:S(2)}) collective-permute-start(f32[4,4,3,3]{3,2,1,0:T(4,128)S(1)} %get-tuple-element.52), channel_id=1, source_target_pairs={{0,28},{8,4},{16,12},{24,20},{4,24},{12,0},{20,8},{28,16},{1,29},{... | collective-permute-start | bytes 1736 | tf_op jit(solution)/shard_map/ppermute | solution.py:133
  32.9 3.5 %copy-start.9 = (s32[4,128]{1,0:T(4,128)S(1)}, s32[4,128]{1,0:T(4,128)}, u32[]{:S(2)}) copy-start(s32[4,128]{1,0:T(4,128)} %param.17) | copy-start | bytes 6148
  32.9 3.5 %collective-permute-start.10 = (f32[4,3,22,134]{3,2,1,0:T(8,128)S(1)}, f32[4,3,22,134]{3,2,1,0:T(8,128)S(1)}, u32[]{:S(2)}, u32[]{:S(2)}) collective-permute-start(f32[4,3,22,134]{3,2,1,0:T(8,128)S(1)} %get-tuple-element.35), channel_id=1, source_target_pairs={{0,1},{1,2},{2,3},{4,5},{5,6},{6,7},{8,9},{9,10},{10,11},{12,13},{... | collective-permute-start | bytes 424520 | tf_op jit(solution)/shard_map/ppermute | solution.py:120
  35.1 4.9 %collective-permute-start.11 = (f32[4,3,22,134]{3,2,1,0:T(8,128)S(1)}, f32[4,3,22,134]{3,2,1,0:T(8,128)S(1)}, u32[]{:S(2)}, u32[]{:S(2)}) collective-permute-start(f32[4,3,22,134]{3,2,1,0:T(8,128)S(1)} %get-tuple-element.36), channel_id=1, source_target_pairs={{1,0},{2,1},{3,2},{5,4},{6,5},{7,6},{9,8},{10,9},{11,10},{13,12},{... | collective-permute-start | bytes 424520 | tf_op jit(solution)/shard_map/ppermute | solution.py:120
  42.0 0.9 %copy-start.5 = (f32[4,16,128]{2,1,0:T(8,128)S(1)}, f32[4,16,128]{2,1,0:T(8,128)}, u32[]{:S(2)}) copy-start(f32[4,16,128]{2,1,0:T(8,128)} %param.16) | copy-start | bytes 98308
  44.2 14.0 %collective-permute-start.12 = (f32[3,128]{1,0:T(4,128)S(1)}, f32[3,128]{1,0:T(4,128)S(1)}, u32[]{:S(2)}, u32[]{:S(2)}) collective-permute-start(f32[3,128]{1,0:T(4,128)S(1)} %get-tuple-element.79), channel_id=1, source_target_pairs={{0,1},{1,2},{2,3},{4,5},{5,6},{6,7},{8,9},{9,10},{10,11},{12,13},{... | collective-permute-start | bytes 4616 | tf_op jit(solution)/shard_map/ppermute | solution.py:196
  51.2 7.1 %collective-permute-start.13 = (f32[3,128]{1,0:T(4,128)S(1)}, f32[3,128]{1,0:T(4,128)S(1)}, u32[]{:S(2)}, u32[]{:S(2)}) collective-permute-start(f32[3,128]{1,0:T(4,128)S(1)} %get-tuple-element.78), channel_id=1, source_target_pairs={{1,0},{2,1},{3,2},{5,4},{6,5},{7,6},{9,8},{10,9},{11,10},{13,12},{... | collective-permute-start | bytes 4616 | tf_op jit(solution)/shard_map/ppermute | solution.py:196
  52.5 5.8 %collective-permute-start.14 = (f32[3,128]{1,0:T(4,128)S(1)}, f32[3,128]{1,0:T(4,128)S(1)}, u32[]{:S(2)}, u32[]{:S(2)}) collective-permute-start(f32[3,128]{1,0:T(4,128)S(1)} %get-tuple-element.77), channel_id=1, source_target_pairs={{0,4},{4,0},{1,5},{5,1},{2,6},{6,2},{3,7},{7,3},{8,12},{12,8},{9,1... | collective-permute-start | bytes 4616 | tf_op jit(solution)/shard_map/ppermute | solution.py:196
  53.3 4.9 %collective-permute-start.15 = (f32[3,128]{1,0:T(4,128)S(1)}, f32[3,128]{1,0:T(4,128)S(1)}, u32[]{:S(2)}, u32[]{:S(2)}) collective-permute-start(f32[3,128]{1,0:T(4,128)S(1)} %get-tuple-element.79), channel_id=1, source_target_pairs={{0,5},{1,6},{2,7},{4,1},{5,2},{6,3},{8,13},{9,14},{10,15},{12,9},{... | collective-permute-start | bytes 4616 | tf_op jit(solution)/shard_map/ppermute | solution.py:196
  56.9 4.9 %collective-permute-start.16 = (f32[3,128]{1,0:T(4,128)S(1)}, f32[3,128]{1,0:T(4,128)S(1)}, u32[]{:S(2)}, u32[]{:S(2)}) collective-permute-start(f32[3,128]{1,0:T(4,128)S(1)} %get-tuple-element.78), channel_id=1, source_target_pairs={{1,4},{2,5},{3,6},{5,0},{6,1},{7,2},{9,12},{10,13},{11,14},{13,8},... | collective-permute-start | bytes 4616 | tf_op jit(solution)/shard_map/ppermute | solution.py:196
  61.8 5.4 %collective-permute-start.17 = (f32[3,128]{1,0:T(4,128)S(1)}, f32[3,128]{1,0:T(4,128)S(1)}, u32[]{:S(2)}, u32[]{:S(2)}) collective-permute-start(f32[3,128]{1,0:T(4,128)S(1)} %add_add_fusion.1), channel_id=1, source_target_pairs={{0,8},{8,16},{16,24},{24,0},{1,9},{9,17},{17,25},{25,1},{2,10},{10... | collective-permute-start | bytes 4616 | tf_op jit(solution)/shard_map/ppermute | solution.py:196
  62.8 4.9 %collective-permute-start.18 = (f32[3,128]{1,0:T(4,128)S(1)}, f32[3,128]{1,0:T(4,128)S(1)}, u32[]{:S(2)}, u32[]{:S(2)}) collective-permute-start(f32[3,128]{1,0:T(4,128)S(1)} %add_add_fusion.1), channel_id=1, source_target_pairs={{0,16},{8,24},{16,0},{24,8},{1,17},{9,25},{17,1},{25,9},{2,18},{10... | collective-permute-start | bytes 4616 | tf_op jit(solution)/shard_map/ppermute | solution.py:196
  66.1 3.6 %collective-permute-start.19 = (f32[3,128]{1,0:T(4,128)S(1)}, f32[3,128]{1,0:T(4,128)S(1)}, u32[]{:S(2)}, u32[]{:S(2)}) collective-permute-start(f32[3,128]{1,0:T(4,128)S(1)} %add_add_fusion.1), channel_id=1, source_target_pairs={{0,24},{8,0},{16,8},{24,16},{1,25},{9,1},{17,9},{25,17},{2,26},{10... | collective-permute-start | bytes 4616 | tf_op jit(solution)/shard_map/ppermute | solution.py:196

commit v10 on v7

--- a/solution.py
+++ b/solution.py
@@ -199,6 +199,14 @@
 
 def reduce_panels(terms):
     below, own, above = (terms[:, i * PANEL_DEV : (i + 1) * PANEL_DEV] for i in range(3))
+    devices = math.prod(lax.axis_size(a) for a in ORDER)
+    if devices <= 64:
+        spans = lax.axis_size("span")
+        relative = jnp.arange(devices, dtype=jnp.int32) % spans - lax.axis_index("span") + 1
+        chunks = jnp.zeros((devices,) + own.shape, own.dtype)
+        for index, block in enumerate((below, own, above)):
+            chunks = jnp.where((relative == index)[:, None, None], block[None], chunks)
+        return jnp.sum(lax.all_to_all(chunks, ORDER, 0, 0, tiled=False), axis=0)
     if lax.axis_size("normal") != 2 or lax.axis_size("circ") > 4:
         own = lax.psum(own + shifted(above, {"span": 1}) + shifted(below, {"span": -1}), ("circ", "normal"))
         return own

time: 70.3 us -> 61.8 us (0.88)
  starting transfers between devices: 38.8 us -> 21 us
  blocking collectives: 0 us -> 15 us
  waiting for transfers between devices: 15.1 us -> 8.64 us
    ppermute x8 -> x0, starting transfers between devices: 17.8 us -> none  [shifted(): return lax.ppermute(array, axes, pairs)]
    all_to_all x0 -> x1, blocking collectives: none -> 15 us  [reduce_panels(): return jnp.sum(lax.all_to_all(chunks, ORDER, 0, 0, tiled=False), axis=0)]
    ppermute x8 -> x0, waiting for transfers between devices: 6.45 us -> none  [shifted(): return lax.ppermute(array, axes, pairs)]
  transfers between devices with their start and end apart: 20 -> 12, of which waited for: 5 -> 2; matrix products, arithmetic and copies ran while one was open for 5% -> 5% of each run, Pallas kernels for 0% -> 0%
where the time goes in v10:
time: 61.8 us; the launch traced here: 61.3 us
  starting transfers between devices  21 us (34%)
  blocking collectives  15 us (24%)
  waiting for transfers between devices  8.64 us (14%)
  local copies, waits for them, and re-layouts  7.84 us (13%)
  other arithmetic  7.03 us (11%)
  between operations  1.33 us (2%)
    all_to_all x1, blocking collectives, reduce_panels(): return jnp.sum(lax.all_to_all(chunks, ORDER, 0, 0, tiled=False), axis=0)  15 us
    ppermute x8, starting transfers between devices, receive(): return lax.ppermute(take(array, rel, dims, width), axes, pairs)  14.2 us
    ppermute x4, starting transfers between devices, receive_pair(): got = lax.ppermute(sent, axes, pairs + back)  6.77 us
    unnamed x34, local copies, waits for them, and re-layouts  4.96 us
    ppermute x4, waiting for transfers between devices, receive_pair(): got = lax.ppermute(sent, axes, pairs + back)  4.61 us
    ppermute x8, waiting for transfers between devices, receive(): return lax.ppermute(take(array, rel, dims, width), axes, pairs)  4.03 us
    mul x3, other arithmetic, relax(): weighted = stiff_pad[None] * mesh_pad  2.17 us
    slice x9, local copies, waits for them, and re-layouts, edge(): return lax.slice_in_dim(array, start, start + width, axis=dim)  2.08 us
  transfers between devices with their start and end apart: 12, of which 2 were waited for; matrix products, arithmetic and copies ran while one was open for 5% of the time, Pallas kernels for 0%

profile of v10, /device:TPU:0, one launch (start us, length us, event | category | flops | bytes accessed | tf_op | source)
XLA Modules:
  0.0 61.3 jit_solution(373118234901711289)
XLA Ops:
  0.6 1.0 %fusion.51 = (f32[5,4,1,128]{3,2,1,0:T(1,128)S(1)}, f32[5,4,1,128]{3,2,1,0:T(1,128)S(1)}) fusion(f32[5,4,16,128]{3,2,1,0:T(8,128)} %param.9), kind=kLoop, calls=%fused_computation.148 | loop fusion | bytes 40960 | tf_op jit(solution)/shard_map/slice | solution.py:88
  1.7 0.8 %fusion.55 = (f32[3,4,1,128]{3,2,1,0:T(1,128)S(1)}, f32[3,4,1,128]{3,2,1,0:T(1,128)S(1)}) fusion(f32[3,4,16,128]{3,2,1,0:T(8,128)} %param.11), kind=kLoop, calls=%fused_computation.152 | loop fusion | bytes 24576 | tf_op jit(solution)/shard_map/slice | solution.py:88
  2.6 3.0 %collective-permute-start.2 = (f32[8,4,1,128]{3,0,2,1:T(8,128)S(1)}, f32[8,4,1,128]{3,0,2,1:T(8,128)S(1)}, u32[]{:S(2)}, u32[]{:S(2)}) collective-permute-start(f32[8,4,1,128]{3,0,2,1:T(8,128)S(1)} %slice_select_fusion.1), channel_id=1, source_target_pairs={{0,4},{4,0},{1,5},{5,1},{2,6},{6,2},{3,7},{7,3},{8,12},{12,8},{9,1... | collective-permute-start | bytes 49160 | tf_op jit(solution)/shard_map/ppermute | solution.py:133
  5.7 1.5 %collective-permute-start.1 = (f32[8,1,16,128]{3,2,1,0:T(8,128)S(1)}, f32[8,1,16,128]{3,2,1,0:T(8,128)S(1)}, u32[]{:S(2)}, u32[]{:S(2)}) collective-permute-start(f32[8,1,16,128]{3,2,1,0:T(8,128)S(1)} %get-tuple-element.49), channel_id=1, source_target_pairs={{0,1},{1,2},{2,3},{4,5},{5,6},{6,7},{8,9},{9,10},{10,11},{12,13},{... | collective-permute-start | bytes 196616 | tf_op jit(solution)/shard_map/ppermute | solution.py:120
  7.1 1.3 %collective-permute-start = (f32[8,1,16,128]{3,2,1,0:T(8,128)S(1)}, f32[8,1,16,128]{3,2,1,0:T(8,128)S(1)}, u32[]{:S(2)}, u32[]{:S(2)}) collective-permute-start(f32[8,1,16,128]{3,2,1,0:T(8,128)S(1)} %get-tuple-element.50), channel_id=1, source_target_pairs={{1,0},{2,1},{3,2},{5,4},{6,5},{7,6},{9,8},{10,9},{11,10},{13,12},{... | collective-permute-start | bytes 196616 | tf_op jit(solution)/shard_map/ppermute | solution.py:120
  8.5 0.1 fusion.50
  8.6 0.1 copy.117
  8.8 0.1 copy.118
  9.0 0.2 copy.115
  9.2 0.3 copy.116
  9.5 1.6 %collective-permute-start.4 = (f32[8,4,16,1]{2,0,3,1:T(8,128)S(1)}, f32[8,4,16,1]{2,0,3,1:T(8,128)S(1)}, u32[]{:S(2)}, u32[]{:S(2)}) collective-permute-start(f32[8,4,16,1]{2,0,3,1:T(8,128)S(1)} %get-tuple-element.65), channel_id=1, source_target_pairs={{0,8},{8,16},{16,24},{24,0},{1,9},{9,17},{17,25},{25,1},{2,10},{10... | collective-permute-start | bytes 6152 | tf_op jit(solution)/shard_map/ppermute | solution.py:120
  11.1 2.2 %collective-permute-start.3 = (f32[8,4,16,1]{2,0,3,1:T(8,128)S(1)}, f32[8,4,16,1]{2,0,3,1:T(8,128)S(1)}, u32[]{:S(2)}, u32[]{:S(2)}) collective-permute-start(f32[8,4,16,1]{2,0,3,1:T(8,128)S(1)} %get-tuple-element.66), channel_id=1, source_target_pairs={{0,24},{8,0},{16,8},{24,16},{1,25},{9,1},{17,9},{25,17},{2,26},{10... | collective-permute-start | bytes 6152 | tf_op jit(solution)/shard_map/ppermute | solution.py:120
  13.4 0.7 %copy-done.6 = f32[3,5,5]{2,0,1:T(4,128)S(1)} copy-done((f32[3,5,5]{2,0,1:T(4,128)S(1)}, f32[3,5,5]{2,0,1:T(4,128)}, u32[]{:S(2)}) %copy-start.6) | copy-done | bytes 324
  14.1 0.7 %copy-done.7 = f32[3,5,5]{2,0,1:T(4,128)S(1)} copy-done((f32[3,5,5]{2,0,1:T(4,128)S(1)}, f32[3,5,5]{2,0,1:T(4,128)}, u32[]{:S(2)}) %copy-start.7) | copy-done | bytes 324
  14.9 0.1 subtract_multiply_fusion
  15.1 0.7 %copy-done.9 = s32[4,128]{1,0:T(4,128)S(1)} copy-done((s32[4,128]{1,0:T(4,128)S(1)}, s32[4,128]{1,0:T(4,128)}, u32[]{:S(2)}) %copy-start.9) | copy-done | bytes 2072
  15.8 0.5 multiply_reduce_fusion.2
  16.3 0.2 multiply_reduce_fusion
  16.5 0.1 multiply_reduce_fusion.4
  16.7 0.2 slice_reduce_fusion
  16.9 0.6 %copy-done.8 = f32[3,5]{1,0:T(4,128)S(1)} copy-done((f32[3,5]{1,0:T(4,128)S(1)}, f32[3,5]{1,0:T(4,128)}, u32[]{:S(2)}) %copy-start.8) | copy-done | bytes 84
  17.9 0.2 copy.100
  18.1 0.2 copy.98
  18.6 0.1 multiply_reduce_fusion.7
  18.8 0.7 %copy-done.4 = f32[5,4,16,128]{3,2,1,0:T(8,128)S(1)} copy-done((f32[5,4,16,128]{3,2,1,0:T(8,128)S(1)}, f32[5,4,16,128]{3,2,1,0:T(8,128)}, u32[]{:S(2)}) %copy-start.4) | copy-done | bytes 163864
  19.5 0.2 fusion.15
  19.8 0.7 %copy-done.2 = f32[4,16,128]{2,1,0:T(8,128)S(1)} copy-done((f32[4,16,128]{2,1,0:T(8,128)S(1)}, f32[4,16,128]{2,1,0:T(8,128)}, u32[]{:S(2)}) %copy-start.2) | copy-done | bytes 32792
  20.7 0.3 collective-permute-start.5
  21.1 1.6 %collective-permute-start.8 = (f32[4,4,16,3]{3,2,1,0:T(8,128)S(1)}, f32[4,4,16,3]{3,2,1,0:T(8,128)S(1)}, u32[]{:S(2)}, u32[]{:S(2)}) collective-permute-start(f32[4,4,16,3]{3,2,1,0:T(8,128)S(1)} %get-tuple-element.45), channel_id=1, source_target_pairs={{0,8},{8,16},{16,24},{24,0},{1,9},{9,17},{17,25},{25,1},{2,10},{10... | collective-permute-start | bytes 9224 | tf_op jit(solution)/shard_map/ppermute | solution.py:120
  22.7 2.5 %collective-permute-start.9 = (f32[4,4,16,3]{3,2,1,0:T(8,128)S(1)}, f32[4,4,16,3]{3,2,1,0:T(8,128)S(1)}, u32[]{:S(2)}, u32[]{:S(2)}) collective-permute-start(f32[4,4,16,3]{3,2,1,0:T(8,128)S(1)} %get-tuple-element.46), channel_id=1, source_target_pairs={{0,24},{8,0},{16,8},{24,16},{1,25},{9,1},{17,9},{25,17},{2,26},{10... | collective-permute-start | bytes 9224 | tf_op jit(solution)/shard_map/ppermute | solution.py:120
  25.2 2.4 %collective-permute-start.7 = (f32[4,4,3,3]{3,2,1,0:T(4,128)S(1)}, f32[4,4,3,3]{3,2,1,0:T(4,128)S(1)}, u32[]{:S(2)}, u32[]{:S(2)}) collective-permute-start(f32[4,4,3,3]{3,2,1,0:T(4,128)S(1)} %get-tuple-element.48), channel_id=1, source_target_pairs={{0,28},{8,4},{16,12},{24,20},{4,24},{12,0},{20,8},{28,16},{1,29},{... | collective-permute-start | bytes 1736 | tf_op jit(solution)/shard_map/ppermute | solution.py:133
  27.6 1.0 %collective-permute-start.6 = (f32[4,4,3,128]{3,2,1,0:T(4,128)S(1)}, f32[4,4,3,128]{3,2,1,0:T(4,128)S(1)}, u32[]{:S(2)}, u32[]{:S(2)}) collective-permute-start(f32[4,4,3,128]{3,2,1,0:T(4,128)S(1)} %fusion.29), channel_id=1, source_target_pairs={{0,4},{4,0},{1,5},{5,1},{2,6},{6,2},{3,7},{7,3},{8,12},{12,8},{9,1... | collective-permute-start | bytes 73736 | tf_op jit(solution)/shard_map/ppermute | solution.py:133
  28.7 4.6 %collective-permute-done.7 = f32[4,4,3,3]{3,2,1,0:T(4,128)S(1)} collective-permute-done((f32[4,4,3,3]{3,2,1,0:T(4,128)S(1)}, f32[4,4,3,3]{3,2,1,0:T(4,128)S(1)}, u32[]{:S(2)}, u32[]{:S(2)}) %collective-permute-start.7) | collective-permute-done | bytes 608 | tf_op jit(solution)/shard_map/ppermute | solution.py:133
  33.3 0.3 maximum_maximum_fusion
  33.7 2.2 %collective-permute-start.10 = (f32[4,3,22,134]{3,2,1,0:T(8,128)S(1)}, f32[4,3,22,134]{3,2,1,0:T(8,128)S(1)}, u32[]{:S(2)}, u32[]{:S(2)}) collective-permute-start(f32[4,3,22,134]{3,2,1,0:T(8,128)S(1)} %get-tuple-element.31), channel_id=1, source_target_pairs={{0,1},{1,2},{2,3},{4,5},{5,6},{6,7},{8,9},{9,10},{10,11},{12,13},{... | collective-permute-start | bytes 424520 | tf_op jit(solution)/shard_map/ppermute | solution.py:120
  35.9 1.3 %collective-permute-start.11 = (f32[4,3,22,134]{3,2,1,0:T(8,128)S(1)}, f32[4,3,22,134]{3,2,1,0:T(8,128)S(1)}, u32[]{:S(2)}, u32[]{:S(2)}) collective-permute-start(f32[4,3,22,134]{3,2,1,0:T(8,128)S(1)} %get-tuple-element.32), channel_id=1, source_target_pairs={{1,0},{2,1},{3,2},{5,4},{6,5},{7,6},{9,8},{10,9},{11,10},{13,12},{... | collective-permute-start | bytes 424520 | tf_op jit(solution)/shard_map/ppermute | solution.py:120
  37.2 4.0 %collective-permute-done.11 = f32[4,3,22,134]{3,2,1,0:T(8,128)S(1)} collective-permute-done((f32[4,3,22,134]{3,2,1,0:T(8,128)S(1)}, f32[4,3,22,134]{3,2,1,0:T(8,128)S(1)}, u32[]{:S(2)}, u32[]{:S(2)}) %collective-permute-start.11) | collective-permute-done | bytes 141536 | tf_op jit(solution)/shard_map/ppermute | solution.py:120
  41.2 0.3 pad_maximum_fusion
  41.6 0.1 multiply_add_fusion
  41.7 0.1 multiply_add_fusion.1
  41.9 0.1 broadcast_multiply_fusion
  42.1 1.2 %broadcast_multiply_fusion.1 = (f32[3,8,20,132]{3,2,1,0:T(8,128)S(1)}, f32[3,8,20,132]{3,2,1,0:T(8,128)S(1)}) fusion(f32[8,20,132]{2,1,0:T(8,128)S(1)} %get-tuple-element.36, f32[3,10,22,134]{3,2,1,0:T(8,128)S(1)} %get-tuple-element.27, f32[8,20,132]{2,1,0:T(8,128)S(1)} %get-tuple-element.35, f32[4,10,22,134]{3,2,1,0:T(8,128)S(1)} %pad_maximum_fusion, ...), kind=kLoop, calls=%fused_computation.42 | loop fusion | flops 760320 | bytes 2703360 | tf_op jit(solution)/shard_map/mul | solution.py:60
  43.3 0.9 %broadcast_multiply_fusion.2 = (f32[3,6,18,130]{3,2,1,0:T(8,128)S(1)}, f32[3,6,18,130]{3,2,1,0:T(8,128)S(1)}) fusion(f32[6,18,130]{2,1,0:T(8,128)S(1)} %get-tuple-element.34, f32[3,8,20,132]{3,2,1,0:T(8,128)S(1)} %get-tuple-element.25, f32[6,18,130]{2,1,0:T(8,128)S(1)} %get-tuple-element.33, f32[4,10,22,134]{3,2,1,0:T(8,128)S(1)} %pad_maximum_fusion, ...), kind=kLoop, calls=%fused_computation.45 | loop fusion | flops 505440 | bytes 1797120 | tf_op jit(solution)/shard_map/mul | solution.py:60
  44.2 0.9 %multiply_reduce_fusion.9 = (f32[3,4,128]{2,1,0:T(4,128)S(1)}, f32[3,4,16,128]{3,2,1,0:T(8,128)}) fusion(f32[4,16,128]{2,1,0:T(8,128)S(1)} %copy-done.5, f32[3,6,18,130]{3,2,1,0:T(8,128)S(1)} %get-tuple-element.23, f32[3,4,16,128]{3,2,1,0:T(8,128)S(1)} %multiply_reduce_fusion.6, f32[4,16,128]{2,1,0:T(8,128)S(1)} %fusion.34, ...), kind=kLoop, calls=%fused_computation.79 | loop fusion | flops 317952 | bytes 956416 | tf_op jit(solution)/shard_map/reduce_sum | solution.py:246
  45.0 0.4 convolution_bitcast_fusion
  45.5 0.2 select_select_fusion
  45.7 15.0 %all_to_all.5 = f32[32,3,128]{2,1,0:T(4,128)S(1)} all-to-all(f32[32,3,128]{2,1,0:T(4,128)S(1)} %select_select_fusion), channel_id=1, replica_groups=mesh['circ'=4,'normal'=2,'span'=4] {'circ','normal','span'}, dimensions={0} | all-to-all | bytes 98304 | tf_op jit(solution)/shard_map/all_to_all | solution.py:209
  60.6 0.6 %reduce_sum.167 = f32[3,128]{1,0:T(4,128)} reduce(f32[32,3,128]{2,1,0:T(4,128)S(1)} %all_to_all.5, f32[]{:T(128)} %constant.14.clone.1), dimensions={0}, to_apply=%region_14.15 | reduce | flops 11904 | bytes 50692 | tf_op jit(solution)/shard_map/reduce_sum | solution.py:209
  (87 shorter events, 1.6 us)
Async XLA Ops:
  0.6 5.0 %copy-start = (f32[5,4,16,128]{3,2,1,0:T(8,128)S(1)}, f32[5,4,16,128]{3,2,1,0:T(8,128)}, u32[]{:S(2)}) copy-start(f32[5,4,16,128]{3,2,1,0:T(8,128)} %param.9) | copy-start | bytes 491524
  2.5 3.1 %copy-start.1 = (f32[3,4,16,128]{3,2,1,0:T(8,128)S(1)}, f32[3,4,16,128]{3,2,1,0:T(8,128)}, u32[]{:S(2)}) copy-start(f32[3,4,16,128]{3,2,1,0:T(8,128)} %param.11) | copy-start | bytes 294916
  2.6 15.7 %collective-permute-start.2 = (f32[8,4,1,128]{3,0,2,1:T(8,128)S(1)}, f32[8,4,1,128]{3,0,2,1:T(8,128)S(1)}, u32[]{:S(2)}, u32[]{:S(2)}) collective-permute-start(f32[8,4,1,128]{3,0,2,1:T(8,128)S(1)} %slice_select_fusion.1), channel_id=1, source_target_pairs={{0,4},{4,0},{1,5},{5,1},{2,6},{6,2},{3,7},{7,3},{8,12},{12,8},{9,1... | collective-permute-start | bytes 49160 | tf_op jit(solution)/shard_map/ppermute | solution.py:133
  5.7 12.9 %collective-permute-start.1 = (f32[8,1,16,128]{3,2,1,0:T(8,128)S(1)}, f32[8,1,16,128]{3,2,1,0:T(8,128)S(1)}, u32[]{:S(2)}, u32[]{:S(2)}) collective-permute-start(f32[8,1,16,128]{3,2,1,0:T(8,128)S(1)} %get-tuple-element.49), channel_id=1, source_target_pairs={{0,1},{1,2},{2,3},{4,5},{5,6},{6,7},{8,9},{9,10},{10,11},{12,13},{... | collective-permute-start | bytes 196616 | tf_op jit(solution)/shard_map/ppermute | solution.py:120
  7.1 11.5 %collective-permute-start = (f32[8,1,16,128]{3,2,1,0:T(8,128)S(1)}, f32[8,1,16,128]{3,2,1,0:T(8,128)S(1)}, u32[]{:S(2)}, u32[]{:S(2)}) collective-permute-start(f32[8,1,16,128]{3,2,1,0:T(8,128)S(1)} %get-tuple-element.50), channel_id=1, source_target_pairs={{1,0},{2,1},{3,2},{5,4},{6,5},{7,6},{9,8},{10,9},{11,10},{13,12},{... | collective-permute-start | bytes 196616 | tf_op jit(solution)/shard_map/ppermute | solution.py:120
  9.5 8.1 %collective-permute-start.4 = (f32[8,4,16,1]{2,0,3,1:T(8,128)S(1)}, f32[8,4,16,1]{2,0,3,1:T(8,128)S(1)}, u32[]{:S(2)}, u32[]{:S(2)}) collective-permute-start(f32[8,4,16,1]{2,0,3,1:T(8,128)S(1)} %get-tuple-element.65), channel_id=1, source_target_pairs={{0,8},{8,16},{16,24},{24,0},{1,9},{9,17},{17,25},{25,1},{2,10},{10... | collective-permute-start | bytes 6152 | tf_op jit(solution)/shard_map/ppermute | solution.py:120
  11.1 6.6 %collective-permute-start.3 = (f32[8,4,16,1]{2,0,3,1:T(8,128)S(1)}, f32[8,4,16,1]{2,0,3,1:T(8,128)S(1)}, u32[]{:S(2)}, u32[]{:S(2)}) collective-permute-start(f32[8,4,16,1]{2,0,3,1:T(8,128)S(1)} %get-tuple-element.66), channel_id=1, source_target_pairs={{0,24},{8,0},{16,8},{24,16},{1,25},{9,1},{17,9},{25,17},{2,26},{10... | collective-permute-start | bytes 6152 | tf_op jit(solution)/shard_map/ppermute | solution.py:120
  13.4 0.7 %copy-start.6 = (f32[3,5,5]{2,0,1:T(4,128)S(1)}, f32[3,5,5]{2,0,1:T(4,128)}, u32[]{:S(2)}) copy-start(f32[3,5,5]{2,0,1:T(4,128)} %param.12) | copy-start | bytes 904
  14.1 0.7 %copy-start.7 = (f32[3,5,5]{2,0,1:T(4,128)S(1)}, f32[3,5,5]{2,0,1:T(4,128)}, u32[]{:S(2)}) copy-start(f32[3,5,5]{2,0,1:T(4,128)} %param.13) | copy-start | bytes 904
  15.1 0.7 %copy-start.9 = (s32[4,128]{1,0:T(4,128)S(1)}, s32[4,128]{1,0:T(4,128)}, u32[]{:S(2)}) copy-start(s32[4,128]{1,0:T(4,128)} %param.17) | copy-start | bytes 6148
  16.9 0.7 %copy-start.8 = (f32[3,5]{1,0:T(4,128)S(1)}, f32[3,5]{1,0:T(4,128)}, u32[]{:S(2)}) copy-start(f32[3,5]{1,0:T(4,128)} %param.14) | copy-start | bytes 184
  18.6 0.9 %copy-start.4 = (f32[5,4,16,128]{3,2,1,0:T(8,128)S(1)}, f32[5,4,16,128]{3,2,1,0:T(8,128)}, u32[]{:S(2)}) copy-start(f32[5,4,16,128]{3,2,1,0:T(8,128)} %param.10) | copy-start | bytes 491524
  19.7 0.9 %copy-start.3 = (f32[5,4,16,128]{3,2,1,0:T(8,128)}, f32[5,4,16,128]{3,2,1,0:T(8,128)S(1)}, u32[]{:S(2)}) copy-start(f32[5,4,16,128]{3,2,1,0:T(8,128)S(1)} %fusion.15) | copy-start | bytes 491524
  19.7 0.8 %copy-start.2 = (f32[4,16,128]{2,1,0:T(8,128)S(1)}, f32[4,16,128]{2,1,0:T(8,128)}, u32[]{:S(2)}) copy-start(f32[4,16,128]{2,1,0:T(8,128)} %param.15) | copy-start | bytes 98308
  20.7 7.9 %collective-permute-start.5 = (f32[4,4,3,3]{3,2,1,0:T(4,128)S(1)}, f32[4,4,3,3]{3,2,1,0:T(4,128)S(1)}, u32[]{:S(2)}, u32[]{:S(2)}) collective-permute-start(f32[4,4,3,3]{3,2,1,0:T(4,128)S(1)} %get-tuple-element.47), channel_id=1, source_target_pairs={{0,12},{8,20},{16,28},{24,4},{4,8},{12,16},{20,24},{28,0},{1,13},{... | collective-permute-start | bytes 1736 | tf_op jit(solution)/shard_map/ppermute | solution.py:133
  21.1 12.3 %collective-permute-start.8 = (f32[4,4,16,3]{3,2,1,0:T(8,128)S(1)}, f32[4,4,16,3]{3,2,1,0:T(8,128)S(1)}, u32[]{:S(2)}, u32[]{:S(2)}) collective-permute-start(f32[4,4,16,3]{3,2,1,0:T(8,128)S(1)} %get-tuple-element.45), channel_id=1, source_target_pairs={{0,8},{8,16},{16,24},{24,0},{1,9},{9,17},{17,25},{25,1},{2,10},{10... | collective-permute-start | bytes 9224 | tf_op jit(solution)/shard_map/ppermute | solution.py:120
  22.7 10.6 %collective-permute-start.9 = (f32[4,4,16,3]{3,2,1,0:T(8,128)S(1)}, f32[4,4,16,3]{3,2,1,0:T(8,128)S(1)}, u32[]{:S(2)}, u32[]{:S(2)}) collective-permute-start(f32[4,4,16,3]{3,2,1,0:T(8,128)S(1)} %get-tuple-element.46), channel_id=1, source_target_pairs={{0,24},{8,0},{16,8},{24,16},{1,25},{9,1},{17,9},{25,17},{2,26},{10... | collective-permute-start | bytes 9224 | tf_op jit(solution)/shard_map/ppermute | solution.py:120
  25.2 8.0 %collective-permute-start.7 = (f32[4,4,3,3]{3,2,1,0:T(4,128)S(1)}, f32[4,4,3,3]{3,2,1,0:T(4,128)S(1)}, u32[]{:S(2)}, u32[]{:S(2)}) collective-permute-start(f32[4,4,3,3]{3,2,1,0:T(4,128)S(1)} %get-tuple-element.48), channel_id=1, source_target_pairs={{0,28},{8,4},{16,12},{24,20},{4,24},{12,0},{20,8},{28,16},{1,29},{... | collective-permute-start | bytes 1736 | tf_op jit(solution)/shard_map/ppermute | solution.py:133
  27.6 5.7 %collective-permute-start.6 = (f32[4,4,3,128]{3,2,1,0:T(4,128)S(1)}, f32[4,4,3,128]{3,2,1,0:T(4,128)S(1)}, u32[]{:S(2)}, u32[]{:S(2)}) collective-permute-start(f32[4,4,3,128]{3,2,1,0:T(4,128)S(1)} %fusion.29), channel_id=1, source_target_pairs={{0,4},{4,0},{1,5},{5,1},{2,6},{6,2},{3,7},{7,3},{8,12},{12,8},{9,1... | collective-permute-start | bytes 73736 | tf_op jit(solution)/shard_map/ppermute | solution.py:133
  33.7 3.5 %collective-permute-start.10 = (f32[4,3,22,134]{3,2,1,0:T(8,128)S(1)}, f32[4,3,22,134]{3,2,1,0:T(8,128)S(1)}, u32[]{:S(2)}, u32[]{:S(2)}) collective-permute-start(f32[4,3,22,134]{3,2,1,0:T(8,128)S(1)} %get-tuple-element.31), channel_id=1, source_target_pairs={{0,1},{1,2},{2,3},{4,5},{5,6},{6,7},{8,9},{9,10},{10,11},{12,13},{... | collective-permute-start | bytes 424520 | tf_op jit(solution)/shard_map/ppermute | solution.py:120
  35.9 5.4 %collective-permute-start.11 = (f32[4,3,22,134]{3,2,1,0:T(8,128)S(1)}, f32[4,3,22,134]{3,2,1,0:T(8,128)S(1)}, u32[]{:S(2)}, u32[]{:S(2)}) collective-permute-start(f32[4,3,22,134]{3,2,1,0:T(8,128)S(1)} %get-tuple-element.32), channel_id=1, source_target_pairs={{1,0},{2,1},{3,2},{5,4},{6,5},{7,6},{9,8},{10,9},{11,10},{13,12},{... | collective-permute-start | bytes 424520 | tf_op jit(solution)/shard_map/ppermute | solution.py:120
  43.2 0.9 %copy-start.5 = (f32[4,16,128]{2,1,0:T(8,128)S(1)}, f32[4,16,128]{2,1,0:T(8,128)}, u32[]{:S(2)}) copy-start(f32[4,16,128]{2,1,0:T(8,128)} %param.16) | copy-start | bytes 98308

commit v11 on v10

--- a/solution.py
+++ b/solution.py
@@ -149,6 +149,51 @@
     low_n, high_n = receive_pair(joined, {}, "normal", dims, width)
     low_lc, high_lc = receive_pair(joined, {"circ": -1}, "normal", dims, width)
     low_hc, high_hc = receive_pair(joined, {"circ": 1}, "normal", dims, width)
+    top = jnp.concatenate([low_lc, low_n, low_hc], axis=3)
+    middle = jnp.concatenate([before_c, joined, after_c], axis=3)
+    bottom = jnp.concatenate([high_lc, high_n, high_hc], axis=3)
+    plane = jnp.concatenate([top, middle, bottom], axis=2)
+    before_s = receive(plane, {"span": -1}, dims, width)
+    after_s = receive(plane, {"span": 1}, dims, width)
+    return jnp.concatenate([before_s, plane, after_s], axis=1)
+
+
+def padded_sweeps_a2a(joined, width):
+    dims = {"span": 1, "normal": 2, "circ": 3}
+    ring = lax.axis_size("circ")
+    c, n = lax.axis_index("circ"), lax.axis_index("normal")
+    rows = {side: take(joined, {"normal": side}, dims, width) for side in (-1, 1)}
+    facing = jnp.where(n == 0, rows[-1], rows[1])
+    pieces = {
+        (1, 0): take(joined, {"circ": -1}, dims, width),
+        (ring - 1, 0): take(joined, {"circ": 1}, dims, width),
+        (0, 1): facing,
+        (1, 1): take(facing, {"circ": -1}, dims, width),
+        (ring - 1, 1): take(facing, {"circ": 1}, dims, width),
+    }
+    size = max(p.size for p in pieces.values())
+    table = jnp.zeros((ring, 2, size), joined.dtype)
+    for (dc, dn), piece in pieces.items():
+        flat = jnp.pad(piece.reshape(-1), (0, size - piece.size))
+        table = table.at[dc, dn].set(flat)
+    table = jnp.roll(jnp.roll(table, c, axis=0), n, axis=1).reshape(ring * 2, size)
+    got = lax.all_to_all(table, ("circ", "normal"), 0, 0, tiled=False).reshape(ring, 2, size)
+    got = jnp.roll(jnp.roll(got, -c, axis=0), -n, axis=1)
+
+    def unpack(dc, dn, like):
+        return got[dc, dn, : like.size].reshape(like.shape)
+
+    before_c = unpack(ring - 1, 0, pieces[(1, 0)])
+    after_c = unpack(1, 0, pieces[(ring - 1, 0)])
+    zero_rows = jnp.zeros_like(facing)
+    partner = unpack(0, 1, facing)
+    low_n, high_n = jnp.where(n == 1, partner, zero_rows), jnp.where(n == 0, partner, zero_rows)
+    corner = pieces[(1, 1)]
+    zero_corner = jnp.zeros_like(corner)
+    from_lc = unpack(ring - 1, 1, corner)
+    from_hc = unpack(1, 1, corner)
+    low_lc, high_lc = jnp.where(n == 1, from_lc, zero_corner), jnp.where(n == 0, from_lc, zero_corner)
+    low_hc, high_hc = jnp.where(n == 1, from_hc, zero_corner), jnp.where(n == 0, from_hc, zero_corner)
     top = jnp.concatenate([low_lc, low_n, low_hc], axis=3)
     middle = jnp.concatenate([before_c, joined, after_c], axis=3)
     bottom = jnp.concatenate([high_lc, high_n, high_hc], axis=3)
@@ -241,7 +286,10 @@
     forcing = jac_apply(coupling.T, residual)
     margin = SWEEPS - 1
     joined = jnp.concatenate([stiffness[None], forcing], axis=0)
-    full_pad = padded_sweeps(joined, margin)
+    if lax.axis_size("normal") == 2 and 3 <= lax.axis_size("circ") <= 4:
+        full_pad = padded_sweeps_a2a(joined, margin)
+    else:
+        full_pad = padded_sweeps(joined, margin)
     mesh = run_sweeps(full_pad[0], full_pad[1:])
     wall_sens = jnp.sum(wall_kernel[None] * mesh, axis=2)
     span = lax.axis_index("span")

time: 61.8 us -> 67.7 us (1.095)
  local copies, waits for them, and re-layouts: 7.84 us -> 13.6 us
  starting transfers between devices: 21 us -> 17.5 us
  waiting for transfers between devices: 8.64 us -> 11.8 us
  other arithmetic: 7.03 us -> 8.54 us
  blocking collectives: 15 us -> 13.6 us
    all_to_all x0 -> x1, waiting for transfers between devices: none -> 7.42 us  [padded_sweeps_a2a(): lax.all_to_all(table, ('circ', 'normal'), 0, 0, tiled=False)]
    ppermute x4 -> x1, waiting for transfers between devices: 4.61 us -> 0.01 us  [receive_pair(): got = lax.ppermute(sent, axes, pairs + back)]
    ppermute x4 -> x1, starting transfers between devices: 6.77 us -> 3.03 us  [receive_pair(): got = lax.ppermute(sent, axes, pairs + back)]
    all_to_all x0 -> x1, starting transfers between devices: none -> 3.56 us  [padded_sweeps_a2a(): lax.all_to_all(table, ('circ', 'normal'), 0, 0, tiled=False)]
    ppermute x8 -> x6, starting transfers between devices: 14.2 us -> 10.9 us  [receive(): return lax.ppermute(take(array, rel, dims, width), axes, pairs)]
    scatter x0 -> x5, local copies, waits for them, and re-layouts: none -> 2.31 us  [padded_sweeps_a2a(): table = table.at[dc, dn].set(flat)]
    all_to_all x1, blocking collectives: 15 us -> 13.6 us  [reduce_panels(): return jnp.sum(lax.all_to_all(chunks, ORDER, 0, 0, tiled=False), axis=0)]
    concatenate x2 -> x6, other arithmetic: 0.66 us -> 1.68 us  [the longest x2 0.51 us: padded_sweeps_a2a(): got = jnp.roll(jnp.roll(got, -c, axis=0), -n, axis=1)]
  transfers between devices with their start and end apart: 12 -> 8, of which waited for: 2 -> 2; matrix products, arithmetic and copies ran while one was open for 5% -> 6% of each run, Pallas kernels for 0% -> 0%
where the time goes in v11:
time: 67.7 us; the launch traced here: 67 us
  starting transfers between devices  17.5 us (26%)
  local copies, waits for them, and re-layouts  13.6 us (20%)
  blocking collectives  13.6 us (20%)
  waiting for transfers between devices  11.8 us (17%)
  other arithmetic  8.54 us (13%)
  between operations  1.48 us (2%)
    all_to_all x1, blocking collectives, reduce_panels(): return jnp.sum(lax.all_to_all(chunks, ORDER, 0, 0, tiled=False), axis=0)  13.6 us
    ppermute x6, starting transfers between devices, receive(): return lax.ppermute(take(array, rel, dims, width), axes, pairs)  10.9 us
    all_to_all x1, waiting for transfers between devices, padded_sweeps_a2a(): lax.all_to_all(table, ('circ', 'normal'), 0, 0, tiled=False)  7.42 us
    unnamed x34, local copies, waits for them, and re-layouts  4.96 us
    ppermute x6, waiting for transfers between devices, receive(): return lax.ppermute(take(array, rel, dims, width), axes, pairs)  4.42 us
    all_to_all x1, starting transfers between devices, padded_sweeps_a2a(): lax.all_to_all(table, ('circ', 'normal'), 0, 0, tiled=False)  3.56 us
    ppermute x1, starting transfers between devices, receive_pair(): got = lax.ppermute(sent, axes, pairs + back)  3.03 us
    scatter x5, local copies, waits for them, and re-layouts, padded_sweeps_a2a(): table = table.at[dc, dn].set(flat)  2.31 us
  transfers between devices with their start and end apart: 8, of which 2 were waited for; matrix products, arithmetic and copies ran while one was open for 6% of the time, Pallas kernels for 0%

profile of v11, /device:TPU:0, one launch (start us, length us, event | category | flops | bytes accessed | tf_op | source)
XLA Modules:
  0.0 67.0 jit_solution(17649181732712219417)
XLA Ops:
  0.6 1.0 %fusion.55 = (f32[5,4,1,128]{3,2,1,0:T(1,128)S(1)}, f32[5,4,1,128]{3,2,1,0:T(1,128)S(1)}) fusion(f32[5,4,16,128]{3,2,1,0:T(8,128)} %param.23), kind=kLoop, calls=%fused_computation.154 | loop fusion | bytes 40960 | tf_op jit(solution)/shard_map/slice | solution.py:88
  1.7 0.8 %fusion.59 = (f32[3,4,1,128]{3,2,1,0:T(1,128)S(1)}, f32[3,4,1,128]{3,2,1,0:T(1,128)S(1)}) fusion(f32[3,4,16,128]{3,2,1,0:T(8,128)} %param.25), kind=kLoop, calls=%fused_computation.158 | loop fusion | bytes 24576 | tf_op jit(solution)/shard_map/slice | solution.py:88
  2.6 3.0 %collective-permute-start.2 = (f32[8,4,1,128]{3,0,2,1:T(8,128)S(1)}, f32[8,4,1,128]{3,0,2,1:T(8,128)S(1)}, u32[]{:S(2)}, u32[]{:S(2)}) collective-permute-start(f32[8,4,1,128]{3,0,2,1:T(8,128)S(1)} %slice_select_fusion.1), channel_id=1, source_target_pairs={{0,4},{4,0},{1,5},{5,1},{2,6},{6,2},{3,7},{7,3},{8,12},{12,8},{9,1... | collective-permute-start | bytes 49160 | tf_op jit(solution)/shard_map/ppermute | solution.py:133
  5.7 1.5 %collective-permute-start.1 = (f32[8,1,16,128]{3,2,1,0:T(8,128)S(1)}, f32[8,1,16,128]{3,2,1,0:T(8,128)S(1)}, u32[]{:S(2)}, u32[]{:S(2)}) collective-permute-start(f32[8,1,16,128]{3,2,1,0:T(8,128)S(1)} %get-tuple-element.117), channel_id=1, source_target_pairs={{0,1},{1,2},{2,3},{4,5},{5,6},{6,7},{8,9},{9,10},{10,11},{12,13},{... | collective-permute-start | bytes 196616 | tf_op jit(solution)/shard_map/ppermute | solution.py:120
  7.1 1.3 %collective-permute-start = (f32[8,1,16,128]{3,2,1,0:T(8,128)S(1)}, f32[8,1,16,128]{3,2,1,0:T(8,128)S(1)}, u32[]{:S(2)}, u32[]{:S(2)}) collective-permute-start(f32[8,1,16,128]{3,2,1,0:T(8,128)S(1)} %get-tuple-element.118), channel_id=1, source_target_pairs={{1,0},{2,1},{3,2},{5,4},{6,5},{7,6},{9,8},{10,9},{11,10},{13,12},{... | collective-permute-start | bytes 196616 | tf_op jit(solution)/shard_map/ppermute | solution.py:120
  9.0 0.2 copy.116
  9.2 0.3 copy.117
  9.5 1.6 %collective-permute-start.4 = (f32[8,4,16,1]{2,0,3,1:T(8,128)S(1)}, f32[8,4,16,1]{2,0,3,1:T(8,128)S(1)}, u32[]{:S(2)}, u32[]{:S(2)}) collective-permute-start(f32[8,4,16,1]{2,0,3,1:T(8,128)S(1)} %get-tuple-element.129), channel_id=1, source_target_pairs={{0,8},{8,16},{16,24},{24,0},{1,9},{9,17},{17,25},{25,1},{2,10},{10... | collective-permute-start | bytes 6152 | tf_op jit(solution)/shard_map/ppermute | solution.py:120
  11.1 2.2 %collective-permute-start.3 = (f32[8,4,16,1]{2,0,3,1:T(8,128)S(1)}, f32[8,4,16,1]{2,0,3,1:T(8,128)S(1)}, u32[]{:S(2)}, u32[]{:S(2)}) collective-permute-start(f32[8,4,16,1]{2,0,3,1:T(8,128)S(1)} %get-tuple-element.130), channel_id=1, source_target_pairs={{0,24},{8,0},{16,8},{24,16},{1,25},{9,1},{17,9},{25,17},{2,26},{10... | collective-permute-start | bytes 6152 | tf_op jit(solution)/shard_map/ppermute | solution.py:120
  13.4 0.7 %copy-done.6 = f32[3,5,5]{2,0,1:T(4,128)S(1)} copy-done((f32[3,5,5]{2,0,1:T(4,128)S(1)}, f32[3,5,5]{2,0,1:T(4,128)}, u32[]{:S(2)}) %copy-start.6) | copy-done | bytes 324
  14.1 0.7 %copy-done.7 = f32[3,5,5]{2,0,1:T(4,128)S(1)} copy-done((f32[3,5,5]{2,0,1:T(4,128)S(1)}, f32[3,5,5]{2,0,1:T(4,128)}, u32[]{:S(2)}) %copy-start.7) | copy-done | bytes 324
  15.3 0.6 fusion.66
  15.9 0.5 multiply_reduce_fusion.2
  16.4 0.2 multiply_reduce_fusion
  16.8 0.6 copy-done.8
  17.8 0.2 copy.100
  18.0 0.2 copy.98
  18.7 0.7 %copy-done.4 = f32[5,4,16,128]{3,2,1,0:T(8,128)S(1)} copy-done((f32[5,4,16,128]{3,2,1,0:T(8,128)S(1)}, f32[5,4,16,128]{3,2,1,0:T(8,128)}, u32[]{:S(2)}) %copy-start.4) | copy-done | bytes 163864
  19.8 0.7 copy-done.3
  20.7 0.2 reshape.331
  21.0 0.2 reshape.333
  21.5 0.2 scatter.19
  21.7 1.5 %scatter.20 = f32[4,2,6144]{2,1,0:T(2,128)S(1)} dynamic-update-slice(f32[4,2,6144]{2,1,0:T(2,128)S(1)} %scatter.19, f32[1,1,6144]{2,1,0:T(1,128)S(1)} %reshape.335, s32[]{:T(128)} %bitcast.30, s32[]{:T(128)} %bitcast.31, s32[]{:T(128)} %constant.231.clone.1) | dynamic-update-slice | bytes 49156 | tf_op jit(solution)/shard_map/scatter | solution.py:178
  23.2 0.2 scatter.21
  23.5 0.2 scatter.24
  23.7 0.2 fusion.13
  24.0 0.3 fusion.12
  24.3 1.0 %all_to_all.9 = f32[8,1,6144]{2,1,0:T(1,128)} reshape(f32[4,2,6144]{2,1,0:T(2,128)S(1)} %fusion.12) | data formatting | bytes 393216 | tf_op jit(solution)/shard_map/all_to_all | solution.py:180
  25.2 3.6 %all-to-all-start = ((f32[8,1,6144]{2,1,0:T(1,128)}), f32[8,1,6144]{2,1,0:T(1,128)S(1)}, u32[]{:S(2)}, u32[]{:S(2)}) async-start(f32[8,1,6144]{2,1,0:T(1,128)} %all_to_all.9), calls=%async_computation | async-start | bytes 393216 | tf_op jit(solution)/shard_map/all_to_all | solution.py:180
  28.8 0.7 %copy-done.9 = s32[4,128]{1,0:T(4,128)S(1)} copy-done((s32[4,128]{1,0:T(4,128)S(1)}, s32[4,128]{1,0:T(4,128)}, u32[]{:S(2)}) %copy-start.9) | copy-done | bytes 2072
  29.5 7.4 %all-to-all-done = f32[8,1,6144]{2,1,0:T(1,128)S(1)} async-done(((f32[8,1,6144]{2,1,0:T(1,128)}), f32[8,1,6144]{2,1,0:T(1,128)S(1)}, u32[]{:S(2)}, u32[]{:S(2)}) %all-to-all-start) | async-done | bytes 196640 | tf_op jit(solution)/shard_map/all_to_all | solution.py:180
  36.9 0.5 reduce.17
  37.5 0.2 fusion.11
  37.7 0.3 fusion.10
  38.2 0.2 reshape_squeeze.10
  38.4 0.2 reshape_squeeze.4
  39.2 0.3 maximum_maximum_fusion
  39.6 3.0 %collective-permute-start.5 = (f32[4,3,22,134]{3,2,1,0:T(8,128)S(1)}, f32[4,3,22,134]{3,2,1,0:T(8,128)S(1)}, u32[]{:S(2)}, u32[]{:S(2)}) collective-permute-start(f32[4,3,22,134]{3,2,1,0:T(8,128)S(1)} %get-tuple-element.101), channel_id=1, source_target_pairs={{0,1},{1,2},{2,3},{4,5},{5,6},{6,7},{8,9},{9,10},{10,11},{12,13},{... | collective-permute-start | bytes 424520 | tf_op jit(solution)/shard_map/ppermute | solution.py:120
  42.6 1.3 %collective-permute-start.6 = (f32[4,3,22,134]{3,2,1,0:T(8,128)S(1)}, f32[4,3,22,134]{3,2,1,0:T(8,128)S(1)}, u32[]{:S(2)}, u32[]{:S(2)}) collective-permute-start(f32[4,3,22,134]{3,2,1,0:T(8,128)S(1)} %get-tuple-element.102), channel_id=1, source_target_pairs={{1,0},{2,1},{3,2},{5,4},{6,5},{7,6},{9,8},{10,9},{11,10},{13,12},{... | collective-permute-start | bytes 424520 | tf_op jit(solution)/shard_map/ppermute | solution.py:120
  44.0 4.4 %collective-permute-done.6 = f32[4,3,22,134]{3,2,1,0:T(8,128)S(1)} collective-permute-done((f32[4,3,22,134]{3,2,1,0:T(8,128)S(1)}, f32[4,3,22,134]{3,2,1,0:T(8,128)S(1)}, u32[]{:S(2)}, u32[]{:S(2)}) %collective-permute-start.6) | collective-permute-done | bytes 141536 | tf_op jit(solution)/shard_map/ppermute | solution.py:120
  48.4 0.3 pad_maximum_fusion
  49.2 1.2 %broadcast_multiply_fusion.1 = (f32[3,8,20,132]{3,2,1,0:T(8,128)S(1)}, f32[3,8,20,132]{3,2,1,0:T(8,128)S(1)}) fusion(f32[8,20,132]{2,1,0:T(8,128)S(1)} %get-tuple-element.106, f32[3,10,22,134]{3,2,1,0:T(8,128)S(1)} %get-tuple-element.97, f32[8,20,132]{2,1,0:T(8,128)S(1)} %get-tuple-element.105, f32[4,10,22,134]{3,2,1,0:T(8,128)S(1)} %pad_maximum_fusion, ...), kind=kLoop, calls=%fused_computation.43 | loop fusion | flops 760320 | bytes 2703360 | tf_op jit(solution)/shard_map/mul | solution.py:60
  50.4 0.9 %broadcast_multiply_fusion.2 = (f32[3,6,18,130]{3,2,1,0:T(8,128)S(1)}, f32[3,6,18,130]{3,2,1,0:T(8,128)S(1)}) fusion(f32[6,18,130]{2,1,0:T(8,128)S(1)} %get-tuple-element.104, f32[3,8,20,132]{3,2,1,0:T(8,128)S(1)} %get-tuple-element.95, f32[6,18,130]{2,1,0:T(8,128)S(1)} %get-tuple-element.103, f32[4,10,22,134]{3,2,1,0:T(8,128)S(1)} %pad_maximum_fusion, ...), kind=kLoop, calls=%fused_computation.46 | loop fusion | flops 505440 | bytes 1797120 | tf_op jit(solution)/shard_map/mul | solution.py:60
  51.3 0.9 %multiply_reduce_fusion.9 = (f32[3,4,128]{2,1,0:T(4,128)S(1)}, f32[3,4,16,128]{3,2,1,0:T(8,128)}) fusion(f32[4,16,128]{2,1,0:T(8,128)S(1)} %copy-done.5, f32[3,6,18,130]{3,2,1,0:T(8,128)S(1)} %get-tuple-element.93, f32[3,4,16,128]{3,2,1,0:T(8,128)S(1)} %multiply_reduce_fusion.6, f32[4,16,128]{2,1,0:T(8,128)S(1)} %fusion.32, ...), kind=kLoop, calls=%fused_computation.83 | loop fusion | flops 317952 | bytes 956416 | tf_op jit(solution)/shard_map/reduce_sum | solution.py:294
  52.2 0.4 convolution_bitcast_fusion
  52.6 0.2 select_select_fusion
  52.8 13.6 %all_to_all.14 = f32[32,3,128]{2,1,0:T(4,128)S(1)} all-to-all(f32[32,3,128]{2,1,0:T(4,128)S(1)} %select_select_fusion), channel_id=1, replica_groups=mesh['circ'=4,'normal'=2,'span'=4] {'circ','normal','span'}, dimensions={0} | all-to-all | bytes 98304 | tf_op jit(solution)/shard_map/all_to_all | solution.py:254
  66.4 0.6 reduce_sum.167
  (110 shorter events, 4.2 us)
Async XLA Ops:
  0.6 5.0 %copy-start = (f32[5,4,16,128]{3,2,1,0:T(8,128)S(1)}, f32[5,4,16,128]{3,2,1,0:T(8,128)}, u32[]{:S(2)}) copy-start(f32[5,4,16,128]{3,2,1,0:T(8,128)} %param.23) | copy-start | bytes 491524
  2.5 3.1 %copy-start.1 = (f32[3,4,16,128]{3,2,1,0:T(8,128)S(1)}, f32[3,4,16,128]{3,2,1,0:T(8,128)}, u32[]{:S(2)}) copy-start(f32[3,4,16,128]{3,2,1,0:T(8,128)} %param.25) | copy-start | bytes 294916
  2.6 15.7 %collective-permute-start.2 = (f32[8,4,1,128]{3,0,2,1:T(8,128)S(1)}, f32[8,4,1,128]{3,0,2,1:T(8,128)S(1)}, u32[]{:S(2)}, u32[]{:S(2)}) collective-permute-start(f32[8,4,1,128]{3,0,2,1:T(8,128)S(1)} %slice_select_fusion.1), channel_id=1, source_target_pairs={{0,4},{4,0},{1,5},{5,1},{2,6},{6,2},{3,7},{7,3},{8,12},{12,8},{9,1... | collective-permute-start | bytes 49160 | tf_op jit(solution)/shard_map/ppermute | solution.py:133
  5.7 12.8 %collective-permute-start.1 = (f32[8,1,16,128]{3,2,1,0:T(8,128)S(1)}, f32[8,1,16,128]{3,2,1,0:T(8,128)S(1)}, u32[]{:S(2)}, u32[]{:S(2)}) collective-permute-start(f32[8,1,16,128]{3,2,1,0:T(8,128)S(1)} %get-tuple-element.117), channel_id=1, source_target_pairs={{0,1},{1,2},{2,3},{4,5},{5,6},{6,7},{8,9},{9,10},{10,11},{12,13},{... | collective-permute-start | bytes 196616 | tf_op jit(solution)/shard_map/ppermute | solution.py:120
  7.1 11.4 %collective-permute-start = (f32[8,1,16,128]{3,2,1,0:T(8,128)S(1)}, f32[8,1,16,128]{3,2,1,0:T(8,128)S(1)}, u32[]{:S(2)}, u32[]{:S(2)}) collective-permute-start(f32[8,1,16,128]{3,2,1,0:T(8,128)S(1)} %get-tuple-element.118), channel_id=1, source_target_pairs={{1,0},{2,1},{3,2},{5,4},{6,5},{7,6},{9,8},{10,9},{11,10},{13,12},{... | collective-permute-start | bytes 196616 | tf_op jit(solution)/shard_map/ppermute | solution.py:120
  9.5 8.0 %collective-permute-start.4 = (f32[8,4,16,1]{2,0,3,1:T(8,128)S(1)}, f32[8,4,16,1]{2,0,3,1:T(8,128)S(1)}, u32[]{:S(2)}, u32[]{:S(2)}) collective-permute-start(f32[8,4,16,1]{2,0,3,1:T(8,128)S(1)} %get-tuple-element.129), channel_id=1, source_target_pairs={{0,8},{8,16},{16,24},{24,0},{1,9},{9,17},{17,25},{25,1},{2,10},{10... | collective-permute-start | bytes 6152 | tf_op jit(solution)/shard_map/ppermute | solution.py:120
  11.1 6.6 %collective-permute-start.3 = (f32[8,4,16,1]{2,0,3,1:T(8,128)S(1)}, f32[8,4,16,1]{2,0,3,1:T(8,128)S(1)}, u32[]{:S(2)}, u32[]{:S(2)}) collective-permute-start(f32[8,4,16,1]{2,0,3,1:T(8,128)S(1)} %get-tuple-element.130), channel_id=1, source_target_pairs={{0,24},{8,0},{16,8},{24,16},{1,25},{9,1},{17,9},{25,17},{2,26},{10... | collective-permute-start | bytes 6152 | tf_op jit(solution)/shard_map/ppermute | solution.py:120
  13.4 0.7 %copy-start.6 = (f32[3,5,5]{2,0,1:T(4,128)S(1)}, f32[3,5,5]{2,0,1:T(4,128)}, u32[]{:S(2)}) copy-start(f32[3,5,5]{2,0,1:T(4,128)} %param.26) | copy-start | bytes 904
  14.1 0.7 %copy-start.7 = (f32[3,5,5]{2,0,1:T(4,128)S(1)}, f32[3,5,5]{2,0,1:T(4,128)}, u32[]{:S(2)}) copy-start(f32[3,5,5]{2,0,1:T(4,128)} %param.27) | copy-start | bytes 904
  16.8 0.7 %copy-start.8 = (f32[3,5]{1,0:T(4,128)S(1)}, f32[3,5]{1,0:T(4,128)}, u32[]{:S(2)}) copy-start(f32[3,5]{1,0:T(4,128)} %param.28) | copy-start | bytes 184
  18.5 0.9 %copy-start.4 = (f32[5,4,16,128]{3,2,1,0:T(8,128)S(1)}, f32[5,4,16,128]{3,2,1,0:T(8,128)}, u32[]{:S(2)}) copy-start(f32[5,4,16,128]{3,2,1,0:T(8,128)} %param.24) | copy-start | bytes 491524
  19.6 0.9 %copy-start.2 = (f32[5,4,16,128]{3,2,1,0:T(8,128)}, f32[5,4,16,128]{3,2,1,0:T(8,128)S(1)}, u32[]{:S(2)}) copy-start(f32[5,4,16,128]{3,2,1,0:T(8,128)S(1)} %fusion.19) | copy-start | bytes 491524
  19.6 0.8 %copy-start.3 = (f32[4,16,128]{2,1,0:T(8,128)S(1)}, f32[4,16,128]{2,1,0:T(8,128)}, u32[]{:S(2)}) copy-start(f32[4,16,128]{2,1,0:T(8,128)} %param.29) | copy-start | bytes 98308
  25.2 11.7 %all-to-all-start = ((f32[8,1,6144]{2,1,0:T(1,128)}), f32[8,1,6144]{2,1,0:T(1,128)S(1)}, u32[]{:S(2)}, u32[]{:S(2)}) async-start(f32[8,1,6144]{2,1,0:T(1,128)} %all_to_all.9), calls=%async_computation | async-start | bytes 393216 | tf_op jit(solution)/shard_map/all_to_all | solution.py:180
  28.8 0.7 %copy-start.9 = (s32[4,128]{1,0:T(4,128)S(1)}, s32[4,128]{1,0:T(4,128)}, u32[]{:S(2)}) copy-start(s32[4,128]{1,0:T(4,128)} %param.31) | copy-start | bytes 6148
  39.6 4.3 %collective-permute-start.5 = (f32[4,3,22,134]{3,2,1,0:T(8,128)S(1)}, f32[4,3,22,134]{3,2,1,0:T(8,128)S(1)}, u32[]{:S(2)}, u32[]{:S(2)}) collective-permute-start(f32[4,3,22,134]{3,2,1,0:T(8,128)S(1)} %get-tuple-element.101), channel_id=1, source_target_pairs={{0,1},{1,2},{2,3},{4,5},{5,6},{6,7},{8,9},{9,10},{10,11},{12,13},{... | collective-permute-start | bytes 424520 | tf_op jit(solution)/shard_map/ppermute | solution.py:120
  42.6 5.7 %collective-permute-start.6 = (f32[4,3,22,134]{3,2,1,0:T(8,128)S(1)}, f32[4,3,22,134]{3,2,1,0:T(8,128)S(1)}, u32[]{:S(2)}, u32[]{:S(2)}) collective-permute-start(f32[4,3,22,134]{3,2,1,0:T(8,128)S(1)} %get-tuple-element.102), channel_id=1, source_target_pairs={{1,0},{2,1},{3,2},{5,4},{6,5},{7,6},{9,8},{10,9},{11,10},{13,12},{... | collective-permute-start | bytes 424520 | tf_op jit(solution)/shard_map/ppermute | solution.py:120
  50.4 0.9 %copy-start.5 = (f32[4,16,128]{2,1,0:T(8,128)S(1)}, f32[4,16,128]{2,1,0:T(8,128)}, u32[]{:S(2)}) copy-start(f32[4,16,128]{2,1,0:T(8,128)} %param.30) | copy-start | bytes 98308

commit v12 on v10

--- a/solution.py
+++ b/solution.py
@@ -255,26 +255,29 @@
     return (residual, mesh, panels)
 
 
+def joined_inputs(coeffs, loads, *rest):
+    coeffs, loads = lax.optimization_barrier((coeffs, loads))
+    jac = coeffs[: 2 * JAC].reshape(2, 3, 5, 5)
+    coupling = coeffs[2 * JAC :].reshape(3, 5)
+    return on_device(rest[0], loads[:5], rest[1], jac[0], jac[1], coupling, loads[5], rest[2], rest[3])
+
+
+JAC = 75
+
+
 def solution(mesh):
-    placed = (
-        P(None, "span", "normal", "circ"),
-        P(None, "span", "normal", "circ"),
-        P(None, "span", "normal", "circ"),
-        P(),
-        P(),
-        P(),
-        P("span", "normal", "circ"),
-        P("span", "normal", "circ"),
-        P("span", "circ"),
-    )
-    return jax.shard_map(
-        on_device,
+    field = P(None, "span", "normal", "circ")
+    inner = jax.shard_map(
+        joined_inputs,
         mesh=mesh,
-        in_specs=placed,
-        out_specs=(
-            P(None, "span", "normal", "circ"),
-            P(None, "span", "normal", "circ"),
-            P(None, "span"),
-        ),
+        in_specs=(P(), field, field, field, P("span", "normal", "circ"), P("span", "circ")),
+        out_specs=(field, field, P(None, "span")),
         check_vma=False,
     )
+
+    def run(adjoint, objective_grad, face_weights, owner_jac, neighbor_jac, coupling, stiffness, wall_kernel, panel_owner):
+        coeffs = jnp.concatenate([owner_jac.reshape(-1), neighbor_jac.reshape(-1), coupling.reshape(-1)])
+        loads = jnp.concatenate([objective_grad, stiffness[None]], axis=0)
+        return inner(coeffs, loads, adjoint, face_weights, wall_kernel, panel_owner)
+
+    return run

time: 61.8 us -> 61.7 us (level)
  blocking collectives: 15 us -> 16.2 us
  local copies, waits for them, and re-layouts: 7.84 us -> 7.05 us
    unnamed x34 -> x30, local copies, waits for them, and re-layouts: 4.96 us -> 3.24 us
    all_to_all x1, blocking collectives: 15 us -> 16.2 us  [reduce_panels(): return jnp.sum(lax.all_to_all(chunks, ORDER, 0, 0, tiled=False), axis=0)]
  transfers between devices with their start and end apart: 12 -> 12, of which waited for: 2 -> 2; matrix products, arithmetic and copies ran while one was open for 5% -> 7% of each run, Pallas kernels for 0% -> 0%
where the time goes in v12:
time: 61.7 us; the launch traced here: 61.3 us
  starting transfers between devices  21 us (34%)
  blocking collectives  16.2 us (26%)
  waiting for transfers between devices  8.18 us (13%)
  other arithmetic  7.12 us (12%)
  local copies, waits for them, and re-layouts  7.05 us (11%)
  between operations  1.33 us (2%)
    all_to_all x1, blocking collectives, reduce_panels(): return jnp.sum(lax.all_to_all(chunks, ORDER, 0, 0, tiled=False), axis=0)  16.2 us
    ppermute x8, starting transfers between devices, receive(): return lax.ppermute(take(array, rel, dims, width), axes, pairs)  14.2 us
    ppermute x4, starting transfers between devices, receive_pair(): got = lax.ppermute(sent, axes, pairs + back)  6.77 us
    ppermute x4, waiting for transfers between devices, receive_pair(): got = lax.ppermute(sent, axes, pairs + back)  4.61 us
    ppermute x8, waiting for transfers between devices, receive(): return lax.ppermute(take(array, rel, dims, width), axes, pairs)  3.57 us
    unnamed x30, local copies, waits for them, and re-layouts  3.24 us
    mul x3, other arithmetic, relax(): weighted = stiff_pad[None] * mesh_pad  2.17 us
    slice x9, local copies, waits for them, and re-layouts, edge(): return lax.slice_in_dim(array, start, start + width, axis=dim)  2.08 us
  transfers between devices with their start and end apart: 12, of which 2 were waited for; matrix products, arithmetic and copies ran while one was open for 7% of the time, Pallas kernels for 0%

profile of v12, /device:TPU:0, one launch (start us, length us, event | category | flops | bytes accessed | tf_op | source)
XLA Modules:
  0.0 61.3 jit_solution(16207420700171121316)
XLA Ops:
  0.6 1.0 %fusion.51 = (f32[5,4,1,128]{3,2,1,0:T(1,128)S(1)}, f32[5,4,1,128]{3,2,1,0:T(1,128)S(1)}) fusion(f32[5,4,16,128]{3,2,1,0:T(8,128)} %param.11), kind=kLoop, calls=%fused_computation.144 | loop fusion | bytes 40960 | tf_op jit(solution)/shard_map/slice | solution.py:88
  1.7 0.8 %fusion.55 = (f32[3,4,1,128]{3,2,1,0:T(1,128)S(1)}, f32[3,4,1,128]{3,2,1,0:T(1,128)S(1)}) fusion(f32[3,4,16,128]{3,2,1,0:T(8,128)} %param.12), kind=kLoop, calls=%fused_computation.148 | loop fusion | bytes 24576 | tf_op jit(solution)/shard_map/slice | solution.py:88
  2.6 3.0 %collective-permute-start.2 = (f32[8,4,1,128]{3,0,2,1:T(8,128)S(1)}, f32[8,4,1,128]{3,0,2,1:T(8,128)S(1)}, u32[]{:S(2)}, u32[]{:S(2)}) collective-permute-start(f32[8,4,1,128]{3,0,2,1:T(8,128)S(1)} %slice_select_fusion.1), channel_id=1, source_target_pairs={{0,4},{4,0},{1,5},{5,1},{2,6},{6,2},{3,7},{7,3},{8,12},{12,8},{9,1... | collective-permute-start | bytes 49160 | tf_op jit(solution)/shard_map/ppermute | solution.py:133
  5.7 1.5 %collective-permute-start.1 = (f32[8,1,16,128]{3,2,1,0:T(8,128)S(1)}, f32[8,1,16,128]{3,2,1,0:T(8,128)S(1)}, u32[]{:S(2)}, u32[]{:S(2)}) collective-permute-start(f32[8,1,16,128]{3,2,1,0:T(8,128)S(1)} %get-tuple-element.53), channel_id=1, source_target_pairs={{0,1},{1,2},{2,3},{4,5},{5,6},{6,7},{8,9},{9,10},{10,11},{12,13},{... | collective-permute-start | bytes 196616 | tf_op jit(solution)/shard_map/ppermute | solution.py:120
  7.1 1.3 %collective-permute-start = (f32[8,1,16,128]{3,2,1,0:T(8,128)S(1)}, f32[8,1,16,128]{3,2,1,0:T(8,128)S(1)}, u32[]{:S(2)}, u32[]{:S(2)}) collective-permute-start(f32[8,1,16,128]{3,2,1,0:T(8,128)S(1)} %get-tuple-element.54), channel_id=1, source_target_pairs={{1,0},{2,1},{3,2},{5,4},{6,5},{7,6},{9,8},{10,9},{11,10},{13,12},{... | collective-permute-start | bytes 196616 | tf_op jit(solution)/shard_map/ppermute | solution.py:120
  8.5 0.1 fusion.50
  8.6 0.1 copy.88
  8.8 0.1 copy.89
  9.0 0.2 copy.86
  9.2 0.3 copy.87
  9.5 1.6 %collective-permute-start.4 = (f32[8,4,16,1]{2,0,3,1:T(8,128)S(1)}, f32[8,4,16,1]{2,0,3,1:T(8,128)S(1)}, u32[]{:S(2)}, u32[]{:S(2)}) collective-permute-start(f32[8,4,16,1]{2,0,3,1:T(8,128)S(1)} %get-tuple-element.69), channel_id=1, source_target_pairs={{0,8},{8,16},{16,24},{24,0},{1,9},{9,17},{17,25},{25,1},{2,10},{10... | collective-permute-start | bytes 6152 | tf_op jit(solution)/shard_map/ppermute | solution.py:120
  11.2 2.2 %collective-permute-start.3 = (f32[8,4,16,1]{2,0,3,1:T(8,128)S(1)}, f32[8,4,16,1]{2,0,3,1:T(8,128)S(1)}, u32[]{:S(2)}, u32[]{:S(2)}) collective-permute-start(f32[8,4,16,1]{2,0,3,1:T(8,128)S(1)} %get-tuple-element.70), channel_id=1, source_target_pairs={{0,24},{8,0},{16,8},{24,16},{1,25},{9,1},{17,9},{25,17},{2,26},{10... | collective-permute-start | bytes 6152 | tf_op jit(solution)/shard_map/ppermute | solution.py:120
  13.5 0.7 %copy-done.6 = f32[3,5,5]{2,0,1:T(4,128)S(1)} copy-done((f32[3,5,5]{2,0,1:T(4,128)S(1)}, f32[3,5,5]{2,0,1:T(4,128)}, u32[]{:S(2)}) %copy-start.6) | copy-done | bytes 324
  14.3 0.6 copy-done.8
  15.6 0.1 subtract_multiply_fusion
  15.9 0.7 %copy-done.9 = s32[4,128]{1,0:T(4,128)S(1)} copy-done((s32[4,128]{1,0:T(4,128)S(1)}, s32[4,128]{1,0:T(4,128)}, u32[]{:S(2)}) %copy-start.9) | copy-done | bytes 2072
  16.6 0.5 multiply_reduce_fusion.2
  17.1 0.2 multiply_reduce_fusion
  17.3 0.1 multiply_reduce_fusion.4
  17.4 0.2 slice_reduce_fusion
  18.0 0.1 multiply_reduce_fusion.10
  18.2 0.2 copy.77
  18.4 0.2 copy.75
  18.9 0.1 multiply_reduce_fusion.7
  19.0 0.2 fusion.15
  19.5 0.5 copy-done.2
  19.9 0.1 fusion.26
  20.0 0.3 collective-permute-start.5
  20.3 1.6 %collective-permute-start.8 = (f32[4,4,16,3]{3,2,1,0:T(8,128)S(1)}, f32[4,4,16,3]{3,2,1,0:T(8,128)S(1)}, u32[]{:S(2)}, u32[]{:S(2)}) collective-permute-start(f32[4,4,16,3]{3,2,1,0:T(8,128)S(1)} %get-tuple-element.49), channel_id=1, source_target_pairs={{0,8},{8,16},{16,24},{24,0},{1,9},{9,17},{17,25},{25,1},{2,10},{10... | collective-permute-start | bytes 9224 | tf_op jit(solution)/shard_map/ppermute | solution.py:120
  22.0 2.5 %collective-permute-start.9 = (f32[4,4,16,3]{3,2,1,0:T(8,128)S(1)}, f32[4,4,16,3]{3,2,1,0:T(8,128)S(1)}, u32[]{:S(2)}, u32[]{:S(2)}) collective-permute-start(f32[4,4,16,3]{3,2,1,0:T(8,128)S(1)} %get-tuple-element.50), channel_id=1, source_target_pairs={{0,24},{8,0},{16,8},{24,16},{1,25},{9,1},{17,9},{25,17},{2,26},{10... | collective-permute-start | bytes 9224 | tf_op jit(solution)/shard_map/ppermute | solution.py:120
  24.5 1.0 %collective-permute-start.6 = (f32[4,4,3,128]{3,2,1,0:T(4,128)S(1)}, f32[4,4,3,128]{3,2,1,0:T(4,128)S(1)}, u32[]{:S(2)}, u32[]{:S(2)}) collective-permute-start(f32[4,4,3,128]{3,2,1,0:T(4,128)S(1)} %fusion.29), channel_id=1, source_target_pairs={{0,4},{4,0},{1,5},{5,1},{2,6},{6,2},{3,7},{7,3},{8,12},{12,8},{9,1... | collective-permute-start | bytes 73736 | tf_op jit(solution)/shard_map/ppermute | solution.py:133
  25.5 2.4 %collective-permute-start.7 = (f32[4,4,3,3]{3,2,1,0:T(4,128)S(1)}, f32[4,4,3,3]{3,2,1,0:T(4,128)S(1)}, u32[]{:S(2)}, u32[]{:S(2)}) collective-permute-start(f32[4,4,3,3]{3,2,1,0:T(4,128)S(1)} %get-tuple-element.52), channel_id=1, source_target_pairs={{0,28},{8,4},{16,12},{24,20},{4,24},{12,0},{20,8},{28,16},{1,29},{... | collective-permute-start | bytes 1736 | tf_op jit(solution)/shard_map/ppermute | solution.py:133
  28.0 4.6 %collective-permute-done.7 = f32[4,4,3,3]{3,2,1,0:T(4,128)S(1)} collective-permute-done((f32[4,4,3,3]{3,2,1,0:T(4,128)S(1)}, f32[4,4,3,3]{3,2,1,0:T(4,128)S(1)}, u32[]{:S(2)}, u32[]{:S(2)}) %collective-permute-start.7) | collective-permute-done | bytes 608 | tf_op jit(solution)/shard_map/ppermute | solution.py:133
  32.6 0.3 maximum_maximum_fusion
  33.0 2.2 %collective-permute-start.10 = (f32[4,3,22,134]{3,2,1,0:T(8,128)S(1)}, f32[4,3,22,134]{3,2,1,0:T(8,128)S(1)}, u32[]{:S(2)}, u32[]{:S(2)}) collective-permute-start(f32[4,3,22,134]{3,2,1,0:T(8,128)S(1)} %get-tuple-element.35), channel_id=1, source_target_pairs={{0,1},{1,2},{2,3},{4,5},{5,6},{6,7},{8,9},{9,10},{10,11},{12,13},{... | collective-permute-start | bytes 424520 | tf_op jit(solution)/shard_map/ppermute | solution.py:120
  35.2 1.3 %collective-permute-start.11 = (f32[4,3,22,134]{3,2,1,0:T(8,128)S(1)}, f32[4,3,22,134]{3,2,1,0:T(8,128)S(1)}, u32[]{:S(2)}, u32[]{:S(2)}) collective-permute-start(f32[4,3,22,134]{3,2,1,0:T(8,128)S(1)} %get-tuple-element.36), channel_id=1, source_target_pairs={{1,0},{2,1},{3,2},{5,4},{6,5},{7,6},{9,8},{10,9},{11,10},{13,12},{... | collective-permute-start | bytes 424520 | tf_op jit(solution)/shard_map/ppermute | solution.py:120
  36.5 3.5 %collective-permute-done.11 = f32[4,3,22,134]{3,2,1,0:T(8,128)S(1)} collective-permute-done((f32[4,3,22,134]{3,2,1,0:T(8,128)S(1)}, f32[4,3,22,134]{3,2,1,0:T(8,128)S(1)}, u32[]{:S(2)}, u32[]{:S(2)}) %collective-permute-start.11) | collective-permute-done | bytes 141536 | tf_op jit(solution)/shard_map/ppermute | solution.py:120
  40.1 0.3 pad_maximum_fusion
  40.4 0.1 multiply_add_fusion
  40.6 0.1 multiply_add_fusion.1
  40.8 0.1 broadcast_multiply_fusion
  40.9 1.2 %broadcast_multiply_fusion.1 = (f32[3,8,20,132]{3,2,1,0:T(8,128)S(1)}, f32[3,8,20,132]{3,2,1,0:T(8,128)S(1)}) fusion(f32[8,20,132]{2,1,0:T(8,128)S(1)} %get-tuple-element.40, f32[3,10,22,134]{3,2,1,0:T(8,128)S(1)} %get-tuple-element.31, f32[8,20,132]{2,1,0:T(8,128)S(1)} %get-tuple-element.39, f32[4,10,22,134]{3,2,1,0:T(8,128)S(1)} %pad_maximum_fusion, ...), kind=kLoop, calls=%fused_computation.42 | loop fusion | flops 760320 | bytes 2703360 | tf_op jit(solution)/shard_map/mul | solution.py:60
  42.1 0.9 %broadcast_multiply_fusion.2 = (f32[3,6,18,130]{3,2,1,0:T(8,128)S(1)}, f32[3,6,18,130]{3,2,1,0:T(8,128)S(1)}) fusion(f32[6,18,130]{2,1,0:T(8,128)S(1)} %get-tuple-element.38, f32[3,8,20,132]{3,2,1,0:T(8,128)S(1)} %get-tuple-element.29, f32[6,18,130]{2,1,0:T(8,128)S(1)} %get-tuple-element.37, f32[4,10,22,134]{3,2,1,0:T(8,128)S(1)} %pad_maximum_fusion, ...), kind=kLoop, calls=%fused_computation.45 | loop fusion | flops 505440 | bytes 1797120 | tf_op jit(solution)/shard_map/mul | solution.py:60
  43.0 0.9 %multiply_reduce_fusion.9 = (f32[3,4,128]{2,1,0:T(4,128)S(1)}, f32[3,4,16,128]{3,2,1,0:T(8,128)}) fusion(f32[4,16,128]{2,1,0:T(8,128)S(1)} %copy-done.5, f32[3,6,18,130]{3,2,1,0:T(8,128)S(1)} %get-tuple-element.27, f32[3,4,16,128]{3,2,1,0:T(8,128)S(1)} %multiply_reduce_fusion.6, f32[4,16,128]{2,1,0:T(8,128)S(1)} %fusion.34, ...), kind=kLoop, calls=%fused_computation.80 | loop fusion | flops 317952 | bytes 956416 | tf_op jit(solution)/shard_map/reduce_sum | solution.py:246
  43.9 0.4 convolution_bitcast_fusion
  44.3 0.2 select_select_fusion
  44.5 16.2 %all_to_all.5 = f32[32,3,128]{2,1,0:T(4,128)S(1)} all-to-all(f32[32,3,128]{2,1,0:T(4,128)S(1)} %select_select_fusion), channel_id=1, replica_groups=mesh['circ'=4,'normal'=2,'span'=4] {'circ','normal','span'}, dimensions={0} | all-to-all | bytes 98304 | tf_op jit(solution)/shard_map/all_to_all | solution.py:209
  60.7 0.6 %reduce_sum.167 = f32[3,128]{1,0:T(4,128)} reduce(f32[32,3,128]{2,1,0:T(4,128)S(1)} %all_to_all.5, f32[]{:T(128)} %constant.14.clone.1), dimensions={0}, to_apply=%region_14.15 | reduce | flops 11904 | bytes 50692 | tf_op jit(solution)/shard_map/reduce_sum | solution.py:209
  (96 shorter events, 2.4 us)
Async XLA Ops:
  0.6 5.0 %copy-start = (f32[5,4,16,128]{3,2,1,0:T(8,128)S(1)}, f32[5,4,16,128]{3,2,1,0:T(8,128)}, u32[]{:S(2)}) copy-start(f32[5,4,16,128]{3,2,1,0:T(8,128)} %param.11) | copy-start | bytes 491524
  2.5 3.1 %copy-start.1 = (f32[3,4,16,128]{3,2,1,0:T(8,128)S(1)}, f32[3,4,16,128]{3,2,1,0:T(8,128)}, u32[]{:S(2)}) copy-start(f32[3,4,16,128]{3,2,1,0:T(8,128)} %param.12) | copy-start | bytes 294916
  2.6 16.0 %collective-permute-start.2 = (f32[8,4,1,128]{3,0,2,1:T(8,128)S(1)}, f32[8,4,1,128]{3,0,2,1:T(8,128)S(1)}, u32[]{:S(2)}, u32[]{:S(2)}) collective-permute-start(f32[8,4,1,128]{3,0,2,1:T(8,128)S(1)} %slice_select_fusion.1), channel_id=1, source_target_pairs={{0,4},{4,0},{1,5},{5,1},{2,6},{6,2},{3,7},{7,3},{8,12},{12,8},{9,1... | collective-permute-start | bytes 49160 | tf_op jit(solution)/shard_map/ppermute | solution.py:133
  5.7 13.2 %collective-permute-start.1 = (f32[8,1,16,128]{3,2,1,0:T(8,128)S(1)}, f32[8,1,16,128]{3,2,1,0:T(8,128)S(1)}, u32[]{:S(2)}, u32[]{:S(2)}) collective-permute-start(f32[8,1,16,128]{3,2,1,0:T(8,128)S(1)} %get-tuple-element.53), channel_id=1, source_target_pairs={{0,1},{1,2},{2,3},{4,5},{5,6},{6,7},{8,9},{9,10},{10,11},{12,13},{... | collective-permute-start | bytes 196616 | tf_op jit(solution)/shard_map/ppermute | solution.py:120
  7.1 11.7 %collective-permute-start = (f32[8,1,16,128]{3,2,1,0:T(8,128)S(1)}, f32[8,1,16,128]{3,2,1,0:T(8,128)S(1)}, u32[]{:S(2)}, u32[]{:S(2)}) collective-permute-start(f32[8,1,16,128]{3,2,1,0:T(8,128)S(1)} %get-tuple-element.54), channel_id=1, source_target_pairs={{1,0},{2,1},{3,2},{5,4},{6,5},{7,6},{9,8},{10,9},{11,10},{13,12},{... | collective-permute-start | bytes 196616 | tf_op jit(solution)/shard_map/ppermute | solution.py:120
  9.5 5.5 %copy-start.3 = (f32[5,4,16,128]{3,2,1,0:T(8,128)S(1)}, f32[5,4,16,128]{3,2,1,0:T(8,128)}, u32[]{:S(2)}) copy-start(f32[5,4,16,128]{3,2,1,0:T(8,128)} %param.9) | copy-start | bytes 491524
  9.5 8.4 %collective-permute-start.4 = (f32[8,4,16,1]{2,0,3,1:T(8,128)S(1)}, f32[8,4,16,1]{2,0,3,1:T(8,128)S(1)}, u32[]{:S(2)}, u32[]{:S(2)}) collective-permute-start(f32[8,4,16,1]{2,0,3,1:T(8,128)S(1)} %get-tuple-element.69), channel_id=1, source_target_pairs={{0,8},{8,16},{16,24},{24,0},{1,9},{9,17},{17,25},{25,1},{2,10},{10... | collective-permute-start | bytes 6152 | tf_op jit(solution)/shard_map/ppermute | solution.py:120
  11.2 6.9 %collective-permute-start.3 = (f32[8,4,16,1]{2,0,3,1:T(8,128)S(1)}, f32[8,4,16,1]{2,0,3,1:T(8,128)S(1)}, u32[]{:S(2)}, u32[]{:S(2)}) collective-permute-start(f32[8,4,16,1]{2,0,3,1:T(8,128)S(1)} %get-tuple-element.70), channel_id=1, source_target_pairs={{0,24},{8,0},{16,8},{24,16},{1,25},{9,1},{17,9},{25,17},{2,26},{10... | collective-permute-start | bytes 6152 | tf_op jit(solution)/shard_map/ppermute | solution.py:120
  13.4 0.7 %copy-start.6 = (f32[3,5,5]{2,0,1:T(4,128)S(1)}, f32[3,5,5]{2,0,1:T(4,128)}, u32[]{:S(2)}) copy-start(f32[3,5,5]{2,0,1:T(4,128)} %param.6) | copy-start | bytes 904
  13.4 0.8 %copy-start.7 = (f32[3,5,5]{2,0,1:T(4,128)S(1)}, f32[3,5,5]{2,0,1:T(4,128)}, u32[]{:S(2)}) copy-start(f32[3,5,5]{2,0,1:T(4,128)} %param.7) | copy-start | bytes 904
  14.1 0.9 %copy-start.4 = (f32[4,16,128]{2,1,0:T(8,128)S(1)}, f32[4,16,128]{2,1,0:T(8,128)}, u32[]{:S(2)}) copy-start(f32[4,16,128]{2,1,0:T(8,128)} %param.10) | copy-start | bytes 98308
  14.2 0.7 %copy-start.8 = (f32[3,5]{1,0:T(4,128)S(1)}, f32[3,5]{1,0:T(4,128)}, u32[]{:S(2)}) copy-start(f32[3,5]{1,0:T(4,128)} %param.8) | copy-start | bytes 184
  15.9 0.7 %copy-start.9 = (s32[4,128]{1,0:T(4,128)S(1)}, s32[4,128]{1,0:T(4,128)}, u32[]{:S(2)}) copy-start(s32[4,128]{1,0:T(4,128)} %param.14) | copy-start | bytes 6148
  19.2 0.7 %copy-start.2 = (f32[5,4,16,128]{3,2,1,0:T(8,128)}, f32[5,4,16,128]{3,2,1,0:T(8,128)S(1)}, u32[]{:S(2)}) copy-start(f32[5,4,16,128]{3,2,1,0:T(8,128)S(1)} %fusion.15) | copy-start | bytes 491524
  20.0 7.9 %collective-permute-start.5 = (f32[4,4,3,3]{3,2,1,0:T(4,128)S(1)}, f32[4,4,3,3]{3,2,1,0:T(4,128)S(1)}, u32[]{:S(2)}, u32[]{:S(2)}) collective-permute-start(f32[4,4,3,3]{3,2,1,0:T(4,128)S(1)} %get-tuple-element.51), channel_id=1, source_target_pairs={{0,12},{8,20},{16,28},{24,4},{4,8},{12,16},{20,24},{28,0},{1,13},{... | collective-permute-start | bytes 1736 | tf_op jit(solution)/shard_map/ppermute | solution.py:133
  20.3 12.3 %collective-permute-start.8 = (f32[4,4,16,3]{3,2,1,0:T(8,128)S(1)}, f32[4,4,16,3]{3,2,1,0:T(8,128)S(1)}, u32[]{:S(2)}, u32[]{:S(2)}) collective-permute-start(f32[4,4,16,3]{3,2,1,0:T(8,128)S(1)} %get-tuple-element.49), channel_id=1, source_target_pairs={{0,8},{8,16},{16,24},{24,0},{1,9},{9,17},{17,25},{25,1},{2,10},{10... | collective-permute-start | bytes 9224 | tf_op jit(solution)/shard_map/ppermute | solution.py:120
  22.0 10.6 %collective-permute-start.9 = (f32[4,4,16,3]{3,2,1,0:T(8,128)S(1)}, f32[4,4,16,3]{3,2,1,0:T(8,128)S(1)}, u32[]{:S(2)}, u32[]{:S(2)}) collective-permute-start(f32[4,4,16,3]{3,2,1,0:T(8,128)S(1)} %get-tuple-element.50), channel_id=1, source_target_pairs={{0,24},{8,0},{16,8},{24,16},{1,25},{9,1},{17,9},{25,17},{2,26},{10... | collective-permute-start | bytes 9224 | tf_op jit(solution)/shard_map/ppermute | solution.py:120
  24.5 8.1 %collective-permute-start.6 = (f32[4,4,3,128]{3,2,1,0:T(4,128)S(1)}, f32[4,4,3,128]{3,2,1,0:T(4,128)S(1)}, u32[]{:S(2)}, u32[]{:S(2)}) collective-permute-start(f32[4,4,3,128]{3,2,1,0:T(4,128)S(1)} %fusion.29), channel_id=1, source_target_pairs={{0,4},{4,0},{1,5},{5,1},{2,6},{6,2},{3,7},{7,3},{8,12},{12,8},{9,1... | collective-permute-start | bytes 73736 | tf_op jit(solution)/shard_map/ppermute | solution.py:133
  25.5 7.1 %collective-permute-start.7 = (f32[4,4,3,3]{3,2,1,0:T(4,128)S(1)}, f32[4,4,3,3]{3,2,1,0:T(4,128)S(1)}, u32[]{:S(2)}, u32[]{:S(2)}) collective-permute-start(f32[4,4,3,3]{3,2,1,0:T(4,128)S(1)} %get-tuple-element.52), channel_id=1, source_target_pairs={{0,28},{8,4},{16,12},{24,20},{4,24},{12,0},{20,8},{28,16},{1,29},{... | collective-permute-start | bytes 1736 | tf_op jit(solution)/shard_map/ppermute | solution.py:133
  33.0 3.5 %collective-permute-start.10 = (f32[4,3,22,134]{3,2,1,0:T(8,128)S(1)}, f32[4,3,22,134]{3,2,1,0:T(8,128)S(1)}, u32[]{:S(2)}, u32[]{:S(2)}) collective-permute-start(f32[4,3,22,134]{3,2,1,0:T(8,128)S(1)} %get-tuple-element.35), channel_id=1, source_target_pairs={{0,1},{1,2},{2,3},{4,5},{5,6},{6,7},{8,9},{9,10},{10,11},{12,13},{... | collective-permute-start | bytes 424520 | tf_op jit(solution)/shard_map/ppermute | solution.py:120
  35.2 4.9 %collective-permute-start.11 = (f32[4,3,22,134]{3,2,1,0:T(8,128)S(1)}, f32[4,3,22,134]{3,2,1,0:T(8,128)S(1)}, u32[]{:S(2)}, u32[]{:S(2)}) collective-permute-start(f32[4,3,22,134]{3,2,1,0:T(8,128)S(1)} %get-tuple-element.36), channel_id=1, source_target_pairs={{1,0},{2,1},{3,2},{5,4},{6,5},{7,6},{9,8},{10,9},{11,10},{13,12},{... | collective-permute-start | bytes 424520 | tf_op jit(solution)/shard_map/ppermute | solution.py:120
  42.1 0.9 %copy-start.5 = (f32[4,16,128]{2,1,0:T(8,128)S(1)}, f32[4,16,128]{2,1,0:T(8,128)}, u32[]{:S(2)}) copy-start(f32[4,16,128]{2,1,0:T(8,128)} %param.13) | copy-start | bytes 98308

commit v13 on v10

--- a/solution.py
+++ b/solution.py
@@ -56,24 +56,22 @@
     return total
 
 
-def relax(mesh_pad, stiff_pad, force_pad):
+def relax(mesh_pad, stiff_pad, force_pad, scale_pad):
     weighted = stiff_pad[None] * mesh_pad
     stiff_in = stiff_pad[1:-1, 1:-1, 1:-1]
     diag_term = 6.0 * stiff_in + 1.0
     mesh_in = inner(mesh_pad)
-    return (
-        mesh_in
-        + 0.8
-        * (inner(force_pad) - diag_term[None] * mesh_in + neighbor_sum(weighted))
-        / diag_term[None]
-    )
+    scale = scale_pad[1:-1, 1:-1, 1:-1]
+    return mesh_in + scale[None] * (inner(force_pad) - diag_term[None] * mesh_in + neighbor_sum(weighted))
 
 
 def run_sweeps(stiff_pad, force_pad):
-    mesh_pad = 0.8 * force_pad / (6.0 * stiff_pad[None] + 1.0)
+    scale_pad = 0.8 / (6.0 * stiff_pad + 1.0)
+    mesh_pad = force_pad * scale_pad[None]
     for sweep in range(1, SWEEPS):
-        mesh_pad = relax(mesh_pad, stiff_pad, force_pad)
+        mesh_pad = relax(mesh_pad, stiff_pad, force_pad, scale_pad)
         stiff_pad = stiff_pad[1:-1, 1:-1, 1:-1]
+        scale_pad = scale_pad[1:-1, 1:-1, 1:-1]
         force_pad = inner(force_pad)
     return mesh_pad
 

time: 61.8 us -> 62.2 us (level)
  no operation moved by 1% of the time
where the time goes in v13:
time: 62.2 us; the launch traced here: 61.6 us
  starting transfers between devices  21 us (34%)
  blocking collectives  15 us (24%)
  waiting for transfers between devices  8.64 us (14%)
  local copies, waits for them, and re-layouts  8.13 us (13%)
  other arithmetic  7.07 us (11%)
  between operations  1.36 us (2%)
    all_to_all x1, blocking collectives, reduce_panels(): return jnp.sum(lax.all_to_all(chunks, ORDER, 0, 0, tiled=False), axis=0)  15 us
    ppermute x8, starting transfers between devices, receive(): return lax.ppermute(take(array, rel, dims, width), axes, pairs)  14.2 us
    ppermute x4, starting transfers between devices, receive_pair(): got = lax.ppermute(sent, axes, pairs + back)  6.77 us
    unnamed x34, local copies, waits for them, and re-layouts  4.96 us
    ppermute x4, waiting for transfers between devices, receive_pair(): got = lax.ppermute(sent, axes, pairs + back)  4.61 us
    ppermute x8, waiting for transfers between devices, receive(): return lax.ppermute(take(array, rel, dims, width), axes, pairs)  4.03 us
    mul x3, other arithmetic, relax(): weighted = stiff_pad[None] * mesh_pad  2.16 us
    slice x9, local copies, waits for them, and re-layouts, edge(): return lax.slice_in_dim(array, start, start + width, axis=dim)  2.08 us
  transfers between devices with their start and end apart: 12, of which 2 were waited for; matrix products, arithmetic and copies ran while one was open for 5% of the time, Pallas kernels for 0%

profile of v13, /device:TPU:0, one launch (start us, length us, event | category | flops | bytes accessed | tf_op | source)
XLA Modules:
  0.0 61.6 jit_solution(10571432746385695246)
XLA Ops:
  0.6 1.0 %fusion.46 = (f32[5,4,1,128]{3,2,1,0:T(1,128)S(1)}, f32[5,4,1,128]{3,2,1,0:T(1,128)S(1)}) fusion(f32[5,4,16,128]{3,2,1,0:T(8,128)} %param.9), kind=kLoop, calls=%fused_computation.145 | loop fusion | bytes 40960 | tf_op jit(solution)/shard_map/slice | solution.py:86
  1.7 0.8 %fusion.50 = (f32[3,4,1,128]{3,2,1,0:T(1,128)S(1)}, f32[3,4,1,128]{3,2,1,0:T(1,128)S(1)}) fusion(f32[3,4,16,128]{3,2,1,0:T(8,128)} %param.11), kind=kLoop, calls=%fused_computation.149 | loop fusion | bytes 24576 | tf_op jit(solution)/shard_map/slice | solution.py:86
  2.6 3.0 %collective-permute-start.2 = (f32[8,4,1,128]{3,0,2,1:T(8,128)S(1)}, f32[8,4,1,128]{3,0,2,1:T(8,128)S(1)}, u32[]{:S(2)}, u32[]{:S(2)}) collective-permute-start(f32[8,4,1,128]{3,0,2,1:T(8,128)S(1)} %slice_select_fusion.1), channel_id=1, source_target_pairs={{0,4},{4,0},{1,5},{5,1},{2,6},{6,2},{3,7},{7,3},{8,12},{12,8},{9,1... | collective-permute-start | bytes 49160 | tf_op jit(solution)/shard_map/ppermute | solution.py:131
  5.7 1.5 %collective-permute-start.1 = (f32[8,1,16,128]{3,2,1,0:T(8,128)S(1)}, f32[8,1,16,128]{3,2,1,0:T(8,128)S(1)}, u32[]{:S(2)}, u32[]{:S(2)}) collective-permute-start(f32[8,1,16,128]{3,2,1,0:T(8,128)S(1)} %get-tuple-element.49), channel_id=1, source_target_pairs={{0,1},{1,2},{2,3},{4,5},{5,6},{6,7},{8,9},{9,10},{10,11},{12,13},{... | collective-permute-start | bytes 196616 | tf_op jit(solution)/shard_map/ppermute | solution.py:118
  7.1 1.3 %collective-permute-start = (f32[8,1,16,128]{3,2,1,0:T(8,128)S(1)}, f32[8,1,16,128]{3,2,1,0:T(8,128)S(1)}, u32[]{:S(2)}, u32[]{:S(2)}) collective-permute-start(f32[8,1,16,128]{3,2,1,0:T(8,128)S(1)} %get-tuple-element.50), channel_id=1, source_target_pairs={{1,0},{2,1},{3,2},{5,4},{6,5},{7,6},{9,8},{10,9},{11,10},{13,12},{... | collective-permute-start | bytes 196616 | tf_op jit(solution)/shard_map/ppermute | solution.py:118
  8.6 0.1 copy.117
  8.8 0.1 copy.118
  9.0 0.2 copy.115
  9.2 0.3 copy.116
  9.5 1.6 %collective-permute-start.4 = (f32[8,4,16,1]{2,0,3,1:T(8,128)S(1)}, f32[8,4,16,1]{2,0,3,1:T(8,128)S(1)}, u32[]{:S(2)}, u32[]{:S(2)}) collective-permute-start(f32[8,4,16,1]{2,0,3,1:T(8,128)S(1)} %get-tuple-element.65), channel_id=1, source_target_pairs={{0,8},{8,16},{16,24},{24,0},{1,9},{9,17},{17,25},{25,1},{2,10},{10... | collective-permute-start | bytes 6152 | tf_op jit(solution)/shard_map/ppermute | solution.py:118
  11.1 2.2 %collective-permute-start.3 = (f32[8,4,16,1]{2,0,3,1:T(8,128)S(1)}, f32[8,4,16,1]{2,0,3,1:T(8,128)S(1)}, u32[]{:S(2)}, u32[]{:S(2)}) collective-permute-start(f32[8,4,16,1]{2,0,3,1:T(8,128)S(1)} %get-tuple-element.66), channel_id=1, source_target_pairs={{0,24},{8,0},{16,8},{24,16},{1,25},{9,1},{17,9},{25,17},{2,26},{10... | collective-permute-start | bytes 6152 | tf_op jit(solution)/shard_map/ppermute | solution.py:118
  13.4 0.7 %copy-done.6 = f32[3,5,5]{2,0,1:T(4,128)S(1)} copy-done((f32[3,5,5]{2,0,1:T(4,128)S(1)}, f32[3,5,5]{2,0,1:T(4,128)}, u32[]{:S(2)}) %copy-start.6) | copy-done | bytes 324
  14.1 0.7 %copy-done.7 = f32[3,5,5]{2,0,1:T(4,128)S(1)} copy-done((f32[3,5,5]{2,0,1:T(4,128)S(1)}, f32[3,5,5]{2,0,1:T(4,128)}, u32[]{:S(2)}) %copy-start.7) | copy-done | bytes 324
  14.9 0.1 subtract_multiply_fusion
  15.1 0.7 %copy-done.9 = s32[4,128]{1,0:T(4,128)S(1)} copy-done((s32[4,128]{1,0:T(4,128)S(1)}, s32[4,128]{1,0:T(4,128)}, u32[]{:S(2)}) %copy-start.9) | copy-done | bytes 2072
  15.8 0.5 multiply_reduce_fusion.2
  16.3 0.2 multiply_reduce_fusion
  16.5 0.1 multiply_reduce_fusion.4
  16.7 0.2 slice_reduce_fusion
  16.9 0.6 %copy-done.8 = f32[3,5]{1,0:T(4,128)S(1)} copy-done((f32[3,5]{1,0:T(4,128)S(1)}, f32[3,5]{1,0:T(4,128)}, u32[]{:S(2)}) %copy-start.8) | copy-done | bytes 84
  17.9 0.2 copy.100
  18.1 0.2 copy.98
  18.6 0.1 multiply_reduce_fusion.7
  18.8 0.7 %copy-done.4 = f32[5,4,16,128]{3,2,1,0:T(8,128)S(1)} copy-done((f32[5,4,16,128]{3,2,1,0:T(8,128)S(1)}, f32[5,4,16,128]{3,2,1,0:T(8,128)}, u32[]{:S(2)}) %copy-start.4) | copy-done | bytes 163864
  19.5 0.2 fusion.12
  19.8 0.7 %copy-done.2 = f32[4,16,128]{2,1,0:T(8,128)S(1)} copy-done((f32[4,16,128]{2,1,0:T(8,128)S(1)}, f32[4,16,128]{2,1,0:T(8,128)}, u32[]{:S(2)}) %copy-start.2) | copy-done | bytes 32792
  20.7 0.3 collective-permute-start.5
  21.1 1.6 %collective-permute-start.8 = (f32[4,4,16,3]{3,2,1,0:T(8,128)S(1)}, f32[4,4,16,3]{3,2,1,0:T(8,128)S(1)}, u32[]{:S(2)}, u32[]{:S(2)}) collective-permute-start(f32[4,4,16,3]{3,2,1,0:T(8,128)S(1)} %get-tuple-element.45), channel_id=1, source_target_pairs={{0,8},{8,16},{16,24},{24,0},{1,9},{9,17},{17,25},{25,1},{2,10},{10... | collective-permute-start | bytes 9224 | tf_op jit(solution)/shard_map/ppermute | solution.py:118
  22.7 2.5 %collective-permute-start.9 = (f32[4,4,16,3]{3,2,1,0:T(8,128)S(1)}, f32[4,4,16,3]{3,2,1,0:T(8,128)S(1)}, u32[]{:S(2)}, u32[]{:S(2)}) collective-permute-start(f32[4,4,16,3]{3,2,1,0:T(8,128)S(1)} %get-tuple-element.46), channel_id=1, source_target_pairs={{0,24},{8,0},{16,8},{24,16},{1,25},{9,1},{17,9},{25,17},{2,26},{10... | collective-permute-start | bytes 9224 | tf_op jit(solution)/shard_map/ppermute | solution.py:118
  25.2 2.4 %collective-permute-start.7 = (f32[4,4,3,3]{3,2,1,0:T(4,128)S(1)}, f32[4,4,3,3]{3,2,1,0:T(4,128)S(1)}, u32[]{:S(2)}, u32[]{:S(2)}) collective-permute-start(f32[4,4,3,3]{3,2,1,0:T(4,128)S(1)} %get-tuple-element.48), channel_id=1, source_target_pairs={{0,28},{8,4},{16,12},{24,20},{4,24},{12,0},{20,8},{28,16},{1,29},{... | collective-permute-start | bytes 1736 | tf_op jit(solution)/shard_map/ppermute | solution.py:131
  27.6 1.0 %collective-permute-start.6 = (f32[4,4,3,128]{3,2,1,0:T(4,128)S(1)}, f32[4,4,3,128]{3,2,1,0:T(4,128)S(1)}, u32[]{:S(2)}, u32[]{:S(2)}) collective-permute-start(f32[4,4,3,128]{3,2,1,0:T(4,128)S(1)} %fusion.25), channel_id=1, source_target_pairs={{0,4},{4,0},{1,5},{5,1},{2,6},{6,2},{3,7},{7,3},{8,12},{12,8},{9,1... | collective-permute-start | bytes 73736 | tf_op jit(solution)/shard_map/ppermute | solution.py:131
  28.7 4.6 %collective-permute-done.7 = f32[4,4,3,3]{3,2,1,0:T(4,128)S(1)} collective-permute-done((f32[4,4,3,3]{3,2,1,0:T(4,128)S(1)}, f32[4,4,3,3]{3,2,1,0:T(4,128)S(1)}, u32[]{:S(2)}, u32[]{:S(2)}) %collective-permute-start.7) | collective-permute-done | bytes 608 | tf_op jit(solution)/shard_map/ppermute | solution.py:131
  33.3 0.3 maximum_maximum_fusion
  33.7 2.2 %collective-permute-start.10 = (f32[4,3,22,134]{3,2,1,0:T(8,128)S(1)}, f32[4,3,22,134]{3,2,1,0:T(8,128)S(1)}, u32[]{:S(2)}, u32[]{:S(2)}) collective-permute-start(f32[4,3,22,134]{3,2,1,0:T(8,128)S(1)} %get-tuple-element.31), channel_id=1, source_target_pairs={{0,1},{1,2},{2,3},{4,5},{5,6},{6,7},{8,9},{9,10},{10,11},{12,13},{... | collective-permute-start | bytes 424520 | tf_op jit(solution)/shard_map/ppermute | solution.py:118
  35.9 1.3 %collective-permute-start.11 = (f32[4,3,22,134]{3,2,1,0:T(8,128)S(1)}, f32[4,3,22,134]{3,2,1,0:T(8,128)S(1)}, u32[]{:S(2)}, u32[]{:S(2)}) collective-permute-start(f32[4,3,22,134]{3,2,1,0:T(8,128)S(1)} %get-tuple-element.32), channel_id=1, source_target_pairs={{1,0},{2,1},{3,2},{5,4},{6,5},{7,6},{9,8},{10,9},{11,10},{13,12},{... | collective-permute-start | bytes 424520 | tf_op jit(solution)/shard_map/ppermute | solution.py:118
  37.2 4.0 %collective-permute-done.11 = f32[4,3,22,134]{3,2,1,0:T(8,128)S(1)} collective-permute-done((f32[4,3,22,134]{3,2,1,0:T(8,128)S(1)}, f32[4,3,22,134]{3,2,1,0:T(8,128)S(1)}, u32[]{:S(2)}, u32[]{:S(2)}) %collective-permute-start.11) | collective-permute-done | bytes 141536 | tf_op jit(solution)/shard_map/ppermute | solution.py:118
  41.2 0.3 pad_maximum_fusion
  41.7 0.1 multiply_add_fusion
  41.8 0.1 multiply_add_fusion.1
  41.9 0.1 slice.447
  42.3 0.1 broadcast_multiply_fusion
  42.4 1.2 %broadcast_multiply_fusion.1 = (f32[3,8,20,132]{3,2,1,0:T(8,128)S(1)}, f32[3,8,20,132]{3,2,1,0:T(8,128)S(1)}) fusion(f32[8,20,132]{2,1,0:T(8,128)S(1)} %get-tuple-element.36, f32[3,10,22,134]{3,2,1,0:T(8,128)S(1)} %get-tuple-element.27, f32[8,20,132]{2,1,0:T(8,128)S(1)} %get-tuple-element.35, f32[4,10,22,134]{3,2,1,0:T(8,128)S(1)} %pad_maximum_fusion, ...), kind=kLoop, calls=%fused_computation.39 | loop fusion | flops 696960 | bytes 2787840 | tf_op jit(solution)/shard_map/mul | solution.py:60
  43.6 0.9 %broadcast_multiply_fusion.2 = (f32[3,6,18,130]{3,2,1,0:T(8,128)S(1)}, f32[3,6,18,130]{3,2,1,0:T(8,128)S(1)}) fusion(f32[6,18,130]{2,1,0:T(8,128)S(1)} %get-tuple-element.34, f32[3,8,20,132]{3,2,1,0:T(8,128)S(1)} %get-tuple-element.25, f32[6,18,130]{2,1,0:T(8,128)S(1)} %get-tuple-element.33, f32[4,10,22,134]{3,2,1,0:T(8,128)S(1)} %pad_maximum_fusion, ...), kind=kLoop, calls=%fused_computation.43 | loop fusion | flops 463320 | bytes 1853280 | tf_op jit(solution)/shard_map/mul | solution.py:60
  44.5 0.9 %multiply_reduce_fusion.9 = (f32[3,4,128]{2,1,0:T(4,128)S(1)}, f32[3,4,16,128]{3,2,1,0:T(8,128)}) fusion(f32[4,16,128]{2,1,0:T(8,128)S(1)} %copy-done.5, f32[3,6,18,130]{3,2,1,0:T(8,128)S(1)} %get-tuple-element.23, f32[3,4,16,128]{3,2,1,0:T(8,128)S(1)} %multiply_reduce_fusion.6, f32[4,16,128]{2,1,0:T(8,128)S(1)} %fusion.30, f32[4,16,128]{2,1,0:T(8,128)S(1)} %slice.467, ...), kind=kLoop, calls=%fused_computation.76 | loop fusion | flops 293376 | bytes 989184 | tf_op jit(solution)/shard_map/reduce_sum | solution.py:244
  45.4 0.4 convolution_bitcast_fusion
  45.8 0.2 select_select_fusion
  46.0 15.0 %all_to_all.5 = f32[32,3,128]{2,1,0:T(4,128)S(1)} all-to-all(f32[32,3,128]{2,1,0:T(4,128)S(1)} %select_select_fusion), channel_id=1, replica_groups=mesh['circ'=4,'normal'=2,'span'=4] {'circ','normal','span'}, dimensions={0} | all-to-all | bytes 98304 | tf_op jit(solution)/shard_map/all_to_all | solution.py:207
  61.0 0.6 %reduce_sum.167 = f32[3,128]{1,0:T(4,128)} reduce(f32[32,3,128]{2,1,0:T(4,128)S(1)} %all_to_all.5, f32[]{:T(128)} %constant.14.clone.1), dimensions={0}, to_apply=%region_14.15 | reduce | flops 11904 | bytes 50692 | tf_op jit(solution)/shard_map/reduce_sum | solution.py:207
  (91 shorter events, 1.9 us)
Async XLA Ops:
  0.6 5.0 %copy-start = (f32[5,4,16,128]{3,2,1,0:T(8,128)S(1)}, f32[5,4,16,128]{3,2,1,0:T(8,128)}, u32[]{:S(2)}) copy-start(f32[5,4,16,128]{3,2,1,0:T(8,128)} %param.9) | copy-start | bytes 491524
  2.5 3.1 %copy-start.1 = (f32[3,4,16,128]{3,2,1,0:T(8,128)S(1)}, f32[3,4,16,128]{3,2,1,0:T(8,128)}, u32[]{:S(2)}) copy-start(f32[3,4,16,128]{3,2,1,0:T(8,128)} %param.11) | copy-start | bytes 294916
  2.6 15.7 %collective-permute-start.2 = (f32[8,4,1,128]{3,0,2,1:T(8,128)S(1)}, f32[8,4,1,128]{3,0,2,1:T(8,128)S(1)}, u32[]{:S(2)}, u32[]{:S(2)}) collective-permute-start(f32[8,4,1,128]{3,0,2,1:T(8,128)S(1)} %slice_select_fusion.1), channel_id=1, source_target_pairs={{0,4},{4,0},{1,5},{5,1},{2,6},{6,2},{3,7},{7,3},{8,12},{12,8},{9,1... | collective-permute-start | bytes 49160 | tf_op jit(solution)/shard_map/ppermute | solution.py:131
  5.7 12.9 %collective-permute-start.1 = (f32[8,1,16,128]{3,2,1,0:T(8,128)S(1)}, f32[8,1,16,128]{3,2,1,0:T(8,128)S(1)}, u32[]{:S(2)}, u32[]{:S(2)}) collective-permute-start(f32[8,1,16,128]{3,2,1,0:T(8,128)S(1)} %get-tuple-element.49), channel_id=1, source_target_pairs={{0,1},{1,2},{2,3},{4,5},{5,6},{6,7},{8,9},{9,10},{10,11},{12,13},{... | collective-permute-start | bytes 196616 | tf_op jit(solution)/shard_map/ppermute | solution.py:118
  7.1 11.5 %collective-permute-start = (f32[8,1,16,128]{3,2,1,0:T(8,128)S(1)}, f32[8,1,16,128]{3,2,1,0:T(8,128)S(1)}, u32[]{:S(2)}, u32[]{:S(2)}) collective-permute-start(f32[8,1,16,128]{3,2,1,0:T(8,128)S(1)} %get-tuple-element.50), channel_id=1, source_target_pairs={{1,0},{2,1},{3,2},{5,4},{6,5},{7,6},{9,8},{10,9},{11,10},{13,12},{... | collective-permute-start | bytes 196616 | tf_op jit(solution)/shard_map/ppermute | solution.py:118
  9.5 8.1 %collective-permute-start.4 = (f32[8,4,16,1]{2,0,3,1:T(8,128)S(1)}, f32[8,4,16,1]{2,0,3,1:T(8,128)S(1)}, u32[]{:S(2)}, u32[]{:S(2)}) collective-permute-start(f32[8,4,16,1]{2,0,3,1:T(8,128)S(1)} %get-tuple-element.65), channel_id=1, source_target_pairs={{0,8},{8,16},{16,24},{24,0},{1,9},{9,17},{17,25},{25,1},{2,10},{10... | collective-permute-start | bytes 6152 | tf_op jit(solution)/shard_map/ppermute | solution.py:118
  11.1 6.6 %collective-permute-start.3 = (f32[8,4,16,1]{2,0,3,1:T(8,128)S(1)}, f32[8,4,16,1]{2,0,3,1:T(8,128)S(1)}, u32[]{:S(2)}, u32[]{:S(2)}) collective-permute-start(f32[8,4,16,1]{2,0,3,1:T(8,128)S(1)} %get-tuple-element.66), channel_id=1, source_target_pairs={{0,24},{8,0},{16,8},{24,16},{1,25},{9,1},{17,9},{25,17},{2,26},{10... | collective-permute-start | bytes 6152 | tf_op jit(solution)/shard_map/ppermute | solution.py:118
  13.4 0.7 %copy-start.6 = (f32[3,5,5]{2,0,1:T(4,128)S(1)}, f32[3,5,5]{2,0,1:T(4,128)}, u32[]{:S(2)}) copy-start(f32[3,5,5]{2,0,1:T(4,128)} %param.12) | copy-start | bytes 904
  14.1 0.7 %copy-start.7 = (f32[3,5,5]{2,0,1:T(4,128)S(1)}, f32[3,5,5]{2,0,1:T(4,128)}, u32[]{:S(2)}) copy-start(f32[3,5,5]{2,0,1:T(4,128)} %param.13) | copy-start | bytes 904
  15.1 0.7 %copy-start.9 = (s32[4,128]{1,0:T(4,128)S(1)}, s32[4,128]{1,0:T(4,128)}, u32[]{:S(2)}) copy-start(s32[4,128]{1,0:T(4,128)} %param.17) | copy-start | bytes 6148
  16.9 0.7 %copy-start.8 = (f32[3,5]{1,0:T(4,128)S(1)}, f32[3,5]{1,0:T(4,128)}, u32[]{:S(2)}) copy-start(f32[3,5]{1,0:T(4,128)} %param.14) | copy-start | bytes 184
  18.6 0.9 %copy-start.4 = (f32[5,4,16,128]{3,2,1,0:T(8,128)S(1)}, f32[5,4,16,128]{3,2,1,0:T(8,128)}, u32[]{:S(2)}) copy-start(f32[5,4,16,128]{3,2,1,0:T(8,128)} %param.10) | copy-start | bytes 491524
  19.7 0.9 %copy-start.3 = (f32[5,4,16,128]{3,2,1,0:T(8,128)}, f32[5,4,16,128]{3,2,1,0:T(8,128)S(1)}, u32[]{:S(2)}) copy-start(f32[5,4,16,128]{3,2,1,0:T(8,128)S(1)} %fusion.12) | copy-start | bytes 491524
  19.7 0.8 %copy-start.2 = (f32[4,16,128]{2,1,0:T(8,128)S(1)}, f32[4,16,128]{2,1,0:T(8,128)}, u32[]{:S(2)}) copy-start(f32[4,16,128]{2,1,0:T(8,128)} %param.15) | copy-start | bytes 98308
  20.7 7.9 %collective-permute-start.5 = (f32[4,4,3,3]{3,2,1,0:T(4,128)S(1)}, f32[4,4,3,3]{3,2,1,0:T(4,128)S(1)}, u32[]{:S(2)}, u32[]{:S(2)}) collective-permute-start(f32[4,4,3,3]{3,2,1,0:T(4,128)S(1)} %get-tuple-element.47), channel_id=1, source_target_pairs={{0,12},{8,20},{16,28},{24,4},{4,8},{12,16},{20,24},{28,0},{1,13},{... | collective-permute-start | bytes 1736 | tf_op jit(solution)/shard_map/ppermute | solution.py:131
  21.1 12.3 %collective-permute-start.8 = (f32[4,4,16,3]{3,2,1,0:T(8,128)S(1)}, f32[4,4,16,3]{3,2,1,0:T(8,128)S(1)}, u32[]{:S(2)}, u32[]{:S(2)}) collective-permute-start(f32[4,4,16,3]{3,2,1,0:T(8,128)S(1)} %get-tuple-element.45), channel_id=1, source_target_pairs={{0,8},{8,16},{16,24},{24,0},{1,9},{9,17},{17,25},{25,1},{2,10},{10... | collective-permute-start | bytes 9224 | tf_op jit(solution)/shard_map/ppermute | solution.py:118
  22.7 10.6 %collective-permute-start.9 = (f32[4,4,16,3]{3,2,1,0:T(8,128)S(1)}, f32[4,4,16,3]{3,2,1,0:T(8,128)S(1)}, u32[]{:S(2)}, u32[]{:S(2)}) collective-permute-start(f32[4,4,16,3]{3,2,1,0:T(8,128)S(1)} %get-tuple-element.46), channel_id=1, source_target_pairs={{0,24},{8,0},{16,8},{24,16},{1,25},{9,1},{17,9},{25,17},{2,26},{10... | collective-permute-start | bytes 9224 | tf_op jit(solution)/shard_map/ppermute | solution.py:118
  25.2 8.0 %collective-permute-start.7 = (f32[4,4,3,3]{3,2,1,0:T(4,128)S(1)}, f32[4,4,3,3]{3,2,1,0:T(4,128)S(1)}, u32[]{:S(2)}, u32[]{:S(2)}) collective-permute-start(f32[4,4,3,3]{3,2,1,0:T(4,128)S(1)} %get-tuple-element.48), channel_id=1, source_target_pairs={{0,28},{8,4},{16,12},{24,20},{4,24},{12,0},{20,8},{28,16},{1,29},{... | collective-permute-start | bytes 1736 | tf_op jit(solution)/shard_map/ppermute | solution.py:131
  27.6 5.7 %collective-permute-start.6 = (f32[4,4,3,128]{3,2,1,0:T(4,128)S(1)}, f32[4,4,3,128]{3,2,1,0:T(4,128)S(1)}, u32[]{:S(2)}, u32[]{:S(2)}) collective-permute-start(f32[4,4,3,128]{3,2,1,0:T(4,128)S(1)} %fusion.25), channel_id=1, source_target_pairs={{0,4},{4,0},{1,5},{5,1},{2,6},{6,2},{3,7},{7,3},{8,12},{12,8},{9,1... | collective-permute-start | bytes 73736 | tf_op jit(solution)/shard_map/ppermute | solution.py:131
  33.7 3.5 %collective-permute-start.10 = (f32[4,3,22,134]{3,2,1,0:T(8,128)S(1)}, f32[4,3,22,134]{3,2,1,0:T(8,128)S(1)}, u32[]{:S(2)}, u32[]{:S(2)}) collective-permute-start(f32[4,3,22,134]{3,2,1,0:T(8,128)S(1)} %get-tuple-element.31), channel_id=1, source_target_pairs={{0,1},{1,2},{2,3},{4,5},{5,6},{6,7},{8,9},{9,10},{10,11},{12,13},{... | collective-permute-start | bytes 424520 | tf_op jit(solution)/shard_map/ppermute | solution.py:118
  35.9 5.4 %collective-permute-start.11 = (f32[4,3,22,134]{3,2,1,0:T(8,128)S(1)}, f32[4,3,22,134]{3,2,1,0:T(8,128)S(1)}, u32[]{:S(2)}, u32[]{:S(2)}) collective-permute-start(f32[4,3,22,134]{3,2,1,0:T(8,128)S(1)} %get-tuple-element.32), channel_id=1, source_target_pairs={{1,0},{2,1},{3,2},{5,4},{6,5},{7,6},{9,8},{10,9},{11,10},{13,12},{... | collective-permute-start | bytes 424520 | tf_op jit(solution)/shard_map/ppermute | solution.py:118
  43.6 0.9 %copy-start.5 = (f32[4,16,128]{2,1,0:T(8,128)S(1)}, f32[4,16,128]{2,1,0:T(8,128)}, u32[]{:S(2)}) copy-start(f32[4,16,128]{2,1,0:T(8,128)} %param.16) | copy-start | bytes 98308

commit v14 on v10

--- a/solution.py
+++ b/solution.py
@@ -202,11 +202,11 @@
     devices = math.prod(lax.axis_size(a) for a in ORDER)
     if devices <= 64:
         spans = lax.axis_size("span")
-        relative = jnp.arange(devices, dtype=jnp.int32) % spans - lax.axis_index("span") + 1
+        relative = jnp.arange(devices, dtype=jnp.int32) // (devices // spans) - lax.axis_index("span") + 1
         chunks = jnp.zeros((devices,) + own.shape, own.dtype)
         for index, block in enumerate((below, own, above)):
             chunks = jnp.where((relative == index)[:, None, None], block[None], chunks)
-        return jnp.sum(lax.all_to_all(chunks, ORDER, 0, 0, tiled=False), axis=0)
+        return jnp.sum(lax.all_to_all(chunks, ORDER[::-1], 0, 0, tiled=False), axis=0)
     if lax.axis_size("normal") != 2 or lax.axis_size("circ") > 4:
         own = lax.psum(own + shifted(above, {"span": 1}) + shifted(below, {"span": -1}), ("circ", "normal"))
         return own

time: 61.8 us -> 61.7 us (level)
  transfers between devices with their start and end apart: 12 -> 12, of which waited for: 2 -> 2; matrix products, arithmetic and copies ran while one was open for 5% -> 6% of each run, Pallas kernels for 0% -> 0%
where the time goes in v14:
time: 61.7 us; the launch traced here: 61.1 us
  starting transfers between devices  21 us (34%)
  blocking collectives  14.8 us (24%)
  waiting for transfers between devices  8.64 us (14%)
  local copies, waits for them, and re-layouts  7.84 us (13%)
  other arithmetic  7.03 us (11%)
  between operations  1.33 us (2%)
    all_to_all x1, blocking collectives, reduce_panels(): lax.all_to_all(chunks, ORDER[::-1], 0, 0, tiled=False)  14.8 us
    ppermute x8, starting transfers between devices, receive(): return lax.ppermute(take(array, rel, dims, width), axes, pairs)  14.2 us
    ppermute x4, starting transfers between devices, receive_pair(): got = lax.ppermute(sent, axes, pairs + back)  6.77 us
    unnamed x34, local copies, waits for them, and re-layouts  4.96 us
    ppermute x4, waiting for transfers between devices, receive_pair(): got = lax.ppermute(sent, axes, pairs + back)  4.61 us
    ppermute x8, waiting for transfers between devices, receive(): return lax.ppermute(take(array, rel, dims, width), axes, pairs)  4.03 us
    mul x3, other arithmetic, relax(): weighted = stiff_pad[None] * mesh_pad  2.17 us
    slice x9, local copies, waits for them, and re-layouts, edge(): return lax.slice_in_dim(array, start, start + width, axis=dim)  2.08 us
  transfers between devices with their start and end apart: 12, of which 2 were waited for; matrix products, arithmetic and copies ran while one was open for 6% of the time, Pallas kernels for 0%

profile of v14, /device:TPU:0, one launch (start us, length us, event | category | flops | bytes accessed | tf_op | source)
XLA Modules:
  0.0 61.1 jit_solution(3768686861025660367)
XLA Ops:
  0.6 1.0 %fusion.51 = (f32[5,4,1,128]{3,2,1,0:T(1,128)S(1)}, f32[5,4,1,128]{3,2,1,0:T(1,128)S(1)}) fusion(f32[5,4,16,128]{3,2,1,0:T(8,128)} %param.9), kind=kLoop, calls=%fused_computation.151 | loop fusion | bytes 40960 | tf_op jit(solution)/shard_map/slice | solution.py:88
  1.7 0.8 %fusion.55 = (f32[3,4,1,128]{3,2,1,0:T(1,128)S(1)}, f32[3,4,1,128]{3,2,1,0:T(1,128)S(1)}) fusion(f32[3,4,16,128]{3,2,1,0:T(8,128)} %param.11), kind=kLoop, calls=%fused_computation.155 | loop fusion | bytes 24576 | tf_op jit(solution)/shard_map/slice | solution.py:88
  2.6 3.0 %collective-permute-start.2 = (f32[8,4,1,128]{3,0,2,1:T(8,128)S(1)}, f32[8,4,1,128]{3,0,2,1:T(8,128)S(1)}, u32[]{:S(2)}, u32[]{:S(2)}) collective-permute-start(f32[8,4,1,128]{3,0,2,1:T(8,128)S(1)} %slice_select_fusion.1), channel_id=1, source_target_pairs={{0,4},{4,0},{1,5},{5,1},{2,6},{6,2},{3,7},{7,3},{8,12},{12,8},{9,1... | collective-permute-start | bytes 49160 | tf_op jit(solution)/shard_map/ppermute | solution.py:133
  5.7 1.5 %collective-permute-start.1 = (f32[8,1,16,128]{3,2,1,0:T(8,128)S(1)}, f32[8,1,16,128]{3,2,1,0:T(8,128)S(1)}, u32[]{:S(2)}, u32[]{:S(2)}) collective-permute-start(f32[8,1,16,128]{3,2,1,0:T(8,128)S(1)} %get-tuple-element.49), channel_id=1, source_target_pairs={{0,1},{1,2},{2,3},{4,5},{5,6},{6,7},{8,9},{9,10},{10,11},{12,13},{... | collective-permute-start | bytes 196616 | tf_op jit(solution)/shard_map/ppermute | solution.py:120
  7.1 1.3 %collective-permute-start = (f32[8,1,16,128]{3,2,1,0:T(8,128)S(1)}, f32[8,1,16,128]{3,2,1,0:T(8,128)S(1)}, u32[]{:S(2)}, u32[]{:S(2)}) collective-permute-start(f32[8,1,16,128]{3,2,1,0:T(8,128)S(1)} %get-tuple-element.50), channel_id=1, source_target_pairs={{1,0},{2,1},{3,2},{5,4},{6,5},{7,6},{9,8},{10,9},{11,10},{13,12},{... | collective-permute-start | bytes 196616 | tf_op jit(solution)/shard_map/ppermute | solution.py:120
  8.5 0.1 fusion.50
  8.6 0.1 copy.117
  8.8 0.1 copy.118
  9.0 0.2 copy.115
  9.2 0.3 copy.116
  9.5 1.6 %collective-permute-start.4 = (f32[8,4,16,1]{2,0,3,1:T(8,128)S(1)}, f32[8,4,16,1]{2,0,3,1:T(8,128)S(1)}, u32[]{:S(2)}, u32[]{:S(2)}) collective-permute-start(f32[8,4,16,1]{2,0,3,1:T(8,128)S(1)} %get-tuple-element.65), channel_id=1, source_target_pairs={{0,8},{8,16},{16,24},{24,0},{1,9},{9,17},{17,25},{25,1},{2,10},{10... | collective-permute-start | bytes 6152 | tf_op jit(solution)/shard_map/ppermute | solution.py:120
  11.1 2.2 %collective-permute-start.3 = (f32[8,4,16,1]{2,0,3,1:T(8,128)S(1)}, f32[8,4,16,1]{2,0,3,1:T(8,128)S(1)}, u32[]{:S(2)}, u32[]{:S(2)}) collective-permute-start(f32[8,4,16,1]{2,0,3,1:T(8,128)S(1)} %get-tuple-element.66), channel_id=1, source_target_pairs={{0,24},{8,0},{16,8},{24,16},{1,25},{9,1},{17,9},{25,17},{2,26},{10... | collective-permute-start | bytes 6152 | tf_op jit(solution)/shard_map/ppermute | solution.py:120
  13.4 0.7 %copy-done.6 = f32[3,5,5]{2,0,1:T(4,128)S(1)} copy-done((f32[3,5,5]{2,0,1:T(4,128)S(1)}, f32[3,5,5]{2,0,1:T(4,128)}, u32[]{:S(2)}) %copy-start.6) | copy-done | bytes 324
  14.1 0.7 %copy-done.7 = f32[3,5,5]{2,0,1:T(4,128)S(1)} copy-done((f32[3,5,5]{2,0,1:T(4,128)S(1)}, f32[3,5,5]{2,0,1:T(4,128)}, u32[]{:S(2)}) %copy-start.7) | copy-done | bytes 324
  14.9 0.1 subtract_multiply_fusion
  15.1 0.7 %copy-done.9 = s32[4,128]{1,0:T(4,128)S(1)} copy-done((s32[4,128]{1,0:T(4,128)S(1)}, s32[4,128]{1,0:T(4,128)}, u32[]{:S(2)}) %copy-start.9) | copy-done | bytes 2072
  15.8 0.5 multiply_reduce_fusion.2
  16.3 0.2 multiply_reduce_fusion
  16.5 0.1 multiply_reduce_fusion.4
  16.7 0.2 slice_reduce_fusion
  16.9 0.6 %copy-done.8 = f32[3,5]{1,0:T(4,128)S(1)} copy-done((f32[3,5]{1,0:T(4,128)S(1)}, f32[3,5]{1,0:T(4,128)}, u32[]{:S(2)}) %copy-start.8) | copy-done | bytes 84
  17.9 0.2 copy.100
  18.1 0.2 copy.98
  18.6 0.1 multiply_reduce_fusion.7
  18.8 0.7 %copy-done.4 = f32[5,4,16,128]{3,2,1,0:T(8,128)S(1)} copy-done((f32[5,4,16,128]{3,2,1,0:T(8,128)S(1)}, f32[5,4,16,128]{3,2,1,0:T(8,128)}, u32[]{:S(2)}) %copy-start.4) | copy-done | bytes 163864
  19.5 0.2 fusion.15
  19.8 0.7 %copy-done.2 = f32[4,16,128]{2,1,0:T(8,128)S(1)} copy-done((f32[4,16,128]{2,1,0:T(8,128)S(1)}, f32[4,16,128]{2,1,0:T(8,128)}, u32[]{:S(2)}) %copy-start.2) | copy-done | bytes 32792
  20.7 0.3 collective-permute-start.5
  21.1 1.6 %collective-permute-start.8 = (f32[4,4,16,3]{3,2,1,0:T(8,128)S(1)}, f32[4,4,16,3]{3,2,1,0:T(8,128)S(1)}, u32[]{:S(2)}, u32[]{:S(2)}) collective-permute-start(f32[4,4,16,3]{3,2,1,0:T(8,128)S(1)} %get-tuple-element.45), channel_id=1, source_target_pairs={{0,8},{8,16},{16,24},{24,0},{1,9},{9,17},{17,25},{25,1},{2,10},{10... | collective-permute-start | bytes 9224 | tf_op jit(solution)/shard_map/ppermute | solution.py:120
  22.7 2.5 %collective-permute-start.9 = (f32[4,4,16,3]{3,2,1,0:T(8,128)S(1)}, f32[4,4,16,3]{3,2,1,0:T(8,128)S(1)}, u32[]{:S(2)}, u32[]{:S(2)}) collective-permute-start(f32[4,4,16,3]{3,2,1,0:T(8,128)S(1)} %get-tuple-element.46), channel_id=1, source_target_pairs={{0,24},{8,0},{16,8},{24,16},{1,25},{9,1},{17,9},{25,17},{2,26},{10... | collective-permute-start | bytes 9224 | tf_op jit(solution)/shard_map/ppermute | solution.py:120
  25.2 2.4 %collective-permute-start.7 = (f32[4,4,3,3]{3,2,1,0:T(4,128)S(1)}, f32[4,4,3,3]{3,2,1,0:T(4,128)S(1)}, u32[]{:S(2)}, u32[]{:S(2)}) collective-permute-start(f32[4,4,3,3]{3,2,1,0:T(4,128)S(1)} %get-tuple-element.48), channel_id=1, source_target_pairs={{0,28},{8,4},{16,12},{24,20},{4,24},{12,0},{20,8},{28,16},{1,29},{... | collective-permute-start | bytes 1736 | tf_op jit(solution)/shard_map/ppermute | solution.py:133
  27.6 1.0 %collective-permute-start.6 = (f32[4,4,3,128]{3,2,1,0:T(4,128)S(1)}, f32[4,4,3,128]{3,2,1,0:T(4,128)S(1)}, u32[]{:S(2)}, u32[]{:S(2)}) collective-permute-start(f32[4,4,3,128]{3,2,1,0:T(4,128)S(1)} %fusion.29), channel_id=1, source_target_pairs={{0,4},{4,0},{1,5},{5,1},{2,6},{6,2},{3,7},{7,3},{8,12},{12,8},{9,1... | collective-permute-start | bytes 73736 | tf_op jit(solution)/shard_map/ppermute | solution.py:133
  28.7 4.6 %collective-permute-done.7 = f32[4,4,3,3]{3,2,1,0:T(4,128)S(1)} collective-permute-done((f32[4,4,3,3]{3,2,1,0:T(4,128)S(1)}, f32[4,4,3,3]{3,2,1,0:T(4,128)S(1)}, u32[]{:S(2)}, u32[]{:S(2)}) %collective-permute-start.7) | collective-permute-done | bytes 608 | tf_op jit(solution)/shard_map/ppermute | solution.py:133
  33.3 0.3 maximum_maximum_fusion
  33.7 2.2 %collective-permute-start.10 = (f32[4,3,22,134]{3,2,1,0:T(8,128)S(1)}, f32[4,3,22,134]{3,2,1,0:T(8,128)S(1)}, u32[]{:S(2)}, u32[]{:S(2)}) collective-permute-start(f32[4,3,22,134]{3,2,1,0:T(8,128)S(1)} %get-tuple-element.31), channel_id=1, source_target_pairs={{0,1},{1,2},{2,3},{4,5},{5,6},{6,7},{8,9},{9,10},{10,11},{12,13},{... | collective-permute-start | bytes 424520 | tf_op jit(solution)/shard_map/ppermute | solution.py:120
  35.9 1.3 %collective-permute-start.11 = (f32[4,3,22,134]{3,2,1,0:T(8,128)S(1)}, f32[4,3,22,134]{3,2,1,0:T(8,128)S(1)}, u32[]{:S(2)}, u32[]{:S(2)}) collective-permute-start(f32[4,3,22,134]{3,2,1,0:T(8,128)S(1)} %get-tuple-element.32), channel_id=1, source_target_pairs={{1,0},{2,1},{3,2},{5,4},{6,5},{7,6},{9,8},{10,9},{11,10},{13,12},{... | collective-permute-start | bytes 424520 | tf_op jit(solution)/shard_map/ppermute | solution.py:120
  37.2 4.0 %collective-permute-done.11 = f32[4,3,22,134]{3,2,1,0:T(8,128)S(1)} collective-permute-done((f32[4,3,22,134]{3,2,1,0:T(8,128)S(1)}, f32[4,3,22,134]{3,2,1,0:T(8,128)S(1)}, u32[]{:S(2)}, u32[]{:S(2)}) %collective-permute-start.11) | collective-permute-done | bytes 141536 | tf_op jit(solution)/shard_map/ppermute | solution.py:120
  41.2 0.3 pad_maximum_fusion
  41.6 0.1 multiply_add_fusion
  41.7 0.1 multiply_add_fusion.1
  41.9 0.1 broadcast_multiply_fusion
  42.1 1.2 %broadcast_multiply_fusion.1 = (f32[3,8,20,132]{3,2,1,0:T(8,128)S(1)}, f32[3,8,20,132]{3,2,1,0:T(8,128)S(1)}) fusion(f32[8,20,132]{2,1,0:T(8,128)S(1)} %get-tuple-element.36, f32[3,10,22,134]{3,2,1,0:T(8,128)S(1)} %get-tuple-element.27, f32[8,20,132]{2,1,0:T(8,128)S(1)} %get-tuple-element.35, f32[4,10,22,134]{3,2,1,0:T(8,128)S(1)} %pad_maximum_fusion, ...), kind=kLoop, calls=%fused_computation.42 | loop fusion | flops 760320 | bytes 2703360 | tf_op jit(solution)/shard_map/mul | solution.py:60
  43.3 0.9 %broadcast_multiply_fusion.2 = (f32[3,6,18,130]{3,2,1,0:T(8,128)S(1)}, f32[3,6,18,130]{3,2,1,0:T(8,128)S(1)}) fusion(f32[6,18,130]{2,1,0:T(8,128)S(1)} %get-tuple-element.34, f32[3,8,20,132]{3,2,1,0:T(8,128)S(1)} %get-tuple-element.25, f32[6,18,130]{2,1,0:T(8,128)S(1)} %get-tuple-element.33, f32[4,10,22,134]{3,2,1,0:T(8,128)S(1)} %pad_maximum_fusion, ...), kind=kLoop, calls=%fused_computation.45 | loop fusion | flops 505440 | bytes 1797120 | tf_op jit(solution)/shard_map/mul | solution.py:60
  44.2 0.9 %multiply_reduce_fusion.9 = (f32[3,4,128]{2,1,0:T(4,128)S(1)}, f32[3,4,16,128]{3,2,1,0:T(8,128)}) fusion(f32[4,16,128]{2,1,0:T(8,128)S(1)} %copy-done.5, f32[3,6,18,130]{3,2,1,0:T(8,128)S(1)} %get-tuple-element.23, f32[3,4,16,128]{3,2,1,0:T(8,128)S(1)} %multiply_reduce_fusion.6, f32[4,16,128]{2,1,0:T(8,128)S(1)} %fusion.34, ...), kind=kLoop, calls=%fused_computation.79 | loop fusion | flops 317952 | bytes 956416 | tf_op jit(solution)/shard_map/reduce_sum | solution.py:246
  45.0 0.4 convolution_bitcast_fusion
  45.5 0.2 select_select_fusion
  45.7 14.8 %all_to_all.5 = f32[32,3,128]{2,1,0:T(4,128)S(1)} all-to-all(f32[32,3,128]{2,1,0:T(4,128)S(1)} %select_select_fusion), channel_id=1, replica_groups=mesh['circ'=4,'normal'=2,'span'=4] {'span','normal','circ'}, dimensions={0} | all-to-all | bytes 98304 | tf_op jit(solution)/shard_map/all_to_all | solution.py:209
  60.5 0.6 %reduce_sum.167 = f32[3,128]{1,0:T(4,128)} reduce(f32[32,3,128]{2,1,0:T(4,128)S(1)} %all_to_all.5, f32[]{:T(128)} %constant.18.clone.1), dimensions={0}, to_apply=%region_14.15 | reduce | flops 11904 | bytes 50692 | tf_op jit(solution)/shard_map/reduce_sum | solution.py:209
  (87 shorter events, 1.6 us)
Async XLA Ops:
  0.6 5.0 %copy-start = (f32[5,4,16,128]{3,2,1,0:T(8,128)S(1)}, f32[5,4,16,128]{3,2,1,0:T(8,128)}, u32[]{:S(2)}) copy-start(f32[5,4,16,128]{3,2,1,0:T(8,128)} %param.9) | copy-start | bytes 491524
  2.5 3.1 %copy-start.1 = (f32[3,4,16,128]{3,2,1,0:T(8,128)S(1)}, f32[3,4,16,128]{3,2,1,0:T(8,128)}, u32[]{:S(2)}) copy-start(f32[3,4,16,128]{3,2,1,0:T(8,128)} %param.11) | copy-start | bytes 294916
  2.6 15.7 %collective-permute-start.2 = (f32[8,4,1,128]{3,0,2,1:T(8,128)S(1)}, f32[8,4,1,128]{3,0,2,1:T(8,128)S(1)}, u32[]{:S(2)}, u32[]{:S(2)}) collective-permute-start(f32[8,4,1,128]{3,0,2,1:T(8,128)S(1)} %slice_select_fusion.1), channel_id=1, source_target_pairs={{0,4},{4,0},{1,5},{5,1},{2,6},{6,2},{3,7},{7,3},{8,12},{12,8},{9,1... | collective-permute-start | bytes 49160 | tf_op jit(solution)/shard_map/ppermute | solution.py:133
  5.7 12.9 %collective-permute-start.1 = (f32[8,1,16,128]{3,2,1,0:T(8,128)S(1)}, f32[8,1,16,128]{3,2,1,0:T(8,128)S(1)}, u32[]{:S(2)}, u32[]{:S(2)}) collective-permute-start(f32[8,1,16,128]{3,2,1,0:T(8,128)S(1)} %get-tuple-element.49), channel_id=1, source_target_pairs={{0,1},{1,2},{2,3},{4,5},{5,6},{6,7},{8,9},{9,10},{10,11},{12,13},{... | collective-permute-start | bytes 196616 | tf_op jit(solution)/shard_map/ppermute | solution.py:120
  7.1 11.5 %collective-permute-start = (f32[8,1,16,128]{3,2,1,0:T(8,128)S(1)}, f32[8,1,16,128]{3,2,1,0:T(8,128)S(1)}, u32[]{:S(2)}, u32[]{:S(2)}) collective-permute-start(f32[8,1,16,128]{3,2,1,0:T(8,128)S(1)} %get-tuple-element.50), channel_id=1, source_target_pairs={{1,0},{2,1},{3,2},{5,4},{6,5},{7,6},{9,8},{10,9},{11,10},{13,12},{... | collective-permute-start | bytes 196616 | tf_op jit(solution)/shard_map/ppermute | solution.py:120
  9.5 8.1 %collective-permute-start.4 = (f32[8,4,16,1]{2,0,3,1:T(8,128)S(1)}, f32[8,4,16,1]{2,0,3,1:T(8,128)S(1)}, u32[]{:S(2)}, u32[]{:S(2)}) collective-permute-start(f32[8,4,16,1]{2,0,3,1:T(8,128)S(1)} %get-tuple-element.65), channel_id=1, source_target_pairs={{0,8},{8,16},{16,24},{24,0},{1,9},{9,17},{17,25},{25,1},{2,10},{10... | collective-permute-start | bytes 6152 | tf_op jit(solution)/shard_map/ppermute | solution.py:120
  11.1 6.6 %collective-permute-start.3 = (f32[8,4,16,1]{2,0,3,1:T(8,128)S(1)}, f32[8,4,16,1]{2,0,3,1:T(8,128)S(1)}, u32[]{:S(2)}, u32[]{:S(2)}) collective-permute-start(f32[8,4,16,1]{2,0,3,1:T(8,128)S(1)} %get-tuple-element.66), channel_id=1, source_target_pairs={{0,24},{8,0},{16,8},{24,16},{1,25},{9,1},{17,9},{25,17},{2,26},{10... | collective-permute-start | bytes 6152 | tf_op jit(solution)/shard_map/ppermute | solution.py:120
  13.4 0.7 %copy-start.6 = (f32[3,5,5]{2,0,1:T(4,128)S(1)}, f32[3,5,5]{2,0,1:T(4,128)}, u32[]{:S(2)}) copy-start(f32[3,5,5]{2,0,1:T(4,128)} %param.12) | copy-start | bytes 904
  14.1 0.7 %copy-start.7 = (f32[3,5,5]{2,0,1:T(4,128)S(1)}, f32[3,5,5]{2,0,1:T(4,128)}, u32[]{:S(2)}) copy-start(f32[3,5,5]{2,0,1:T(4,128)} %param.13) | copy-start | bytes 904
  15.1 0.7 %copy-start.9 = (s32[4,128]{1,0:T(4,128)S(1)}, s32[4,128]{1,0:T(4,128)}, u32[]{:S(2)}) copy-start(s32[4,128]{1,0:T(4,128)} %param.17) | copy-start | bytes 6148
  16.9 0.7 %copy-start.8 = (f32[3,5]{1,0:T(4,128)S(1)}, f32[3,5]{1,0:T(4,128)}, u32[]{:S(2)}) copy-start(f32[3,5]{1,0:T(4,128)} %param.14) | copy-start | bytes 184
  18.6 0.9 %copy-start.4 = (f32[5,4,16,128]{3,2,1,0:T(8,128)S(1)}, f32[5,4,16,128]{3,2,1,0:T(8,128)}, u32[]{:S(2)}) copy-start(f32[5,4,16,128]{3,2,1,0:T(8,128)} %param.10) | copy-start | bytes 491524
  19.7 0.9 %copy-start.3 = (f32[5,4,16,128]{3,2,1,0:T(8,128)}, f32[5,4,16,128]{3,2,1,0:T(8,128)S(1)}, u32[]{:S(2)}) copy-start(f32[5,4,16,128]{3,2,1,0:T(8,128)S(1)} %fusion.15) | copy-start | bytes 491524
  19.7 0.8 %copy-start.2 = (f32[4,16,128]{2,1,0:T(8,128)S(1)}, f32[4,16,128]{2,1,0:T(8,128)}, u32[]{:S(2)}) copy-start(f32[4,16,128]{2,1,0:T(8,128)} %param.15) | copy-start | bytes 98308
  20.7 7.9 %collective-permute-start.5 = (f32[4,4,3,3]{3,2,1,0:T(4,128)S(1)}, f32[4,4,3,3]{3,2,1,0:T(4,128)S(1)}, u32[]{:S(2)}, u32[]{:S(2)}) collective-permute-start(f32[4,4,3,3]{3,2,1,0:T(4,128)S(1)} %get-tuple-element.47), channel_id=1, source_target_pairs={{0,12},{8,20},{16,28},{24,4},{4,8},{12,16},{20,24},{28,0},{1,13},{... | collective-permute-start | bytes 1736 | tf_op jit(solution)/shard_map/ppermute | solution.py:133
  21.1 12.3 %collective-permute-start.8 = (f32[4,4,16,3]{3,2,1,0:T(8,128)S(1)}, f32[4,4,16,3]{3,2,1,0:T(8,128)S(1)}, u32[]{:S(2)}, u32[]{:S(2)}) collective-permute-start(f32[4,4,16,3]{3,2,1,0:T(8,128)S(1)} %get-tuple-element.45), channel_id=1, source_target_pairs={{0,8},{8,16},{16,24},{24,0},{1,9},{9,17},{17,25},{25,1},{2,10},{10... | collective-permute-start | bytes 9224 | tf_op jit(solution)/shard_map/ppermute | solution.py:120
  22.7 10.6 %collective-permute-start.9 = (f32[4,4,16,3]{3,2,1,0:T(8,128)S(1)}, f32[4,4,16,3]{3,2,1,0:T(8,128)S(1)}, u32[]{:S(2)}, u32[]{:S(2)}) collective-permute-start(f32[4,4,16,3]{3,2,1,0:T(8,128)S(1)} %get-tuple-element.46), channel_id=1, source_target_pairs={{0,24},{8,0},{16,8},{24,16},{1,25},{9,1},{17,9},{25,17},{2,26},{10... | collective-permute-start | bytes 9224 | tf_op jit(solution)/shard_map/ppermute | solution.py:120
  25.2 8.0 %collective-permute-start.7 = (f32[4,4,3,3]{3,2,1,0:T(4,128)S(1)}, f32[4,4,3,3]{3,2,1,0:T(4,128)S(1)}, u32[]{:S(2)}, u32[]{:S(2)}) collective-permute-start(f32[4,4,3,3]{3,2,1,0:T(4,128)S(1)} %get-tuple-element.48), channel_id=1, source_target_pairs={{0,28},{8,4},{16,12},{24,20},{4,24},{12,0},{20,8},{28,16},{1,29},{... | collective-permute-start | bytes 1736 | tf_op jit(solution)/shard_map/ppermute | solution.py:133
  27.6 5.7 %collective-permute-start.6 = (f32[4,4,3,128]{3,2,1,0:T(4,128)S(1)}, f32[4,4,3,128]{3,2,1,0:T(4,128)S(1)}, u32[]{:S(2)}, u32[]{:S(2)}) collective-permute-start(f32[4,4,3,128]{3,2,1,0:T(4,128)S(1)} %fusion.29), channel_id=1, source_target_pairs={{0,4},{4,0},{1,5},{5,1},{2,6},{6,2},{3,7},{7,3},{8,12},{12,8},{9,1... | collective-permute-start | bytes 73736 | tf_op jit(solution)/shard_map/ppermute | solution.py:133
  33.7 3.5 %collective-permute-start.10 = (f32[4,3,22,134]{3,2,1,0:T(8,128)S(1)}, f32[4,3,22,134]{3,2,1,0:T(8,128)S(1)}, u32[]{:S(2)}, u32[]{:S(2)}) collective-permute-start(f32[4,3,22,134]{3,2,1,0:T(8,128)S(1)} %get-tuple-element.31), channel_id=1, source_target_pairs={{0,1},{1,2},{2,3},{4,5},{5,6},{6,7},{8,9},{9,10},{10,11},{12,13},{... | collective-permute-start | bytes 424520 | tf_op jit(solution)/shard_map/ppermute | solution.py:120
  35.9 5.4 %collective-permute-start.11 = (f32[4,3,22,134]{3,2,1,0:T(8,128)S(1)}, f32[4,3,22,134]{3,2,1,0:T(8,128)S(1)}, u32[]{:S(2)}, u32[]{:S(2)}) collective-permute-start(f32[4,3,22,134]{3,2,1,0:T(8,128)S(1)} %get-tuple-element.32), channel_id=1, source_target_pairs={{1,0},{2,1},{3,2},{5,4},{6,5},{7,6},{9,8},{10,9},{11,10},{13,12},{... | collective-permute-start | bytes 424520 | tf_op jit(solution)/shard_map/ppermute | solution.py:120
  43.2 0.9 %copy-start.5 = (f32[4,16,128]{2,1,0:T(8,128)S(1)}, f32[4,16,128]{2,1,0:T(8,128)}, u32[]{:S(2)}) copy-start(f32[4,16,128]{2,1,0:T(8,128)} %param.16) | copy-start | bytes 98308

commit v15 on v14

--- a/solution.py
+++ b/solution.py
@@ -135,7 +135,22 @@
     return jnp.where(me == 1, got, zero), jnp.where(me == 0, got, zero)
 
 
+def tile_halos(fields, axis, dim, length):
+    rows = 8
+    me = lax.axis_index(axis)
+    start = (1 - me) * (length - rows)
+    sent = jnp.concatenate([lax.dynamic_slice_in_dim(f, start, rows, axis=dim) for f in fields], axis=0)
+    got = lax.ppermute(sent, axis, [(0, 1), (1, 0)])
+    low = lax.slice_in_dim(got, rows - 1, rows, axis=dim)
+    high = lax.slice_in_dim(got, 0, 1, axis=dim)
+    zero = jnp.zeros_like(low)
+    return jnp.where(me == 1, low, zero), jnp.where(me == 0, high, zero)
+
+
 def face_halos(fields, axis, dim, wrap):
+    length = fields[0].shape[dim]
+    if axis == "normal" and lax.axis_size(axis) == 2 and length >= 8:
+        return tile_halos(fields, axis, dim, length)
     thin = jnp.concatenate(
         [jnp.concatenate([edge(f, dim, 1, 1), edge(f, dim, -1, 1)], axis=dim) for f in fields], axis=0
     )

time: 61.7 us -> 60.4 us (0.979)
  local copies, waits for them, and re-layouts: 7.84 us -> 6.67 us
    ppermute x0 -> x1, starting transfers between devices: none -> 3.03 us  [tile_halos(): got = lax.ppermute(sent, axis, [(0, 1), (1, 0)])]
    ppermute x4 -> x3, starting transfers between devices: 6.77 us -> 3.76 us  [receive_pair(): got = lax.ppermute(sent, axes, pairs + back)]
    slice x9 -> x7, local copies, waits for them, and re-layouts: 2.08 us -> 0.26 us  [edge(): return lax.slice_in_dim(array, start, start + width, axis=dim)]
    dynamic_slice x0 -> x2, local copies, waits for them, and re-layouts: none -> 0.94 us  [tile_halos(): lax.dynamic_slice_in_dim(f, start, rows, axis=dim)]
    unnamed x34 -> x28, local copies, waits for them, and re-layouts: 4.96 us -> 4.68 us
    ppermute x4 -> x3, waiting for transfers between devices: 4.61 us -> 4.59 us  [receive_pair(): got = lax.ppermute(sent, axes, pairs + back)]
  transfers between devices with their start and end apart: 12 -> 12, of which waited for: 2 -> 2; matrix products, arithmetic and copies ran while one was open for 6% -> 5% of each run, Pallas kernels for 0% -> 0%
where the time goes in v15:
time: 60.4 us; the launch traced here: 59.9 us
  starting transfers between devices  21 us (35%)
  blocking collectives  14.8 us (25%)
  waiting for transfers between devices  8.62 us (14%)
  other arithmetic  7.07 us (12%)
  local copies, waits for them, and re-layouts  6.67 us (11%)
  between operations  1.26 us (2%)
    all_to_all x1, blocking collectives, reduce_panels(): lax.all_to_all(chunks, ORDER[::-1], 0, 0, tiled=False)  14.8 us
    ppermute x8, starting transfers between devices, receive(): return lax.ppermute(take(array, rel, dims, width), axes, pairs)  14.2 us
    unnamed x28, local copies, waits for them, and re-layouts  4.68 us
    ppermute x3, waiting for transfers between devices, receive_pair(): got = lax.ppermute(sent, axes, pairs + back)  4.59 us
    ppermute x8, waiting for transfers between devices, receive(): return lax.ppermute(take(array, rel, dims, width), axes, pairs)  4.03 us
    ppermute x3, starting transfers between devices, receive_pair(): got = lax.ppermute(sent, axes, pairs + back)  3.76 us
    ppermute x1, starting transfers between devices, tile_halos(): got = lax.ppermute(sent, axis, [(0, 1), (1, 0)])  3.03 us
    mul x3, other arithmetic, relax(): weighted = stiff_pad[None] * mesh_pad  2.17 us
  transfers between devices with their start and end apart: 12, of which 2 were waited for; matrix products, arithmetic and copies ran while one was open for 5% of the time, Pallas kernels for 0%

profile of v15, /device:TPU:0, one launch (start us, length us, event | category | flops | bytes accessed | tf_op | source)
XLA Modules:
  0.0 59.9 jit_solution(11819947655271324454)
XLA Ops:
  0.6 0.9 %constant_dynamic-slice_fusion.1 = f32[5,4,8,128]{3,2,1,0:T(8,128)S(1)} fusion(f32[5,4,16,128]{3,2,1,0:T(8,128)} %param.9, s32[]{:T(128)S(6)} %select_n.92), kind=kLoop, calls=%fused_computation.144 | loop fusion | bytes 163844 | tf_op jit(solution)/shard_map/dynamic_slice | solution.py:142
  1.6 3.0 %collective-permute-start.2 = (f32[8,4,8,128]{3,2,1,0:T(8,128)S(1)}, f32[8,4,8,128]{3,2,1,0:T(8,128)S(1)}, u32[]{:S(2)}, u32[]{:S(2)}) collective-permute-start(f32[8,4,8,128]{3,2,1,0:T(8,128)S(1)} %pad_maximum_fusion.2), channel_id=1, source_target_pairs={{0,4},{4,0},{1,5},{5,1},{2,6},{6,2},{3,7},{7,3},{8,12},{12,8},{9,1... | collective-permute-start | bytes 393224 | tf_op jit(solution)/shard_map/ppermute | solution.py:143
  4.7 1.5 %collective-permute-start.1 = (f32[8,1,16,128]{3,2,1,0:T(8,128)S(1)}, f32[8,1,16,128]{3,2,1,0:T(8,128)S(1)}, u32[]{:S(2)}, u32[]{:S(2)}) collective-permute-start(f32[8,1,16,128]{3,2,1,0:T(8,128)S(1)} %get-tuple-element.51), channel_id=1, source_target_pairs={{0,1},{1,2},{2,3},{4,5},{5,6},{6,7},{8,9},{9,10},{10,11},{12,13},{... | collective-permute-start | bytes 196616 | tf_op jit(solution)/shard_map/ppermute | solution.py:120
  6.2 1.3 %collective-permute-start = (f32[8,1,16,128]{3,2,1,0:T(8,128)S(1)}, f32[8,1,16,128]{3,2,1,0:T(8,128)S(1)}, u32[]{:S(2)}, u32[]{:S(2)}) collective-permute-start(f32[8,1,16,128]{3,2,1,0:T(8,128)S(1)} %get-tuple-element.52), channel_id=1, source_target_pairs={{1,0},{2,1},{3,2},{5,4},{6,5},{7,6},{9,8},{10,9},{11,10},{13,12},{... | collective-permute-start | bytes 196616 | tf_op jit(solution)/shard_map/ppermute | solution.py:120
  7.6 0.1 fusion.48
  7.7 0.1 copy.95
  7.8 0.1 copy.96
  8.0 0.2 copy.93
  8.3 0.3 copy.94
  8.6 1.6 %collective-permute-start.4 = (f32[8,4,16,1]{2,0,3,1:T(8,128)S(1)}, f32[8,4,16,1]{2,0,3,1:T(8,128)S(1)}, u32[]{:S(2)}, u32[]{:S(2)}) collective-permute-start(f32[8,4,16,1]{2,0,3,1:T(8,128)S(1)} %get-tuple-element.65), channel_id=1, source_target_pairs={{0,8},{8,16},{16,24},{24,0},{1,9},{9,17},{17,25},{25,1},{2,10},{10... | collective-permute-start | bytes 6152 | tf_op jit(solution)/shard_map/ppermute | solution.py:120
  10.2 2.2 %collective-permute-start.3 = (f32[8,4,16,1]{2,0,3,1:T(8,128)S(1)}, f32[8,4,16,1]{2,0,3,1:T(8,128)S(1)}, u32[]{:S(2)}, u32[]{:S(2)}) collective-permute-start(f32[8,4,16,1]{2,0,3,1:T(8,128)S(1)} %get-tuple-element.66), channel_id=1, source_target_pairs={{0,24},{8,0},{16,8},{24,16},{1,25},{9,1},{17,9},{25,17},{2,26},{10... | collective-permute-start | bytes 6152 | tf_op jit(solution)/shard_map/ppermute | solution.py:120
  12.5 0.7 %copy-done.6 = f32[3,5,5]{2,0,1:T(4,128)S(1)} copy-done((f32[3,5,5]{2,0,1:T(4,128)S(1)}, f32[3,5,5]{2,0,1:T(4,128)}, u32[]{:S(2)}) %copy-start.6) | copy-done | bytes 324
  13.2 0.7 %copy-done.7 = f32[3,5,5]{2,0,1:T(4,128)S(1)} copy-done((f32[3,5,5]{2,0,1:T(4,128)S(1)}, f32[3,5,5]{2,0,1:T(4,128)}, u32[]{:S(2)}) %copy-start.7) | copy-done | bytes 324
  14.0 0.1 subtract_multiply_fusion
  14.2 0.7 %copy-done.9 = s32[4,128]{1,0:T(4,128)S(1)} copy-done((s32[4,128]{1,0:T(4,128)S(1)}, s32[4,128]{1,0:T(4,128)}, u32[]{:S(2)}) %copy-start.9) | copy-done | bytes 2072
  14.9 0.5 multiply_reduce_fusion.2
  15.3 0.2 multiply_reduce_fusion
  15.6 0.1 multiply_reduce_fusion.4
  15.7 0.2 slice_reduce_fusion
  16.0 0.6 %copy-done.8 = f32[3,5]{1,0:T(4,128)S(1)} copy-done((f32[3,5]{1,0:T(4,128)S(1)}, f32[3,5]{1,0:T(4,128)}, u32[]{:S(2)}) %copy-start.8) | copy-done | bytes 84
  16.8 0.2 copy.82
  17.2 0.2 copy.80
  17.4 0.1 multiply_reduce_fusion.7
  17.8 0.5 copy-done.4
  18.3 0.2 fusion.15
  18.6 0.7 %copy-done.2 = f32[4,16,128]{2,1,0:T(8,128)S(1)} copy-done((f32[4,16,128]{2,1,0:T(8,128)S(1)}, f32[4,16,128]{2,1,0:T(8,128)}, u32[]{:S(2)}) %copy-start.2) | copy-done | bytes 32792
  19.4 0.1 fusion.26
  19.5 0.3 collective-permute-start.5
  19.9 1.6 %collective-permute-start.8 = (f32[4,4,16,3]{3,2,1,0:T(8,128)S(1)}, f32[4,4,16,3]{3,2,1,0:T(8,128)S(1)}, u32[]{:S(2)}, u32[]{:S(2)}) collective-permute-start(f32[4,4,16,3]{3,2,1,0:T(8,128)S(1)} %get-tuple-element.45), channel_id=1, source_target_pairs={{0,8},{8,16},{16,24},{24,0},{1,9},{9,17},{17,25},{25,1},{2,10},{10... | collective-permute-start | bytes 9224 | tf_op jit(solution)/shard_map/ppermute | solution.py:120
  21.5 2.5 %collective-permute-start.9 = (f32[4,4,16,3]{3,2,1,0:T(8,128)S(1)}, f32[4,4,16,3]{3,2,1,0:T(8,128)S(1)}, u32[]{:S(2)}, u32[]{:S(2)}) collective-permute-start(f32[4,4,16,3]{3,2,1,0:T(8,128)S(1)} %get-tuple-element.46), channel_id=1, source_target_pairs={{0,24},{8,0},{16,8},{24,16},{1,25},{9,1},{17,9},{25,17},{2,26},{10... | collective-permute-start | bytes 9224 | tf_op jit(solution)/shard_map/ppermute | solution.py:120
  24.0 2.4 %collective-permute-start.7 = (f32[4,4,3,3]{3,2,1,0:T(4,128)S(1)}, f32[4,4,3,3]{3,2,1,0:T(4,128)S(1)}, u32[]{:S(2)}, u32[]{:S(2)}) collective-permute-start(f32[4,4,3,3]{3,2,1,0:T(4,128)S(1)} %get-tuple-element.48), channel_id=1, source_target_pairs={{0,28},{8,4},{16,12},{24,20},{4,24},{12,0},{20,8},{28,16},{1,29},{... | collective-permute-start | bytes 1736 | tf_op jit(solution)/shard_map/ppermute | solution.py:133
  26.4 1.1 %collective-permute-start.6 = (f32[4,4,3,128]{3,2,1,0:T(4,128)S(1)}, f32[4,4,3,128]{3,2,1,0:T(4,128)S(1)}, u32[]{:S(2)}, u32[]{:S(2)}) collective-permute-start(f32[4,4,3,128]{3,2,1,0:T(4,128)S(1)} %fusion.29), channel_id=1, source_target_pairs={{0,4},{4,0},{1,5},{5,1},{2,6},{6,2},{3,7},{7,3},{8,12},{12,8},{9,1... | collective-permute-start | bytes 73736 | tf_op jit(solution)/shard_map/ppermute | solution.py:133
  27.5 4.6 %collective-permute-done.7 = f32[4,4,3,3]{3,2,1,0:T(4,128)S(1)} collective-permute-done((f32[4,4,3,3]{3,2,1,0:T(4,128)S(1)}, f32[4,4,3,3]{3,2,1,0:T(4,128)S(1)}, u32[]{:S(2)}, u32[]{:S(2)}) %collective-permute-start.7) | collective-permute-done | bytes 608 | tf_op jit(solution)/shard_map/ppermute | solution.py:133
  32.1 0.3 maximum_maximum_fusion
  32.5 2.2 %collective-permute-start.10 = (f32[4,3,22,134]{3,2,1,0:T(8,128)S(1)}, f32[4,3,22,134]{3,2,1,0:T(8,128)S(1)}, u32[]{:S(2)}, u32[]{:S(2)}) collective-permute-start(f32[4,3,22,134]{3,2,1,0:T(8,128)S(1)} %get-tuple-element.31), channel_id=1, source_target_pairs={{0,1},{1,2},{2,3},{4,5},{5,6},{6,7},{8,9},{9,10},{10,11},{12,13},{... | collective-permute-start | bytes 424520 | tf_op jit(solution)/shard_map/ppermute | solution.py:120
  34.7 1.3 %collective-permute-start.11 = (f32[4,3,22,134]{3,2,1,0:T(8,128)S(1)}, f32[4,3,22,134]{3,2,1,0:T(8,128)S(1)}, u32[]{:S(2)}, u32[]{:S(2)}) collective-permute-start(f32[4,3,22,134]{3,2,1,0:T(8,128)S(1)} %get-tuple-element.32), channel_id=1, source_target_pairs={{1,0},{2,1},{3,2},{5,4},{6,5},{7,6},{9,8},{10,9},{11,10},{13,12},{... | collective-permute-start | bytes 424520 | tf_op jit(solution)/shard_map/ppermute | solution.py:120
  36.0 4.0 %collective-permute-done.11 = f32[4,3,22,134]{3,2,1,0:T(8,128)S(1)} collective-permute-done((f32[4,3,22,134]{3,2,1,0:T(8,128)S(1)}, f32[4,3,22,134]{3,2,1,0:T(8,128)S(1)}, u32[]{:S(2)}, u32[]{:S(2)}) %collective-permute-start.11) | collective-permute-done | bytes 141536 | tf_op jit(solution)/shard_map/ppermute | solution.py:120
  40.0 0.3 pad_maximum_fusion
  40.4 0.1 multiply_add_fusion
  40.5 0.1 multiply_add_fusion.1
  40.7 0.1 broadcast_multiply_fusion
  40.9 1.2 %broadcast_multiply_fusion.1 = (f32[3,8,20,132]{3,2,1,0:T(8,128)S(1)}, f32[3,8,20,132]{3,2,1,0:T(8,128)S(1)}) fusion(f32[8,20,132]{2,1,0:T(8,128)S(1)} %get-tuple-element.36, f32[3,10,22,134]{3,2,1,0:T(8,128)S(1)} %get-tuple-element.27, f32[8,20,132]{2,1,0:T(8,128)S(1)} %get-tuple-element.35, f32[4,10,22,134]{3,2,1,0:T(8,128)S(1)} %pad_maximum_fusion, ...), kind=kLoop, calls=%fused_computation.42 | loop fusion | flops 760320 | bytes 2703360 | tf_op jit(solution)/shard_map/mul | solution.py:60
  42.1 0.9 %broadcast_multiply_fusion.2 = (f32[3,6,18,130]{3,2,1,0:T(8,128)S(1)}, f32[3,6,18,130]{3,2,1,0:T(8,128)S(1)}) fusion(f32[6,18,130]{2,1,0:T(8,128)S(1)} %get-tuple-element.34, f32[3,8,20,132]{3,2,1,0:T(8,128)S(1)} %get-tuple-element.25, f32[6,18,130]{2,1,0:T(8,128)S(1)} %get-tuple-element.33, f32[4,10,22,134]{3,2,1,0:T(8,128)S(1)} %pad_maximum_fusion, ...), kind=kLoop, calls=%fused_computation.45 | loop fusion | flops 505440 | bytes 1797120 | tf_op jit(solution)/shard_map/mul | solution.py:60
  43.0 0.9 %multiply_reduce_fusion.9 = (f32[3,4,128]{2,1,0:T(4,128)S(1)}, f32[3,4,16,128]{3,2,1,0:T(8,128)}) fusion(f32[4,16,128]{2,1,0:T(8,128)S(1)} %copy-done.5, f32[3,6,18,130]{3,2,1,0:T(8,128)S(1)} %get-tuple-element.23, f32[3,4,16,128]{3,2,1,0:T(8,128)S(1)} %multiply_reduce_fusion.6, f32[4,16,128]{2,1,0:T(8,128)S(1)} %fusion.34, ...), kind=kLoop, calls=%fused_computation.80 | loop fusion | flops 317952 | bytes 956416 | tf_op jit(solution)/shard_map/reduce_sum | solution.py:261
  43.8 0.4 convolution_bitcast_fusion
  44.3 0.2 select_select_fusion
  44.4 14.8 %all_to_all.5 = f32[32,3,128]{2,1,0:T(4,128)S(1)} all-to-all(f32[32,3,128]{2,1,0:T(4,128)S(1)} %select_select_fusion), channel_id=1, replica_groups=mesh['circ'=4,'normal'=2,'span'=4] {'span','normal','circ'}, dimensions={0} | all-to-all | bytes 98304 | tf_op jit(solution)/shard_map/all_to_all | solution.py:224
  59.3 0.6 %reduce_sum.167 = f32[3,128]{1,0:T(4,128)} reduce(f32[32,3,128]{2,1,0:T(4,128)S(1)} %all_to_all.5, f32[]{:T(128)} %constant.18.clone.1), dimensions={0}, to_apply=%region_14.15 | reduce | flops 11904 | bytes 50692 | tf_op jit(solution)/shard_map/reduce_sum | solution.py:224
  (79 shorter events, 1.5 us)
Async XLA Ops:
  0.6 0.9 %copy-start.1 = (f32[3,4,16,128]{3,2,1,0:T(8,128)S(1)}, f32[3,4,16,128]{3,2,1,0:T(8,128)}, u32[]{:S(2)}) copy-start(f32[3,4,16,128]{3,2,1,0:T(8,128)} %param.11) | copy-start | bytes 294916
  1.6 3.1 %copy-start = (f32[5,4,16,128]{3,2,1,0:T(8,128)S(1)}, f32[5,4,16,128]{3,2,1,0:T(8,128)}, u32[]{:S(2)}) copy-start(f32[5,4,16,128]{3,2,1,0:T(8,128)} %param.9) | copy-start | bytes 491524
  1.6 15.9 %collective-permute-start.2 = (f32[8,4,8,128]{3,2,1,0:T(8,128)S(1)}, f32[8,4,8,128]{3,2,1,0:T(8,128)S(1)}, u32[]{:S(2)}, u32[]{:S(2)}) collective-permute-start(f32[8,4,8,128]{3,2,1,0:T(8,128)S(1)} %pad_maximum_fusion.2), channel_id=1, source_target_pairs={{0,4},{4,0},{1,5},{5,1},{2,6},{6,2},{3,7},{7,3},{8,12},{12,8},{9,1... | collective-permute-start | bytes 393224 | tf_op jit(solution)/shard_map/ppermute | solution.py:143
  4.7 12.6 %collective-permute-start.1 = (f32[8,1,16,128]{3,2,1,0:T(8,128)S(1)}, f32[8,1,16,128]{3,2,1,0:T(8,128)S(1)}, u32[]{:S(2)}, u32[]{:S(2)}) collective-permute-start(f32[8,1,16,128]{3,2,1,0:T(8,128)S(1)} %get-tuple-element.51), channel_id=1, source_target_pairs={{0,1},{1,2},{2,3},{4,5},{5,6},{6,7},{8,9},{9,10},{10,11},{12,13},{... | collective-permute-start | bytes 196616 | tf_op jit(solution)/shard_map/ppermute | solution.py:120
  6.2 11.2 %collective-permute-start = (f32[8,1,16,128]{3,2,1,0:T(8,128)S(1)}, f32[8,1,16,128]{3,2,1,0:T(8,128)S(1)}, u32[]{:S(2)}, u32[]{:S(2)}) collective-permute-start(f32[8,1,16,128]{3,2,1,0:T(8,128)S(1)} %get-tuple-element.52), channel_id=1, source_target_pairs={{1,0},{2,1},{3,2},{5,4},{6,5},{7,6},{9,8},{10,9},{11,10},{13,12},{... | collective-permute-start | bytes 196616 | tf_op jit(solution)/shard_map/ppermute | solution.py:120
  8.6 8.1 %collective-permute-start.4 = (f32[8,4,16,1]{2,0,3,1:T(8,128)S(1)}, f32[8,4,16,1]{2,0,3,1:T(8,128)S(1)}, u32[]{:S(2)}, u32[]{:S(2)}) collective-permute-start(f32[8,4,16,1]{2,0,3,1:T(8,128)S(1)} %get-tuple-element.65), channel_id=1, source_target_pairs={{0,8},{8,16},{16,24},{24,0},{1,9},{9,17},{17,25},{25,1},{2,10},{10... | collective-permute-start | bytes 6152 | tf_op jit(solution)/shard_map/ppermute | solution.py:120
  10.2 6.8 %collective-permute-start.3 = (f32[8,4,16,1]{2,0,3,1:T(8,128)S(1)}, f32[8,4,16,1]{2,0,3,1:T(8,128)S(1)}, u32[]{:S(2)}, u32[]{:S(2)}) collective-permute-start(f32[8,4,16,1]{2,0,3,1:T(8,128)S(1)} %get-tuple-element.66), channel_id=1, source_target_pairs={{0,24},{8,0},{16,8},{24,16},{1,25},{9,1},{17,9},{25,17},{2,26},{10... | collective-permute-start | bytes 6152 | tf_op jit(solution)/shard_map/ppermute | solution.py:120
  12.5 0.7 %copy-start.6 = (f32[3,5,5]{2,0,1:T(4,128)S(1)}, f32[3,5,5]{2,0,1:T(4,128)}, u32[]{:S(2)}) copy-start(f32[3,5,5]{2,0,1:T(4,128)} %param.12) | copy-start | bytes 904
  13.2 0.7 %copy-start.7 = (f32[3,5,5]{2,0,1:T(4,128)S(1)}, f32[3,5,5]{2,0,1:T(4,128)}, u32[]{:S(2)}) copy-start(f32[3,5,5]{2,0,1:T(4,128)} %param.13) | copy-start | bytes 904
  14.2 0.7 %copy-start.9 = (s32[4,128]{1,0:T(4,128)S(1)}, s32[4,128]{1,0:T(4,128)}, u32[]{:S(2)}) copy-start(s32[4,128]{1,0:T(4,128)} %param.17) | copy-start | bytes 6148
  15.9 0.7 %copy-start.8 = (f32[3,5]{1,0:T(4,128)S(1)}, f32[3,5]{1,0:T(4,128)}, u32[]{:S(2)}) copy-start(f32[3,5]{1,0:T(4,128)} %param.14) | copy-start | bytes 184
  17.4 0.9 %copy-start.4 = (f32[5,4,16,128]{3,2,1,0:T(8,128)S(1)}, f32[5,4,16,128]{3,2,1,0:T(8,128)}, u32[]{:S(2)}) copy-start(f32[5,4,16,128]{3,2,1,0:T(8,128)} %param.10) | copy-start | bytes 491524
  18.5 0.9 %copy-start.3 = (f32[5,4,16,128]{3,2,1,0:T(8,128)}, f32[5,4,16,128]{3,2,1,0:T(8,128)S(1)}, u32[]{:S(2)}) copy-start(f32[5,4,16,128]{3,2,1,0:T(8,128)S(1)} %fusion.15) | copy-start | bytes 491524
  18.5 0.8 %copy-start.2 = (f32[4,16,128]{2,1,0:T(8,128)S(1)}, f32[4,16,128]{2,1,0:T(8,128)}, u32[]{:S(2)}) copy-start(f32[4,16,128]{2,1,0:T(8,128)} %param.15) | copy-start | bytes 98308
  19.5 7.9 %collective-permute-start.5 = (f32[4,4,3,3]{3,2,1,0:T(4,128)S(1)}, f32[4,4,3,3]{3,2,1,0:T(4,128)S(1)}, u32[]{:S(2)}, u32[]{:S(2)}) collective-permute-start(f32[4,4,3,3]{3,2,1,0:T(4,128)S(1)} %get-tuple-element.47), channel_id=1, source_target_pairs={{0,12},{8,20},{16,28},{24,4},{4,8},{12,16},{20,24},{28,0},{1,13},{... | collective-permute-start | bytes 1736 | tf_op jit(solution)/shard_map/ppermute | solution.py:133
  19.9 12.2 %collective-permute-start.8 = (f32[4,4,16,3]{3,2,1,0:T(8,128)S(1)}, f32[4,4,16,3]{3,2,1,0:T(8,128)S(1)}, u32[]{:S(2)}, u32[]{:S(2)}) collective-permute-start(f32[4,4,16,3]{3,2,1,0:T(8,128)S(1)} %get-tuple-element.45), channel_id=1, source_target_pairs={{0,8},{8,16},{16,24},{24,0},{1,9},{9,17},{17,25},{25,1},{2,10},{10... | collective-permute-start | bytes 9224 | tf_op jit(solution)/shard_map/ppermute | solution.py:120
  21.5 10.6 %collective-permute-start.9 = (f32[4,4,16,3]{3,2,1,0:T(8,128)S(1)}, f32[4,4,16,3]{3,2,1,0:T(8,128)S(1)}, u32[]{:S(2)}, u32[]{:S(2)}) collective-permute-start(f32[4,4,16,3]{3,2,1,0:T(8,128)S(1)} %get-tuple-element.46), channel_id=1, source_target_pairs={{0,24},{8,0},{16,8},{24,16},{1,25},{9,1},{17,9},{25,17},{2,26},{10... | collective-permute-start | bytes 9224 | tf_op jit(solution)/shard_map/ppermute | solution.py:120
  24.0 8.0 %collective-permute-start.7 = (f32[4,4,3,3]{3,2,1,0:T(4,128)S(1)}, f32[4,4,3,3]{3,2,1,0:T(4,128)S(1)}, u32[]{:S(2)}, u32[]{:S(2)}) collective-permute-start(f32[4,4,3,3]{3,2,1,0:T(4,128)S(1)} %get-tuple-element.48), channel_id=1, source_target_pairs={{0,28},{8,4},{16,12},{24,20},{4,24},{12,0},{20,8},{28,16},{1,29},{... | collective-permute-start | bytes 1736 | tf_op jit(solution)/shard_map/ppermute | solution.py:133
  26.4 5.7 %collective-permute-start.6 = (f32[4,4,3,128]{3,2,1,0:T(4,128)S(1)}, f32[4,4,3,128]{3,2,1,0:T(4,128)S(1)}, u32[]{:S(2)}, u32[]{:S(2)}) collective-permute-start(f32[4,4,3,128]{3,2,1,0:T(4,128)S(1)} %fusion.29), channel_id=1, source_target_pairs={{0,4},{4,0},{1,5},{5,1},{2,6},{6,2},{3,7},{7,3},{8,12},{12,8},{9,1... | collective-permute-start | bytes 73736 | tf_op jit(solution)/shard_map/ppermute | solution.py:133
  32.5 3.5 %collective-permute-start.10 = (f32[4,3,22,134]{3,2,1,0:T(8,128)S(1)}, f32[4,3,22,134]{3,2,1,0:T(8,128)S(1)}, u32[]{:S(2)}, u32[]{:S(2)}) collective-permute-start(f32[4,3,22,134]{3,2,1,0:T(8,128)S(1)} %get-tuple-element.31), channel_id=1, source_target_pairs={{0,1},{1,2},{2,3},{4,5},{5,6},{6,7},{8,9},{9,10},{10,11},{12,13},{... | collective-permute-start | bytes 424520 | tf_op jit(solution)/shard_map/ppermute | solution.py:120
  34.7 5.4 %collective-permute-start.11 = (f32[4,3,22,134]{3,2,1,0:T(8,128)S(1)}, f32[4,3,22,134]{3,2,1,0:T(8,128)S(1)}, u32[]{:S(2)}, u32[]{:S(2)}) collective-permute-start(f32[4,3,22,134]{3,2,1,0:T(8,128)S(1)} %get-tuple-element.32), channel_id=1, source_target_pairs={{1,0},{2,1},{3,2},{5,4},{6,5},{7,6},{9,8},{10,9},{11,10},{13,12},{... | collective-permute-start | bytes 424520 | tf_op jit(solution)/shard_map/ppermute | solution.py:120
  42.0 0.9 %copy-start.5 = (f32[4,16,128]{2,1,0:T(8,128)S(1)}, f32[4,16,128]{2,1,0:T(8,128)}, u32[]{:S(2)}) copy-start(f32[4,16,128]{2,1,0:T(8,128)} %param.16) | copy-start | bytes 98308

commit v16 on v12

--- a/solution.py
+++ b/solution.py
@@ -135,7 +135,22 @@
     return jnp.where(me == 1, got, zero), jnp.where(me == 0, got, zero)
 
 
+def tile_halos(fields, axis, dim, length):
+    rows = 8
+    me = lax.axis_index(axis)
+    start = (1 - me) * (length - rows)
+    sent = jnp.concatenate([lax.dynamic_slice_in_dim(f, start, rows, axis=dim) for f in fields], axis=0)
+    got = lax.ppermute(sent, axis, [(0, 1), (1, 0)])
+    low = lax.slice_in_dim(got, rows - 1, rows, axis=dim)
+    high = lax.slice_in_dim(got, 0, 1, axis=dim)
+    zero = jnp.zeros_like(low)
+    return jnp.where(me == 1, low, zero), jnp.where(me == 0, high, zero)
+
+
 def face_halos(fields, axis, dim, wrap):
+    length = fields[0].shape[dim]
+    if axis == "normal" and lax.axis_size(axis) == 2 and length >= 8:
+        return tile_halos(fields, axis, dim, length)
     thin = jnp.concatenate(
         [jnp.concatenate([edge(f, dim, 1, 1), edge(f, dim, -1, 1)], axis=dim) for f in fields], axis=0
     )
@@ -202,11 +217,11 @@
     devices = math.prod(lax.axis_size(a) for a in ORDER)
     if devices <= 64:
         spans = lax.axis_size("span")
-        relative = jnp.arange(devices, dtype=jnp.int32) % spans - lax.axis_index("span") + 1
+        relative = jnp.arange(devices, dtype=jnp.int32) // (devices // spans) - lax.axis_index("span") + 1
         chunks = jnp.zeros((devices,) + own.shape, own.dtype)
         for index, block in enumerate((below, own, above)):
             chunks = jnp.where((relative == index)[:, None, None], block[None], chunks)
-        return jnp.sum(lax.all_to_all(chunks, ORDER, 0, 0, tiled=False), axis=0)
+        return jnp.sum(lax.all_to_all(chunks, ORDER[::-1], 0, 0, tiled=False), axis=0)
     if lax.axis_size("normal") != 2 or lax.axis_size("circ") > 4:
         own = lax.psum(own + shifted(above, {"span": 1}) + shifted(below, {"span": -1}), ("circ", "normal"))
         return own

time: 61.7 us -> 60.7 us (0.984)
  local copies, waits for them, and re-layouts: 7.05 us -> 6.15 us
    ppermute x0 -> x1, starting transfers between devices: none -> 3.03 us  [tile_halos(): got = lax.ppermute(sent, axis, [(0, 1), (1, 0)])]
    ppermute x4 -> x3, starting transfers between devices: 6.77 us -> 3.76 us  [receive_pair(): got = lax.ppermute(sent, axes, pairs + back)]
    slice x9 -> x7, local copies, waits for them, and re-layouts: 2.08 us -> 0.26 us  [edge(): return lax.slice_in_dim(array, start, start + width, axis=dim)]
    dynamic_slice x0 -> x2, local copies, waits for them, and re-layouts: none -> 0.94 us  [tile_halos(): lax.dynamic_slice_in_dim(f, start, rows, axis=dim)]
    ppermute x4 -> x3, waiting for transfers between devices: 4.61 us -> 4.59 us  [receive_pair(): got = lax.ppermute(sent, axes, pairs + back)]
    unnamed x30 -> x26, local copies, waits for them, and re-layouts: 3.24 us -> 3.22 us
where the time goes in v16:
time: 60.7 us; the launch traced here: 60.3 us
  starting transfers between devices  21 us (35%)
  blocking collectives  16.1 us (27%)
  waiting for transfers between devices  8.15 us (13%)
  other arithmetic  7.16 us (12%)
  local copies, waits for them, and re-layouts  6.15 us (10%)
  between operations  1.25 us (2%)
    all_to_all x1, blocking collectives, reduce_panels(): lax.all_to_all(chunks, ORDER[::-1], 0, 0, tiled=False)  16.1 us
    ppermute x8, starting transfers between devices, receive(): return lax.ppermute(take(array, rel, dims, width), axes, pairs)  14.2 us
    ppermute x3, waiting for transfers between devices, receive_pair(): got = lax.ppermute(sent, axes, pairs + back)  4.59 us
    ppermute x3, starting transfers between devices, receive_pair(): got = lax.ppermute(sent, axes, pairs + back)  3.76 us
    ppermute x8, waiting for transfers between devices, receive(): return lax.ppermute(take(array, rel, dims, width), axes, pairs)  3.57 us
    unnamed x26, local copies, waits for them, and re-layouts  3.22 us
    ppermute x1, starting transfers between devices, tile_halos(): got = lax.ppermute(sent, axis, [(0, 1), (1, 0)])  3.03 us
    mul x3, other arithmetic, relax(): weighted = stiff_pad[None] * mesh_pad  2.17 us
  transfers between devices with their start and end apart: 12, of which 2 were waited for; matrix products, arithmetic and copies ran while one was open for 7% of the time, Pallas kernels for 0%

profile of v16, /device:TPU:0, one launch (start us, length us, event | category | flops | bytes accessed | tf_op | source)
XLA Modules:
  0.0 60.3 jit_solution(11454748083128206910)
XLA Ops:
  0.6 0.9 %constant_dynamic-slice_fusion.1 = f32[5,4,8,128]{3,2,1,0:T(8,128)S(1)} fusion(f32[5,4,16,128]{3,2,1,0:T(8,128)} %param.11, s32[]{:T(128)S(6)} %select_n.92), kind=kLoop, calls=%fused_computation.140 | loop fusion | bytes 163844 | tf_op jit(solution)/shard_map/dynamic_slice | solution.py:142
  1.6 3.0 %collective-permute-start.2 = (f32[8,4,8,128]{3,2,1,0:T(8,128)S(1)}, f32[8,4,8,128]{3,2,1,0:T(8,128)S(1)}, u32[]{:S(2)}, u32[]{:S(2)}) collective-permute-start(f32[8,4,8,128]{3,2,1,0:T(8,128)S(1)} %pad_maximum_fusion.3), channel_id=1, source_target_pairs={{0,4},{4,0},{1,5},{5,1},{2,6},{6,2},{3,7},{7,3},{8,12},{12,8},{9,1... | collective-permute-start | bytes 393224 | tf_op jit(solution)/shard_map/ppermute | solution.py:143
  4.7 1.5 %collective-permute-start.1 = (f32[8,1,16,128]{3,2,1,0:T(8,128)S(1)}, f32[8,1,16,128]{3,2,1,0:T(8,128)S(1)}, u32[]{:S(2)}, u32[]{:S(2)}) collective-permute-start(f32[8,1,16,128]{3,2,1,0:T(8,128)S(1)} %get-tuple-element.55), channel_id=1, source_target_pairs={{0,1},{1,2},{2,3},{4,5},{5,6},{6,7},{8,9},{9,10},{10,11},{12,13},{... | collective-permute-start | bytes 196616 | tf_op jit(solution)/shard_map/ppermute | solution.py:120
  6.2 1.3 %collective-permute-start = (f32[8,1,16,128]{3,2,1,0:T(8,128)S(1)}, f32[8,1,16,128]{3,2,1,0:T(8,128)S(1)}, u32[]{:S(2)}, u32[]{:S(2)}) collective-permute-start(f32[8,1,16,128]{3,2,1,0:T(8,128)S(1)} %get-tuple-element.56), channel_id=1, source_target_pairs={{1,0},{2,1},{3,2},{5,4},{6,5},{7,6},{9,8},{10,9},{11,10},{13,12},{... | collective-permute-start | bytes 196616 | tf_op jit(solution)/shard_map/ppermute | solution.py:120
  7.6 0.1 fusion.48
  7.7 0.1 copy.66
  7.8 0.1 copy.67
  8.0 0.2 copy.64
  8.3 0.3 copy.65
  8.6 1.6 %collective-permute-start.4 = (f32[8,4,16,1]{2,0,3,1:T(8,128)S(1)}, f32[8,4,16,1]{2,0,3,1:T(8,128)S(1)}, u32[]{:S(2)}, u32[]{:S(2)}) collective-permute-start(f32[8,4,16,1]{2,0,3,1:T(8,128)S(1)} %get-tuple-element.69), channel_id=1, source_target_pairs={{0,8},{8,16},{16,24},{24,0},{1,9},{9,17},{17,25},{25,1},{2,10},{10... | collective-permute-start | bytes 6152 | tf_op jit(solution)/shard_map/ppermute | solution.py:120
  10.2 2.2 %collective-permute-start.3 = (f32[8,4,16,1]{2,0,3,1:T(8,128)S(1)}, f32[8,4,16,1]{2,0,3,1:T(8,128)S(1)}, u32[]{:S(2)}, u32[]{:S(2)}) collective-permute-start(f32[8,4,16,1]{2,0,3,1:T(8,128)S(1)} %get-tuple-element.70), channel_id=1, source_target_pairs={{0,24},{8,0},{16,8},{24,16},{1,25},{9,1},{17,9},{25,17},{2,26},{10... | collective-permute-start | bytes 6152 | tf_op jit(solution)/shard_map/ppermute | solution.py:120
  12.5 0.7 %copy-done.6 = f32[3,5,5]{2,0,1:T(4,128)S(1)} copy-done((f32[3,5,5]{2,0,1:T(4,128)S(1)}, f32[3,5,5]{2,0,1:T(4,128)}, u32[]{:S(2)}) %copy-start.6) | copy-done | bytes 324
  13.4 0.6 copy-done.8
  14.6 0.1 subtract_multiply_fusion
  15.0 0.7 %copy-done.9 = s32[4,128]{1,0:T(4,128)S(1)} copy-done((s32[4,128]{1,0:T(4,128)S(1)}, s32[4,128]{1,0:T(4,128)}, u32[]{:S(2)}) %copy-start.9) | copy-done | bytes 2072
  15.6 0.5 multiply_reduce_fusion.2
  16.1 0.2 multiply_reduce_fusion
  16.3 0.1 multiply_reduce_fusion.4
  16.5 0.2 slice_reduce_fusion
  17.0 0.1 multiply_reduce_fusion.10
  17.1 0.2 copy.59
  17.4 0.2 copy.57
  17.7 0.1 multiply_reduce_fusion.7
  18.0 0.1 multiply_reduce_fusion.12
  18.1 0.2 fusion.15
  18.5 0.5 copy-done.2
  19.0 0.1 fusion.26
  19.1 0.3 collective-permute-start.5
  19.4 1.6 %collective-permute-start.8 = (f32[4,4,16,3]{3,2,1,0:T(8,128)S(1)}, f32[4,4,16,3]{3,2,1,0:T(8,128)S(1)}, u32[]{:S(2)}, u32[]{:S(2)}) collective-permute-start(f32[4,4,16,3]{3,2,1,0:T(8,128)S(1)} %get-tuple-element.49), channel_id=1, source_target_pairs={{0,8},{8,16},{16,24},{24,0},{1,9},{9,17},{17,25},{25,1},{2,10},{10... | collective-permute-start | bytes 9224 | tf_op jit(solution)/shard_map/ppermute | solution.py:120
  21.1 2.5 %collective-permute-start.9 = (f32[4,4,16,3]{3,2,1,0:T(8,128)S(1)}, f32[4,4,16,3]{3,2,1,0:T(8,128)S(1)}, u32[]{:S(2)}, u32[]{:S(2)}) collective-permute-start(f32[4,4,16,3]{3,2,1,0:T(8,128)S(1)} %get-tuple-element.50), channel_id=1, source_target_pairs={{0,24},{8,0},{16,8},{24,16},{1,25},{9,1},{17,9},{25,17},{2,26},{10... | collective-permute-start | bytes 9224 | tf_op jit(solution)/shard_map/ppermute | solution.py:120
  23.6 1.0 %collective-permute-start.6 = (f32[4,4,3,128]{3,2,1,0:T(4,128)S(1)}, f32[4,4,3,128]{3,2,1,0:T(4,128)S(1)}, u32[]{:S(2)}, u32[]{:S(2)}) collective-permute-start(f32[4,4,3,128]{3,2,1,0:T(4,128)S(1)} %fusion.29), channel_id=1, source_target_pairs={{0,4},{4,0},{1,5},{5,1},{2,6},{6,2},{3,7},{7,3},{8,12},{12,8},{9,1... | collective-permute-start | bytes 73736 | tf_op jit(solution)/shard_map/ppermute | solution.py:133
  24.6 2.5 %collective-permute-start.7 = (f32[4,4,3,3]{3,2,1,0:T(4,128)S(1)}, f32[4,4,3,3]{3,2,1,0:T(4,128)S(1)}, u32[]{:S(2)}, u32[]{:S(2)}) collective-permute-start(f32[4,4,3,3]{3,2,1,0:T(4,128)S(1)} %get-tuple-element.52), channel_id=1, source_target_pairs={{0,28},{8,4},{16,12},{24,20},{4,24},{12,0},{20,8},{28,16},{1,29},{... | collective-permute-start | bytes 1736 | tf_op jit(solution)/shard_map/ppermute | solution.py:133
  27.0 4.6 %collective-permute-done.7 = f32[4,4,3,3]{3,2,1,0:T(4,128)S(1)} collective-permute-done((f32[4,4,3,3]{3,2,1,0:T(4,128)S(1)}, f32[4,4,3,3]{3,2,1,0:T(4,128)S(1)}, u32[]{:S(2)}, u32[]{:S(2)}) %collective-permute-start.7) | collective-permute-done | bytes 608 | tf_op jit(solution)/shard_map/ppermute | solution.py:133
  31.7 0.3 maximum_maximum_fusion
  32.1 2.2 %collective-permute-start.10 = (f32[4,3,22,134]{3,2,1,0:T(8,128)S(1)}, f32[4,3,22,134]{3,2,1,0:T(8,128)S(1)}, u32[]{:S(2)}, u32[]{:S(2)}) collective-permute-start(f32[4,3,22,134]{3,2,1,0:T(8,128)S(1)} %get-tuple-element.35), channel_id=1, source_target_pairs={{0,1},{1,2},{2,3},{4,5},{5,6},{6,7},{8,9},{9,10},{10,11},{12,13},{... | collective-permute-start | bytes 424520 | tf_op jit(solution)/shard_map/ppermute | solution.py:120
  34.2 1.3 %collective-permute-start.11 = (f32[4,3,22,134]{3,2,1,0:T(8,128)S(1)}, f32[4,3,22,134]{3,2,1,0:T(8,128)S(1)}, u32[]{:S(2)}, u32[]{:S(2)}) collective-permute-start(f32[4,3,22,134]{3,2,1,0:T(8,128)S(1)} %get-tuple-element.36), channel_id=1, source_target_pairs={{1,0},{2,1},{3,2},{5,4},{6,5},{7,6},{9,8},{10,9},{11,10},{13,12},{... | collective-permute-start | bytes 424520 | tf_op jit(solution)/shard_map/ppermute | solution.py:120
  35.6 3.5 %collective-permute-done.11 = f32[4,3,22,134]{3,2,1,0:T(8,128)S(1)} collective-permute-done((f32[4,3,22,134]{3,2,1,0:T(8,128)S(1)}, f32[4,3,22,134]{3,2,1,0:T(8,128)S(1)}, u32[]{:S(2)}, u32[]{:S(2)}) %collective-permute-start.11) | collective-permute-done | bytes 141536 | tf_op jit(solution)/shard_map/ppermute | solution.py:120
  39.1 0.3 pad_maximum_fusion
  39.5 0.1 multiply_add_fusion
  39.6 0.1 multiply_add_fusion.1
  39.8 0.1 broadcast_multiply_fusion
  40.0 1.2 %broadcast_multiply_fusion.1 = (f32[3,8,20,132]{3,2,1,0:T(8,128)S(1)}, f32[3,8,20,132]{3,2,1,0:T(8,128)S(1)}) fusion(f32[8,20,132]{2,1,0:T(8,128)S(1)} %get-tuple-element.40, f32[3,10,22,134]{3,2,1,0:T(8,128)S(1)} %get-tuple-element.31, f32[8,20,132]{2,1,0:T(8,128)S(1)} %get-tuple-element.39, f32[4,10,22,134]{3,2,1,0:T(8,128)S(1)} %pad_maximum_fusion, ...), kind=kLoop, calls=%fused_computation.42 | loop fusion | flops 760320 | bytes 2703360 | tf_op jit(solution)/shard_map/mul | solution.py:60
  41.2 0.9 %broadcast_multiply_fusion.2 = (f32[3,6,18,130]{3,2,1,0:T(8,128)S(1)}, f32[3,6,18,130]{3,2,1,0:T(8,128)S(1)}) fusion(f32[6,18,130]{2,1,0:T(8,128)S(1)} %get-tuple-element.38, f32[3,8,20,132]{3,2,1,0:T(8,128)S(1)} %get-tuple-element.29, f32[6,18,130]{2,1,0:T(8,128)S(1)} %get-tuple-element.37, f32[4,10,22,134]{3,2,1,0:T(8,128)S(1)} %pad_maximum_fusion, ...), kind=kLoop, calls=%fused_computation.45 | loop fusion | flops 505440 | bytes 1797120 | tf_op jit(solution)/shard_map/mul | solution.py:60
  42.1 0.9 %multiply_reduce_fusion.9 = (f32[3,4,128]{2,1,0:T(4,128)S(1)}, f32[3,4,16,128]{3,2,1,0:T(8,128)}) fusion(f32[4,16,128]{2,1,0:T(8,128)S(1)} %copy-done.5, f32[3,6,18,130]{3,2,1,0:T(8,128)S(1)} %get-tuple-element.27, f32[3,4,16,128]{3,2,1,0:T(8,128)S(1)} %multiply_reduce_fusion.6, f32[4,16,128]{2,1,0:T(8,128)S(1)} %fusion.34, ...), kind=kLoop, calls=%fused_computation.81 | loop fusion | flops 317952 | bytes 956416 | tf_op jit(solution)/shard_map/reduce_sum | solution.py:261
  42.9 0.4 convolution_bitcast_fusion
  43.4 0.2 select_select_fusion
  43.5 16.1 %all_to_all.5 = f32[32,3,128]{2,1,0:T(4,128)S(1)} all-to-all(f32[32,3,128]{2,1,0:T(4,128)S(1)} %select_select_fusion), channel_id=1, replica_groups=mesh['circ'=4,'normal'=2,'span'=4] {'span','normal','circ'}, dimensions={0} | all-to-all | bytes 98304 | tf_op jit(solution)/shard_map/all_to_all | solution.py:224
  59.6 0.6 %reduce_sum.167 = f32[3,128]{1,0:T(4,128)} reduce(f32[32,3,128]{2,1,0:T(4,128)S(1)} %all_to_all.5, f32[]{:T(128)} %constant.18.clone.1), dimensions={0}, to_apply=%region_14.15 | reduce | flops 11904 | bytes 50692 | tf_op jit(solution)/shard_map/reduce_sum | solution.py:224
  (89 shorter events, 2.3 us)
Async XLA Ops:
  0.6 0.9 %copy-start.1 = (f32[3,4,16,128]{3,2,1,0:T(8,128)S(1)}, f32[3,4,16,128]{3,2,1,0:T(8,128)}, u32[]{:S(2)}) copy-start(f32[3,4,16,128]{3,2,1,0:T(8,128)} %param.12) | copy-start | bytes 294916
  1.6 3.1 %copy-start = (f32[5,4,16,128]{3,2,1,0:T(8,128)S(1)}, f32[5,4,16,128]{3,2,1,0:T(8,128)}, u32[]{:S(2)}) copy-start(f32[5,4,16,128]{3,2,1,0:T(8,128)} %param.11) | copy-start | bytes 491524
  1.6 16.2 %collective-permute-start.2 = (f32[8,4,8,128]{3,2,1,0:T(8,128)S(1)}, f32[8,4,8,128]{3,2,1,0:T(8,128)S(1)}, u32[]{:S(2)}, u32[]{:S(2)}) collective-permute-start(f32[8,4,8,128]{3,2,1,0:T(8,128)S(1)} %pad_maximum_fusion.3), channel_id=1, source_target_pairs={{0,4},{4,0},{1,5},{5,1},{2,6},{6,2},{3,7},{7,3},{8,12},{12,8},{9,1... | collective-permute-start | bytes 393224 | tf_op jit(solution)/shard_map/ppermute | solution.py:143
  4.7 12.9 %collective-permute-start.1 = (f32[8,1,16,128]{3,2,1,0:T(8,128)S(1)}, f32[8,1,16,128]{3,2,1,0:T(8,128)S(1)}, u32[]{:S(2)}, u32[]{:S(2)}) collective-permute-start(f32[8,1,16,128]{3,2,1,0:T(8,128)S(1)} %get-tuple-element.55), channel_id=1, source_target_pairs={{0,1},{1,2},{2,3},{4,5},{5,6},{6,7},{8,9},{9,10},{10,11},{12,13},{... | collective-permute-start | bytes 196616 | tf_op jit(solution)/shard_map/ppermute | solution.py:120
  6.2 11.5 %collective-permute-start = (f32[8,1,16,128]{3,2,1,0:T(8,128)S(1)}, f32[8,1,16,128]{3,2,1,0:T(8,128)S(1)}, u32[]{:S(2)}, u32[]{:S(2)}) collective-permute-start(f32[8,1,16,128]{3,2,1,0:T(8,128)S(1)} %get-tuple-element.56), channel_id=1, source_target_pairs={{1,0},{2,1},{3,2},{5,4},{6,5},{7,6},{9,8},{10,9},{11,10},{13,12},{... | collective-permute-start | bytes 196616 | tf_op jit(solution)/shard_map/ppermute | solution.py:120
  8.6 5.5 %copy-start.3 = (f32[5,4,16,128]{3,2,1,0:T(8,128)S(1)}, f32[5,4,16,128]{3,2,1,0:T(8,128)}, u32[]{:S(2)}) copy-start(f32[5,4,16,128]{3,2,1,0:T(8,128)} %param.9) | copy-start | bytes 491524
  8.6 8.4 %collective-permute-start.4 = (f32[8,4,16,1]{2,0,3,1:T(8,128)S(1)}, f32[8,4,16,1]{2,0,3,1:T(8,128)S(1)}, u32[]{:S(2)}, u32[]{:S(2)}) collective-permute-start(f32[8,4,16,1]{2,0,3,1:T(8,128)S(1)} %get-tuple-element.69), channel_id=1, source_target_pairs={{0,8},{8,16},{16,24},{24,0},{1,9},{9,17},{17,25},{25,1},{2,10},{10... | collective-permute-start | bytes 6152 | tf_op jit(solution)/shard_map/ppermute | solution.py:120
  10.2 7.1 %collective-permute-start.3 = (f32[8,4,16,1]{2,0,3,1:T(8,128)S(1)}, f32[8,4,16,1]{2,0,3,1:T(8,128)S(1)}, u32[]{:S(2)}, u32[]{:S(2)}) collective-permute-start(f32[8,4,16,1]{2,0,3,1:T(8,128)S(1)} %get-tuple-element.70), channel_id=1, source_target_pairs={{0,24},{8,0},{16,8},{24,16},{1,25},{9,1},{17,9},{25,17},{2,26},{10... | collective-permute-start | bytes 6152 | tf_op jit(solution)/shard_map/ppermute | solution.py:120
  12.5 0.7 %copy-start.6 = (f32[3,5,5]{2,0,1:T(4,128)S(1)}, f32[3,5,5]{2,0,1:T(4,128)}, u32[]{:S(2)}) copy-start(f32[3,5,5]{2,0,1:T(4,128)} %param.6) | copy-start | bytes 904
  12.5 0.8 %copy-start.7 = (f32[3,5,5]{2,0,1:T(4,128)S(1)}, f32[3,5,5]{2,0,1:T(4,128)}, u32[]{:S(2)}) copy-start(f32[3,5,5]{2,0,1:T(4,128)} %param.7) | copy-start | bytes 904
  13.2 0.9 %copy-start.4 = (f32[4,16,128]{2,1,0:T(8,128)S(1)}, f32[4,16,128]{2,1,0:T(8,128)}, u32[]{:S(2)}) copy-start(f32[4,16,128]{2,1,0:T(8,128)} %param.10) | copy-start | bytes 98308
  13.3 0.7 %copy-start.8 = (f32[3,5]{1,0:T(4,128)S(1)}, f32[3,5]{1,0:T(4,128)}, u32[]{:S(2)}) copy-start(f32[3,5]{1,0:T(4,128)} %param.8) | copy-start | bytes 184
  14.9 0.7 %copy-start.9 = (s32[4,128]{1,0:T(4,128)S(1)}, s32[4,128]{1,0:T(4,128)}, u32[]{:S(2)}) copy-start(s32[4,128]{1,0:T(4,128)} %param.14) | copy-start | bytes 6148
  18.3 0.7 %copy-start.2 = (f32[5,4,16,128]{3,2,1,0:T(8,128)}, f32[5,4,16,128]{3,2,1,0:T(8,128)S(1)}, u32[]{:S(2)}) copy-start(f32[5,4,16,128]{3,2,1,0:T(8,128)S(1)} %fusion.15) | copy-start | bytes 491524
  19.1 7.9 %collective-permute-start.5 = (f32[4,4,3,3]{3,2,1,0:T(4,128)S(1)}, f32[4,4,3,3]{3,2,1,0:T(4,128)S(1)}, u32[]{:S(2)}, u32[]{:S(2)}) collective-permute-start(f32[4,4,3,3]{3,2,1,0:T(4,128)S(1)} %get-tuple-element.51), channel_id=1, source_target_pairs={{0,12},{8,20},{16,28},{24,4},{4,8},{12,16},{20,24},{28,0},{1,13},{... | collective-permute-start | bytes 1736 | tf_op jit(solution)/shard_map/ppermute | solution.py:133
  19.4 12.2 %collective-permute-start.8 = (f32[4,4,16,3]{3,2,1,0:T(8,128)S(1)}, f32[4,4,16,3]{3,2,1,0:T(8,128)S(1)}, u32[]{:S(2)}, u32[]{:S(2)}) collective-permute-start(f32[4,4,16,3]{3,2,1,0:T(8,128)S(1)} %get-tuple-element.49), channel_id=1, source_target_pairs={{0,8},{8,16},{16,24},{24,0},{1,9},{9,17},{17,25},{25,1},{2,10},{10... | collective-permute-start | bytes 9224 | tf_op jit(solution)/shard_map/ppermute | solution.py:120
  21.1 10.6 %collective-permute-start.9 = (f32[4,4,16,3]{3,2,1,0:T(8,128)S(1)}, f32[4,4,16,3]{3,2,1,0:T(8,128)S(1)}, u32[]{:S(2)}, u32[]{:S(2)}) collective-permute-start(f32[4,4,16,3]{3,2,1,0:T(8,128)S(1)} %get-tuple-element.50), channel_id=1, source_target_pairs={{0,24},{8,0},{16,8},{24,16},{1,25},{9,1},{17,9},{25,17},{2,26},{10... | collective-permute-start | bytes 9224 | tf_op jit(solution)/shard_map/ppermute | solution.py:120
  23.6 8.0 %collective-permute-start.6 = (f32[4,4,3,128]{3,2,1,0:T(4,128)S(1)}, f32[4,4,3,128]{3,2,1,0:T(4,128)S(1)}, u32[]{:S(2)}, u32[]{:S(2)}) collective-permute-start(f32[4,4,3,128]{3,2,1,0:T(4,128)S(1)} %fusion.29), channel_id=1, source_target_pairs={{0,4},{4,0},{1,5},{5,1},{2,6},{6,2},{3,7},{7,3},{8,12},{12,8},{9,1... | collective-permute-start | bytes 73736 | tf_op jit(solution)/shard_map/ppermute | solution.py:133
  24.6 7.1 %collective-permute-start.7 = (f32[4,4,3,3]{3,2,1,0:T(4,128)S(1)}, f32[4,4,3,3]{3,2,1,0:T(4,128)S(1)}, u32[]{:S(2)}, u32[]{:S(2)}) collective-permute-start(f32[4,4,3,3]{3,2,1,0:T(4,128)S(1)} %get-tuple-element.52), channel_id=1, source_target_pairs={{0,28},{8,4},{16,12},{24,20},{4,24},{12,0},{20,8},{28,16},{1,29},{... | collective-permute-start | bytes 1736 | tf_op jit(solution)/shard_map/ppermute | solution.py:133
  32.1 3.5 %collective-permute-start.10 = (f32[4,3,22,134]{3,2,1,0:T(8,128)S(1)}, f32[4,3,22,134]{3,2,1,0:T(8,128)S(1)}, u32[]{:S(2)}, u32[]{:S(2)}) collective-permute-start(f32[4,3,22,134]{3,2,1,0:T(8,128)S(1)} %get-tuple-element.35), channel_id=1, source_target_pairs={{0,1},{1,2},{2,3},{4,5},{5,6},{6,7},{8,9},{9,10},{10,11},{12,13},{... | collective-permute-start | bytes 424520 | tf_op jit(solution)/shard_map/ppermute | solution.py:120
  34.2 4.9 %collective-permute-start.11 = (f32[4,3,22,134]{3,2,1,0:T(8,128)S(1)}, f32[4,3,22,134]{3,2,1,0:T(8,128)S(1)}, u32[]{:S(2)}, u32[]{:S(2)}) collective-permute-start(f32[4,3,22,134]{3,2,1,0:T(8,128)S(1)} %get-tuple-element.36), channel_id=1, source_target_pairs={{1,0},{2,1},{3,2},{5,4},{6,5},{7,6},{9,8},{10,9},{11,10},{13,12},{... | collective-permute-start | bytes 424520 | tf_op jit(solution)/shard_map/ppermute | solution.py:120
  41.1 0.9 %copy-start.5 = (f32[4,16,128]{2,1,0:T(8,128)S(1)}, f32[4,16,128]{2,1,0:T(8,128)}, u32[]{:S(2)}) copy-start(f32[4,16,128]{2,1,0:T(8,128)} %param.13) | copy-start | bytes 98308

commit v17 on v15

--- a/solution.py
+++ b/solution.py
@@ -198,7 +198,7 @@
         first = lax.slice_in_dim(psi, 0, 1, axis=dim)
         w_last = lax.slice_in_dim(weights[direction], length - 1, length, axis=direction)
         up_edge = w_last[None] * (last - after[:5])
-        down_edge = before[5 + direction][None] * (before[:5] - first)
+        down_edge = before[5][None] * (before[:5] - first)
         up_inner, down_inner = inner_terms[direction]
         up = jnp.concatenate([up_inner, jac_apply(owner_jac[direction], up_edge)], axis=dim)
         down = jnp.concatenate([jac_apply(neighbor_jac[direction], down_edge), down_inner], axis=dim)
@@ -246,11 +246,9 @@
     wall_kernel,
     panel_owner,
 ):
-    fields = (adjoint, face_weights)
     halos = [
-        face_halos(fields, "span", 1, False),
-        face_halos(fields, "normal", 2, False),
-        face_halos(fields, "circ", 3, True),
+        face_halos((adjoint, face_weights[d : d + 1]), axis, d + 1, False)
+        for d, axis in enumerate(("span", "normal", "circ"))
     ]
     residual = flux_faces(adjoint, face_weights, halos, owner_jac, neighbor_jac) + adjoint - objective_grad
     forcing = jac_apply(coupling.T, residual)

time: 60.4 us -> 59.6 us (0.987)
  local copies, waits for them, and re-layouts: 6.67 us -> 5.88 us
    dynamic_slice x2, local copies, waits for them, and re-layouts: 0.94 us -> 0.01 us  [tile_halos(): lax.dynamic_slice_in_dim(f, start, rows, axis=dim)]
    slice x2 -> x3, local copies, waits for them, and re-layouts: 0.01 us -> 0.83 us  [the longest x1 0.82 us: flux_faces(): w_low = lax.slice_in_dim(weights[direction], 0, length - 1, axis=direction)]
    unnamed x28, local copies, waits for them, and re-layouts: 4.68 us -> 4.02 us
where the time goes in v17:
time: 59.6 us; the launch traced here: 59.1 us
  starting transfers between devices  20.9 us (35%)
  blocking collectives  14.8 us (25%)
  waiting for transfers between devices  8.73 us (15%)
  other arithmetic  7.04 us (12%)
  local copies, waits for them, and re-layouts  5.88 us (10%)
  between operations  1.22 us (2%)
    all_to_all x1, blocking collectives, reduce_panels(): lax.all_to_all(chunks, ORDER[::-1], 0, 0, tiled=False)  14.8 us
    ppermute x8, starting transfers between devices, receive(): return lax.ppermute(take(array, rel, dims, width), axes, pairs)  13.9 us
    ppermute x3, waiting for transfers between devices, receive_pair(): got = lax.ppermute(sent, axes, pairs + back)  5.01 us
    unnamed x28, local copies, waits for them, and re-layouts  4.02 us
    ppermute x3, starting transfers between devices, receive_pair(): got = lax.ppermute(sent, axes, pairs + back)  4.02 us
    ppermute x8, waiting for transfers between devices, receive(): return lax.ppermute(take(array, rel, dims, width), axes, pairs)  3.72 us
    ppermute x1, starting transfers between devices, tile_halos(): got = lax.ppermute(sent, axis, [(0, 1), (1, 0)])  3.03 us
    mul x3, other arithmetic, relax(): weighted = stiff_pad[None] * mesh_pad  2.17 us
  transfers between devices with their start and end apart: 12, of which 2 were waited for; matrix products, arithmetic and copies ran while one was open for 5% of the time, Pallas kernels for 0%

profile of v17, /device:TPU:0, one launch (start us, length us, event | category | flops | bytes accessed | tf_op | source)
XLA Modules:
  0.0 59.1 jit_solution(12692566906114268215)
XLA Ops:
  0.6 0.8 %fusion.51 = (f32[1,4,16,128]{3,2,1,0:T(8,128)S(1)}, f32[4,16,128]{2,1,0:T(8,128)S(1)}, f32[4,16,128]{2,1,0:T(8,128)S(1)}) fusion(f32[3,4,16,128]{3,2,1,0:T(8,128)} %param.11), kind=kLoop, calls=%fused_computation.152 | loop fusion | bytes 163840 | tf_op jit(solution)/shard_map/slice | solution.py:188
  1.5 0.1 copy-done
  1.6 3.0 %collective-permute-start.2 = (f32[6,4,8,128]{3,2,1,0:T(8,128)S(1)}, f32[6,4,8,128]{3,2,1,0:T(8,128)S(1)}, u32[]{:S(2)}, u32[]{:S(2)}) collective-permute-start(f32[6,4,8,128]{3,2,1,0:T(8,128)S(1)} %pad_maximum_fusion.2), channel_id=1, source_target_pairs={{0,4},{4,0},{1,5},{5,1},{2,6},{6,2},{3,7},{7,3},{8,12},{12,8},{9,1... | collective-permute-start | bytes 294920 | tf_op jit(solution)/shard_map/ppermute | solution.py:143
  4.7 1.5 %collective-permute-start.1 = (f32[6,1,16,128]{3,2,1,0:T(8,128)S(1)}, f32[6,1,16,128]{3,2,1,0:T(8,128)S(1)}, u32[]{:S(2)}, u32[]{:S(2)}) collective-permute-start(f32[6,1,16,128]{3,2,1,0:T(8,128)S(1)} %get-tuple-element.56), channel_id=1, source_target_pairs={{0,1},{1,2},{2,3},{4,5},{5,6},{6,7},{8,9},{9,10},{10,11},{12,13},{... | collective-permute-start | bytes 147464 | tf_op jit(solution)/shard_map/ppermute | solution.py:120
  6.2 1.3 %collective-permute-start = (f32[6,1,16,128]{3,2,1,0:T(8,128)S(1)}, f32[6,1,16,128]{3,2,1,0:T(8,128)S(1)}, u32[]{:S(2)}, u32[]{:S(2)}) collective-permute-start(f32[6,1,16,128]{3,2,1,0:T(8,128)S(1)} %get-tuple-element.57), channel_id=1, source_target_pairs={{1,0},{2,1},{3,2},{5,4},{6,5},{7,6},{9,8},{10,9},{11,10},{13,12},{... | collective-permute-start | bytes 147464 | tf_op jit(solution)/shard_map/ppermute | solution.py:120
  7.5 0.1 fusion.48
  7.6 0.3 copy.93
  7.9 0.3 copy.94
  8.4 1.6 %collective-permute-start.4 = (f32[6,4,16,1]{2,0,3,1:T(8,128)S(1)}, f32[6,4,16,1]{2,0,3,1:T(8,128)S(1)}, u32[]{:S(2)}, u32[]{:S(2)}) collective-permute-start(f32[6,4,16,1]{2,0,3,1:T(8,128)S(1)} %get-tuple-element.67), channel_id=1, source_target_pairs={{0,8},{8,16},{16,24},{24,0},{1,9},{9,17},{17,25},{25,1},{2,10},{10... | collective-permute-start | bytes 4616 | tf_op jit(solution)/shard_map/ppermute | solution.py:120
  10.1 2.2 %collective-permute-start.3 = (f32[6,4,16,1]{2,0,3,1:T(8,128)S(1)}, f32[6,4,16,1]{2,0,3,1:T(8,128)S(1)}, u32[]{:S(2)}, u32[]{:S(2)}) collective-permute-start(f32[6,4,16,1]{2,0,3,1:T(8,128)S(1)} %get-tuple-element.68), channel_id=1, source_target_pairs={{0,24},{8,0},{16,8},{24,16},{1,25},{9,1},{17,9},{25,17},{2,26},{10... | collective-permute-start | bytes 4616 | tf_op jit(solution)/shard_map/ppermute | solution.py:120
  12.3 0.7 %copy-done.7 = f32[3,5,5]{2,0,1:T(4,128)S(1)} copy-done((f32[3,5,5]{2,0,1:T(4,128)S(1)}, f32[3,5,5]{2,0,1:T(4,128)}, u32[]{:S(2)}) %copy-start.7) | copy-done | bytes 324
  13.1 0.1 subtract_multiply_fusion
  13.3 0.7 %copy-done.9 = s32[4,128]{1,0:T(4,128)S(1)} copy-done((s32[4,128]{1,0:T(4,128)S(1)}, s32[4,128]{1,0:T(4,128)}, u32[]{:S(2)}) %copy-start.9) | copy-done | bytes 2072
  14.0 0.5 multiply_reduce_fusion.2
  14.5 0.2 multiply_reduce_fusion
  14.7 0.1 multiply_reduce_fusion.4
  14.9 0.2 slice_reduce_fusion
  15.1 0.6 %copy-done.8 = f32[3,5]{1,0:T(4,128)S(1)} copy-done((f32[3,5]{1,0:T(4,128)S(1)}, f32[3,5]{1,0:T(4,128)}, u32[]{:S(2)}) %copy-start.8) | copy-done | bytes 84
  16.0 0.1 multiply_reduce_fusion.11
  16.1 0.2 copy.82
  16.3 0.2 copy.80
  16.6 0.1 multiply_reduce_fusion.7
  16.9 0.1 multiply_reduce_fusion.12
  17.0 0.5 copy-done.4
  17.5 0.2 fusion.15
  17.8 0.7 %copy-done.1 = f32[4,16,128]{2,1,0:T(8,128)S(1)} copy-done((f32[4,16,128]{2,1,0:T(8,128)S(1)}, f32[4,16,128]{2,1,0:T(8,128)}, u32[]{:S(2)}) %copy-start.1) | copy-done | bytes 32792
  18.6 0.1 fusion.26
  18.7 0.6 %collective-permute-start.5 = (f32[4,4,3,3]{3,2,1,0:T(4,128)S(1)}, f32[4,4,3,3]{3,2,1,0:T(4,128)S(1)}, u32[]{:S(2)}, u32[]{:S(2)}) collective-permute-start(f32[4,4,3,3]{3,2,1,0:T(4,128)S(1)} %get-tuple-element.47), channel_id=1, source_target_pairs={{0,12},{8,20},{16,28},{24,4},{4,8},{12,16},{20,24},{28,0},{1,13},{... | collective-permute-start | bytes 1736 | tf_op jit(solution)/shard_map/ppermute | solution.py:133
  19.3 1.6 %collective-permute-start.8 = (f32[4,4,16,3]{3,2,1,0:T(8,128)S(1)}, f32[4,4,16,3]{3,2,1,0:T(8,128)S(1)}, u32[]{:S(2)}, u32[]{:S(2)}) collective-permute-start(f32[4,4,16,3]{3,2,1,0:T(8,128)S(1)} %get-tuple-element.45), channel_id=1, source_target_pairs={{0,8},{8,16},{16,24},{24,0},{1,9},{9,17},{17,25},{25,1},{2,10},{10... | collective-permute-start | bytes 9224 | tf_op jit(solution)/shard_map/ppermute | solution.py:120
  20.9 2.3 %collective-permute-start.9 = (f32[4,4,16,3]{3,2,1,0:T(8,128)S(1)}, f32[4,4,16,3]{3,2,1,0:T(8,128)S(1)}, u32[]{:S(2)}, u32[]{:S(2)}) collective-permute-start(f32[4,4,16,3]{3,2,1,0:T(8,128)S(1)} %get-tuple-element.46), channel_id=1, source_target_pairs={{0,24},{8,0},{16,8},{24,16},{1,25},{9,1},{17,9},{25,17},{2,26},{10... | collective-permute-start | bytes 9224 | tf_op jit(solution)/shard_map/ppermute | solution.py:120
  23.2 2.3 %collective-permute-start.7 = (f32[4,4,3,3]{3,2,1,0:T(4,128)S(1)}, f32[4,4,3,3]{3,2,1,0:T(4,128)S(1)}, u32[]{:S(2)}, u32[]{:S(2)}) collective-permute-start(f32[4,4,3,3]{3,2,1,0:T(4,128)S(1)} %get-tuple-element.48), channel_id=1, source_target_pairs={{0,28},{8,4},{16,12},{24,20},{4,24},{12,0},{20,8},{28,16},{1,29},{... | collective-permute-start | bytes 1736 | tf_op jit(solution)/shard_map/ppermute | solution.py:133
  25.5 1.1 %collective-permute-start.6 = (f32[4,4,3,128]{3,2,1,0:T(4,128)S(1)}, f32[4,4,3,128]{3,2,1,0:T(4,128)S(1)}, u32[]{:S(2)}, u32[]{:S(2)}) collective-permute-start(f32[4,4,3,128]{3,2,1,0:T(4,128)S(1)} %fusion.29), channel_id=1, source_target_pairs={{0,4},{4,0},{1,5},{5,1},{2,6},{6,2},{3,7},{7,3},{8,12},{12,8},{9,1... | collective-permute-start | bytes 73736 | tf_op jit(solution)/shard_map/ppermute | solution.py:133
  26.6 5.0 %collective-permute-done.7 = f32[4,4,3,3]{3,2,1,0:T(4,128)S(1)} collective-permute-done((f32[4,4,3,3]{3,2,1,0:T(4,128)S(1)}, f32[4,4,3,3]{3,2,1,0:T(4,128)S(1)}, u32[]{:S(2)}, u32[]{:S(2)}) %collective-permute-start.7) | collective-permute-done | bytes 608 | tf_op jit(solution)/shard_map/ppermute | solution.py:133
  31.7 0.3 maximum_maximum_fusion
  32.1 2.0 %collective-permute-start.10 = (f32[4,3,22,134]{3,2,1,0:T(8,128)S(1)}, f32[4,3,22,134]{3,2,1,0:T(8,128)S(1)}, u32[]{:S(2)}, u32[]{:S(2)}) collective-permute-start(f32[4,3,22,134]{3,2,1,0:T(8,128)S(1)} %get-tuple-element.31), channel_id=1, source_target_pairs={{0,1},{1,2},{2,3},{4,5},{5,6},{6,7},{8,9},{9,10},{10,11},{12,13},{... | collective-permute-start | bytes 424520 | tf_op jit(solution)/shard_map/ppermute | solution.py:120
  34.1 1.3 %collective-permute-start.11 = (f32[4,3,22,134]{3,2,1,0:T(8,128)S(1)}, f32[4,3,22,134]{3,2,1,0:T(8,128)S(1)}, u32[]{:S(2)}, u32[]{:S(2)}) collective-permute-start(f32[4,3,22,134]{3,2,1,0:T(8,128)S(1)} %get-tuple-element.32), channel_id=1, source_target_pairs={{1,0},{2,1},{3,2},{5,4},{6,5},{7,6},{9,8},{10,9},{11,10},{13,12},{... | collective-permute-start | bytes 424520 | tf_op jit(solution)/shard_map/ppermute | solution.py:120
  35.5 3.7 %collective-permute-done.11 = f32[4,3,22,134]{3,2,1,0:T(8,128)S(1)} collective-permute-done((f32[4,3,22,134]{3,2,1,0:T(8,128)S(1)}, f32[4,3,22,134]{3,2,1,0:T(8,128)S(1)}, u32[]{:S(2)}, u32[]{:S(2)}) %collective-permute-start.11) | collective-permute-done | bytes 141536 | tf_op jit(solution)/shard_map/ppermute | solution.py:120
  39.2 0.3 pad_maximum_fusion
  39.6 0.1 multiply_add_fusion
  39.7 0.1 multiply_add_fusion.1
  39.9 0.1 broadcast_multiply_fusion
  40.0 1.2 %broadcast_multiply_fusion.1 = (f32[3,8,20,132]{3,2,1,0:T(8,128)S(1)}, f32[3,8,20,132]{3,2,1,0:T(8,128)S(1)}) fusion(f32[8,20,132]{2,1,0:T(8,128)S(1)} %get-tuple-element.36, f32[3,10,22,134]{3,2,1,0:T(8,128)S(1)} %get-tuple-element.27, f32[8,20,132]{2,1,0:T(8,128)S(1)} %get-tuple-element.35, f32[4,10,22,134]{3,2,1,0:T(8,128)S(1)} %pad_maximum_fusion, ...), kind=kLoop, calls=%fused_computation.42 | loop fusion | flops 760320 | bytes 2703360 | tf_op jit(solution)/shard_map/mul | solution.py:60
  41.2 0.9 %broadcast_multiply_fusion.2 = (f32[3,6,18,130]{3,2,1,0:T(8,128)S(1)}, f32[3,6,18,130]{3,2,1,0:T(8,128)S(1)}) fusion(f32[6,18,130]{2,1,0:T(8,128)S(1)} %get-tuple-element.34, f32[3,8,20,132]{3,2,1,0:T(8,128)S(1)} %get-tuple-element.25, f32[6,18,130]{2,1,0:T(8,128)S(1)} %get-tuple-element.33, f32[4,10,22,134]{3,2,1,0:T(8,128)S(1)} %pad_maximum_fusion, ...), kind=kLoop, calls=%fused_computation.45 | loop fusion | flops 505440 | bytes 1797120 | tf_op jit(solution)/shard_map/mul | solution.py:60
  42.1 0.9 %multiply_reduce_fusion.9 = (f32[3,4,128]{2,1,0:T(4,128)S(1)}, f32[3,4,16,128]{3,2,1,0:T(8,128)}) fusion(f32[4,16,128]{2,1,0:T(8,128)S(1)} %copy-done.5, f32[3,6,18,130]{3,2,1,0:T(8,128)S(1)} %get-tuple-element.23, f32[3,4,16,128]{3,2,1,0:T(8,128)S(1)} %multiply_reduce_fusion.6, f32[4,16,128]{2,1,0:T(8,128)S(1)} %fusion.34, ...), kind=kLoop, calls=%fused_computation.80 | loop fusion | flops 317952 | bytes 956416 | tf_op jit(solution)/shard_map/reduce_sum | solution.py:259
  43.0 0.4 convolution_bitcast_fusion
  43.4 0.2 select_select_fusion
  43.6 14.8 %all_to_all.5 = f32[32,3,128]{2,1,0:T(4,128)S(1)} all-to-all(f32[32,3,128]{2,1,0:T(4,128)S(1)} %select_select_fusion), channel_id=1, replica_groups=mesh['circ'=4,'normal'=2,'span'=4] {'span','normal','circ'}, dimensions={0} | all-to-all | bytes 98304 | tf_op jit(solution)/shard_map/all_to_all | solution.py:224
  58.4 0.6 %reduce_sum.167 = f32[3,128]{1,0:T(4,128)} reduce(f32[32,3,128]{2,1,0:T(4,128)S(1)} %all_to_all.5, f32[]{:T(128)} %constant.18.clone.1), dimensions={0}, to_apply=%region_14.15 | reduce | flops 11904 | bytes 50692 | tf_op jit(solution)/shard_map/reduce_sum | solution.py:224
  (78 shorter events, 1.4 us)
Async XLA Ops:
  0.6 0.9 %copy-start = (f32[5,4,16,128]{3,2,1,0:T(8,128)S(1)}, f32[5,4,16,128]{3,2,1,0:T(8,128)}, u32[]{:S(2)}) copy-start(f32[5,4,16,128]{3,2,1,0:T(8,128)} %param.9) | copy-start | bytes 491524
  1.6 3.1 %copy-start.3 = (f32[3,4,16,128]{3,2,1,0:T(8,128)S(1)}, f32[3,4,16,128]{3,2,1,0:T(8,128)}, u32[]{:S(2)}) copy-start(f32[3,4,16,128]{3,2,1,0:T(8,128)} %param.11) | copy-start | bytes 294916
  1.6 15.1 %collective-permute-start.2 = (f32[6,4,8,128]{3,2,1,0:T(8,128)S(1)}, f32[6,4,8,128]{3,2,1,0:T(8,128)S(1)}, u32[]{:S(2)}, u32[]{:S(2)}) collective-permute-start(f32[6,4,8,128]{3,2,1,0:T(8,128)S(1)} %pad_maximum_fusion.2), channel_id=1, source_target_pairs={{0,4},{4,0},{1,5},{5,1},{2,6},{6,2},{3,7},{7,3},{8,12},{12,8},{9,1... | collective-permute-start | bytes 294920 | tf_op jit(solution)/shard_map/ppermute | solution.py:143
  4.7 11.8 %collective-permute-start.1 = (f32[6,1,16,128]{3,2,1,0:T(8,128)S(1)}, f32[6,1,16,128]{3,2,1,0:T(8,128)S(1)}, u32[]{:S(2)}, u32[]{:S(2)}) collective-permute-start(f32[6,1,16,128]{3,2,1,0:T(8,128)S(1)} %get-tuple-element.56), channel_id=1, source_target_pairs={{0,1},{1,2},{2,3},{4,5},{5,6},{6,7},{8,9},{9,10},{10,11},{12,13},{... | collective-permute-start | bytes 147464 | tf_op jit(solution)/shard_map/ppermute | solution.py:120
  6.2 10.4 %collective-permute-start = (f32[6,1,16,128]{3,2,1,0:T(8,128)S(1)}, f32[6,1,16,128]{3,2,1,0:T(8,128)S(1)}, u32[]{:S(2)}, u32[]{:S(2)}) collective-permute-start(f32[6,1,16,128]{3,2,1,0:T(8,128)S(1)} %get-tuple-element.57), channel_id=1, source_target_pairs={{1,0},{2,1},{3,2},{5,4},{6,5},{7,6},{9,8},{10,9},{11,10},{13,12},{... | collective-permute-start | bytes 147464 | tf_op jit(solution)/shard_map/ppermute | solution.py:120
  8.4 7.4 %collective-permute-start.4 = (f32[6,4,16,1]{2,0,3,1:T(8,128)S(1)}, f32[6,4,16,1]{2,0,3,1:T(8,128)S(1)}, u32[]{:S(2)}, u32[]{:S(2)}) collective-permute-start(f32[6,4,16,1]{2,0,3,1:T(8,128)S(1)} %get-tuple-element.67), channel_id=1, source_target_pairs={{0,8},{8,16},{16,24},{24,0},{1,9},{9,17},{17,25},{25,1},{2,10},{10... | collective-permute-start | bytes 4616 | tf_op jit(solution)/shard_map/ppermute | solution.py:120
  10.0 2.3 %copy-start.6 = (f32[3,5,5]{2,0,1:T(4,128)S(1)}, f32[3,5,5]{2,0,1:T(4,128)}, u32[]{:S(2)}) copy-start(f32[3,5,5]{2,0,1:T(4,128)} %param.12) | copy-start | bytes 904
  10.1 5.9 %collective-permute-start.3 = (f32[6,4,16,1]{2,0,3,1:T(8,128)S(1)}, f32[6,4,16,1]{2,0,3,1:T(8,128)S(1)}, u32[]{:S(2)}, u32[]{:S(2)}) collective-permute-start(f32[6,4,16,1]{2,0,3,1:T(8,128)S(1)} %get-tuple-element.68), channel_id=1, source_target_pairs={{0,24},{8,0},{16,8},{24,16},{1,25},{9,1},{17,9},{25,17},{2,26},{10... | collective-permute-start | bytes 4616 | tf_op jit(solution)/shard_map/ppermute | solution.py:120
  12.3 0.7 %copy-start.7 = (f32[3,5,5]{2,0,1:T(4,128)S(1)}, f32[3,5,5]{2,0,1:T(4,128)}, u32[]{:S(2)}) copy-start(f32[3,5,5]{2,0,1:T(4,128)} %param.13) | copy-start | bytes 904
  13.3 0.7 %copy-start.9 = (s32[4,128]{1,0:T(4,128)S(1)}, s32[4,128]{1,0:T(4,128)}, u32[]{:S(2)}) copy-start(s32[4,128]{1,0:T(4,128)} %param.17) | copy-start | bytes 6148
  15.1 0.7 %copy-start.8 = (f32[3,5]{1,0:T(4,128)S(1)}, f32[3,5]{1,0:T(4,128)}, u32[]{:S(2)}) copy-start(f32[3,5]{1,0:T(4,128)} %param.14) | copy-start | bytes 184
  16.5 0.9 %copy-start.4 = (f32[5,4,16,128]{3,2,1,0:T(8,128)S(1)}, f32[5,4,16,128]{3,2,1,0:T(8,128)}, u32[]{:S(2)}) copy-start(f32[5,4,16,128]{3,2,1,0:T(8,128)} %param.10) | copy-start | bytes 491524
  17.6 0.9 %copy-start.2 = (f32[5,4,16,128]{3,2,1,0:T(8,128)}, f32[5,4,16,128]{3,2,1,0:T(8,128)S(1)}, u32[]{:S(2)}) copy-start(f32[5,4,16,128]{3,2,1,0:T(8,128)S(1)} %fusion.15) | copy-start | bytes 491524
  17.7 0.8 %copy-start.1 = (f32[4,16,128]{2,1,0:T(8,128)S(1)}, f32[4,16,128]{2,1,0:T(8,128)}, u32[]{:S(2)}) copy-start(f32[4,16,128]{2,1,0:T(8,128)} %param.15) | copy-start | bytes 98308
  18.7 8.0 %collective-permute-start.5 = (f32[4,4,3,3]{3,2,1,0:T(4,128)S(1)}, f32[4,4,3,3]{3,2,1,0:T(4,128)S(1)}, u32[]{:S(2)}, u32[]{:S(2)}) collective-permute-start(f32[4,4,3,3]{3,2,1,0:T(4,128)S(1)} %get-tuple-element.47), channel_id=1, source_target_pairs={{0,12},{8,20},{16,28},{24,4},{4,8},{12,16},{20,24},{28,0},{1,13},{... | collective-permute-start | bytes 1736 | tf_op jit(solution)/shard_map/ppermute | solution.py:133
  19.3 12.4 %collective-permute-start.8 = (f32[4,4,16,3]{3,2,1,0:T(8,128)S(1)}, f32[4,4,16,3]{3,2,1,0:T(8,128)S(1)}, u32[]{:S(2)}, u32[]{:S(2)}) collective-permute-start(f32[4,4,16,3]{3,2,1,0:T(8,128)S(1)} %get-tuple-element.45), channel_id=1, source_target_pairs={{0,8},{8,16},{16,24},{24,0},{1,9},{9,17},{17,25},{25,1},{2,10},{10... | collective-permute-start | bytes 9224 | tf_op jit(solution)/shard_map/ppermute | solution.py:120
  20.9 10.8 %collective-permute-start.9 = (f32[4,4,16,3]{3,2,1,0:T(8,128)S(1)}, f32[4,4,16,3]{3,2,1,0:T(8,128)S(1)}, u32[]{:S(2)}, u32[]{:S(2)}) collective-permute-start(f32[4,4,16,3]{3,2,1,0:T(8,128)S(1)} %get-tuple-element.46), channel_id=1, source_target_pairs={{0,24},{8,0},{16,8},{24,16},{1,25},{9,1},{17,9},{25,17},{2,26},{10... | collective-permute-start | bytes 9224 | tf_op jit(solution)/shard_map/ppermute | solution.py:120
  23.2 8.4 %collective-permute-start.7 = (f32[4,4,3,3]{3,2,1,0:T(4,128)S(1)}, f32[4,4,3,3]{3,2,1,0:T(4,128)S(1)}, u32[]{:S(2)}, u32[]{:S(2)}) collective-permute-start(f32[4,4,3,3]{3,2,1,0:T(4,128)S(1)} %get-tuple-element.48), channel_id=1, source_target_pairs={{0,28},{8,4},{16,12},{24,20},{4,24},{12,0},{20,8},{28,16},{1,29},{... | collective-permute-start | bytes 1736 | tf_op jit(solution)/shard_map/ppermute | solution.py:133
  25.5 6.1 %collective-permute-start.6 = (f32[4,4,3,128]{3,2,1,0:T(4,128)S(1)}, f32[4,4,3,128]{3,2,1,0:T(4,128)S(1)}, u32[]{:S(2)}, u32[]{:S(2)}) collective-permute-start(f32[4,4,3,128]{3,2,1,0:T(4,128)S(1)} %fusion.29), channel_id=1, source_target_pairs={{0,4},{4,0},{1,5},{5,1},{2,6},{6,2},{3,7},{7,3},{8,12},{12,8},{9,1... | collective-permute-start | bytes 73736 | tf_op jit(solution)/shard_map/ppermute | solution.py:133
  32.1 3.4 %collective-permute-start.10 = (f32[4,3,22,134]{3,2,1,0:T(8,128)S(1)}, f32[4,3,22,134]{3,2,1,0:T(8,128)S(1)}, u32[]{:S(2)}, u32[]{:S(2)}) collective-permute-start(f32[4,3,22,134]{3,2,1,0:T(8,128)S(1)} %get-tuple-element.31), channel_id=1, source_target_pairs={{0,1},{1,2},{2,3},{4,5},{5,6},{6,7},{8,9},{9,10},{10,11},{12,13},{... | collective-permute-start | bytes 424520 | tf_op jit(solution)/shard_map/ppermute | solution.py:120
  34.1 5.0 %collective-permute-start.11 = (f32[4,3,22,134]{3,2,1,0:T(8,128)S(1)}, f32[4,3,22,134]{3,2,1,0:T(8,128)S(1)}, u32[]{:S(2)}, u32[]{:S(2)}) collective-permute-start(f32[4,3,22,134]{3,2,1,0:T(8,128)S(1)} %get-tuple-element.32), channel_id=1, source_target_pairs={{1,0},{2,1},{3,2},{5,4},{6,5},{7,6},{9,8},{10,9},{11,10},{13,12},{... | collective-permute-start | bytes 424520 | tf_op jit(solution)/shard_map/ppermute | solution.py:120
  41.2 0.9 %copy-start.5 = (f32[4,16,128]{2,1,0:T(8,128)S(1)}, f32[4,16,128]{2,1,0:T(8,128)}, u32[]{:S(2)}) copy-start(f32[4,16,128]{2,1,0:T(8,128)} %param.16) | copy-start | bytes 98308

commit v18 on v17

--- a/solution.py
+++ b/solution.py
@@ -159,18 +159,18 @@
 
 def padded_sweeps(joined, width):
     dims = {"span": 1, "normal": 2, "circ": 3}
-    before_c = receive(joined, {"circ": -1}, dims, width)
-    after_c = receive(joined, {"circ": 1}, dims, width)
+    before_s = receive(joined, {"span": -1}, dims, width)
+    after_s = receive(joined, {"span": 1}, dims, width)
     low_n, high_n = receive_pair(joined, {}, "normal", dims, width)
-    low_lc, high_lc = receive_pair(joined, {"circ": -1}, "normal", dims, width)
-    low_hc, high_hc = receive_pair(joined, {"circ": 1}, "normal", dims, width)
-    top = jnp.concatenate([low_lc, low_n, low_hc], axis=3)
-    middle = jnp.concatenate([before_c, joined, after_c], axis=3)
-    bottom = jnp.concatenate([high_lc, high_n, high_hc], axis=3)
+    low_ls, high_ls = receive_pair(joined, {"span": -1}, "normal", dims, width)
+    low_hs, high_hs = receive_pair(joined, {"span": 1}, "normal", dims, width)
+    top = jnp.concatenate([low_ls, low_n, low_hs], axis=1)
+    middle = jnp.concatenate([before_s, joined, after_s], axis=1)
+    bottom = jnp.concatenate([high_ls, high_n, high_hs], axis=1)
     plane = jnp.concatenate([top, middle, bottom], axis=2)
-    before_s = receive(plane, {"span": -1}, dims, width)
-    after_s = receive(plane, {"span": 1}, dims, width)
-    return jnp.concatenate([before_s, plane, after_s], axis=1)
+    before_c = receive(plane, {"circ": -1}, dims, width)
+    after_c = receive(plane, {"circ": 1}, dims, width)
+    return jnp.concatenate([before_c, plane, after_c], axis=3)
 
 
 def jac_apply(jac, term):

time: 59.6 us -> 75.5 us (1.27)
  waiting for transfers between devices: 8.73 us -> 24 us
  starting transfers between devices: 20.9 us -> 25.9 us
  blocking collectives: 14.8 us -> 10.5 us
    ppermute x8, waiting for transfers between devices: 3.72 us -> 20.1 us  [receive(): return lax.ppermute(take(array, rel, dims, width), axes, pairs)]
    all_to_all x1, blocking collectives: 14.8 us -> 10.5 us  [reduce_panels(): lax.all_to_all(chunks, ORDER[::-1], 0, 0, tiled=False)]
    ppermute x3, starting transfers between devices: 4.02 us -> 7.14 us  [receive_pair(): got = lax.ppermute(sent, axes, pairs + back)]
    ppermute x8, starting transfers between devices: 13.9 us -> 15.7 us  [receive(): return lax.ppermute(take(array, rel, dims, width), axes, pairs)]
    ppermute x3, waiting for transfers between devices: 5.01 us -> 3.82 us  [receive_pair(): got = lax.ppermute(sent, axes, pairs + back)]
  transfers between devices with their start and end apart: 12 -> 12, of which waited for: 2 -> 3; matrix products, arithmetic and copies ran while one was open for 5% -> 4% of each run, Pallas kernels for 0% -> 0%
where the time goes in v18:
time: 75.5 us; the launch traced here: 75 us
  starting transfers between devices  25.9 us (34%)
  waiting for transfers between devices  24 us (32%)
  blocking collectives  10.5 us (14%)
  other arithmetic  6.93 us (9%)
  local copies, waits for them, and re-layouts  6.03 us (8%)
  between operations  1.23 us (2%)
    ppermute x8, waiting for transfers between devices, receive(): return lax.ppermute(take(array, rel, dims, width), axes, pairs)  20.1 us
    ppermute x8, starting transfers between devices, receive(): return lax.ppermute(take(array, rel, dims, width), axes, pairs)  15.7 us
    all_to_all x1, blocking collectives, reduce_panels(): lax.all_to_all(chunks, ORDER[::-1], 0, 0, tiled=False)  10.5 us
    ppermute x3, starting transfers between devices, receive_pair(): got = lax.ppermute(sent, axes, pairs + back)  7.14 us
    unnamed x28, local copies, waits for them, and re-layouts  4.02 us
    ppermute x3, waiting for transfers between devices, receive_pair(): got = lax.ppermute(sent, axes, pairs + back)  3.82 us
    ppermute x1, starting transfers between devices, tile_halos(): got = lax.ppermute(sent, axis, [(0, 1), (1, 0)])  3.03 us
    mul x3, other arithmetic, relax(): weighted = stiff_pad[None] * mesh_pad  2.17 us
  transfers between devices with their start and end apart: 12, of which 3 were waited for; matrix products, arithmetic and copies ran while one was open for 4% of the time, Pallas kernels for 0%

profile of v18, /device:TPU:0, one launch (start us, length us, event | category | flops | bytes accessed | tf_op | source)
XLA Modules:
  0.0 75.0 jit_solution(5150478512258952480)
XLA Ops:
  0.6 0.8 %fusion.51 = (f32[1,4,16,128]{3,2,1,0:T(8,128)S(1)}, f32[4,16,128]{2,1,0:T(8,128)S(1)}, f32[4,16,128]{2,1,0:T(8,128)S(1)}) fusion(f32[3,4,16,128]{3,2,1,0:T(8,128)} %param.11), kind=kLoop, calls=%fused_computation.152 | loop fusion | bytes 163840 | tf_op jit(solution)/shard_map/slice | solution.py:188
  1.5 0.1 copy-done
  1.6 3.0 %collective-permute-start.2 = (f32[6,4,8,128]{3,2,1,0:T(8,128)S(1)}, f32[6,4,8,128]{3,2,1,0:T(8,128)S(1)}, u32[]{:S(2)}, u32[]{:S(2)}) collective-permute-start(f32[6,4,8,128]{3,2,1,0:T(8,128)S(1)} %pad_maximum_fusion.2), channel_id=1, source_target_pairs={{0,4},{4,0},{1,5},{5,1},{2,6},{6,2},{3,7},{7,3},{8,12},{12,8},{9,1... | collective-permute-start | bytes 294920 | tf_op jit(solution)/shard_map/ppermute | solution.py:143
  4.7 1.5 %collective-permute-start.1 = (f32[6,1,16,128]{3,2,1,0:T(8,128)S(1)}, f32[6,1,16,128]{3,2,1,0:T(8,128)S(1)}, u32[]{:S(2)}, u32[]{:S(2)}) collective-permute-start(f32[6,1,16,128]{3,2,1,0:T(8,128)S(1)} %get-tuple-element.56), channel_id=1, source_target_pairs={{0,1},{1,2},{2,3},{4,5},{5,6},{6,7},{8,9},{9,10},{10,11},{12,13},{... | collective-permute-start | bytes 147464 | tf_op jit(solution)/shard_map/ppermute | solution.py:120
  6.2 1.3 %collective-permute-start = (f32[6,1,16,128]{3,2,1,0:T(8,128)S(1)}, f32[6,1,16,128]{3,2,1,0:T(8,128)S(1)}, u32[]{:S(2)}, u32[]{:S(2)}) collective-permute-start(f32[6,1,16,128]{3,2,1,0:T(8,128)S(1)} %get-tuple-element.57), channel_id=1, source_target_pairs={{1,0},{2,1},{3,2},{5,4},{6,5},{7,6},{9,8},{10,9},{11,10},{13,12},{... | collective-permute-start | bytes 147464 | tf_op jit(solution)/shard_map/ppermute | solution.py:120
  7.5 0.1 fusion.48
  7.6 0.3 copy.93
  7.9 0.3 copy.94
  8.4 1.6 %collective-permute-start.4 = (f32[6,4,16,1]{2,0,3,1:T(8,128)S(1)}, f32[6,4,16,1]{2,0,3,1:T(8,128)S(1)}, u32[]{:S(2)}, u32[]{:S(2)}) collective-permute-start(f32[6,4,16,1]{2,0,3,1:T(8,128)S(1)} %get-tuple-element.63), channel_id=1, source_target_pairs={{0,8},{8,16},{16,24},{24,0},{1,9},{9,17},{17,25},{25,1},{2,10},{10... | collective-permute-start | bytes 4616 | tf_op jit(solution)/shard_map/ppermute | solution.py:120
  10.1 2.2 %collective-permute-start.3 = (f32[6,4,16,1]{2,0,3,1:T(8,128)S(1)}, f32[6,4,16,1]{2,0,3,1:T(8,128)S(1)}, u32[]{:S(2)}, u32[]{:S(2)}) collective-permute-start(f32[6,4,16,1]{2,0,3,1:T(8,128)S(1)} %get-tuple-element.64), channel_id=1, source_target_pairs={{0,24},{8,0},{16,8},{24,16},{1,25},{9,1},{17,9},{25,17},{2,26},{10... | collective-permute-start | bytes 4616 | tf_op jit(solution)/shard_map/ppermute | solution.py:120
  12.3 0.7 copy-done.7
  13.1 0.2 slice_reduce_fusion
  13.3 0.1 subtract_multiply_fusion
  13.5 0.7 copy-done.9
  14.2 0.5 multiply_reduce_fusion.2
  14.6 0.2 multiply_reduce_fusion
  14.9 0.1 multiply_reduce_fusion.4
  15.1 0.6 copy-done.8
  15.9 0.1 multiply_reduce_fusion.10
  16.0 0.1 multiply_reduce_fusion.11
  16.1 0.2 copy.82
  16.3 0.2 copy.80
  16.6 0.1 multiply_reduce_fusion.7
  16.9 0.1 multiply_reduce_fusion.12
  17.0 0.5 copy-done.4
  17.5 0.2 fusion.15
  17.8 0.7 copy-done.1
  18.5 4.6 %collective-permute-start.5 = (f32[4,3,3,128]{3,2,1,0:T(4,128)S(1)}, f32[4,3,3,128]{3,2,1,0:T(4,128)S(1)}, u32[]{:S(2)}, u32[]{:S(2)}) collective-permute-start(f32[4,3,3,128]{3,2,1,0:T(4,128)S(1)} %get-tuple-element.47), channel_id=1, source_target_pairs={{0,5},{1,6},{2,7},{4,1},{5,2},{6,3},{8,13},{9,14},{10,15},{12,9},{... | collective-permute-start | bytes 55304 | tf_op jit(solution)/shard_map/ppermute | solution.py:133
  23.1 3.9 %collective-permute-start.8 = (f32[4,3,16,128]{3,2,1,0:T(8,128)S(1)}, f32[4,3,16,128]{3,2,1,0:T(8,128)S(1)}, u32[]{:S(2)}, u32[]{:S(2)}) collective-permute-start(f32[4,3,16,128]{3,2,1,0:T(8,128)S(1)} %get-tuple-element.45), channel_id=1, source_target_pairs={{0,1},{1,2},{2,3},{4,5},{5,6},{6,7},{8,9},{9,10},{10,11},{12,13},{... | collective-permute-start | bytes 294920 | tf_op jit(solution)/shard_map/ppermute | solution.py:120
  27.0 1.3 %collective-permute-start.9 = (f32[4,3,16,128]{3,2,1,0:T(8,128)S(1)}, f32[4,3,16,128]{3,2,1,0:T(8,128)S(1)}, u32[]{:S(2)}, u32[]{:S(2)}) collective-permute-start(f32[4,3,16,128]{3,2,1,0:T(8,128)S(1)} %get-tuple-element.46), channel_id=1, source_target_pairs={{1,0},{2,1},{3,2},{5,4},{6,5},{7,6},{9,8},{10,9},{11,10},{13,12},{... | collective-permute-start | bytes 294920 | tf_op jit(solution)/shard_map/ppermute | solution.py:120
  28.3 1.3 %collective-permute-start.6 = (f32[4,4,3,128]{3,2,1,0:T(4,128)S(1)}, f32[4,4,3,128]{3,2,1,0:T(4,128)S(1)}, u32[]{:S(2)}, u32[]{:S(2)}) collective-permute-start(f32[4,4,3,128]{3,2,1,0:T(4,128)S(1)} %fusion.26), channel_id=1, source_target_pairs={{0,4},{4,0},{1,5},{5,1},{2,6},{6,2},{3,7},{7,3},{8,12},{12,8},{9,1... | collective-permute-start | bytes 73736 | tf_op jit(solution)/shard_map/ppermute | solution.py:133
  29.6 1.3 %collective-permute-start.7 = (f32[4,3,3,128]{3,2,1,0:T(4,128)S(1)}, f32[4,3,3,128]{3,2,1,0:T(4,128)S(1)}, u32[]{:S(2)}, u32[]{:S(2)}) collective-permute-start(f32[4,3,3,128]{3,2,1,0:T(4,128)S(1)} %get-tuple-element.48), channel_id=1, source_target_pairs={{1,4},{2,5},{3,6},{5,0},{6,1},{7,2},{9,12},{10,13},{11,14},{13,8},... | collective-permute-start | bytes 55304 | tf_op jit(solution)/shard_map/ppermute | solution.py:133
  30.9 3.8 %collective-permute-done.7 = f32[4,3,3,128]{3,2,1,0:T(4,128)S(1)} collective-permute-done((f32[4,3,3,128]{3,2,1,0:T(4,128)S(1)}, f32[4,3,3,128]{3,2,1,0:T(4,128)S(1)}, u32[]{:S(2)}, u32[]{:S(2)}) %collective-permute-start.7) | collective-permute-done | bytes 18464 | tf_op jit(solution)/shard_map/ppermute | solution.py:133
  34.9 0.2 fusion.47
  35.2 3.8 %collective-permute-start.11 = (f32[4,10,22,3]{3,2,1,0:T(8,128)S(1)}, f32[4,10,22,3]{3,2,1,0:T(8,128)S(1)}, u32[]{:S(2)}, u32[]{:S(2)}) collective-permute-start(f32[4,10,22,3]{3,2,1,0:T(8,128)S(1)} %get-tuple-element.32), channel_id=1, source_target_pairs={{0,24},{8,0},{16,8},{24,16},{1,25},{9,1},{17,9},{25,17},{2,26},{10... | collective-permute-start | bytes 31688 | tf_op jit(solution)/shard_map/ppermute | solution.py:120
  39.0 11.5 %collective-permute-done.10 = f32[4,10,22,3]{3,2,1,0:T(8,128)S(1)} collective-permute-done((f32[4,10,22,3]{3,2,1,0:T(8,128)S(1)}, f32[4,10,22,3]{3,2,1,0:T(8,128)S(1)}, u32[]{:S(2)}, u32[]{:S(2)}) %collective-permute-start.10) | collective-permute-done | bytes 10592 | tf_op jit(solution)/shard_map/ppermute | solution.py:120
  50.4 8.7 %collective-permute-done.11 = f32[4,10,22,3]{3,2,1,0:T(8,128)S(1)} collective-permute-done((f32[4,10,22,3]{3,2,1,0:T(8,128)S(1)}, f32[4,10,22,3]{3,2,1,0:T(8,128)S(1)}, u32[]{:S(2)}, u32[]{:S(2)}) %collective-permute-start.11) | collective-permute-done | bytes 10592 | tf_op jit(solution)/shard_map/ppermute | solution.py:120
  59.1 0.6 pad_maximum_fusion
  59.8 0.1 multiply_add_fusion
  59.9 0.1 multiply_add_fusion.1
  60.1 0.1 broadcast_multiply_fusion
  60.2 1.2 %broadcast_multiply_fusion.1 = (f32[3,8,20,132]{3,2,1,0:T(8,128)S(1)}, f32[3,8,20,132]{3,2,1,0:T(8,128)S(1)}) fusion(f32[8,20,132]{2,1,0:T(8,128)S(1)} %get-tuple-element.36, f32[3,10,22,134]{3,2,1,0:T(8,128)S(1)} %get-tuple-element.27, f32[8,20,132]{2,1,0:T(8,128)S(1)} %get-tuple-element.35, f32[4,10,22,134]{3,2,1,0:T(8,128)S(1)} %pad_maximum_fusion, ...), kind=kLoop, calls=%fused_computation.42 | loop fusion | flops 760320 | bytes 2703360 | tf_op jit(solution)/shard_map/mul | solution.py:60
  61.4 0.9 %broadcast_multiply_fusion.2 = (f32[3,6,18,130]{3,2,1,0:T(8,128)S(1)}, f32[3,6,18,130]{3,2,1,0:T(8,128)S(1)}) fusion(f32[6,18,130]{2,1,0:T(8,128)S(1)} %get-tuple-element.34, f32[3,8,20,132]{3,2,1,0:T(8,128)S(1)} %get-tuple-element.25, f32[6,18,130]{2,1,0:T(8,128)S(1)} %get-tuple-element.33, f32[4,10,22,134]{3,2,1,0:T(8,128)S(1)} %pad_maximum_fusion, ...), kind=kLoop, calls=%fused_computation.45 | loop fusion | flops 505440 | bytes 1797120 | tf_op jit(solution)/shard_map/mul | solution.py:60
  62.3 0.9 %multiply_reduce_fusion.9 = (f32[3,4,128]{2,1,0:T(4,128)S(1)}, f32[3,4,16,128]{3,2,1,0:T(8,128)}) fusion(f32[4,16,128]{2,1,0:T(8,128)S(1)} %copy-done.5, f32[3,6,18,130]{3,2,1,0:T(8,128)S(1)} %get-tuple-element.23, f32[3,4,16,128]{3,2,1,0:T(8,128)S(1)} %multiply_reduce_fusion.6, f32[4,16,128]{2,1,0:T(8,128)S(1)} %fusion.28, ...), kind=kLoop, calls=%fused_computation.80 | loop fusion | flops 317952 | bytes 956416 | tf_op jit(solution)/shard_map/reduce_sum | solution.py:259
  63.2 0.4 convolution_bitcast_fusion
  63.6 0.2 select_select_fusion
  63.8 10.5 %all_to_all.5 = f32[32,3,128]{2,1,0:T(4,128)S(1)} all-to-all(f32[32,3,128]{2,1,0:T(4,128)S(1)} %select_select_fusion), channel_id=1, replica_groups=mesh['circ'=4,'normal'=2,'span'=4] {'span','normal','circ'}, dimensions={0} | all-to-all | bytes 98304 | tf_op jit(solution)/shard_map/all_to_all | solution.py:224
  74.3 0.6 reduce_sum.167
  (78 shorter events, 1.4 us)
Async XLA Ops:
  0.6 0.9 %copy-start = (f32[5,4,16,128]{3,2,1,0:T(8,128)S(1)}, f32[5,4,16,128]{3,2,1,0:T(8,128)}, u32[]{:S(2)}) copy-start(f32[5,4,16,128]{3,2,1,0:T(8,128)} %param.9) | copy-start | bytes 491524
  1.6 3.1 %copy-start.3 = (f32[3,4,16,128]{3,2,1,0:T(8,128)S(1)}, f32[3,4,16,128]{3,2,1,0:T(8,128)}, u32[]{:S(2)}) copy-start(f32[3,4,16,128]{3,2,1,0:T(8,128)} %param.11) | copy-start | bytes 294916
  1.6 15.1 %collective-permute-start.2 = (f32[6,4,8,128]{3,2,1,0:T(8,128)S(1)}, f32[6,4,8,128]{3,2,1,0:T(8,128)S(1)}, u32[]{:S(2)}, u32[]{:S(2)}) collective-permute-start(f32[6,4,8,128]{3,2,1,0:T(8,128)S(1)} %pad_maximum_fusion.2), channel_id=1, source_target_pairs={{0,4},{4,0},{1,5},{5,1},{2,6},{6,2},{3,7},{7,3},{8,12},{12,8},{9,1... | collective-permute-start | bytes 294920 | tf_op jit(solution)/shard_map/ppermute | solution.py:143
  4.7 11.8 %collective-permute-start.1 = (f32[6,1,16,128]{3,2,1,0:T(8,128)S(1)}, f32[6,1,16,128]{3,2,1,0:T(8,128)S(1)}, u32[]{:S(2)}, u32[]{:S(2)}) collective-permute-start(f32[6,1,16,128]{3,2,1,0:T(8,128)S(1)} %get-tuple-element.56), channel_id=1, source_target_pairs={{0,1},{1,2},{2,3},{4,5},{5,6},{6,7},{8,9},{9,10},{10,11},{12,13},{... | collective-permute-start | bytes 147464 | tf_op jit(solution)/shard_map/ppermute | solution.py:120
  6.2 10.4 %collective-permute-start = (f32[6,1,16,128]{3,2,1,0:T(8,128)S(1)}, f32[6,1,16,128]{3,2,1,0:T(8,128)S(1)}, u32[]{:S(2)}, u32[]{:S(2)}) collective-permute-start(f32[6,1,16,128]{3,2,1,0:T(8,128)S(1)} %get-tuple-element.57), channel_id=1, source_target_pairs={{1,0},{2,1},{3,2},{5,4},{6,5},{7,6},{9,8},{10,9},{11,10},{13,12},{... | collective-permute-start | bytes 147464 | tf_op jit(solution)/shard_map/ppermute | solution.py:120
  8.4 7.4 %collective-permute-start.4 = (f32[6,4,16,1]{2,0,3,1:T(8,128)S(1)}, f32[6,4,16,1]{2,0,3,1:T(8,128)S(1)}, u32[]{:S(2)}, u32[]{:S(2)}) collective-permute-start(f32[6,4,16,1]{2,0,3,1:T(8,128)S(1)} %get-tuple-element.63), channel_id=1, source_target_pairs={{0,8},{8,16},{16,24},{24,0},{1,9},{9,17},{17,25},{25,1},{2,10},{10... | collective-permute-start | bytes 4616 | tf_op jit(solution)/shard_map/ppermute | solution.py:120
  10.0 2.3 %copy-start.6 = (f32[3,5,5]{2,0,1:T(4,128)S(1)}, f32[3,5,5]{2,0,1:T(4,128)}, u32[]{:S(2)}) copy-start(f32[3,5,5]{2,0,1:T(4,128)} %param.12) | copy-start | bytes 904
  10.1 6.0 %collective-permute-start.3 = (f32[6,4,16,1]{2,0,3,1:T(8,128)S(1)}, f32[6,4,16,1]{2,0,3,1:T(8,128)S(1)}, u32[]{:S(2)}, u32[]{:S(2)}) collective-permute-start(f32[6,4,16,1]{2,0,3,1:T(8,128)S(1)} %get-tuple-element.64), channel_id=1, source_target_pairs={{0,24},{8,0},{16,8},{24,16},{1,25},{9,1},{17,9},{25,17},{2,26},{10... | collective-permute-start | bytes 4616 | tf_op jit(solution)/shard_map/ppermute | solution.py:120
  12.3 0.7 copy-start.7
  13.5 0.7 copy-start.9
  15.1 0.7 copy-start.8
  16.6 0.9 %copy-start.4 = (f32[5,4,16,128]{3,2,1,0:T(8,128)S(1)}, f32[5,4,16,128]{3,2,1,0:T(8,128)}, u32[]{:S(2)}) copy-start(f32[5,4,16,128]{3,2,1,0:T(8,128)} %param.10) | copy-start | bytes 491524
  17.7 0.8 %copy-start.2 = (f32[5,4,16,128]{3,2,1,0:T(8,128)}, f32[5,4,16,128]{3,2,1,0:T(8,128)S(1)}, u32[]{:S(2)}) copy-start(f32[5,4,16,128]{3,2,1,0:T(8,128)S(1)} %fusion.15) | copy-start | bytes 491524
  17.7 0.8 %copy-start.1 = (f32[4,16,128]{2,1,0:T(8,128)S(1)}, f32[4,16,128]{2,1,0:T(8,128)}, u32[]{:S(2)}) copy-start(f32[4,16,128]{2,1,0:T(8,128)} %param.15) | copy-start | bytes 98308
  18.5 12.4 %collective-permute-start.5 = (f32[4,3,3,128]{3,2,1,0:T(4,128)S(1)}, f32[4,3,3,128]{3,2,1,0:T(4,128)S(1)}, u32[]{:S(2)}, u32[]{:S(2)}) collective-permute-start(f32[4,3,3,128]{3,2,1,0:T(4,128)S(1)} %get-tuple-element.47), channel_id=1, source_target_pairs={{0,5},{1,6},{2,7},{4,1},{5,2},{6,3},{8,13},{9,14},{10,15},{12,9},{... | collective-permute-start | bytes 55304 | tf_op jit(solution)/shard_map/ppermute | solution.py:133
  23.1 11.7 %collective-permute-start.8 = (f32[4,3,16,128]{3,2,1,0:T(8,128)S(1)}, f32[4,3,16,128]{3,2,1,0:T(8,128)S(1)}, u32[]{:S(2)}, u32[]{:S(2)}) collective-permute-start(f32[4,3,16,128]{3,2,1,0:T(8,128)S(1)} %get-tuple-element.45), channel_id=1, source_target_pairs={{0,1},{1,2},{2,3},{4,5},{5,6},{6,7},{8,9},{9,10},{10,11},{12,13},{... | collective-permute-start | bytes 294920 | tf_op jit(solution)/shard_map/ppermute | solution.py:120
  27.0 7.8 %collective-permute-start.9 = (f32[4,3,16,128]{3,2,1,0:T(8,128)S(1)}, f32[4,3,16,128]{3,2,1,0:T(8,128)S(1)}, u32[]{:S(2)}, u32[]{:S(2)}) collective-permute-start(f32[4,3,16,128]{3,2,1,0:T(8,128)S(1)} %get-tuple-element.46), channel_id=1, source_target_pairs={{1,0},{2,1},{3,2},{5,4},{6,5},{7,6},{9,8},{10,9},{11,10},{13,12},{... | collective-permute-start | bytes 294920 | tf_op jit(solution)/shard_map/ppermute | solution.py:120
  28.3 6.4 %collective-permute-start.6 = (f32[4,4,3,128]{3,2,1,0:T(4,128)S(1)}, f32[4,4,3,128]{3,2,1,0:T(4,128)S(1)}, u32[]{:S(2)}, u32[]{:S(2)}) collective-permute-start(f32[4,4,3,128]{3,2,1,0:T(4,128)S(1)} %fusion.26), channel_id=1, source_target_pairs={{0,4},{4,0},{1,5},{5,1},{2,6},{6,2},{3,7},{7,3},{8,12},{12,8},{9,1... | collective-permute-start | bytes 73736 | tf_op jit(solution)/shard_map/ppermute | solution.py:133
  29.6 5.1 %collective-permute-start.7 = (f32[4,3,3,128]{3,2,1,0:T(4,128)S(1)}, f32[4,3,3,128]{3,2,1,0:T(4,128)S(1)}, u32[]{:S(2)}, u32[]{:S(2)}) collective-permute-start(f32[4,3,3,128]{3,2,1,0:T(4,128)S(1)} %get-tuple-element.48), channel_id=1, source_target_pairs={{1,4},{2,5},{3,6},{5,0},{6,1},{7,2},{9,12},{10,13},{11,14},{13,8},... | collective-permute-start | bytes 55304 | tf_op jit(solution)/shard_map/ppermute | solution.py:133
  35.1 15.3 %collective-permute-start.10 = (f32[4,10,22,3]{3,2,1,0:T(8,128)S(1)}, f32[4,10,22,3]{3,2,1,0:T(8,128)S(1)}, u32[]{:S(2)}, u32[]{:S(2)}) collective-permute-start(f32[4,10,22,3]{3,2,1,0:T(8,128)S(1)} %get-tuple-element.31), channel_id=1, source_target_pairs={{0,8},{8,16},{16,24},{24,0},{1,9},{9,17},{17,25},{25,1},{2,10},{10... | collective-permute-start | bytes 31688 | tf_op jit(solution)/shard_map/ppermute | solution.py:120
  35.2 23.9 %collective-permute-start.11 = (f32[4,10,22,3]{3,2,1,0:T(8,128)S(1)}, f32[4,10,22,3]{3,2,1,0:T(8,128)S(1)}, u32[]{:S(2)}, u32[]{:S(2)}) collective-permute-start(f32[4,10,22,3]{3,2,1,0:T(8,128)S(1)} %get-tuple-element.32), channel_id=1, source_target_pairs={{0,24},{8,0},{16,8},{24,16},{1,25},{9,1},{17,9},{25,17},{2,26},{10... | collective-permute-start | bytes 31688 | tf_op jit(solution)/shard_map/ppermute | solution.py:120
  61.4 0.9 %copy-start.5 = (f32[4,16,128]{2,1,0:T(8,128)S(1)}, f32[4,16,128]{2,1,0:T(8,128)}, u32[]{:S(2)}) copy-start(f32[4,16,128]{2,1,0:T(8,128)} %param.16) | copy-start | bytes 98308

commit v19 on v17

--- a/solution.py
+++ b/solution.py
@@ -114,10 +114,16 @@
     return array
 
 
-def receive(array, rel, dims, width):
+def receive(array, rel, dims, width, pack=False):
     rel = {a: r for a, r in rel.items() if r}
     axes, pairs = pairs_for({a: -r for a, r in rel.items()})
-    return lax.ppermute(take(array, rel, dims, width), axes, pairs)
+    slab = take(array, rel, dims, width)
+    if not pack:
+        return lax.ppermute(slab, axes, pairs)
+    size = slab.size
+    rows = -(-size // 1024) * 8
+    flat = jnp.pad(slab.reshape(-1), (0, rows * 128 - size)).reshape(rows, 128)
+    return lax.ppermute(flat, axes, pairs).reshape(-1)[:size].reshape(slab.shape)
 
 
 def receive_pair(array, rel, axis, dims, width):
@@ -168,8 +174,8 @@
     middle = jnp.concatenate([before_c, joined, after_c], axis=3)
     bottom = jnp.concatenate([high_lc, high_n, high_hc], axis=3)
     plane = jnp.concatenate([top, middle, bottom], axis=2)
-    before_s = receive(plane, {"span": -1}, dims, width)
-    after_s = receive(plane, {"span": 1}, dims, width)
+    before_s = receive(plane, {"span": -1}, dims, width, True)
+    after_s = receive(plane, {"span": 1}, dims, width, True)
     return jnp.concatenate([before_s, plane, after_s], axis=1)
 
 

time: 59.6 us -> 58.6 us (0.983)
  blocking collectives: 14.8 us -> 13.4 us
  local copies, waits for them, and re-layouts: 5.88 us -> 6.76 us
    all_to_all x1, blocking collectives: 14.8 us -> 13.4 us  [reduce_panels(): lax.all_to_all(chunks, ORDER[::-1], 0, 0, tiled=False)]
    reshape x0 -> x6, local copies, waits for them, and re-layouts: none -> 0.88 us  [the longest x2 0.45 us: receive(): lax.ppermute(flat, axes, pairs).reshape(-1)[:size].reshape(slab.shape)]
  transfers between devices with their start and end apart: 12 -> 12, of which waited for: 2 -> 2; matrix products, arithmetic and copies ran while one was open for 5% -> 6% of each run, Pallas kernels for 0% -> 0%
where the time goes in v19:
time: 58.6 us; the launch traced here: 58.1 us
  starting transfers between devices  20.9 us (36%)
  blocking collectives  13.4 us (23%)
  waiting for transfers between devices  8.29 us (14%)
  other arithmetic  7.04 us (12%)
  local copies, waits for them, and re-layouts  6.76 us (12%)
  between operations  1.27 us (2%)
    all_to_all x1, blocking collectives, reduce_panels(): lax.all_to_all(chunks, ORDER[::-1], 0, 0, tiled=False)  13.4 us
    ppermute x6, starting transfers between devices, receive(): return lax.ppermute(slab, axes, pairs)  10.5 us
    ppermute x3, waiting for transfers between devices, receive_pair(): got = lax.ppermute(sent, axes, pairs + back)  5.01 us
    unnamed x28, local copies, waits for them, and re-layouts  4.02 us
    ppermute x3, starting transfers between devices, receive_pair(): got = lax.ppermute(sent, axes, pairs + back)  4.02 us
    ppermute x2, starting transfers between devices, receive(): lax.ppermute(flat, axes, pairs).reshape(-1)[:size].reshape(slab.shape)  3.32 us
    ppermute x2, waiting for transfers between devices, receive(): lax.ppermute(flat, axes, pairs).reshape(-1)[:size].reshape(slab.shape)  3.27 us
    ppermute x1, starting transfers between devices, tile_halos(): got = lax.ppermute(sent, axis, [(0, 1), (1, 0)])  3.03 us
  transfers between devices with their start and end apart: 12, of which 2 were waited for; matrix products, arithmetic and copies ran while one was open for 6% of the time, Pallas kernels for 0%

profile of v19, /device:TPU:0, one launch (start us, length us, event | category | flops | bytes accessed | tf_op | source)
XLA Modules:
  0.0 58.1 jit_solution(6204057807770051736)
XLA Ops:
  0.6 0.8 %fusion.51 = (f32[1,4,16,128]{3,2,1,0:T(8,128)S(1)}, f32[4,16,128]{2,1,0:T(8,128)S(1)}, f32[4,16,128]{2,1,0:T(8,128)S(1)}) fusion(f32[3,4,16,128]{3,2,1,0:T(8,128)} %param.11), kind=kLoop, calls=%fused_computation.154 | loop fusion | bytes 163840 | tf_op jit(solution)/shard_map/slice | solution.py:194
  1.5 0.1 copy-done
  1.6 3.0 %collective-permute-start.2 = (f32[6,4,8,128]{3,2,1,0:T(8,128)S(1)}, f32[6,4,8,128]{3,2,1,0:T(8,128)S(1)}, u32[]{:S(2)}, u32[]{:S(2)}) collective-permute-start(f32[6,4,8,128]{3,2,1,0:T(8,128)S(1)} %pad_maximum_fusion.2), channel_id=1, source_target_pairs={{0,4},{4,0},{1,5},{5,1},{2,6},{6,2},{3,7},{7,3},{8,12},{12,8},{9,1... | collective-permute-start | bytes 294920 | tf_op jit(solution)/shard_map/ppermute | solution.py:149
  4.7 1.5 %collective-permute-start.1 = (f32[6,1,16,128]{3,2,1,0:T(8,128)S(1)}, f32[6,1,16,128]{3,2,1,0:T(8,128)S(1)}, u32[]{:S(2)}, u32[]{:S(2)}) collective-permute-start(f32[6,1,16,128]{3,2,1,0:T(8,128)S(1)} %get-tuple-element.56), channel_id=1, source_target_pairs={{0,1},{1,2},{2,3},{4,5},{5,6},{6,7},{8,9},{9,10},{10,11},{12,13},{... | collective-permute-start | bytes 147464 | tf_op jit(solution)/shard_map/ppermute | solution.py:122
  6.2 1.3 %collective-permute-start = (f32[6,1,16,128]{3,2,1,0:T(8,128)S(1)}, f32[6,1,16,128]{3,2,1,0:T(8,128)S(1)}, u32[]{:S(2)}, u32[]{:S(2)}) collective-permute-start(f32[6,1,16,128]{3,2,1,0:T(8,128)S(1)} %get-tuple-element.57), channel_id=1, source_target_pairs={{1,0},{2,1},{3,2},{5,4},{6,5},{7,6},{9,8},{10,9},{11,10},{13,12},{... | collective-permute-start | bytes 147464 | tf_op jit(solution)/shard_map/ppermute | solution.py:122
  7.6 0.3 copy.113
  7.9 0.3 copy.114
  8.4 1.6 %collective-permute-start.4 = (f32[6,4,16,1]{2,0,3,1:T(8,128)S(1)}, f32[6,4,16,1]{2,0,3,1:T(8,128)S(1)}, u32[]{:S(2)}, u32[]{:S(2)}) collective-permute-start(f32[6,4,16,1]{2,0,3,1:T(8,128)S(1)} %get-tuple-element.67), channel_id=1, source_target_pairs={{0,8},{8,16},{16,24},{24,0},{1,9},{9,17},{17,25},{25,1},{2,10},{10... | collective-permute-start | bytes 4616 | tf_op jit(solution)/shard_map/ppermute | solution.py:122
  10.1 2.2 %collective-permute-start.3 = (f32[6,4,16,1]{2,0,3,1:T(8,128)S(1)}, f32[6,4,16,1]{2,0,3,1:T(8,128)S(1)}, u32[]{:S(2)}, u32[]{:S(2)}) collective-permute-start(f32[6,4,16,1]{2,0,3,1:T(8,128)S(1)} %get-tuple-element.68), channel_id=1, source_target_pairs={{0,24},{8,0},{16,8},{24,16},{1,25},{9,1},{17,9},{25,17},{2,26},{10... | collective-permute-start | bytes 4616 | tf_op jit(solution)/shard_map/ppermute | solution.py:122
  12.3 0.7 %copy-done.7 = f32[3,5,5]{2,0,1:T(4,128)S(1)} copy-done((f32[3,5,5]{2,0,1:T(4,128)S(1)}, f32[3,5,5]{2,0,1:T(4,128)}, u32[]{:S(2)}) %copy-start.7) | copy-done | bytes 324
  13.1 0.1 subtract_multiply_fusion
  13.3 0.7 %copy-done.9 = s32[4,128]{1,0:T(4,128)S(1)} copy-done((s32[4,128]{1,0:T(4,128)S(1)}, s32[4,128]{1,0:T(4,128)}, u32[]{:S(2)}) %copy-start.9) | copy-done | bytes 2072
  14.0 0.5 multiply_reduce_fusion.2
  14.5 0.2 multiply_reduce_fusion
  14.7 0.1 multiply_reduce_fusion.4
  14.9 0.2 slice_reduce_fusion
  15.1 0.6 %copy-done.8 = f32[3,5]{1,0:T(4,128)S(1)} copy-done((f32[3,5]{1,0:T(4,128)S(1)}, f32[3,5]{1,0:T(4,128)}, u32[]{:S(2)}) %copy-start.8) | copy-done | bytes 84
  16.1 0.2 copy.102
  16.3 0.2 copy.100
  16.6 0.1 multiply_reduce_fusion.7
  17.0 0.5 copy-done.4
  17.5 0.2 fusion.15
  17.8 0.7 %copy-done.1 = f32[4,16,128]{2,1,0:T(8,128)S(1)} copy-done((f32[4,16,128]{2,1,0:T(8,128)S(1)}, f32[4,16,128]{2,1,0:T(8,128)}, u32[]{:S(2)}) %copy-start.1) | copy-done | bytes 32792
  18.7 0.6 %collective-permute-start.5 = (f32[4,4,3,3]{3,2,1,0:T(4,128)S(1)}, f32[4,4,3,3]{3,2,1,0:T(4,128)S(1)}, u32[]{:S(2)}, u32[]{:S(2)}) collective-permute-start(f32[4,4,3,3]{3,2,1,0:T(4,128)S(1)} %get-tuple-element.47), channel_id=1, source_target_pairs={{0,12},{8,20},{16,28},{24,4},{4,8},{12,16},{20,24},{28,0},{1,13},{... | collective-permute-start | bytes 1736 | tf_op jit(solution)/shard_map/ppermute | solution.py:139
  19.3 1.6 %collective-permute-start.8 = (f32[4,4,16,3]{3,2,1,0:T(8,128)S(1)}, f32[4,4,16,3]{3,2,1,0:T(8,128)S(1)}, u32[]{:S(2)}, u32[]{:S(2)}) collective-permute-start(f32[4,4,16,3]{3,2,1,0:T(8,128)S(1)} %get-tuple-element.45), channel_id=1, source_target_pairs={{0,8},{8,16},{16,24},{24,0},{1,9},{9,17},{17,25},{25,1},{2,10},{10... | collective-permute-start | bytes 9224 | tf_op jit(solution)/shard_map/ppermute | solution.py:122
  20.9 2.3 %collective-permute-start.9 = (f32[4,4,16,3]{3,2,1,0:T(8,128)S(1)}, f32[4,4,16,3]{3,2,1,0:T(8,128)S(1)}, u32[]{:S(2)}, u32[]{:S(2)}) collective-permute-start(f32[4,4,16,3]{3,2,1,0:T(8,128)S(1)} %get-tuple-element.46), channel_id=1, source_target_pairs={{0,24},{8,0},{16,8},{24,16},{1,25},{9,1},{17,9},{25,17},{2,26},{10... | collective-permute-start | bytes 9224 | tf_op jit(solution)/shard_map/ppermute | solution.py:122
  23.2 2.3 %collective-permute-start.7 = (f32[4,4,3,3]{3,2,1,0:T(4,128)S(1)}, f32[4,4,3,3]{3,2,1,0:T(4,128)S(1)}, u32[]{:S(2)}, u32[]{:S(2)}) collective-permute-start(f32[4,4,3,3]{3,2,1,0:T(4,128)S(1)} %get-tuple-element.48), channel_id=1, source_target_pairs={{0,28},{8,4},{16,12},{24,20},{4,24},{12,0},{20,8},{28,16},{1,29},{... | collective-permute-start | bytes 1736 | tf_op jit(solution)/shard_map/ppermute | solution.py:139
  25.5 1.1 %collective-permute-start.6 = (f32[4,4,3,128]{3,2,1,0:T(4,128)S(1)}, f32[4,4,3,128]{3,2,1,0:T(4,128)S(1)}, u32[]{:S(2)}, u32[]{:S(2)}) collective-permute-start(f32[4,4,3,128]{3,2,1,0:T(4,128)S(1)} %fusion.29), channel_id=1, source_target_pairs={{0,4},{4,0},{1,5},{5,1},{2,6},{6,2},{3,7},{7,3},{8,12},{12,8},{9,1... | collective-permute-start | bytes 73736 | tf_op jit(solution)/shard_map/ppermute | solution.py:139
  26.6 5.0 %collective-permute-done.7 = f32[4,4,3,3]{3,2,1,0:T(4,128)S(1)} collective-permute-done((f32[4,4,3,3]{3,2,1,0:T(4,128)S(1)}, f32[4,4,3,3]{3,2,1,0:T(4,128)S(1)}, u32[]{:S(2)}, u32[]{:S(2)}) %collective-permute-start.7) | collective-permute-done | bytes 608 | tf_op jit(solution)/shard_map/ppermute | solution.py:139
  31.7 0.3 maximum_maximum_fusion
  32.1 0.2 reshape.159
  32.3 2.0 %collective-permute-start.10 = (f32[280,128]{1,0:T(8,128)S(1)}, f32[280,128]{1,0:T(8,128)S(1)}, u32[]{:S(2)}, u32[]{:S(2)}) collective-permute-start(f32[280,128]{1,0:T(8,128)S(1)} %pad_bitcast_fusion.1), channel_id=1, source_target_pairs={{0,1},{1,2},{2,3},{4,5},{5,6},{6,7},{8,9},{9,10},{10,11},{12,13},{... | collective-permute-start | bytes 430088 | tf_op jit(solution)/shard_map/ppermute | solution.py:126
  34.4 0.2 reshape.163
  34.6 1.3 %collective-permute-start.11 = (f32[280,128]{1,0:T(8,128)S(1)}, f32[280,128]{1,0:T(8,128)S(1)}, u32[]{:S(2)}, u32[]{:S(2)}) collective-permute-start(f32[280,128]{1,0:T(8,128)S(1)} %pad_bitcast_fusion), channel_id=1, source_target_pairs={{1,0},{2,1},{3,2},{5,4},{6,5},{7,6},{9,8},{10,9},{11,10},{13,12},{... | collective-permute-start | bytes 430088 | tf_op jit(solution)/shard_map/ppermute | solution.py:126
  35.9 0.2 reshape.162
  36.2 3.3 %collective-permute-done.11 = f32[280,128]{1,0:T(8,128)S(1)} collective-permute-done((f32[280,128]{1,0:T(8,128)S(1)}, f32[280,128]{1,0:T(8,128)S(1)}, u32[]{:S(2)}, u32[]{:S(2)}) %collective-permute-start.11) | collective-permute-done | bytes 143392 | tf_op jit(solution)/shard_map/ppermute | solution.py:126
  39.4 0.2 reshape.166
  39.7 0.3 pad_maximum_fusion
  40.0 0.1 multiply_add_fusion
  40.2 0.1 multiply_add_fusion.1
  40.4 0.1 broadcast_multiply_fusion
  40.5 1.2 %broadcast_multiply_fusion.1 = (f32[3,8,20,132]{3,2,1,0:T(8,128)S(1)}, f32[3,8,20,132]{3,2,1,0:T(8,128)S(1)}) fusion(f32[8,20,132]{2,1,0:T(8,128)S(1)} %get-tuple-element.36, f32[3,10,22,134]{3,2,1,0:T(8,128)S(1)} %get-tuple-element.27, f32[8,20,132]{2,1,0:T(8,128)S(1)} %get-tuple-element.35, f32[4,10,22,134]{3,2,1,0:T(8,128)S(1)} %pad_maximum_fusion, ...), kind=kLoop, calls=%fused_computation.42 | loop fusion | flops 760320 | bytes 2703360 | tf_op jit(solution)/shard_map/mul | solution.py:60
  41.7 0.9 %broadcast_multiply_fusion.2 = (f32[3,6,18,130]{3,2,1,0:T(8,128)S(1)}, f32[3,6,18,130]{3,2,1,0:T(8,128)S(1)}) fusion(f32[6,18,130]{2,1,0:T(8,128)S(1)} %get-tuple-element.34, f32[3,8,20,132]{3,2,1,0:T(8,128)S(1)} %get-tuple-element.25, f32[6,18,130]{2,1,0:T(8,128)S(1)} %get-tuple-element.33, f32[4,10,22,134]{3,2,1,0:T(8,128)S(1)} %pad_maximum_fusion, ...), kind=kLoop, calls=%fused_computation.45 | loop fusion | flops 505440 | bytes 1797120 | tf_op jit(solution)/shard_map/mul | solution.py:60
  42.6 0.9 %multiply_reduce_fusion.9 = (f32[3,4,128]{2,1,0:T(4,128)S(1)}, f32[3,4,16,128]{3,2,1,0:T(8,128)}) fusion(f32[4,16,128]{2,1,0:T(8,128)S(1)} %copy-done.5, f32[3,6,18,130]{3,2,1,0:T(8,128)S(1)} %get-tuple-element.23, f32[3,4,16,128]{3,2,1,0:T(8,128)S(1)} %multiply_reduce_fusion.6, f32[4,16,128]{2,1,0:T(8,128)S(1)} %fusion.34, ...), kind=kLoop, calls=%fused_computation.82 | loop fusion | flops 317952 | bytes 956416 | tf_op jit(solution)/shard_map/reduce_sum | solution.py:265
  43.5 0.4 convolution_bitcast_fusion
  43.9 0.2 select_select_fusion
  44.1 13.4 %all_to_all.5 = f32[32,3,128]{2,1,0:T(4,128)S(1)} all-to-all(f32[32,3,128]{2,1,0:T(4,128)S(1)} %select_select_fusion), channel_id=1, replica_groups=mesh['circ'=4,'normal'=2,'span'=4] {'span','normal','circ'}, dimensions={0} | all-to-all | bytes 98304 | tf_op jit(solution)/shard_map/all_to_all | solution.py:230
  57.5 0.6 %reduce_sum.167 = f32[3,128]{1,0:T(4,128)} reduce(f32[32,3,128]{2,1,0:T(4,128)S(1)} %all_to_all.5, f32[]{:T(128)} %constant.19.clone.1), dimensions={0}, to_apply=%region_14.15 | reduce | flops 11904 | bytes 50692 | tf_op jit(solution)/shard_map/reduce_sum | solution.py:230
  (84 shorter events, 1.8 us)
Async XLA Ops:
  0.6 0.9 %copy-start = (f32[5,4,16,128]{3,2,1,0:T(8,128)S(1)}, f32[5,4,16,128]{3,2,1,0:T(8,128)}, u32[]{:S(2)}) copy-start(f32[5,4,16,128]{3,2,1,0:T(8,128)} %param.9) | copy-start | bytes 491524
  1.6 3.1 %copy-start.3 = (f32[3,4,16,128]{3,2,1,0:T(8,128)S(1)}, f32[3,4,16,128]{3,2,1,0:T(8,128)}, u32[]{:S(2)}) copy-start(f32[3,4,16,128]{3,2,1,0:T(8,128)} %param.11) | copy-start | bytes 294916
  1.6 15.1 %collective-permute-start.2 = (f32[6,4,8,128]{3,2,1,0:T(8,128)S(1)}, f32[6,4,8,128]{3,2,1,0:T(8,128)S(1)}, u32[]{:S(2)}, u32[]{:S(2)}) collective-permute-start(f32[6,4,8,128]{3,2,1,0:T(8,128)S(1)} %pad_maximum_fusion.2), channel_id=1, source_target_pairs={{0,4},{4,0},{1,5},{5,1},{2,6},{6,2},{3,7},{7,3},{8,12},{12,8},{9,1... | collective-permute-start | bytes 294920 | tf_op jit(solution)/shard_map/ppermute | solution.py:149
  4.7 11.8 %collective-permute-start.1 = (f32[6,1,16,128]{3,2,1,0:T(8,128)S(1)}, f32[6,1,16,128]{3,2,1,0:T(8,128)S(1)}, u32[]{:S(2)}, u32[]{:S(2)}) collective-permute-start(f32[6,1,16,128]{3,2,1,0:T(8,128)S(1)} %get-tuple-element.56), channel_id=1, source_target_pairs={{0,1},{1,2},{2,3},{4,5},{5,6},{6,7},{8,9},{9,10},{10,11},{12,13},{... | collective-permute-start | bytes 147464 | tf_op jit(solution)/shard_map/ppermute | solution.py:122
  6.2 10.4 %collective-permute-start = (f32[6,1,16,128]{3,2,1,0:T(8,128)S(1)}, f32[6,1,16,128]{3,2,1,0:T(8,128)S(1)}, u32[]{:S(2)}, u32[]{:S(2)}) collective-permute-start(f32[6,1,16,128]{3,2,1,0:T(8,128)S(1)} %get-tuple-element.57), channel_id=1, source_target_pairs={{1,0},{2,1},{3,2},{5,4},{6,5},{7,6},{9,8},{10,9},{11,10},{13,12},{... | collective-permute-start | bytes 147464 | tf_op jit(solution)/shard_map/ppermute | solution.py:122
  8.4 7.4 %collective-permute-start.4 = (f32[6,4,16,1]{2,0,3,1:T(8,128)S(1)}, f32[6,4,16,1]{2,0,3,1:T(8,128)S(1)}, u32[]{:S(2)}, u32[]{:S(2)}) collective-permute-start(f32[6,4,16,1]{2,0,3,1:T(8,128)S(1)} %get-tuple-element.67), channel_id=1, source_target_pairs={{0,8},{8,16},{16,24},{24,0},{1,9},{9,17},{17,25},{25,1},{2,10},{10... | collective-permute-start | bytes 4616 | tf_op jit(solution)/shard_map/ppermute | solution.py:122
  10.0 2.3 %copy-start.6 = (f32[3,5,5]{2,0,1:T(4,128)S(1)}, f32[3,5,5]{2,0,1:T(4,128)}, u32[]{:S(2)}) copy-start(f32[3,5,5]{2,0,1:T(4,128)} %param.12) | copy-start | bytes 904
  10.1 5.9 %collective-permute-start.3 = (f32[6,4,16,1]{2,0,3,1:T(8,128)S(1)}, f32[6,4,16,1]{2,0,3,1:T(8,128)S(1)}, u32[]{:S(2)}, u32[]{:S(2)}) collective-permute-start(f32[6,4,16,1]{2,0,3,1:T(8,128)S(1)} %get-tuple-element.68), channel_id=1, source_target_pairs={{0,24},{8,0},{16,8},{24,16},{1,25},{9,1},{17,9},{25,17},{2,26},{10... | collective-permute-start | bytes 4616 | tf_op jit(solution)/shard_map/ppermute | solution.py:122
  12.3 0.7 %copy-start.7 = (f32[3,5,5]{2,0,1:T(4,128)S(1)}, f32[3,5,5]{2,0,1:T(4,128)}, u32[]{:S(2)}) copy-start(f32[3,5,5]{2,0,1:T(4,128)} %param.13) | copy-start | bytes 904
  13.3 0.7 %copy-start.9 = (s32[4,128]{1,0:T(4,128)S(1)}, s32[4,128]{1,0:T(4,128)}, u32[]{:S(2)}) copy-start(s32[4,128]{1,0:T(4,128)} %param.17) | copy-start | bytes 6148
  15.1 0.7 %copy-start.8 = (f32[3,5]{1,0:T(4,128)S(1)}, f32[3,5]{1,0:T(4,128)}, u32[]{:S(2)}) copy-start(f32[3,5]{1,0:T(4,128)} %param.14) | copy-start | bytes 184
  16.5 0.9 %copy-start.4 = (f32[5,4,16,128]{3,2,1,0:T(8,128)S(1)}, f32[5,4,16,128]{3,2,1,0:T(8,128)}, u32[]{:S(2)}) copy-start(f32[5,4,16,128]{3,2,1,0:T(8,128)} %param.10) | copy-start | bytes 491524
  17.6 0.9 %copy-start.2 = (f32[5,4,16,128]{3,2,1,0:T(8,128)}, f32[5,4,16,128]{3,2,1,0:T(8,128)S(1)}, u32[]{:S(2)}) copy-start(f32[5,4,16,128]{3,2,1,0:T(8,128)S(1)} %fusion.15) | copy-start | bytes 491524
  17.7 0.8 %copy-start.1 = (f32[4,16,128]{2,1,0:T(8,128)S(1)}, f32[4,16,128]{2,1,0:T(8,128)}, u32[]{:S(2)}) copy-start(f32[4,16,128]{2,1,0:T(8,128)} %param.15) | copy-start | bytes 98308
  18.7 8.0 %collective-permute-start.5 = (f32[4,4,3,3]{3,2,1,0:T(4,128)S(1)}, f32[4,4,3,3]{3,2,1,0:T(4,128)S(1)}, u32[]{:S(2)}, u32[]{:S(2)}) collective-permute-start(f32[4,4,3,3]{3,2,1,0:T(4,128)S(1)} %get-tuple-element.47), channel_id=1, source_target_pairs={{0,12},{8,20},{16,28},{24,4},{4,8},{12,16},{20,24},{28,0},{1,13},{... | collective-permute-start | bytes 1736 | tf_op jit(solution)/shard_map/ppermute | solution.py:139
  19.3 12.4 %collective-permute-start.8 = (f32[4,4,16,3]{3,2,1,0:T(8,128)S(1)}, f32[4,4,16,3]{3,2,1,0:T(8,128)S(1)}, u32[]{:S(2)}, u32[]{:S(2)}) collective-permute-start(f32[4,4,16,3]{3,2,1,0:T(8,128)S(1)} %get-tuple-element.45), channel_id=1, source_target_pairs={{0,8},{8,16},{16,24},{24,0},{1,9},{9,17},{17,25},{25,1},{2,10},{10... | collective-permute-start | bytes 9224 | tf_op jit(solution)/shard_map/ppermute | solution.py:122
  20.9 10.8 %collective-permute-start.9 = (f32[4,4,16,3]{3,2,1,0:T(8,128)S(1)}, f32[4,4,16,3]{3,2,1,0:T(8,128)S(1)}, u32[]{:S(2)}, u32[]{:S(2)}) collective-permute-start(f32[4,4,16,3]{3,2,1,0:T(8,128)S(1)} %get-tuple-element.46), channel_id=1, source_target_pairs={{0,24},{8,0},{16,8},{24,16},{1,25},{9,1},{17,9},{25,17},{2,26},{10... | collective-permute-start | bytes 9224 | tf_op jit(solution)/shard_map/ppermute | solution.py:122
  23.2 8.4 %collective-permute-start.7 = (f32[4,4,3,3]{3,2,1,0:T(4,128)S(1)}, f32[4,4,3,3]{3,2,1,0:T(4,128)S(1)}, u32[]{:S(2)}, u32[]{:S(2)}) collective-permute-start(f32[4,4,3,3]{3,2,1,0:T(4,128)S(1)} %get-tuple-element.48), channel_id=1, source_target_pairs={{0,28},{8,4},{16,12},{24,20},{4,24},{12,0},{20,8},{28,16},{1,29},{... | collective-permute-start | bytes 1736 | tf_op jit(solution)/shard_map/ppermute | solution.py:139
  25.5 6.1 %collective-permute-start.6 = (f32[4,4,3,128]{3,2,1,0:T(4,128)S(1)}, f32[4,4,3,128]{3,2,1,0:T(4,128)S(1)}, u32[]{:S(2)}, u32[]{:S(2)}) collective-permute-start(f32[4,4,3,128]{3,2,1,0:T(4,128)S(1)} %fusion.29), channel_id=1, source_target_pairs={{0,4},{4,0},{1,5},{5,1},{2,6},{6,2},{3,7},{7,3},{8,12},{12,8},{9,1... | collective-permute-start | bytes 73736 | tf_op jit(solution)/shard_map/ppermute | solution.py:139
  32.3 3.6 %collective-permute-start.10 = (f32[280,128]{1,0:T(8,128)S(1)}, f32[280,128]{1,0:T(8,128)S(1)}, u32[]{:S(2)}, u32[]{:S(2)}) collective-permute-start(f32[280,128]{1,0:T(8,128)S(1)} %pad_bitcast_fusion.1), channel_id=1, source_target_pairs={{0,1},{1,2},{2,3},{4,5},{5,6},{6,7},{8,9},{9,10},{10,11},{12,13},{... | collective-permute-start | bytes 430088 | tf_op jit(solution)/shard_map/ppermute | solution.py:126
  34.6 4.8 %collective-permute-start.11 = (f32[280,128]{1,0:T(8,128)S(1)}, f32[280,128]{1,0:T(8,128)S(1)}, u32[]{:S(2)}, u32[]{:S(2)}) collective-permute-start(f32[280,128]{1,0:T(8,128)S(1)} %pad_bitcast_fusion), channel_id=1, source_target_pairs={{1,0},{2,1},{3,2},{5,4},{6,5},{7,6},{9,8},{10,9},{11,10},{13,12},{... | collective-permute-start | bytes 430088 | tf_op jit(solution)/shard_map/ppermute | solution.py:126
  41.7 0.9 %copy-start.5 = (f32[4,16,128]{2,1,0:T(8,128)S(1)}, f32[4,16,128]{2,1,0:T(8,128)}, u32[]{:S(2)}) copy-start(f32[4,16,128]{2,1,0:T(8,128)} %param.16) | copy-start | bytes 98308

commit v20 on v19

--- a/solution.py
+++ b/solution.py
@@ -165,8 +165,8 @@
 
 def padded_sweeps(joined, width):
     dims = {"span": 1, "normal": 2, "circ": 3}
-    before_c = receive(joined, {"circ": -1}, dims, width)
-    after_c = receive(joined, {"circ": 1}, dims, width)
+    before_c = receive(joined, {"circ": -1}, dims, width, True)
+    after_c = receive(joined, {"circ": 1}, dims, width, True)
     low_n, high_n = receive_pair(joined, {}, "normal", dims, width)
     low_lc, high_lc = receive_pair(joined, {"circ": -1}, "normal", dims, width)
     low_hc, high_hc = receive_pair(joined, {"circ": 1}, "normal", dims, width)

time: 58.6 us -> 59.5 us (1.015)
  local copies, waits for them, and re-layouts: 6.76 us -> 7.56 us
    ppermute x6 -> x4, starting transfers between devices: 10.5 us -> 6.63 us  [receive(): return lax.ppermute(slab, axes, pairs)]
    ppermute x3, waiting for transfers between devices: 5.01 us -> 2.55 us  [receive_pair(): got = lax.ppermute(sent, axes, pairs + back)]
    ppermute x2 -> x4, starting transfers between devices: 3.32 us -> 5.64 us  [receive(): lax.ppermute(flat, axes, pairs).reshape(-1)[:size].reshape(slab.shape)]
    ppermute x2 -> x4, waiting for transfers between devices: 3.27 us -> 5.31 us  [receive(): lax.ppermute(flat, axes, pairs).reshape(-1)[:size].reshape(slab.shape)]
    ppermute x3, starting transfers between devices: 4.02 us -> 5.61 us  [receive_pair(): got = lax.ppermute(sent, axes, pairs + back)]
  transfers between devices with their start and end apart: 12 -> 12, of which waited for: 2 -> 3; matrix products, arithmetic and copies ran while one was open for 6% -> 7% of each run, Pallas kernels for 0% -> 0%
where the time goes in v20:
time: 59.5 us; the launch traced here: 59 us
  starting transfers between devices  20.9 us (35%)
  blocking collectives  13.9 us (23%)
  waiting for transfers between devices  7.88 us (13%)
  local copies, waits for them, and re-layouts  7.56 us (13%)
  other arithmetic  7.04 us (12%)
  between operations  1.29 us (2%)
    all_to_all x1, blocking collectives, reduce_panels(): lax.all_to_all(chunks, ORDER[::-1], 0, 0, tiled=False)  13.9 us
    ppermute x4, starting transfers between devices, receive(): return lax.ppermute(slab, axes, pairs)  6.63 us
    ppermute x4, starting transfers between devices, receive(): lax.ppermute(flat, axes, pairs).reshape(-1)[:size].reshape(slab.shape)  5.64 us
    ppermute x3, starting transfers between devices, receive_pair(): got = lax.ppermute(sent, axes, pairs + back)  5.61 us
    ppermute x4, waiting for transfers between devices, receive(): lax.ppermute(flat, axes, pairs).reshape(-1)[:size].reshape(slab.shape)  5.31 us
    unnamed x28, local copies, waits for them, and re-layouts  4.02 us
    ppermute x1, starting transfers between devices, tile_halos(): got = lax.ppermute(sent, axis, [(0, 1), (1, 0)])  3.03 us
    ppermute x3, waiting for transfers between devices, receive_pair(): got = lax.ppermute(sent, axes, pairs + back)  2.55 us
  transfers between devices with their start and end apart: 12, of which 3 were waited for; matrix products, arithmetic and copies ran while one was open for 7% of the time, Pallas kernels for 0%

profile of v20, /device:TPU:0, one launch (start us, length us, event | category | flops | bytes accessed | tf_op | source)
XLA Modules:
  0.0 59.0 jit_solution(13053461355940239194)
XLA Ops:
  0.6 0.8 %fusion.51 = (f32[1,4,16,128]{3,2,1,0:T(8,128)S(1)}, f32[4,16,128]{2,1,0:T(8,128)S(1)}, f32[4,16,128]{2,1,0:T(8,128)S(1)}) fusion(f32[3,4,16,128]{3,2,1,0:T(8,128)} %param.11), kind=kLoop, calls=%fused_computation.156 | loop fusion | bytes 163840 | tf_op jit(solution)/shard_map/slice | solution.py:194
  1.6 3.0 %collective-permute-start.2 = (f32[6,4,8,128]{3,2,1,0:T(8,128)S(1)}, f32[6,4,8,128]{3,2,1,0:T(8,128)S(1)}, u32[]{:S(2)}, u32[]{:S(2)}) collective-permute-start(f32[6,4,8,128]{3,2,1,0:T(8,128)S(1)} %pad_maximum_fusion.2), channel_id=1, source_target_pairs={{0,4},{4,0},{1,5},{5,1},{2,6},{6,2},{3,7},{7,3},{8,12},{12,8},{9,1... | collective-permute-start | bytes 294920 | tf_op jit(solution)/shard_map/ppermute | solution.py:149
  4.7 1.5 %collective-permute-start.1 = (f32[6,1,16,128]{3,2,1,0:T(8,128)S(1)}, f32[6,1,16,128]{3,2,1,0:T(8,128)S(1)}, u32[]{:S(2)}, u32[]{:S(2)}) collective-permute-start(f32[6,1,16,128]{3,2,1,0:T(8,128)S(1)} %get-tuple-element.56), channel_id=1, source_target_pairs={{0,1},{1,2},{2,3},{4,5},{5,6},{6,7},{8,9},{9,10},{10,11},{12,13},{... | collective-permute-start | bytes 147464 | tf_op jit(solution)/shard_map/ppermute | solution.py:122
  6.2 1.3 %collective-permute-start = (f32[6,1,16,128]{3,2,1,0:T(8,128)S(1)}, f32[6,1,16,128]{3,2,1,0:T(8,128)S(1)}, u32[]{:S(2)}, u32[]{:S(2)}) collective-permute-start(f32[6,1,16,128]{3,2,1,0:T(8,128)S(1)} %get-tuple-element.57), channel_id=1, source_target_pairs={{1,0},{2,1},{3,2},{5,4},{6,5},{7,6},{9,8},{10,9},{11,10},{13,12},{... | collective-permute-start | bytes 147464 | tf_op jit(solution)/shard_map/ppermute | solution.py:122
  7.6 0.3 copy.113
  7.9 0.3 copy.114
  8.4 1.6 %collective-permute-start.4 = (f32[6,4,16,1]{2,0,3,1:T(8,128)S(1)}, f32[6,4,16,1]{2,0,3,1:T(8,128)S(1)}, u32[]{:S(2)}, u32[]{:S(2)}) collective-permute-start(f32[6,4,16,1]{2,0,3,1:T(8,128)S(1)} %get-tuple-element.67), channel_id=1, source_target_pairs={{0,8},{8,16},{16,24},{24,0},{1,9},{9,17},{17,25},{25,1},{2,10},{10... | collective-permute-start | bytes 4616 | tf_op jit(solution)/shard_map/ppermute | solution.py:122
  10.1 2.2 %collective-permute-start.3 = (f32[6,4,16,1]{2,0,3,1:T(8,128)S(1)}, f32[6,4,16,1]{2,0,3,1:T(8,128)S(1)}, u32[]{:S(2)}, u32[]{:S(2)}) collective-permute-start(f32[6,4,16,1]{2,0,3,1:T(8,128)S(1)} %get-tuple-element.68), channel_id=1, source_target_pairs={{0,24},{8,0},{16,8},{24,16},{1,25},{9,1},{17,9},{25,17},{2,26},{10... | collective-permute-start | bytes 4616 | tf_op jit(solution)/shard_map/ppermute | solution.py:122
  12.3 0.7 %copy-done.7 = f32[3,5,5]{2,0,1:T(4,128)S(1)} copy-done((f32[3,5,5]{2,0,1:T(4,128)S(1)}, f32[3,5,5]{2,0,1:T(4,128)}, u32[]{:S(2)}) %copy-start.7) | copy-done | bytes 324
  13.3 0.7 %copy-done.9 = s32[4,128]{1,0:T(4,128)S(1)} copy-done((s32[4,128]{1,0:T(4,128)S(1)}, s32[4,128]{1,0:T(4,128)}, u32[]{:S(2)}) %copy-start.9) | copy-done | bytes 2072
  14.0 0.5 multiply_reduce_fusion.2
  14.5 0.2 multiply_reduce_fusion
  14.7 0.1 multiply_reduce_fusion.4
  14.9 0.2 slice_reduce_fusion
  15.1 0.6 %copy-done.8 = f32[3,5]{1,0:T(4,128)S(1)} copy-done((f32[3,5]{1,0:T(4,128)S(1)}, f32[3,5]{1,0:T(4,128)}, u32[]{:S(2)}) %copy-start.8) | copy-done | bytes 84
  16.1 0.2 copy.102
  16.3 0.2 copy.100
  17.0 0.5 copy-done.4
  17.5 0.2 fusion.15
  17.8 0.7 %copy-done.1 = f32[4,16,128]{2,1,0:T(8,128)S(1)} copy-done((f32[4,16,128]{2,1,0:T(8,128)S(1)}, f32[4,16,128]{2,1,0:T(8,128)}, u32[]{:S(2)}) %copy-start.1) | copy-done | bytes 32792
  18.7 0.2 reshape.183
  19.0 0.2 reshape.186
  19.2 2.1 %collective-permute-start.5 = (f32[4,4,3,3]{3,2,1,0:T(4,128)S(1)}, f32[4,4,3,3]{3,2,1,0:T(4,128)S(1)}, u32[]{:S(2)}, u32[]{:S(2)}) collective-permute-start(f32[4,4,3,3]{3,2,1,0:T(4,128)S(1)} %get-tuple-element.47), channel_id=1, source_target_pairs={{0,12},{8,20},{16,28},{24,4},{4,8},{12,16},{20,24},{28,0},{1,13},{... | collective-permute-start | bytes 1736 | tf_op jit(solution)/shard_map/ppermute | solution.py:139
  21.3 2.2 %collective-permute-start.9 = (f32[8,128]{1,0:T(8,128)S(1)}, f32[8,128]{1,0:T(8,128)S(1)}, u32[]{:S(2)}, u32[]{:S(2)}) collective-permute-start(f32[8,128]{1,0:T(8,128)S(1)} %pad_bitcast_fusion.2), channel_id=1, source_target_pairs={{0,24},{8,0},{16,8},{24,16},{1,25},{9,1},{17,9},{25,17},{2,26},{10... | collective-permute-start | bytes 12296 | tf_op jit(solution)/shard_map/ppermute | solution.py:126
  23.6 2.4 %collective-permute-start.7 = (f32[4,4,3,3]{3,2,1,0:T(4,128)S(1)}, f32[4,4,3,3]{3,2,1,0:T(4,128)S(1)}, u32[]{:S(2)}, u32[]{:S(2)}) collective-permute-start(f32[4,4,3,3]{3,2,1,0:T(4,128)S(1)} %get-tuple-element.48), channel_id=1, source_target_pairs={{0,28},{8,4},{16,12},{24,20},{4,24},{12,0},{20,8},{28,16},{1,29},{... | collective-permute-start | bytes 1736 | tf_op jit(solution)/shard_map/ppermute | solution.py:139
  26.0 1.1 %collective-permute-start.6 = (f32[4,4,3,128]{3,2,1,0:T(4,128)S(1)}, f32[4,4,3,128]{3,2,1,0:T(4,128)S(1)}, u32[]{:S(2)}, u32[]{:S(2)}) collective-permute-start(f32[4,4,3,128]{3,2,1,0:T(4,128)S(1)} %fusion.29), channel_id=1, source_target_pairs={{0,4},{4,0},{1,5},{5,1},{2,6},{6,2},{3,7},{7,3},{8,12},{12,8},{9,1... | collective-permute-start | bytes 73736 | tf_op jit(solution)/shard_map/ppermute | solution.py:139
  27.1 1.3 %collective-permute-done.7 = f32[4,4,3,3]{3,2,1,0:T(4,128)S(1)} collective-permute-done((f32[4,4,3,3]{3,2,1,0:T(4,128)S(1)}, f32[4,4,3,3]{3,2,1,0:T(4,128)S(1)}, u32[]{:S(2)}, u32[]{:S(2)}) %collective-permute-start.7) | collective-permute-done | bytes 608 | tf_op jit(solution)/shard_map/ppermute | solution.py:139
  28.4 0.2 reshape.185
  28.6 0.2 reshape.188
  28.8 1.2 %collective-permute-done.6 = f32[4,4,3,128]{3,2,1,0:T(4,128)S(1)} collective-permute-done((f32[4,4,3,128]{3,2,1,0:T(4,128)S(1)}, f32[4,4,3,128]{3,2,1,0:T(4,128)S(1)}, u32[]{:S(2)}, u32[]{:S(2)}) %collective-permute-start.6) | collective-permute-done | bytes 24608 | tf_op jit(solution)/shard_map/ppermute | solution.py:139
  30.1 0.3 maximum_maximum_fusion
  30.5 0.2 reshape.189
  30.7 2.0 %collective-permute-start.10 = (f32[280,128]{1,0:T(8,128)S(1)}, f32[280,128]{1,0:T(8,128)S(1)}, u32[]{:S(2)}, u32[]{:S(2)}) collective-permute-start(f32[280,128]{1,0:T(8,128)S(1)} %pad_bitcast_fusion.1), channel_id=1, source_target_pairs={{0,1},{1,2},{2,3},{4,5},{5,6},{6,7},{8,9},{9,10},{10,11},{12,13},{... | collective-permute-start | bytes 430088 | tf_op jit(solution)/shard_map/ppermute | solution.py:126
  32.7 0.2 reshape.193
  33.0 1.3 %collective-permute-start.11 = (f32[280,128]{1,0:T(8,128)S(1)}, f32[280,128]{1,0:T(8,128)S(1)}, u32[]{:S(2)}, u32[]{:S(2)}) collective-permute-start(f32[280,128]{1,0:T(8,128)S(1)} %pad_bitcast_fusion), channel_id=1, source_target_pairs={{1,0},{2,1},{3,2},{5,4},{6,5},{7,6},{9,8},{10,9},{11,10},{13,12},{... | collective-permute-start | bytes 430088 | tf_op jit(solution)/shard_map/ppermute | solution.py:126
  34.3 0.2 reshape.192
  34.5 5.3 %collective-permute-done.11 = f32[280,128]{1,0:T(8,128)S(1)} collective-permute-done((f32[280,128]{1,0:T(8,128)S(1)}, f32[280,128]{1,0:T(8,128)S(1)}, u32[]{:S(2)}, u32[]{:S(2)}) %collective-permute-start.11) | collective-permute-done | bytes 143392 | tf_op jit(solution)/shard_map/ppermute | solution.py:126
  39.8 0.2 reshape.196
  40.1 0.3 pad_maximum_fusion
  40.4 0.1 multiply_add_fusion
  40.8 0.1 broadcast_multiply_fusion
  40.9 1.2 %broadcast_multiply_fusion.1 = (f32[3,8,20,132]{3,2,1,0:T(8,128)S(1)}, f32[3,8,20,132]{3,2,1,0:T(8,128)S(1)}) fusion(f32[8,20,132]{2,1,0:T(8,128)S(1)} %get-tuple-element.36, f32[3,10,22,134]{3,2,1,0:T(8,128)S(1)} %get-tuple-element.27, f32[8,20,132]{2,1,0:T(8,128)S(1)} %get-tuple-element.35, f32[4,10,22,134]{3,2,1,0:T(8,128)S(1)} %pad_maximum_fusion, ...), kind=kLoop, calls=%fused_computation.42 | loop fusion | flops 760320 | bytes 2703360 | tf_op jit(solution)/shard_map/mul | solution.py:60
  42.1 0.9 %broadcast_multiply_fusion.2 = (f32[3,6,18,130]{3,2,1,0:T(8,128)S(1)}, f32[3,6,18,130]{3,2,1,0:T(8,128)S(1)}) fusion(f32[6,18,130]{2,1,0:T(8,128)S(1)} %get-tuple-element.34, f32[3,8,20,132]{3,2,1,0:T(8,128)S(1)} %get-tuple-element.25, f32[6,18,130]{2,1,0:T(8,128)S(1)} %get-tuple-element.33, f32[4,10,22,134]{3,2,1,0:T(8,128)S(1)} %pad_maximum_fusion, ...), kind=kLoop, calls=%fused_computation.45 | loop fusion | flops 505440 | bytes 1797120 | tf_op jit(solution)/shard_map/mul | solution.py:60
  43.0 0.9 %multiply_reduce_fusion.9 = (f32[3,4,128]{2,1,0:T(4,128)S(1)}, f32[3,4,16,128]{3,2,1,0:T(8,128)}) fusion(f32[4,16,128]{2,1,0:T(8,128)S(1)} %copy-done.5, f32[3,6,18,130]{3,2,1,0:T(8,128)S(1)} %get-tuple-element.23, f32[3,4,16,128]{3,2,1,0:T(8,128)S(1)} %multiply_reduce_fusion.6, f32[4,16,128]{2,1,0:T(8,128)S(1)} %fusion.34, ...), kind=kLoop, calls=%fused_computation.82 | loop fusion | flops 317952 | bytes 956416 | tf_op jit(solution)/shard_map/reduce_sum | solution.py:265
  43.9 0.4 convolution_bitcast_fusion
  44.3 0.2 select_select_fusion
  44.5 13.9 %all_to_all.5 = f32[32,3,128]{2,1,0:T(4,128)S(1)} all-to-all(f32[32,3,128]{2,1,0:T(4,128)S(1)} %select_select_fusion), channel_id=1, replica_groups=mesh['circ'=4,'normal'=2,'span'=4] {'span','normal','circ'}, dimensions={0} | all-to-all | bytes 98304 | tf_op jit(solution)/shard_map/all_to_all | solution.py:230
  58.3 0.6 %reduce_sum.167 = f32[3,128]{1,0:T(4,128)} reduce(f32[32,3,128]{2,1,0:T(4,128)S(1)} %all_to_all.5, f32[]{:T(128)} %constant.19.clone.1), dimensions={0}, to_apply=%region_14.15 | reduce | flops 11904 | bytes 50692 | tf_op jit(solution)/shard_map/reduce_sum | solution.py:230
  (90 shorter events, 2.4 us)
Async XLA Ops:
  0.6 0.9 %copy-start = (f32[5,4,16,128]{3,2,1,0:T(8,128)S(1)}, f32[5,4,16,128]{3,2,1,0:T(8,128)}, u32[]{:S(2)}) copy-start(f32[5,4,16,128]{3,2,1,0:T(8,128)} %param.9) | copy-start | bytes 491524
  1.6 3.1 %copy-start.3 = (f32[3,4,16,128]{3,2,1,0:T(8,128)S(1)}, f32[3,4,16,128]{3,2,1,0:T(8,128)}, u32[]{:S(2)}) copy-start(f32[3,4,16,128]{3,2,1,0:T(8,128)} %param.11) | copy-start | bytes 294916
  1.6 15.1 %collective-permute-start.2 = (f32[6,4,8,128]{3,2,1,0:T(8,128)S(1)}, f32[6,4,8,128]{3,2,1,0:T(8,128)S(1)}, u32[]{:S(2)}, u32[]{:S(2)}) collective-permute-start(f32[6,4,8,128]{3,2,1,0:T(8,128)S(1)} %pad_maximum_fusion.2), channel_id=1, source_target_pairs={{0,4},{4,0},{1,5},{5,1},{2,6},{6,2},{3,7},{7,3},{8,12},{12,8},{9,1... | collective-permute-start | bytes 294920 | tf_op jit(solution)/shard_map/ppermute | solution.py:149
  4.7 11.8 %collective-permute-start.1 = (f32[6,1,16,128]{3,2,1,0:T(8,128)S(1)}, f32[6,1,16,128]{3,2,1,0:T(8,128)S(1)}, u32[]{:S(2)}, u32[]{:S(2)}) collective-permute-start(f32[6,1,16,128]{3,2,1,0:T(8,128)S(1)} %get-tuple-element.56), channel_id=1, source_target_pairs={{0,1},{1,2},{2,3},{4,5},{5,6},{6,7},{8,9},{9,10},{10,11},{12,13},{... | collective-permute-start | bytes 147464 | tf_op jit(solution)/shard_map/ppermute | solution.py:122
  6.2 10.4 %collective-permute-start = (f32[6,1,16,128]{3,2,1,0:T(8,128)S(1)}, f32[6,1,16,128]{3,2,1,0:T(8,128)S(1)}, u32[]{:S(2)}, u32[]{:S(2)}) collective-permute-start(f32[6,1,16,128]{3,2,1,0:T(8,128)S(1)} %get-tuple-element.57), channel_id=1, source_target_pairs={{1,0},{2,1},{3,2},{5,4},{6,5},{7,6},{9,8},{10,9},{11,10},{13,12},{... | collective-permute-start | bytes 147464 | tf_op jit(solution)/shard_map/ppermute | solution.py:122
  8.4 7.4 %collective-permute-start.4 = (f32[6,4,16,1]{2,0,3,1:T(8,128)S(1)}, f32[6,4,16,1]{2,0,3,1:T(8,128)S(1)}, u32[]{:S(2)}, u32[]{:S(2)}) collective-permute-start(f32[6,4,16,1]{2,0,3,1:T(8,128)S(1)} %get-tuple-element.67), channel_id=1, source_target_pairs={{0,8},{8,16},{16,24},{24,0},{1,9},{9,17},{17,25},{25,1},{2,10},{10... | collective-permute-start | bytes 4616 | tf_op jit(solution)/shard_map/ppermute | solution.py:122
  10.0 2.3 %copy-start.6 = (f32[3,5,5]{2,0,1:T(4,128)S(1)}, f32[3,5,5]{2,0,1:T(4,128)}, u32[]{:S(2)}) copy-start(f32[3,5,5]{2,0,1:T(4,128)} %param.12) | copy-start | bytes 904
  10.1 5.9 %collective-permute-start.3 = (f32[6,4,16,1]{2,0,3,1:T(8,128)S(1)}, f32[6,4,16,1]{2,0,3,1:T(8,128)S(1)}, u32[]{:S(2)}, u32[]{:S(2)}) collective-permute-start(f32[6,4,16,1]{2,0,3,1:T(8,128)S(1)} %get-tuple-element.68), channel_id=1, source_target_pairs={{0,24},{8,0},{16,8},{24,16},{1,25},{9,1},{17,9},{25,17},{2,26},{10... | collective-permute-start | bytes 4616 | tf_op jit(solution)/shard_map/ppermute | solution.py:122
  12.3 0.7 %copy-start.7 = (f32[3,5,5]{2,0,1:T(4,128)S(1)}, f32[3,5,5]{2,0,1:T(4,128)}, u32[]{:S(2)}) copy-start(f32[3,5,5]{2,0,1:T(4,128)} %param.13) | copy-start | bytes 904
  13.3 0.7 %copy-start.9 = (s32[4,128]{1,0:T(4,128)S(1)}, s32[4,128]{1,0:T(4,128)}, u32[]{:S(2)}) copy-start(s32[4,128]{1,0:T(4,128)} %param.17) | copy-start | bytes 6148
  15.1 0.7 %copy-start.8 = (f32[3,5]{1,0:T(4,128)S(1)}, f32[3,5]{1,0:T(4,128)}, u32[]{:S(2)}) copy-start(f32[3,5]{1,0:T(4,128)} %param.14) | copy-start | bytes 184
  16.5 0.9 %copy-start.4 = (f32[5,4,16,128]{3,2,1,0:T(8,128)S(1)}, f32[5,4,16,128]{3,2,1,0:T(8,128)}, u32[]{:S(2)}) copy-start(f32[5,4,16,128]{3,2,1,0:T(8,128)} %param.10) | copy-start | bytes 491524
  17.6 0.9 %copy-start.2 = (f32[5,4,16,128]{3,2,1,0:T(8,128)}, f32[5,4,16,128]{3,2,1,0:T(8,128)S(1)}, u32[]{:S(2)}) copy-start(f32[5,4,16,128]{3,2,1,0:T(8,128)S(1)} %fusion.15) | copy-start | bytes 491524
  17.7 0.8 %copy-start.1 = (f32[4,16,128]{2,1,0:T(8,128)S(1)}, f32[4,16,128]{2,1,0:T(8,128)}, u32[]{:S(2)}) copy-start(f32[4,16,128]{2,1,0:T(8,128)} %param.15) | copy-start | bytes 98308
  18.9 9.5 %collective-permute-start.8 = (f32[8,128]{1,0:T(8,128)S(1)}, f32[8,128]{1,0:T(8,128)S(1)}, u32[]{:S(2)}, u32[]{:S(2)}) collective-permute-start(f32[8,128]{1,0:T(8,128)S(1)} %pad_bitcast_fusion.3), channel_id=1, source_target_pairs={{0,8},{8,16},{16,24},{24,0},{1,9},{9,17},{17,25},{25,1},{2,10},{10... | collective-permute-start | bytes 12296 | tf_op jit(solution)/shard_map/ppermute | solution.py:126
  19.2 7.9 %collective-permute-start.5 = (f32[4,4,3,3]{3,2,1,0:T(4,128)S(1)}, f32[4,4,3,3]{3,2,1,0:T(4,128)S(1)}, u32[]{:S(2)}, u32[]{:S(2)}) collective-permute-start(f32[4,4,3,3]{3,2,1,0:T(4,128)S(1)} %get-tuple-element.47), channel_id=1, source_target_pairs={{0,12},{8,20},{16,28},{24,4},{4,8},{12,16},{20,24},{28,0},{1,13},{... | collective-permute-start | bytes 1736 | tf_op jit(solution)/shard_map/ppermute | solution.py:139
  21.3 7.3 %collective-permute-start.9 = (f32[8,128]{1,0:T(8,128)S(1)}, f32[8,128]{1,0:T(8,128)S(1)}, u32[]{:S(2)}, u32[]{:S(2)}) collective-permute-start(f32[8,128]{1,0:T(8,128)S(1)} %pad_bitcast_fusion.2), channel_id=1, source_target_pairs={{0,24},{8,0},{16,8},{24,16},{1,25},{9,1},{17,9},{25,17},{2,26},{10... | collective-permute-start | bytes 12296 | tf_op jit(solution)/shard_map/ppermute | solution.py:126
  23.6 4.8 %collective-permute-start.7 = (f32[4,4,3,3]{3,2,1,0:T(4,128)S(1)}, f32[4,4,3,3]{3,2,1,0:T(4,128)S(1)}, u32[]{:S(2)}, u32[]{:S(2)}) collective-permute-start(f32[4,4,3,3]{3,2,1,0:T(4,128)S(1)} %get-tuple-element.48), channel_id=1, source_target_pairs={{0,28},{8,4},{16,12},{24,20},{4,24},{12,0},{20,8},{28,16},{1,29},{... | collective-permute-start | bytes 1736 | tf_op jit(solution)/shard_map/ppermute | solution.py:139
  26.0 4.1 %collective-permute-start.6 = (f32[4,4,3,128]{3,2,1,0:T(4,128)S(1)}, f32[4,4,3,128]{3,2,1,0:T(4,128)S(1)}, u32[]{:S(2)}, u32[]{:S(2)}) collective-permute-start(f32[4,4,3,128]{3,2,1,0:T(4,128)S(1)} %fusion.29), channel_id=1, source_target_pairs={{0,4},{4,0},{1,5},{5,1},{2,6},{6,2},{3,7},{7,3},{8,12},{12,8},{9,1... | collective-permute-start | bytes 73736 | tf_op jit(solution)/shard_map/ppermute | solution.py:139
  30.7 3.6 %collective-permute-start.10 = (f32[280,128]{1,0:T(8,128)S(1)}, f32[280,128]{1,0:T(8,128)S(1)}, u32[]{:S(2)}, u32[]{:S(2)}) collective-permute-start(f32[280,128]{1,0:T(8,128)S(1)} %pad_bitcast_fusion.1), channel_id=1, source_target_pairs={{0,1},{1,2},{2,3},{4,5},{5,6},{6,7},{8,9},{9,10},{10,11},{12,13},{... | collective-permute-start | bytes 430088 | tf_op jit(solution)/shard_map/ppermute | solution.py:126
  33.0 6.9 %collective-permute-start.11 = (f32[280,128]{1,0:T(8,128)S(1)}, f32[280,128]{1,0:T(8,128)S(1)}, u32[]{:S(2)}, u32[]{:S(2)}) collective-permute-start(f32[280,128]{1,0:T(8,128)S(1)} %pad_bitcast_fusion), channel_id=1, source_target_pairs={{1,0},{2,1},{3,2},{5,4},{6,5},{7,6},{9,8},{10,9},{11,10},{13,12},{... | collective-permute-start | bytes 430088 | tf_op jit(solution)/shard_map/ppermute | solution.py:126
  42.1 0.9 %copy-start.5 = (f32[4,16,128]{2,1,0:T(8,128)S(1)}, f32[4,16,128]{2,1,0:T(8,128)}, u32[]{:S(2)}) copy-start(f32[4,16,128]{2,1,0:T(8,128)} %param.16) | copy-start | bytes 98308

commit v21 on v19

--- a/solution.py
+++ b/solution.py
@@ -224,10 +224,11 @@
     if devices <= 64:
         spans = lax.axis_size("span")
         relative = jnp.arange(devices, dtype=jnp.int32) // (devices // spans) - lax.axis_index("span") + 1
-        chunks = jnp.zeros((devices,) + own.shape, own.dtype)
+        chunks = jnp.zeros((devices, own.size), own.dtype)
         for index, block in enumerate((below, own, above)):
-            chunks = jnp.where((relative == index)[:, None, None], block[None], chunks)
-        return jnp.sum(lax.all_to_all(chunks, ORDER[::-1], 0, 0, tiled=False), axis=0)
+            chunks = jnp.where((relative == index)[:, None], block.reshape(1, -1), chunks)
+        got = lax.all_to_all(chunks, ORDER[::-1], 0, 0, tiled=False)
+        return jnp.sum(got, axis=0).reshape(own.shape)
     if lax.axis_size("normal") != 2 or lax.axis_size("circ") > 4:
         own = lax.psum(own + shifted(above, {"span": 1}) + shifted(below, {"span": -1}), ("circ", "normal"))
         return own

time: 58.6 us -> 58.6 us (level)
  no operation moved by 1% of the time
where the time goes in v21:
time: 58.6 us; the launch traced here: 58.1 us
  starting transfers between devices  20.9 us (36%)
  blocking collectives  13.4 us (23%)
  waiting for transfers between devices  8.29 us (14%)
  other arithmetic  7.06 us (12%)
  local copies, waits for them, and re-layouts  6.76 us (12%)
  between operations  1.27 us (2%)
    all_to_all x1, blocking collectives, reduce_panels(): got = lax.all_to_all(chunks, ORDER[::-1], 0, 0, tiled=False)  13.4 us
    ppermute x6, starting transfers between devices, receive(): return lax.ppermute(slab, axes, pairs)  10.5 us
    ppermute x3, waiting for transfers between devices, receive_pair(): got = lax.ppermute(sent, axes, pairs + back)  5.01 us
    unnamed x28, local copies, waits for them, and re-layouts  4.02 us
    ppermute x3, starting transfers between devices, receive_pair(): got = lax.ppermute(sent, axes, pairs + back)  4.02 us
    ppermute x2, starting transfers between devices, receive(): lax.ppermute(flat, axes, pairs).reshape(-1)[:size].reshape(slab.shape)  3.32 us
    ppermute x2, waiting for transfers between devices, receive(): lax.ppermute(flat, axes, pairs).reshape(-1)[:size].reshape(slab.shape)  3.27 us
    ppermute x1, starting transfers between devices, tile_halos(): got = lax.ppermute(sent, axis, [(0, 1), (1, 0)])  3.03 us
  transfers between devices with their start and end apart: 12, of which 2 were waited for; matrix products, arithmetic and copies ran while one was open for 6% of the time, Pallas kernels for 0%

profile of v21, /device:TPU:0, one launch (start us, length us, event | category | flops | bytes accessed | tf_op | source)
XLA Modules:
  0.0 58.1 jit_solution(4566623456003943215)
XLA Ops:
  0.6 0.8 %fusion.51 = (f32[1,4,16,128]{3,2,1,0:T(8,128)S(1)}, f32[4,16,128]{2,1,0:T(8,128)S(1)}, f32[4,16,128]{2,1,0:T(8,128)S(1)}) fusion(f32[3,4,16,128]{3,2,1,0:T(8,128)} %param.11), kind=kLoop, calls=%fused_computation.159 | loop fusion | bytes 163840 | tf_op jit(solution)/shard_map/slice | solution.py:194
  1.5 0.1 copy-done
  1.6 3.0 %collective-permute-start.2 = (f32[6,4,8,128]{3,2,1,0:T(8,128)S(1)}, f32[6,4,8,128]{3,2,1,0:T(8,128)S(1)}, u32[]{:S(2)}, u32[]{:S(2)}) collective-permute-start(f32[6,4,8,128]{3,2,1,0:T(8,128)S(1)} %pad_maximum_fusion.2), channel_id=1, source_target_pairs={{0,4},{4,0},{1,5},{5,1},{2,6},{6,2},{3,7},{7,3},{8,12},{12,8},{9,1... | collective-permute-start | bytes 294920 | tf_op jit(solution)/shard_map/ppermute | solution.py:149
  4.7 1.5 %collective-permute-start.1 = (f32[6,1,16,128]{3,2,1,0:T(8,128)S(1)}, f32[6,1,16,128]{3,2,1,0:T(8,128)S(1)}, u32[]{:S(2)}, u32[]{:S(2)}) collective-permute-start(f32[6,1,16,128]{3,2,1,0:T(8,128)S(1)} %get-tuple-element.56), channel_id=1, source_target_pairs={{0,1},{1,2},{2,3},{4,5},{5,6},{6,7},{8,9},{9,10},{10,11},{12,13},{... | collective-permute-start | bytes 147464 | tf_op jit(solution)/shard_map/ppermute | solution.py:122
  6.2 1.3 %collective-permute-start = (f32[6,1,16,128]{3,2,1,0:T(8,128)S(1)}, f32[6,1,16,128]{3,2,1,0:T(8,128)S(1)}, u32[]{:S(2)}, u32[]{:S(2)}) collective-permute-start(f32[6,1,16,128]{3,2,1,0:T(8,128)S(1)} %get-tuple-element.57), channel_id=1, source_target_pairs={{1,0},{2,1},{3,2},{5,4},{6,5},{7,6},{9,8},{10,9},{11,10},{13,12},{... | collective-permute-start | bytes 147464 | tf_op jit(solution)/shard_map/ppermute | solution.py:122
  7.6 0.3 copy.113
  7.9 0.3 copy.114
  8.4 1.6 %collective-permute-start.4 = (f32[6,4,16,1]{2,0,3,1:T(8,128)S(1)}, f32[6,4,16,1]{2,0,3,1:T(8,128)S(1)}, u32[]{:S(2)}, u32[]{:S(2)}) collective-permute-start(f32[6,4,16,1]{2,0,3,1:T(8,128)S(1)} %get-tuple-element.67), channel_id=1, source_target_pairs={{0,8},{8,16},{16,24},{24,0},{1,9},{9,17},{17,25},{25,1},{2,10},{10... | collective-permute-start | bytes 4616 | tf_op jit(solution)/shard_map/ppermute | solution.py:122
  10.1 2.2 %collective-permute-start.3 = (f32[6,4,16,1]{2,0,3,1:T(8,128)S(1)}, f32[6,4,16,1]{2,0,3,1:T(8,128)S(1)}, u32[]{:S(2)}, u32[]{:S(2)}) collective-permute-start(f32[6,4,16,1]{2,0,3,1:T(8,128)S(1)} %get-tuple-element.68), channel_id=1, source_target_pairs={{0,24},{8,0},{16,8},{24,16},{1,25},{9,1},{17,9},{25,17},{2,26},{10... | collective-permute-start | bytes 4616 | tf_op jit(solution)/shard_map/ppermute | solution.py:122
  12.3 0.7 %copy-done.7 = f32[3,5,5]{2,0,1:T(4,128)S(1)} copy-done((f32[3,5,5]{2,0,1:T(4,128)S(1)}, f32[3,5,5]{2,0,1:T(4,128)}, u32[]{:S(2)}) %copy-start.7) | copy-done | bytes 324
  13.1 0.1 subtract_multiply_fusion
  13.3 0.7 %copy-done.9 = s32[4,128]{1,0:T(4,128)S(1)} copy-done((s32[4,128]{1,0:T(4,128)S(1)}, s32[4,128]{1,0:T(4,128)}, u32[]{:S(2)}) %copy-start.9) | copy-done | bytes 2072
  14.0 0.5 multiply_reduce_fusion.2
  14.5 0.2 multiply_reduce_fusion
  14.7 0.1 multiply_reduce_fusion.4
  14.9 0.2 slice_reduce_fusion
  15.1 0.6 %copy-done.8 = f32[3,5]{1,0:T(4,128)S(1)} copy-done((f32[3,5]{1,0:T(4,128)S(1)}, f32[3,5]{1,0:T(4,128)}, u32[]{:S(2)}) %copy-start.8) | copy-done | bytes 84
  16.1 0.2 copy.102
  16.3 0.2 copy.100
  16.6 0.1 multiply_reduce_fusion.7
  17.0 0.5 copy-done.4
  17.5 0.2 fusion.15
  17.8 0.7 %copy-done.1 = f32[4,16,128]{2,1,0:T(8,128)S(1)} copy-done((f32[4,16,128]{2,1,0:T(8,128)S(1)}, f32[4,16,128]{2,1,0:T(8,128)}, u32[]{:S(2)}) %copy-start.1) | copy-done | bytes 32792
  18.7 0.6 %collective-permute-start.5 = (f32[4,4,3,3]{3,2,1,0:T(4,128)S(1)}, f32[4,4,3,3]{3,2,1,0:T(4,128)S(1)}, u32[]{:S(2)}, u32[]{:S(2)}) collective-permute-start(f32[4,4,3,3]{3,2,1,0:T(4,128)S(1)} %get-tuple-element.47), channel_id=1, source_target_pairs={{0,12},{8,20},{16,28},{24,4},{4,8},{12,16},{20,24},{28,0},{1,13},{... | collective-permute-start | bytes 1736 | tf_op jit(solution)/shard_map/ppermute | solution.py:139
  19.3 1.6 %collective-permute-start.8 = (f32[4,4,16,3]{3,2,1,0:T(8,128)S(1)}, f32[4,4,16,3]{3,2,1,0:T(8,128)S(1)}, u32[]{:S(2)}, u32[]{:S(2)}) collective-permute-start(f32[4,4,16,3]{3,2,1,0:T(8,128)S(1)} %get-tuple-element.45), channel_id=1, source_target_pairs={{0,8},{8,16},{16,24},{24,0},{1,9},{9,17},{17,25},{25,1},{2,10},{10... | collective-permute-start | bytes 9224 | tf_op jit(solution)/shard_map/ppermute | solution.py:122
  20.9 2.3 %collective-permute-start.9 = (f32[4,4,16,3]{3,2,1,0:T(8,128)S(1)}, f32[4,4,16,3]{3,2,1,0:T(8,128)S(1)}, u32[]{:S(2)}, u32[]{:S(2)}) collective-permute-start(f32[4,4,16,3]{3,2,1,0:T(8,128)S(1)} %get-tuple-element.46), channel_id=1, source_target_pairs={{0,24},{8,0},{16,8},{24,16},{1,25},{9,1},{17,9},{25,17},{2,26},{10... | collective-permute-start | bytes 9224 | tf_op jit(solution)/shard_map/ppermute | solution.py:122
  23.2 2.3 %collective-permute-start.7 = (f32[4,4,3,3]{3,2,1,0:T(4,128)S(1)}, f32[4,4,3,3]{3,2,1,0:T(4,128)S(1)}, u32[]{:S(2)}, u32[]{:S(2)}) collective-permute-start(f32[4,4,3,3]{3,2,1,0:T(4,128)S(1)} %get-tuple-element.48), channel_id=1, source_target_pairs={{0,28},{8,4},{16,12},{24,20},{4,24},{12,0},{20,8},{28,16},{1,29},{... | collective-permute-start | bytes 1736 | tf_op jit(solution)/shard_map/ppermute | solution.py:139
  25.5 1.1 %collective-permute-start.6 = (f32[4,4,3,128]{3,2,1,0:T(4,128)S(1)}, f32[4,4,3,128]{3,2,1,0:T(4,128)S(1)}, u32[]{:S(2)}, u32[]{:S(2)}) collective-permute-start(f32[4,4,3,128]{3,2,1,0:T(4,128)S(1)} %fusion.29), channel_id=1, source_target_pairs={{0,4},{4,0},{1,5},{5,1},{2,6},{6,2},{3,7},{7,3},{8,12},{12,8},{9,1... | collective-permute-start | bytes 73736 | tf_op jit(solution)/shard_map/ppermute | solution.py:139
  26.6 5.0 %collective-permute-done.7 = f32[4,4,3,3]{3,2,1,0:T(4,128)S(1)} collective-permute-done((f32[4,4,3,3]{3,2,1,0:T(4,128)S(1)}, f32[4,4,3,3]{3,2,1,0:T(4,128)S(1)}, u32[]{:S(2)}, u32[]{:S(2)}) %collective-permute-start.7) | collective-permute-done | bytes 608 | tf_op jit(solution)/shard_map/ppermute | solution.py:139
  31.7 0.3 maximum_maximum_fusion
  32.1 0.2 reshape.314
  32.3 2.0 %collective-permute-start.10 = (f32[280,128]{1,0:T(8,128)S(1)}, f32[280,128]{1,0:T(8,128)S(1)}, u32[]{:S(2)}, u32[]{:S(2)}) collective-permute-start(f32[280,128]{1,0:T(8,128)S(1)} %pad_bitcast_fusion.1), channel_id=1, source_target_pairs={{0,1},{1,2},{2,3},{4,5},{5,6},{6,7},{8,9},{9,10},{10,11},{12,13},{... | collective-permute-start | bytes 430088 | tf_op jit(solution)/shard_map/ppermute | solution.py:126
  34.4 0.2 reshape.318
  34.6 1.3 %collective-permute-start.11 = (f32[280,128]{1,0:T(8,128)S(1)}, f32[280,128]{1,0:T(8,128)S(1)}, u32[]{:S(2)}, u32[]{:S(2)}) collective-permute-start(f32[280,128]{1,0:T(8,128)S(1)} %pad_bitcast_fusion), channel_id=1, source_target_pairs={{1,0},{2,1},{3,2},{5,4},{6,5},{7,6},{9,8},{10,9},{11,10},{13,12},{... | collective-permute-start | bytes 430088 | tf_op jit(solution)/shard_map/ppermute | solution.py:126
  35.9 0.2 reshape.317
  36.2 3.3 %collective-permute-done.11 = f32[280,128]{1,0:T(8,128)S(1)} collective-permute-done((f32[280,128]{1,0:T(8,128)S(1)}, f32[280,128]{1,0:T(8,128)S(1)}, u32[]{:S(2)}, u32[]{:S(2)}) %collective-permute-start.11) | collective-permute-done | bytes 143392 | tf_op jit(solution)/shard_map/ppermute | solution.py:126
  39.4 0.2 reshape.321
  39.7 0.3 pad_maximum_fusion
  40.0 0.1 multiply_add_fusion
  40.2 0.1 multiply_add_fusion.1
  40.4 0.1 broadcast_multiply_fusion
  40.5 1.2 %broadcast_multiply_fusion.1 = (f32[3,8,20,132]{3,2,1,0:T(8,128)S(1)}, f32[3,8,20,132]{3,2,1,0:T(8,128)S(1)}) fusion(f32[8,20,132]{2,1,0:T(8,128)S(1)} %get-tuple-element.36, f32[3,10,22,134]{3,2,1,0:T(8,128)S(1)} %get-tuple-element.27, f32[8,20,132]{2,1,0:T(8,128)S(1)} %get-tuple-element.35, f32[4,10,22,134]{3,2,1,0:T(8,128)S(1)} %pad_maximum_fusion, ...), kind=kLoop, calls=%fused_computation.42 | loop fusion | flops 760320 | bytes 2703360 | tf_op jit(solution)/shard_map/mul | solution.py:60
  41.7 0.9 %broadcast_multiply_fusion.2 = (f32[3,6,18,130]{3,2,1,0:T(8,128)S(1)}, f32[3,6,18,130]{3,2,1,0:T(8,128)S(1)}) fusion(f32[6,18,130]{2,1,0:T(8,128)S(1)} %get-tuple-element.34, f32[3,8,20,132]{3,2,1,0:T(8,128)S(1)} %get-tuple-element.25, f32[6,18,130]{2,1,0:T(8,128)S(1)} %get-tuple-element.33, f32[4,10,22,134]{3,2,1,0:T(8,128)S(1)} %pad_maximum_fusion, ...), kind=kLoop, calls=%fused_computation.45 | loop fusion | flops 505440 | bytes 1797120 | tf_op jit(solution)/shard_map/mul | solution.py:60
  42.6 0.9 %multiply_reduce_fusion.9 = (f32[3,4,128]{2,1,0:T(4,128)S(1)}, f32[3,4,16,128]{3,2,1,0:T(8,128)}) fusion(f32[4,16,128]{2,1,0:T(8,128)S(1)} %copy-done.5, f32[3,6,18,130]{3,2,1,0:T(8,128)S(1)} %get-tuple-element.23, f32[3,4,16,128]{3,2,1,0:T(8,128)S(1)} %multiply_reduce_fusion.6, f32[4,16,128]{2,1,0:T(8,128)S(1)} %fusion.34, ...), kind=kLoop, calls=%fused_computation.82 | loop fusion | flops 317952 | bytes 956416 | tf_op jit(solution)/shard_map/reduce_sum | solution.py:266
  43.5 0.4 convolution_bitcast_fusion
  43.9 0.2 broadcast_select_fusion.1
  44.1 13.4 %all_to_all.6 = f32[32,1,384]{2,1,0:T(1,128)S(1)} all-to-all(f32[32,1,384]{2,1,0:T(1,128)S(1)} %broadcast_select_fusion.1), channel_id=1, replica_groups=mesh['circ'=4,'normal'=2,'span'=4] {'span','normal','circ'}, dimensions={0} | all-to-all | bytes 98304 | tf_op jit(solution)/shard_map/all_to_all | solution.py:230
  57.5 0.6 %reduce_sum.167 = f32[384]{0:T(512)} reduce(f32[32,1,384]{2,1,0:T(1,128)S(1)} %all_to_all.6, f32[]{:T(128)} %constant.19.clone.1), dimensions={0,1}, to_apply=%region_14.15 | reduce | flops 11904 | bytes 50692 | tf_op jit(solution)/shard_map/reduce_sum | solution.py:231
  (84 shorter events, 1.8 us)
Async XLA Ops:
  0.6 0.9 %copy-start = (f32[5,4,16,128]{3,2,1,0:T(8,128)S(1)}, f32[5,4,16,128]{3,2,1,0:T(8,128)}, u32[]{:S(2)}) copy-start(f32[5,4,16,128]{3,2,1,0:T(8,128)} %param.9) | copy-start | bytes 491524
  1.6 3.1 %copy-start.3 = (f32[3,4,16,128]{3,2,1,0:T(8,128)S(1)}, f32[3,4,16,128]{3,2,1,0:T(8,128)}, u32[]{:S(2)}) copy-start(f32[3,4,16,128]{3,2,1,0:T(8,128)} %param.11) | copy-start | bytes 294916
  1.6 15.1 %collective-permute-start.2 = (f32[6,4,8,128]{3,2,1,0:T(8,128)S(1)}, f32[6,4,8,128]{3,2,1,0:T(8,128)S(1)}, u32[]{:S(2)}, u32[]{:S(2)}) collective-permute-start(f32[6,4,8,128]{3,2,1,0:T(8,128)S(1)} %pad_maximum_fusion.2), channel_id=1, source_target_pairs={{0,4},{4,0},{1,5},{5,1},{2,6},{6,2},{3,7},{7,3},{8,12},{12,8},{9,1... | collective-permute-start | bytes 294920 | tf_op jit(solution)/shard_map/ppermute | solution.py:149
  4.7 11.8 %collective-permute-start.1 = (f32[6,1,16,128]{3,2,1,0:T(8,128)S(1)}, f32[6,1,16,128]{3,2,1,0:T(8,128)S(1)}, u32[]{:S(2)}, u32[]{:S(2)}) collective-permute-start(f32[6,1,16,128]{3,2,1,0:T(8,128)S(1)} %get-tuple-element.56), channel_id=1, source_target_pairs={{0,1},{1,2},{2,3},{4,5},{5,6},{6,7},{8,9},{9,10},{10,11},{12,13},{... | collective-permute-start | bytes 147464 | tf_op jit(solution)/shard_map/ppermute | solution.py:122
  6.2 10.4 %collective-permute-start = (f32[6,1,16,128]{3,2,1,0:T(8,128)S(1)}, f32[6,1,16,128]{3,2,1,0:T(8,128)S(1)}, u32[]{:S(2)}, u32[]{:S(2)}) collective-permute-start(f32[6,1,16,128]{3,2,1,0:T(8,128)S(1)} %get-tuple-element.57), channel_id=1, source_target_pairs={{1,0},{2,1},{3,2},{5,4},{6,5},{7,6},{9,8},{10,9},{11,10},{13,12},{... | collective-permute-start | bytes 147464 | tf_op jit(solution)/shard_map/ppermute | solution.py:122
  8.4 7.4 %collective-permute-start.4 = (f32[6,4,16,1]{2,0,3,1:T(8,128)S(1)}, f32[6,4,16,1]{2,0,3,1:T(8,128)S(1)}, u32[]{:S(2)}, u32[]{:S(2)}) collective-permute-start(f32[6,4,16,1]{2,0,3,1:T(8,128)S(1)} %get-tuple-element.67), channel_id=1, source_target_pairs={{0,8},{8,16},{16,24},{24,0},{1,9},{9,17},{17,25},{25,1},{2,10},{10... | collective-permute-start | bytes 4616 | tf_op jit(solution)/shard_map/ppermute | solution.py:122
  10.0 2.3 %copy-start.6 = (f32[3,5,5]{2,0,1:T(4,128)S(1)}, f32[3,5,5]{2,0,1:T(4,128)}, u32[]{:S(2)}) copy-start(f32[3,5,5]{2,0,1:T(4,128)} %param.12) | copy-start | bytes 904
  10.1 5.9 %collective-permute-start.3 = (f32[6,4,16,1]{2,0,3,1:T(8,128)S(1)}, f32[6,4,16,1]{2,0,3,1:T(8,128)S(1)}, u32[]{:S(2)}, u32[]{:S(2)}) collective-permute-start(f32[6,4,16,1]{2,0,3,1:T(8,128)S(1)} %get-tuple-element.68), channel_id=1, source_target_pairs={{0,24},{8,0},{16,8},{24,16},{1,25},{9,1},{17,9},{25,17},{2,26},{10... | collective-permute-start | bytes 4616 | tf_op jit(solution)/shard_map/ppermute | solution.py:122
  12.3 0.7 %copy-start.7 = (f32[3,5,5]{2,0,1:T(4,128)S(1)}, f32[3,5,5]{2,0,1:T(4,128)}, u32[]{:S(2)}) copy-start(f32[3,5,5]{2,0,1:T(4,128)} %param.13) | copy-start | bytes 904
  13.3 0.7 %copy-start.9 = (s32[4,128]{1,0:T(4,128)S(1)}, s32[4,128]{1,0:T(4,128)}, u32[]{:S(2)}) copy-start(s32[4,128]{1,0:T(4,128)} %param.17) | copy-start | bytes 6148
  15.1 0.7 %copy-start.8 = (f32[3,5]{1,0:T(4,128)S(1)}, f32[3,5]{1,0:T(4,128)}, u32[]{:S(2)}) copy-start(f32[3,5]{1,0:T(4,128)} %param.14) | copy-start | bytes 184
  16.5 0.9 %copy-start.4 = (f32[5,4,16,128]{3,2,1,0:T(8,128)S(1)}, f32[5,4,16,128]{3,2,1,0:T(8,128)}, u32[]{:S(2)}) copy-start(f32[5,4,16,128]{3,2,1,0:T(8,128)} %param.10) | copy-start | bytes 491524
  17.6 0.9 %copy-start.2 = (f32[5,4,16,128]{3,2,1,0:T(8,128)}, f32[5,4,16,128]{3,2,1,0:T(8,128)S(1)}, u32[]{:S(2)}) copy-start(f32[5,4,16,128]{3,2,1,0:T(8,128)S(1)} %fusion.15) | copy-start | bytes 491524
  17.7 0.8 %copy-start.1 = (f32[4,16,128]{2,1,0:T(8,128)S(1)}, f32[4,16,128]{2,1,0:T(8,128)}, u32[]{:S(2)}) copy-start(f32[4,16,128]{2,1,0:T(8,128)} %param.15) | copy-start | bytes 98308
  18.7 8.0 %collective-permute-start.5 = (f32[4,4,3,3]{3,2,1,0:T(4,128)S(1)}, f32[4,4,3,3]{3,2,1,0:T(4,128)S(1)}, u32[]{:S(2)}, u32[]{:S(2)}) collective-permute-start(f32[4,4,3,3]{3,2,1,0:T(4,128)S(1)} %get-tuple-element.47), channel_id=1, source_target_pairs={{0,12},{8,20},{16,28},{24,4},{4,8},{12,16},{20,24},{28,0},{1,13},{... | collective-permute-start | bytes 1736 | tf_op jit(solution)/shard_map/ppermute | solution.py:139
  19.3 12.4 %collective-permute-start.8 = (f32[4,4,16,3]{3,2,1,0:T(8,128)S(1)}, f32[4,4,16,3]{3,2,1,0:T(8,128)S(1)}, u32[]{:S(2)}, u32[]{:S(2)}) collective-permute-start(f32[4,4,16,3]{3,2,1,0:T(8,128)S(1)} %get-tuple-element.45), channel_id=1, source_target_pairs={{0,8},{8,16},{16,24},{24,0},{1,9},{9,17},{17,25},{25,1},{2,10},{10... | collective-permute-start | bytes 9224 | tf_op jit(solution)/shard_map/ppermute | solution.py:122
  20.9 10.8 %collective-permute-start.9 = (f32[4,4,16,3]{3,2,1,0:T(8,128)S(1)}, f32[4,4,16,3]{3,2,1,0:T(8,128)S(1)}, u32[]{:S(2)}, u32[]{:S(2)}) collective-permute-start(f32[4,4,16,3]{3,2,1,0:T(8,128)S(1)} %get-tuple-element.46), channel_id=1, source_target_pairs={{0,24},{8,0},{16,8},{24,16},{1,25},{9,1},{17,9},{25,17},{2,26},{10... | collective-permute-start | bytes 9224 | tf_op jit(solution)/shard_map/ppermute | solution.py:122
  23.2 8.4 %collective-permute-start.7 = (f32[4,4,3,3]{3,2,1,0:T(4,128)S(1)}, f32[4,4,3,3]{3,2,1,0:T(4,128)S(1)}, u32[]{:S(2)}, u32[]{:S(2)}) collective-permute-start(f32[4,4,3,3]{3,2,1,0:T(4,128)S(1)} %get-tuple-element.48), channel_id=1, source_target_pairs={{0,28},{8,4},{16,12},{24,20},{4,24},{12,0},{20,8},{28,16},{1,29},{... | collective-permute-start | bytes 1736 | tf_op jit(solution)/shard_map/ppermute | solution.py:139
  25.5 6.1 %collective-permute-start.6 = (f32[4,4,3,128]{3,2,1,0:T(4,128)S(1)}, f32[4,4,3,128]{3,2,1,0:T(4,128)S(1)}, u32[]{:S(2)}, u32[]{:S(2)}) collective-permute-start(f32[4,4,3,128]{3,2,1,0:T(4,128)S(1)} %fusion.29), channel_id=1, source_target_pairs={{0,4},{4,0},{1,5},{5,1},{2,6},{6,2},{3,7},{7,3},{8,12},{12,8},{9,1... | collective-permute-start | bytes 73736 | tf_op jit(solution)/shard_map/ppermute | solution.py:139
  32.3 3.6 %collective-permute-start.10 = (f32[280,128]{1,0:T(8,128)S(1)}, f32[280,128]{1,0:T(8,128)S(1)}, u32[]{:S(2)}, u32[]{:S(2)}) collective-permute-start(f32[280,128]{1,0:T(8,128)S(1)} %pad_bitcast_fusion.1), channel_id=1, source_target_pairs={{0,1},{1,2},{2,3},{4,5},{5,6},{6,7},{8,9},{9,10},{10,11},{12,13},{... | collective-permute-start | bytes 430088 | tf_op jit(solution)/shard_map/ppermute | solution.py:126
  34.6 4.8 %collective-permute-start.11 = (f32[280,128]{1,0:T(8,128)S(1)}, f32[280,128]{1,0:T(8,128)S(1)}, u32[]{:S(2)}, u32[]{:S(2)}) collective-permute-start(f32[280,128]{1,0:T(8,128)S(1)} %pad_bitcast_fusion), channel_id=1, source_target_pairs={{1,0},{2,1},{3,2},{5,4},{6,5},{7,6},{9,8},{10,9},{11,10},{13,12},{... | collective-permute-start | bytes 430088 | tf_op jit(solution)/shard_map/ppermute | solution.py:126
  41.7 0.9 %copy-start.5 = (f32[4,16,128]{2,1,0:T(8,128)S(1)}, f32[4,16,128]{2,1,0:T(8,128)}, u32[]{:S(2)}) copy-start(f32[4,16,128]{2,1,0:T(8,128)} %param.16) | copy-start | bytes 98308

commit v22 on v19

--- a/solution.py
+++ b/solution.py
@@ -269,7 +269,7 @@
     onehot = (
         local[:, :, None] == jnp.arange(3 * PANEL_DEV, dtype=jnp.int32)[None, None, :]
     ).astype(jnp.float32)
-    terms = jnp.einsum("mki,kip->mp", wall_sens, onehot, precision=lax.Precision.HIGHEST)
+    terms = jnp.einsum("mki,kip->mp", wall_sens, onehot, precision=lax.Precision.HIGH)
     panels = reduce_panels(terms)
     return (residual, mesh, panels)
 

time: 58.6 us -> 58.6 us (level)
  no operation moved by 1% of the time
where the time goes in v22:
time: 58.6 us; the launch traced here: 58.1 us
  starting transfers between devices  20.9 us (36%)
  blocking collectives  13.4 us (23%)
  waiting for transfers between devices  8.29 us (14%)
  other arithmetic  7.04 us (12%)
  local copies, waits for them, and re-layouts  6.76 us (12%)
  between operations  1.27 us (2%)
    all_to_all x1, blocking collectives, reduce_panels(): lax.all_to_all(chunks, ORDER[::-1], 0, 0, tiled=False)  13.4 us
    ppermute x6, starting transfers between devices, receive(): return lax.ppermute(slab, axes, pairs)  10.5 us
    ppermute x3, waiting for transfers between devices, receive_pair(): got = lax.ppermute(sent, axes, pairs + back)  5.01 us
    unnamed x28, local copies, waits for them, and re-layouts  4.02 us
    ppermute x3, starting transfers between devices, receive_pair(): got = lax.ppermute(sent, axes, pairs + back)  4.02 us
    ppermute x2, starting transfers between devices, receive(): lax.ppermute(flat, axes, pairs).reshape(-1)[:size].reshape(slab.shape)  3.32 us
    ppermute x2, waiting for transfers between devices, receive(): lax.ppermute(flat, axes, pairs).reshape(-1)[:size].reshape(slab.shape)  3.27 us
    ppermute x1, starting transfers between devices, tile_halos(): got = lax.ppermute(sent, axis, [(0, 1), (1, 0)])  3.03 us
  transfers between devices with their start and end apart: 12, of which 2 were waited for; matrix products, arithmetic and copies ran while one was open for 6% of the time, Pallas kernels for 0%

profile of v22, /device:TPU:0, one launch (start us, length us, event | category | flops | bytes accessed | tf_op | source)
XLA Modules:
  0.0 58.1 jit_solution(12260489928639586127)
XLA Ops:
  0.6 0.8 %fusion.51 = (f32[1,4,16,128]{3,2,1,0:T(8,128)S(1)}, f32[4,16,128]{2,1,0:T(8,128)S(1)}, f32[4,16,128]{2,1,0:T(8,128)S(1)}) fusion(f32[3,4,16,128]{3,2,1,0:T(8,128)} %param.11), kind=kLoop, calls=%fused_computation.154 | loop fusion | bytes 163840 | tf_op jit(solution)/shard_map/slice | solution.py:194
  1.5 0.1 copy-done
  1.6 3.0 %collective-permute-start.2 = (f32[6,4,8,128]{3,2,1,0:T(8,128)S(1)}, f32[6,4,8,128]{3,2,1,0:T(8,128)S(1)}, u32[]{:S(2)}, u32[]{:S(2)}) collective-permute-start(f32[6,4,8,128]{3,2,1,0:T(8,128)S(1)} %pad_maximum_fusion.2), channel_id=1, source_target_pairs={{0,4},{4,0},{1,5},{5,1},{2,6},{6,2},{3,7},{7,3},{8,12},{12,8},{9,1... | collective-permute-start | bytes 294920 | tf_op jit(solution)/shard_map/ppermute | solution.py:149
  4.7 1.5 %collective-permute-start.1 = (f32[6,1,16,128]{3,2,1,0:T(8,128)S(1)}, f32[6,1,16,128]{3,2,1,0:T(8,128)S(1)}, u32[]{:S(2)}, u32[]{:S(2)}) collective-permute-start(f32[6,1,16,128]{3,2,1,0:T(8,128)S(1)} %get-tuple-element.56), channel_id=1, source_target_pairs={{0,1},{1,2},{2,3},{4,5},{5,6},{6,7},{8,9},{9,10},{10,11},{12,13},{... | collective-permute-start | bytes 147464 | tf_op jit(solution)/shard_map/ppermute | solution.py:122
  6.2 1.3 %collective-permute-start = (f32[6,1,16,128]{3,2,1,0:T(8,128)S(1)}, f32[6,1,16,128]{3,2,1,0:T(8,128)S(1)}, u32[]{:S(2)}, u32[]{:S(2)}) collective-permute-start(f32[6,1,16,128]{3,2,1,0:T(8,128)S(1)} %get-tuple-element.57), channel_id=1, source_target_pairs={{1,0},{2,1},{3,2},{5,4},{6,5},{7,6},{9,8},{10,9},{11,10},{13,12},{... | collective-permute-start | bytes 147464 | tf_op jit(solution)/shard_map/ppermute | solution.py:122
  7.6 0.3 copy.113
  7.9 0.3 copy.114
  8.4 1.6 %collective-permute-start.4 = (f32[6,4,16,1]{2,0,3,1:T(8,128)S(1)}, f32[6,4,16,1]{2,0,3,1:T(8,128)S(1)}, u32[]{:S(2)}, u32[]{:S(2)}) collective-permute-start(f32[6,4,16,1]{2,0,3,1:T(8,128)S(1)} %get-tuple-element.67), channel_id=1, source_target_pairs={{0,8},{8,16},{16,24},{24,0},{1,9},{9,17},{17,25},{25,1},{2,10},{10... | collective-permute-start | bytes 4616 | tf_op jit(solution)/shard_map/ppermute | solution.py:122
  10.1 2.2 %collective-permute-start.3 = (f32[6,4,16,1]{2,0,3,1:T(8,128)S(1)}, f32[6,4,16,1]{2,0,3,1:T(8,128)S(1)}, u32[]{:S(2)}, u32[]{:S(2)}) collective-permute-start(f32[6,4,16,1]{2,0,3,1:T(8,128)S(1)} %get-tuple-element.68), channel_id=1, source_target_pairs={{0,24},{8,0},{16,8},{24,16},{1,25},{9,1},{17,9},{25,17},{2,26},{10... | collective-permute-start | bytes 4616 | tf_op jit(solution)/shard_map/ppermute | solution.py:122
  12.3 0.7 %copy-done.7 = f32[3,5,5]{2,0,1:T(4,128)S(1)} copy-done((f32[3,5,5]{2,0,1:T(4,128)S(1)}, f32[3,5,5]{2,0,1:T(4,128)}, u32[]{:S(2)}) %copy-start.7) | copy-done | bytes 324
  13.1 0.1 subtract_multiply_fusion
  13.3 0.7 %copy-done.9 = s32[4,128]{1,0:T(4,128)S(1)} copy-done((s32[4,128]{1,0:T(4,128)S(1)}, s32[4,128]{1,0:T(4,128)}, u32[]{:S(2)}) %copy-start.9) | copy-done | bytes 2072
  14.0 0.5 multiply_reduce_fusion.2
  14.5 0.2 multiply_reduce_fusion
  14.7 0.1 multiply_reduce_fusion.4
  14.9 0.2 slice_reduce_fusion
  15.1 0.6 %copy-done.8 = f32[3,5]{1,0:T(4,128)S(1)} copy-done((f32[3,5]{1,0:T(4,128)S(1)}, f32[3,5]{1,0:T(4,128)}, u32[]{:S(2)}) %copy-start.8) | copy-done | bytes 84
  16.1 0.2 copy.102
  16.3 0.2 copy.100
  16.6 0.1 multiply_reduce_fusion.7
  17.0 0.5 copy-done.4
  17.5 0.2 fusion.15
  17.8 0.7 %copy-done.1 = f32[4,16,128]{2,1,0:T(8,128)S(1)} copy-done((f32[4,16,128]{2,1,0:T(8,128)S(1)}, f32[4,16,128]{2,1,0:T(8,128)}, u32[]{:S(2)}) %copy-start.1) | copy-done | bytes 32792
  18.7 0.6 %collective-permute-start.5 = (f32[4,4,3,3]{3,2,1,0:T(4,128)S(1)}, f32[4,4,3,3]{3,2,1,0:T(4,128)S(1)}, u32[]{:S(2)}, u32[]{:S(2)}) collective-permute-start(f32[4,4,3,3]{3,2,1,0:T(4,128)S(1)} %get-tuple-element.47), channel_id=1, source_target_pairs={{0,12},{8,20},{16,28},{24,4},{4,8},{12,16},{20,24},{28,0},{1,13},{... | collective-permute-start | bytes 1736 | tf_op jit(solution)/shard_map/ppermute | solution.py:139
  19.3 1.6 %collective-permute-start.8 = (f32[4,4,16,3]{3,2,1,0:T(8,128)S(1)}, f32[4,4,16,3]{3,2,1,0:T(8,128)S(1)}, u32[]{:S(2)}, u32[]{:S(2)}) collective-permute-start(f32[4,4,16,3]{3,2,1,0:T(8,128)S(1)} %get-tuple-element.45), channel_id=1, source_target_pairs={{0,8},{8,16},{16,24},{24,0},{1,9},{9,17},{17,25},{25,1},{2,10},{10... | collective-permute-start | bytes 9224 | tf_op jit(solution)/shard_map/ppermute | solution.py:122
  20.9 2.3 %collective-permute-start.9 = (f32[4,4,16,3]{3,2,1,0:T(8,128)S(1)}, f32[4,4,16,3]{3,2,1,0:T(8,128)S(1)}, u32[]{:S(2)}, u32[]{:S(2)}) collective-permute-start(f32[4,4,16,3]{3,2,1,0:T(8,128)S(1)} %get-tuple-element.46), channel_id=1, source_target_pairs={{0,24},{8,0},{16,8},{24,16},{1,25},{9,1},{17,9},{25,17},{2,26},{10... | collective-permute-start | bytes 9224 | tf_op jit(solution)/shard_map/ppermute | solution.py:122
  23.2 2.3 %collective-permute-start.7 = (f32[4,4,3,3]{3,2,1,0:T(4,128)S(1)}, f32[4,4,3,3]{3,2,1,0:T(4,128)S(1)}, u32[]{:S(2)}, u32[]{:S(2)}) collective-permute-start(f32[4,4,3,3]{3,2,1,0:T(4,128)S(1)} %get-tuple-element.48), channel_id=1, source_target_pairs={{0,28},{8,4},{16,12},{24,20},{4,24},{12,0},{20,8},{28,16},{1,29},{... | collective-permute-start | bytes 1736 | tf_op jit(solution)/shard_map/ppermute | solution.py:139
  25.5 1.1 %collective-permute-start.6 = (f32[4,4,3,128]{3,2,1,0:T(4,128)S(1)}, f32[4,4,3,128]{3,2,1,0:T(4,128)S(1)}, u32[]{:S(2)}, u32[]{:S(2)}) collective-permute-start(f32[4,4,3,128]{3,2,1,0:T(4,128)S(1)} %fusion.29), channel_id=1, source_target_pairs={{0,4},{4,0},{1,5},{5,1},{2,6},{6,2},{3,7},{7,3},{8,12},{12,8},{9,1... | collective-permute-start | bytes 73736 | tf_op jit(solution)/shard_map/ppermute | solution.py:139
  26.6 5.0 %collective-permute-done.7 = f32[4,4,3,3]{3,2,1,0:T(4,128)S(1)} collective-permute-done((f32[4,4,3,3]{3,2,1,0:T(4,128)S(1)}, f32[4,4,3,3]{3,2,1,0:T(4,128)S(1)}, u32[]{:S(2)}, u32[]{:S(2)}) %collective-permute-start.7) | collective-permute-done | bytes 608 | tf_op jit(solution)/shard_map/ppermute | solution.py:139
  31.7 0.3 maximum_maximum_fusion
  32.1 0.2 reshape.159
  32.3 2.0 %collective-permute-start.10 = (f32[280,128]{1,0:T(8,128)S(1)}, f32[280,128]{1,0:T(8,128)S(1)}, u32[]{:S(2)}, u32[]{:S(2)}) collective-permute-start(f32[280,128]{1,0:T(8,128)S(1)} %pad_bitcast_fusion.1), channel_id=1, source_target_pairs={{0,1},{1,2},{2,3},{4,5},{5,6},{6,7},{8,9},{9,10},{10,11},{12,13},{... | collective-permute-start | bytes 430088 | tf_op jit(solution)/shard_map/ppermute | solution.py:126
  34.4 0.2 reshape.163
  34.6 1.3 %collective-permute-start.11 = (f32[280,128]{1,0:T(8,128)S(1)}, f32[280,128]{1,0:T(8,128)S(1)}, u32[]{:S(2)}, u32[]{:S(2)}) collective-permute-start(f32[280,128]{1,0:T(8,128)S(1)} %pad_bitcast_fusion), channel_id=1, source_target_pairs={{1,0},{2,1},{3,2},{5,4},{6,5},{7,6},{9,8},{10,9},{11,10},{13,12},{... | collective-permute-start | bytes 430088 | tf_op jit(solution)/shard_map/ppermute | solution.py:126
  35.9 0.2 reshape.162
  36.2 3.3 %collective-permute-done.11 = f32[280,128]{1,0:T(8,128)S(1)} collective-permute-done((f32[280,128]{1,0:T(8,128)S(1)}, f32[280,128]{1,0:T(8,128)S(1)}, u32[]{:S(2)}, u32[]{:S(2)}) %collective-permute-start.11) | collective-permute-done | bytes 143392 | tf_op jit(solution)/shard_map/ppermute | solution.py:126
  39.4 0.2 reshape.166
  39.7 0.3 pad_maximum_fusion
  40.0 0.1 multiply_add_fusion
  40.2 0.1 multiply_add_fusion.1
  40.4 0.1 broadcast_multiply_fusion
  40.5 1.2 %broadcast_multiply_fusion.1 = (f32[3,8,20,132]{3,2,1,0:T(8,128)S(1)}, f32[3,8,20,132]{3,2,1,0:T(8,128)S(1)}) fusion(f32[8,20,132]{2,1,0:T(8,128)S(1)} %get-tuple-element.36, f32[3,10,22,134]{3,2,1,0:T(8,128)S(1)} %get-tuple-element.27, f32[8,20,132]{2,1,0:T(8,128)S(1)} %get-tuple-element.35, f32[4,10,22,134]{3,2,1,0:T(8,128)S(1)} %pad_maximum_fusion, ...), kind=kLoop, calls=%fused_computation.42 | loop fusion | flops 760320 | bytes 2703360 | tf_op jit(solution)/shard_map/mul | solution.py:60
  41.7 0.9 %broadcast_multiply_fusion.2 = (f32[3,6,18,130]{3,2,1,0:T(8,128)S(1)}, f32[3,6,18,130]{3,2,1,0:T(8,128)S(1)}) fusion(f32[6,18,130]{2,1,0:T(8,128)S(1)} %get-tuple-element.34, f32[3,8,20,132]{3,2,1,0:T(8,128)S(1)} %get-tuple-element.25, f32[6,18,130]{2,1,0:T(8,128)S(1)} %get-tuple-element.33, f32[4,10,22,134]{3,2,1,0:T(8,128)S(1)} %pad_maximum_fusion, ...), kind=kLoop, calls=%fused_computation.45 | loop fusion | flops 505440 | bytes 1797120 | tf_op jit(solution)/shard_map/mul | solution.py:60
  42.6 0.9 %multiply_reduce_fusion.9 = (f32[3,4,128]{2,1,0:T(4,128)S(1)}, f32[3,4,16,128]{3,2,1,0:T(8,128)}) fusion(f32[4,16,128]{2,1,0:T(8,128)S(1)} %copy-done.5, f32[3,6,18,130]{3,2,1,0:T(8,128)S(1)} %get-tuple-element.23, f32[3,4,16,128]{3,2,1,0:T(8,128)S(1)} %multiply_reduce_fusion.6, f32[4,16,128]{2,1,0:T(8,128)S(1)} %fusion.34, ...), kind=kLoop, calls=%fused_computation.82 | loop fusion | flops 317952 | bytes 956416 | tf_op jit(solution)/shard_map/reduce_sum | solution.py:265
  43.5 0.4 convolution_bitcast_fusion
  43.8 0.2 select_select_fusion
  44.0 13.4 %all_to_all.5 = f32[32,3,128]{2,1,0:T(4,128)S(1)} all-to-all(f32[32,3,128]{2,1,0:T(4,128)S(1)} %select_select_fusion), channel_id=1, replica_groups=mesh['circ'=4,'normal'=2,'span'=4] {'span','normal','circ'}, dimensions={0} | all-to-all | bytes 98304 | tf_op jit(solution)/shard_map/all_to_all | solution.py:230
  57.5 0.6 %reduce_sum.167 = f32[3,128]{1,0:T(4,128)} reduce(f32[32,3,128]{2,1,0:T(4,128)S(1)} %all_to_all.5, f32[]{:T(128)} %constant.19.clone.1), dimensions={0}, to_apply=%region_14.15 | reduce | flops 11904 | bytes 50692 | tf_op jit(solution)/shard_map/reduce_sum | solution.py:230
  (84 shorter events, 1.8 us)
Async XLA Ops:
  0.6 0.9 %copy-start = (f32[5,4,16,128]{3,2,1,0:T(8,128)S(1)}, f32[5,4,16,128]{3,2,1,0:T(8,128)}, u32[]{:S(2)}) copy-start(f32[5,4,16,128]{3,2,1,0:T(8,128)} %param.9) | copy-start | bytes 491524
  1.6 3.1 %copy-start.3 = (f32[3,4,16,128]{3,2,1,0:T(8,128)S(1)}, f32[3,4,16,128]{3,2,1,0:T(8,128)}, u32[]{:S(2)}) copy-start(f32[3,4,16,128]{3,2,1,0:T(8,128)} %param.11) | copy-start | bytes 294916
  1.6 15.1 %collective-permute-start.2 = (f32[6,4,8,128]{3,2,1,0:T(8,128)S(1)}, f32[6,4,8,128]{3,2,1,0:T(8,128)S(1)}, u32[]{:S(2)}, u32[]{:S(2)}) collective-permute-start(f32[6,4,8,128]{3,2,1,0:T(8,128)S(1)} %pad_maximum_fusion.2), channel_id=1, source_target_pairs={{0,4},{4,0},{1,5},{5,1},{2,6},{6,2},{3,7},{7,3},{8,12},{12,8},{9,1... | collective-permute-start | bytes 294920 | tf_op jit(solution)/shard_map/ppermute | solution.py:149
  4.7 11.8 %collective-permute-start.1 = (f32[6,1,16,128]{3,2,1,0:T(8,128)S(1)}, f32[6,1,16,128]{3,2,1,0:T(8,128)S(1)}, u32[]{:S(2)}, u32[]{:S(2)}) collective-permute-start(f32[6,1,16,128]{3,2,1,0:T(8,128)S(1)} %get-tuple-element.56), channel_id=1, source_target_pairs={{0,1},{1,2},{2,3},{4,5},{5,6},{6,7},{8,9},{9,10},{10,11},{12,13},{... | collective-permute-start | bytes 147464 | tf_op jit(solution)/shard_map/ppermute | solution.py:122
  6.2 10.4 %collective-permute-start = (f32[6,1,16,128]{3,2,1,0:T(8,128)S(1)}, f32[6,1,16,128]{3,2,1,0:T(8,128)S(1)}, u32[]{:S(2)}, u32[]{:S(2)}) collective-permute-start(f32[6,1,16,128]{3,2,1,0:T(8,128)S(1)} %get-tuple-element.57), channel_id=1, source_target_pairs={{1,0},{2,1},{3,2},{5,4},{6,5},{7,6},{9,8},{10,9},{11,10},{13,12},{... | collective-permute-start | bytes 147464 | tf_op jit(solution)/shard_map/ppermute | solution.py:122
  8.4 7.4 %collective-permute-start.4 = (f32[6,4,16,1]{2,0,3,1:T(8,128)S(1)}, f32[6,4,16,1]{2,0,3,1:T(8,128)S(1)}, u32[]{:S(2)}, u32[]{:S(2)}) collective-permute-start(f32[6,4,16,1]{2,0,3,1:T(8,128)S(1)} %get-tuple-element.67), channel_id=1, source_target_pairs={{0,8},{8,16},{16,24},{24,0},{1,9},{9,17},{17,25},{25,1},{2,10},{10... | collective-permute-start | bytes 4616 | tf_op jit(solution)/shard_map/ppermute | solution.py:122
  10.0 2.3 %copy-start.6 = (f32[3,5,5]{2,0,1:T(4,128)S(1)}, f32[3,5,5]{2,0,1:T(4,128)}, u32[]{:S(2)}) copy-start(f32[3,5,5]{2,0,1:T(4,128)} %param.12) | copy-start | bytes 904
  10.1 5.9 %collective-permute-start.3 = (f32[6,4,16,1]{2,0,3,1:T(8,128)S(1)}, f32[6,4,16,1]{2,0,3,1:T(8,128)S(1)}, u32[]{:S(2)}, u32[]{:S(2)}) collective-permute-start(f32[6,4,16,1]{2,0,3,1:T(8,128)S(1)} %get-tuple-element.68), channel_id=1, source_target_pairs={{0,24},{8,0},{16,8},{24,16},{1,25},{9,1},{17,9},{25,17},{2,26},{10... | collective-permute-start | bytes 4616 | tf_op jit(solution)/shard_map/ppermute | solution.py:122
  12.3 0.7 %copy-start.7 = (f32[3,5,5]{2,0,1:T(4,128)S(1)}, f32[3,5,5]{2,0,1:T(4,128)}, u32[]{:S(2)}) copy-start(f32[3,5,5]{2,0,1:T(4,128)} %param.13) | copy-start | bytes 904
  13.3 0.7 %copy-start.9 = (s32[4,128]{1,0:T(4,128)S(1)}, s32[4,128]{1,0:T(4,128)}, u32[]{:S(2)}) copy-start(s32[4,128]{1,0:T(4,128)} %param.17) | copy-start | bytes 6148
  15.1 0.7 %copy-start.8 = (f32[3,5]{1,0:T(4,128)S(1)}, f32[3,5]{1,0:T(4,128)}, u32[]{:S(2)}) copy-start(f32[3,5]{1,0:T(4,128)} %param.14) | copy-start | bytes 184
  16.5 0.9 %copy-start.4 = (f32[5,4,16,128]{3,2,1,0:T(8,128)S(1)}, f32[5,4,16,128]{3,2,1,0:T(8,128)}, u32[]{:S(2)}) copy-start(f32[5,4,16,128]{3,2,1,0:T(8,128)} %param.10) | copy-start | bytes 491524
  17.6 0.9 %copy-start.2 = (f32[5,4,16,128]{3,2,1,0:T(8,128)}, f32[5,4,16,128]{3,2,1,0:T(8,128)S(1)}, u32[]{:S(2)}) copy-start(f32[5,4,16,128]{3,2,1,0:T(8,128)S(1)} %fusion.15) | copy-start | bytes 491524
  17.7 0.8 %copy-start.1 = (f32[4,16,128]{2,1,0:T(8,128)S(1)}, f32[4,16,128]{2,1,0:T(8,128)}, u32[]{:S(2)}) copy-start(f32[4,16,128]{2,1,0:T(8,128)} %param.15) | copy-start | bytes 98308
  18.7 8.0 %collective-permute-start.5 = (f32[4,4,3,3]{3,2,1,0:T(4,128)S(1)}, f32[4,4,3,3]{3,2,1,0:T(4,128)S(1)}, u32[]{:S(2)}, u32[]{:S(2)}) collective-permute-start(f32[4,4,3,3]{3,2,1,0:T(4,128)S(1)} %get-tuple-element.47), channel_id=1, source_target_pairs={{0,12},{8,20},{16,28},{24,4},{4,8},{12,16},{20,24},{28,0},{1,13},{... | collective-permute-start | bytes 1736 | tf_op jit(solution)/shard_map/ppermute | solution.py:139
  19.3 12.4 %collective-permute-start.8 = (f32[4,4,16,3]{3,2,1,0:T(8,128)S(1)}, f32[4,4,16,3]{3,2,1,0:T(8,128)S(1)}, u32[]{:S(2)}, u32[]{:S(2)}) collective-permute-start(f32[4,4,16,3]{3,2,1,0:T(8,128)S(1)} %get-tuple-element.45), channel_id=1, source_target_pairs={{0,8},{8,16},{16,24},{24,0},{1,9},{9,17},{17,25},{25,1},{2,10},{10... | collective-permute-start | bytes 9224 | tf_op jit(solution)/shard_map/ppermute | solution.py:122
  20.9 10.8 %collective-permute-start.9 = (f32[4,4,16,3]{3,2,1,0:T(8,128)S(1)}, f32[4,4,16,3]{3,2,1,0:T(8,128)S(1)}, u32[]{:S(2)}, u32[]{:S(2)}) collective-permute-start(f32[4,4,16,3]{3,2,1,0:T(8,128)S(1)} %get-tuple-element.46), channel_id=1, source_target_pairs={{0,24},{8,0},{16,8},{24,16},{1,25},{9,1},{17,9},{25,17},{2,26},{10... | collective-permute-start | bytes 9224 | tf_op jit(solution)/shard_map/ppermute | solution.py:122
  23.2 8.4 %collective-permute-start.7 = (f32[4,4,3,3]{3,2,1,0:T(4,128)S(1)}, f32[4,4,3,3]{3,2,1,0:T(4,128)S(1)}, u32[]{:S(2)}, u32[]{:S(2)}) collective-permute-start(f32[4,4,3,3]{3,2,1,0:T(4,128)S(1)} %get-tuple-element.48), channel_id=1, source_target_pairs={{0,28},{8,4},{16,12},{24,20},{4,24},{12,0},{20,8},{28,16},{1,29},{... | collective-permute-start | bytes 1736 | tf_op jit(solution)/shard_map/ppermute | solution.py:139
  25.5 6.1 %collective-permute-start.6 = (f32[4,4,3,128]{3,2,1,0:T(4,128)S(1)}, f32[4,4,3,128]{3,2,1,0:T(4,128)S(1)}, u32[]{:S(2)}, u32[]{:S(2)}) collective-permute-start(f32[4,4,3,128]{3,2,1,0:T(4,128)S(1)} %fusion.29), channel_id=1, source_target_pairs={{0,4},{4,0},{1,5},{5,1},{2,6},{6,2},{3,7},{7,3},{8,12},{12,8},{9,1... | collective-permute-start | bytes 73736 | tf_op jit(solution)/shard_map/ppermute | solution.py:139
  32.3 3.6 %collective-permute-start.10 = (f32[280,128]{1,0:T(8,128)S(1)}, f32[280,128]{1,0:T(8,128)S(1)}, u32[]{:S(2)}, u32[]{:S(2)}) collective-permute-start(f32[280,128]{1,0:T(8,128)S(1)} %pad_bitcast_fusion.1), channel_id=1, source_target_pairs={{0,1},{1,2},{2,3},{4,5},{5,6},{6,7},{8,9},{9,10},{10,11},{12,13},{... | collective-permute-start | bytes 430088 | tf_op jit(solution)/shard_map/ppermute | solution.py:126
  34.6 4.8 %collective-permute-start.11 = (f32[280,128]{1,0:T(8,128)S(1)}, f32[280,128]{1,0:T(8,128)S(1)}, u32[]{:S(2)}, u32[]{:S(2)}) collective-permute-start(f32[280,128]{1,0:T(8,128)S(1)} %pad_bitcast_fusion), channel_id=1, source_target_pairs={{1,0},{2,1},{3,2},{5,4},{6,5},{7,6},{9,8},{10,9},{11,10},{13,12},{... | collective-permute-start | bytes 430088 | tf_op jit(solution)/shard_map/ppermute | solution.py:126
  41.7 0.9 %copy-start.5 = (f32[4,16,128]{2,1,0:T(8,128)S(1)}, f32[4,16,128]{2,1,0:T(8,128)}, u32[]{:S(2)}) copy-start(f32[4,16,128]{2,1,0:T(8,128)} %param.16) | copy-start | bytes 98308

commit v23 on v19

--- a/solution.py
+++ b/solution.py
@@ -126,7 +126,7 @@
     return lax.ppermute(flat, axes, pairs).reshape(-1)[:size].reshape(slab.shape)
 
 
-def receive_pair(array, rel, axis, dims, width):
+def receive_pair(array, rel, axis, dims, width, pack=False):
     low = dict(rel, **{axis: -1})
     high = dict(rel, **{axis: 1})
     if lax.axis_size(axis) != 2 or WRAP[axis]:
@@ -136,7 +136,13 @@
     low_nz = {a: r for a, r in low.items() if r}
     axes, pairs = pairs_for({a: -r for a, r in low_nz.items()})
     _, back = pairs_for({a: -r for a, r in dict(low_nz, **{axis: 1}).items()})
-    got = lax.ppermute(sent, axes, pairs + back)
+    if pack:
+        size = sent.size
+        rows = -(-size // 1024) * 8
+        flat = jnp.pad(sent.reshape(-1), (0, rows * 128 - size)).reshape(rows, 128)
+        got = lax.ppermute(flat, axes, pairs + back).reshape(-1)[:size].reshape(sent.shape)
+    else:
+        got = lax.ppermute(sent, axes, pairs + back)
     zero = jnp.zeros_like(got)
     return jnp.where(me == 1, got, zero), jnp.where(me == 0, got, zero)
 
@@ -168,8 +174,8 @@
     before_c = receive(joined, {"circ": -1}, dims, width)
     after_c = receive(joined, {"circ": 1}, dims, width)
     low_n, high_n = receive_pair(joined, {}, "normal", dims, width)
-    low_lc, high_lc = receive_pair(joined, {"circ": -1}, "normal", dims, width)
-    low_hc, high_hc = receive_pair(joined, {"circ": 1}, "normal", dims, width)
+    low_lc, high_lc = receive_pair(joined, {"circ": -1}, "normal", dims, width, True)
+    low_hc, high_hc = receive_pair(joined, {"circ": 1}, "normal", dims, width, True)
     top = jnp.concatenate([low_lc, low_n, low_hc], axis=3)
     middle = jnp.concatenate([before_c, joined, after_c], axis=3)
     bottom = jnp.concatenate([high_lc, high_n, high_hc], axis=3)

time: 58.6 us -> 61.8 us (1.055)
  blocking collectives: 13.4 us -> 15.6 us
  starting transfers between devices: 20.9 us -> 22.8 us
  waiting for transfers between devices: 8.29 us -> 6.62 us
  local copies, waits for them, and re-layouts: 6.76 us -> 7.58 us
    ppermute x3 -> x1, waiting for transfers between devices: 5.01 us -> 0.01 us  [receive_pair(): got = lax.ppermute(sent, axes, pairs + back)]
    ppermute x0 -> x2, starting transfers between devices: none -> 4.82 us  [receive_pair(): lax.ppermute(flat, axes, pairs + back).reshape(-1)[:size]]
    ppermute x3 -> x1, starting transfers between devices: 4.02 us -> 1.08 us  [receive_pair(): got = lax.ppermute(sent, axes, pairs + back)]
    all_to_all x1, blocking collectives: 13.4 us -> 15.6 us  [reduce_panels(): lax.all_to_all(chunks, ORDER[::-1], 0, 0, tiled=False)]
    ppermute x2, waiting for transfers between devices: 3.27 us -> 5.1 us  [receive(): lax.ppermute(flat, axes, pairs).reshape(-1)[:size].reshape(slab.shape)]
    ppermute x0 -> x2, waiting for transfers between devices: none -> 1.5 us  [receive_pair(): lax.ppermute(flat, axes, pairs + back).reshape(-1)[:size]]
  transfers between devices with their start and end apart: 12 -> 12, of which waited for: 2 -> 2; matrix products, arithmetic and copies ran while one was open for 6% -> 7% of each run, Pallas kernels for 0% -> 0%
where the time goes in v23:
time: 61.8 us; the launch traced here: 61.3 us
  starting transfers between devices  22.8 us (37%)
  blocking collectives  15.6 us (25%)
  local copies, waits for them, and re-layouts  7.58 us (12%)
  other arithmetic  7.02 us (11%)
  waiting for transfers between devices  6.62 us (11%)
  between operations  1.3 us (2%)
    all_to_all x1, blocking collectives, reduce_panels(): lax.all_to_all(chunks, ORDER[::-1], 0, 0, tiled=False)  15.6 us
    ppermute x6, starting transfers between devices, receive(): return lax.ppermute(slab, axes, pairs)  10.5 us
    ppermute x2, waiting for transfers between devices, receive(): lax.ppermute(flat, axes, pairs).reshape(-1)[:size].reshape(slab.shape)  5.1 us
    ppermute x2, starting transfers between devices, receive_pair(): lax.ppermute(flat, axes, pairs + back).reshape(-1)[:size]  4.82 us
    unnamed x28, local copies, waits for them, and re-layouts  4.02 us
    ppermute x2, starting transfers between devices, receive(): lax.ppermute(flat, axes, pairs).reshape(-1)[:size].reshape(slab.shape)  3.32 us
    ppermute x1, starting transfers between devices, tile_halos(): got = lax.ppermute(sent, axis, [(0, 1), (1, 0)])  3.03 us
    mul x3, other arithmetic, relax(): weighted = stiff_pad[None] * mesh_pad  2.17 us
  transfers between devices with their start and end apart: 12, of which 2 were waited for; matrix products, arithmetic and copies ran while one was open for 7% of the time, Pallas kernels for 0%

profile of v23, /device:TPU:0, one launch (start us, length us, event | category | flops | bytes accessed | tf_op | source)
XLA Modules:
  0.0 61.3 jit_solution(11114683240443387691)
XLA Ops:
  0.6 0.8 %fusion.51 = (f32[1,4,16,128]{3,2,1,0:T(8,128)S(1)}, f32[4,16,128]{2,1,0:T(8,128)S(1)}, f32[4,16,128]{2,1,0:T(8,128)S(1)}) fusion(f32[3,4,16,128]{3,2,1,0:T(8,128)} %param.11), kind=kLoop, calls=%fused_computation.156 | loop fusion | bytes 163840 | tf_op jit(solution)/shard_map/slice | solution.py:200
  1.6 3.0 %collective-permute-start.2 = (f32[6,4,8,128]{3,2,1,0:T(8,128)S(1)}, f32[6,4,8,128]{3,2,1,0:T(8,128)S(1)}, u32[]{:S(2)}, u32[]{:S(2)}) collective-permute-start(f32[6,4,8,128]{3,2,1,0:T(8,128)S(1)} %pad_maximum_fusion.2), channel_id=1, source_target_pairs={{0,4},{4,0},{1,5},{5,1},{2,6},{6,2},{3,7},{7,3},{8,12},{12,8},{9,1... | collective-permute-start | bytes 294920 | tf_op jit(solution)/shard_map/ppermute | solution.py:155
  4.7 1.5 %collective-permute-start.1 = (f32[6,1,16,128]{3,2,1,0:T(8,128)S(1)}, f32[6,1,16,128]{3,2,1,0:T(8,128)S(1)}, u32[]{:S(2)}, u32[]{:S(2)}) collective-permute-start(f32[6,1,16,128]{3,2,1,0:T(8,128)S(1)} %get-tuple-element.56), channel_id=1, source_target_pairs={{0,1},{1,2},{2,3},{4,5},{5,6},{6,7},{8,9},{9,10},{10,11},{12,13},{... | collective-permute-start | bytes 147464 | tf_op jit(solution)/shard_map/ppermute | solution.py:122
  6.2 1.3 %collective-permute-start = (f32[6,1,16,128]{3,2,1,0:T(8,128)S(1)}, f32[6,1,16,128]{3,2,1,0:T(8,128)S(1)}, u32[]{:S(2)}, u32[]{:S(2)}) collective-permute-start(f32[6,1,16,128]{3,2,1,0:T(8,128)S(1)} %get-tuple-element.57), channel_id=1, source_target_pairs={{1,0},{2,1},{3,2},{5,4},{6,5},{7,6},{9,8},{10,9},{11,10},{13,12},{... | collective-permute-start | bytes 147464 | tf_op jit(solution)/shard_map/ppermute | solution.py:122
  7.6 0.3 copy.113
  7.9 0.3 copy.114
  8.4 1.6 %collective-permute-start.4 = (f32[6,4,16,1]{2,0,3,1:T(8,128)S(1)}, f32[6,4,16,1]{2,0,3,1:T(8,128)S(1)}, u32[]{:S(2)}, u32[]{:S(2)}) collective-permute-start(f32[6,4,16,1]{2,0,3,1:T(8,128)S(1)} %get-tuple-element.63), channel_id=1, source_target_pairs={{0,8},{8,16},{16,24},{24,0},{1,9},{9,17},{17,25},{25,1},{2,10},{10... | collective-permute-start | bytes 4616 | tf_op jit(solution)/shard_map/ppermute | solution.py:122
  10.1 2.2 %collective-permute-start.3 = (f32[6,4,16,1]{2,0,3,1:T(8,128)S(1)}, f32[6,4,16,1]{2,0,3,1:T(8,128)S(1)}, u32[]{:S(2)}, u32[]{:S(2)}) collective-permute-start(f32[6,4,16,1]{2,0,3,1:T(8,128)S(1)} %get-tuple-element.64), channel_id=1, source_target_pairs={{0,24},{8,0},{16,8},{24,16},{1,25},{9,1},{17,9},{25,17},{2,26},{10... | collective-permute-start | bytes 4616 | tf_op jit(solution)/shard_map/ppermute | solution.py:122
  12.3 0.7 %copy-done.7 = f32[3,5,5]{2,0,1:T(4,128)S(1)} copy-done((f32[3,5,5]{2,0,1:T(4,128)S(1)}, f32[3,5,5]{2,0,1:T(4,128)}, u32[]{:S(2)}) %copy-start.7) | copy-done | bytes 324
  13.3 0.7 %copy-done.9 = s32[4,128]{1,0:T(4,128)S(1)} copy-done((s32[4,128]{1,0:T(4,128)S(1)}, s32[4,128]{1,0:T(4,128)}, u32[]{:S(2)}) %copy-start.9) | copy-done | bytes 2072
  14.0 0.5 multiply_reduce_fusion.2
  14.5 0.2 multiply_reduce_fusion
  14.7 0.1 multiply_reduce_fusion.4
  14.9 0.2 slice_reduce_fusion
  15.1 0.6 %copy-done.8 = f32[3,5]{1,0:T(4,128)S(1)} copy-done((f32[3,5]{1,0:T(4,128)S(1)}, f32[3,5]{1,0:T(4,128)}, u32[]{:S(2)}) %copy-start.8) | copy-done | bytes 84
  16.1 0.2 copy.102
  16.3 0.2 copy.100
  17.0 0.5 copy-done.4
  17.5 0.2 fusion.15
  17.8 0.7 %copy-done.1 = f32[4,16,128]{2,1,0:T(8,128)S(1)} copy-done((f32[4,16,128]{2,1,0:T(8,128)S(1)}, f32[4,16,128]{2,1,0:T(8,128)}, u32[]{:S(2)}) %copy-start.1) | copy-done | bytes 32792
  18.8 3.8 %collective-permute-start.9 = (f32[4,4,16,3]{3,2,1,0:T(8,128)S(1)}, f32[4,4,16,3]{3,2,1,0:T(8,128)S(1)}, u32[]{:S(2)}, u32[]{:S(2)}) collective-permute-start(f32[4,4,16,3]{3,2,1,0:T(8,128)S(1)} %get-tuple-element.46), channel_id=1, source_target_pairs={{0,24},{8,0},{16,8},{24,16},{1,25},{9,1},{17,9},{25,17},{2,26},{10... | collective-permute-start | bytes 9224 | tf_op jit(solution)/shard_map/ppermute | solution.py:122
  22.6 1.1 %collective-permute-start.6 = (f32[4,4,3,128]{3,2,1,0:T(4,128)S(1)}, f32[4,4,3,128]{3,2,1,0:T(4,128)S(1)}, u32[]{:S(2)}, u32[]{:S(2)}) collective-permute-start(f32[4,4,3,128]{3,2,1,0:T(4,128)S(1)} %fusion.29), channel_id=1, source_target_pairs={{0,4},{4,0},{1,5},{5,1},{2,6},{6,2},{3,7},{7,3},{8,12},{12,8},{9,1... | collective-permute-start | bytes 73736 | tf_op jit(solution)/shard_map/ppermute | solution.py:145
  23.6 0.1 reshape.191
  23.8 0.1 reshape.194
  24.0 4.8 %collective-permute-start.7 = (f32[8,128]{1,0:T(8,128)S(1)}, f32[8,128]{1,0:T(8,128)S(1)}, u32[]{:S(2)}, u32[]{:S(2)}) collective-permute-start(f32[8,128]{1,0:T(8,128)S(1)} %pad_bitcast_fusion.2), channel_id=1, source_target_pairs={{0,28},{8,4},{16,12},{24,20},{4,24},{12,0},{20,8},{28,16},{1,29},{... | collective-permute-start | bytes 12296 | tf_op jit(solution)/shard_map/ppermute | solution.py:143
  28.7 1.5 %collective-permute-done.5 = f32[8,128]{1,0:T(8,128)S(1)} collective-permute-done((f32[8,128]{1,0:T(8,128)S(1)}, f32[8,128]{1,0:T(8,128)S(1)}, u32[]{:S(2)}, u32[]{:S(2)}) %collective-permute-start.5) | collective-permute-done | bytes 4128 | tf_op jit(solution)/shard_map/ppermute | solution.py:143
  30.3 0.1 select_n.114
  30.4 0.1 select_n.124
  30.5 0.1 select_n.121
  30.7 0.1 select_n.127
  30.9 0.3 maximum_maximum_fusion
  31.3 0.2 reshape.197
  31.5 2.0 %collective-permute-start.10 = (f32[280,128]{1,0:T(8,128)S(1)}, f32[280,128]{1,0:T(8,128)S(1)}, u32[]{:S(2)}, u32[]{:S(2)}) collective-permute-start(f32[280,128]{1,0:T(8,128)S(1)} %pad_bitcast_fusion.1), channel_id=1, source_target_pairs={{0,1},{1,2},{2,3},{4,5},{5,6},{6,7},{8,9},{9,10},{10,11},{12,13},{... | collective-permute-start | bytes 430088 | tf_op jit(solution)/shard_map/ppermute | solution.py:126
  33.5 0.2 reshape.201
  33.8 1.3 %collective-permute-start.11 = (f32[280,128]{1,0:T(8,128)S(1)}, f32[280,128]{1,0:T(8,128)S(1)}, u32[]{:S(2)}, u32[]{:S(2)}) collective-permute-start(f32[280,128]{1,0:T(8,128)S(1)} %pad_bitcast_fusion), channel_id=1, source_target_pairs={{1,0},{2,1},{3,2},{5,4},{6,5},{7,6},{9,8},{10,9},{11,10},{13,12},{... | collective-permute-start | bytes 430088 | tf_op jit(solution)/shard_map/ppermute | solution.py:126
  35.1 0.2 reshape.200
  35.3 5.1 %collective-permute-done.11 = f32[280,128]{1,0:T(8,128)S(1)} collective-permute-done((f32[280,128]{1,0:T(8,128)S(1)}, f32[280,128]{1,0:T(8,128)S(1)}, u32[]{:S(2)}, u32[]{:S(2)}) %collective-permute-start.11) | collective-permute-done | bytes 143392 | tf_op jit(solution)/shard_map/ppermute | solution.py:126
  40.4 0.2 reshape.204
  40.7 0.3 pad_maximum_fusion
  41.0 0.1 multiply_add_fusion
  41.4 0.1 broadcast_multiply_fusion
  41.5 1.2 %broadcast_multiply_fusion.1 = (f32[3,8,20,132]{3,2,1,0:T(8,128)S(1)}, f32[3,8,20,132]{3,2,1,0:T(8,128)S(1)}) fusion(f32[8,20,132]{2,1,0:T(8,128)S(1)} %get-tuple-element.36, f32[3,10,22,134]{3,2,1,0:T(8,128)S(1)} %get-tuple-element.27, f32[8,20,132]{2,1,0:T(8,128)S(1)} %get-tuple-element.35, f32[4,10,22,134]{3,2,1,0:T(8,128)S(1)} %pad_maximum_fusion, ...), kind=kLoop, calls=%fused_computation.42 | loop fusion | flops 760320 | bytes 2703360 | tf_op jit(solution)/shard_map/mul | solution.py:60
  42.7 0.9 %broadcast_multiply_fusion.2 = (f32[3,6,18,130]{3,2,1,0:T(8,128)S(1)}, f32[3,6,18,130]{3,2,1,0:T(8,128)S(1)}) fusion(f32[6,18,130]{2,1,0:T(8,128)S(1)} %get-tuple-element.34, f32[3,8,20,132]{3,2,1,0:T(8,128)S(1)} %get-tuple-element.25, f32[6,18,130]{2,1,0:T(8,128)S(1)} %get-tuple-element.33, f32[4,10,22,134]{3,2,1,0:T(8,128)S(1)} %pad_maximum_fusion, ...), kind=kLoop, calls=%fused_computation.45 | loop fusion | flops 505440 | bytes 1797120 | tf_op jit(solution)/shard_map/mul | solution.py:60
  43.6 0.9 %multiply_reduce_fusion.9 = (f32[3,4,128]{2,1,0:T(4,128)S(1)}, f32[3,4,16,128]{3,2,1,0:T(8,128)}) fusion(f32[4,16,128]{2,1,0:T(8,128)S(1)} %copy-done.5, f32[3,6,18,130]{3,2,1,0:T(8,128)S(1)} %get-tuple-element.23, f32[3,4,16,128]{3,2,1,0:T(8,128)S(1)} %multiply_reduce_fusion.6, f32[4,16,128]{2,1,0:T(8,128)S(1)} %fusion.34, ...), kind=kLoop, calls=%fused_computation.82 | loop fusion | flops 317952 | bytes 956416 | tf_op jit(solution)/shard_map/reduce_sum | solution.py:271
  44.5 0.4 convolution_bitcast_fusion
  44.9 0.2 select_select_fusion
  45.1 15.6 %all_to_all.5 = f32[32,3,128]{2,1,0:T(4,128)S(1)} all-to-all(f32[32,3,128]{2,1,0:T(4,128)S(1)} %select_select_fusion), channel_id=1, replica_groups=mesh['circ'=4,'normal'=2,'span'=4] {'span','normal','circ'}, dimensions={0} | all-to-all | bytes 98304 | tf_op jit(solution)/shard_map/all_to_all | solution.py:236
  60.7 0.6 %reduce_sum.167 = f32[3,128]{1,0:T(4,128)} reduce(f32[32,3,128]{2,1,0:T(4,128)S(1)} %all_to_all.5, f32[]{:T(128)} %constant.19.clone.1), dimensions={0}, to_apply=%region_14.15 | reduce | flops 11904 | bytes 50692 | tf_op jit(solution)/shard_map/reduce_sum | solution.py:236
  (92 shorter events, 2.4 us)
Async XLA Ops:
  0.6 0.9 %copy-start = (f32[5,4,16,128]{3,2,1,0:T(8,128)S(1)}, f32[5,4,16,128]{3,2,1,0:T(8,128)}, u32[]{:S(2)}) copy-start(f32[5,4,16,128]{3,2,1,0:T(8,128)} %param.9) | copy-start | bytes 491524
  1.6 3.1 %copy-start.3 = (f32[3,4,16,128]{3,2,1,0:T(8,128)S(1)}, f32[3,4,16,128]{3,2,1,0:T(8,128)}, u32[]{:S(2)}) copy-start(f32[3,4,16,128]{3,2,1,0:T(8,128)} %param.11) | copy-start | bytes 294916
  1.6 15.1 %collective-permute-start.2 = (f32[6,4,8,128]{3,2,1,0:T(8,128)S(1)}, f32[6,4,8,128]{3,2,1,0:T(8,128)S(1)}, u32[]{:S(2)}, u32[]{:S(2)}) collective-permute-start(f32[6,4,8,128]{3,2,1,0:T(8,128)S(1)} %pad_maximum_fusion.2), channel_id=1, source_target_pairs={{0,4},{4,0},{1,5},{5,1},{2,6},{6,2},{3,7},{7,3},{8,12},{12,8},{9,1... | collective-permute-start | bytes 294920 | tf_op jit(solution)/shard_map/ppermute | solution.py:155
  4.7 11.8 %collective-permute-start.1 = (f32[6,1,16,128]{3,2,1,0:T(8,128)S(1)}, f32[6,1,16,128]{3,2,1,0:T(8,128)S(1)}, u32[]{:S(2)}, u32[]{:S(2)}) collective-permute-start(f32[6,1,16,128]{3,2,1,0:T(8,128)S(1)} %get-tuple-element.56), channel_id=1, source_target_pairs={{0,1},{1,2},{2,3},{4,5},{5,6},{6,7},{8,9},{9,10},{10,11},{12,13},{... | collective-permute-start | bytes 147464 | tf_op jit(solution)/shard_map/ppermute | solution.py:122
  6.2 10.4 %collective-permute-start = (f32[6,1,16,128]{3,2,1,0:T(8,128)S(1)}, f32[6,1,16,128]{3,2,1,0:T(8,128)S(1)}, u32[]{:S(2)}, u32[]{:S(2)}) collective-permute-start(f32[6,1,16,128]{3,2,1,0:T(8,128)S(1)} %get-tuple-element.57), channel_id=1, source_target_pairs={{1,0},{2,1},{3,2},{5,4},{6,5},{7,6},{9,8},{10,9},{11,10},{13,12},{... | collective-permute-start | bytes 147464 | tf_op jit(solution)/shard_map/ppermute | solution.py:122
  8.4 7.4 %collective-permute-start.4 = (f32[6,4,16,1]{2,0,3,1:T(8,128)S(1)}, f32[6,4,16,1]{2,0,3,1:T(8,128)S(1)}, u32[]{:S(2)}, u32[]{:S(2)}) collective-permute-start(f32[6,4,16,1]{2,0,3,1:T(8,128)S(1)} %get-tuple-element.63), channel_id=1, source_target_pairs={{0,8},{8,16},{16,24},{24,0},{1,9},{9,17},{17,25},{25,1},{2,10},{10... | collective-permute-start | bytes 4616 | tf_op jit(solution)/shard_map/ppermute | solution.py:122
  10.0 2.3 %copy-start.6 = (f32[3,5,5]{2,0,1:T(4,128)S(1)}, f32[3,5,5]{2,0,1:T(4,128)}, u32[]{:S(2)}) copy-start(f32[3,5,5]{2,0,1:T(4,128)} %param.12) | copy-start | bytes 904
  10.1 5.9 %collective-permute-start.3 = (f32[6,4,16,1]{2,0,3,1:T(8,128)S(1)}, f32[6,4,16,1]{2,0,3,1:T(8,128)S(1)}, u32[]{:S(2)}, u32[]{:S(2)}) collective-permute-start(f32[6,4,16,1]{2,0,3,1:T(8,128)S(1)} %get-tuple-element.64), channel_id=1, source_target_pairs={{0,24},{8,0},{16,8},{24,16},{1,25},{9,1},{17,9},{25,17},{2,26},{10... | collective-permute-start | bytes 4616 | tf_op jit(solution)/shard_map/ppermute | solution.py:122
  12.3 0.7 %copy-start.7 = (f32[3,5,5]{2,0,1:T(4,128)S(1)}, f32[3,5,5]{2,0,1:T(4,128)}, u32[]{:S(2)}) copy-start(f32[3,5,5]{2,0,1:T(4,128)} %param.13) | copy-start | bytes 904
  13.3 0.7 %copy-start.9 = (s32[4,128]{1,0:T(4,128)S(1)}, s32[4,128]{1,0:T(4,128)}, u32[]{:S(2)}) copy-start(s32[4,128]{1,0:T(4,128)} %param.17) | copy-start | bytes 6148
  15.1 0.7 %copy-start.8 = (f32[3,5]{1,0:T(4,128)S(1)}, f32[3,5]{1,0:T(4,128)}, u32[]{:S(2)}) copy-start(f32[3,5]{1,0:T(4,128)} %param.14) | copy-start | bytes 184
  16.5 0.9 %copy-start.4 = (f32[5,4,16,128]{3,2,1,0:T(8,128)S(1)}, f32[5,4,16,128]{3,2,1,0:T(8,128)}, u32[]{:S(2)}) copy-start(f32[5,4,16,128]{3,2,1,0:T(8,128)} %param.10) | copy-start | bytes 491524
  17.6 0.9 %copy-start.2 = (f32[5,4,16,128]{3,2,1,0:T(8,128)}, f32[5,4,16,128]{3,2,1,0:T(8,128)S(1)}, u32[]{:S(2)}) copy-start(f32[5,4,16,128]{3,2,1,0:T(8,128)S(1)} %fusion.15) | copy-start | bytes 491524
  17.7 0.8 %copy-start.1 = (f32[4,16,128]{2,1,0:T(8,128)S(1)}, f32[4,16,128]{2,1,0:T(8,128)}, u32[]{:S(2)}) copy-start(f32[4,16,128]{2,1,0:T(8,128)} %param.15) | copy-start | bytes 98308
  18.7 12.2 %collective-permute-start.8 = (f32[4,4,16,3]{3,2,1,0:T(8,128)S(1)}, f32[4,4,16,3]{3,2,1,0:T(8,128)S(1)}, u32[]{:S(2)}, u32[]{:S(2)}) collective-permute-start(f32[4,4,16,3]{3,2,1,0:T(8,128)S(1)} %get-tuple-element.45), channel_id=1, source_target_pairs={{0,8},{8,16},{16,24},{24,0},{1,9},{9,17},{17,25},{25,1},{2,10},{10... | collective-permute-start | bytes 9224 | tf_op jit(solution)/shard_map/ppermute | solution.py:122
  18.8 12.1 %collective-permute-start.9 = (f32[4,4,16,3]{3,2,1,0:T(8,128)S(1)}, f32[4,4,16,3]{3,2,1,0:T(8,128)S(1)}, u32[]{:S(2)}, u32[]{:S(2)}) collective-permute-start(f32[4,4,16,3]{3,2,1,0:T(8,128)S(1)} %get-tuple-element.46), channel_id=1, source_target_pairs={{0,24},{8,0},{16,8},{24,16},{1,25},{9,1},{17,9},{25,17},{2,26},{10... | collective-permute-start | bytes 9224 | tf_op jit(solution)/shard_map/ppermute | solution.py:122
  22.6 8.3 %collective-permute-start.6 = (f32[4,4,3,128]{3,2,1,0:T(4,128)S(1)}, f32[4,4,3,128]{3,2,1,0:T(4,128)S(1)}, u32[]{:S(2)}, u32[]{:S(2)}) collective-permute-start(f32[4,4,3,128]{3,2,1,0:T(4,128)S(1)} %fusion.29), channel_id=1, source_target_pairs={{0,4},{4,0},{1,5},{5,1},{2,6},{6,2},{3,7},{7,3},{8,12},{12,8},{9,1... | collective-permute-start | bytes 73736 | tf_op jit(solution)/shard_map/ppermute | solution.py:145
  23.8 6.5 %collective-permute-start.5 = (f32[8,128]{1,0:T(8,128)S(1)}, f32[8,128]{1,0:T(8,128)S(1)}, u32[]{:S(2)}, u32[]{:S(2)}) collective-permute-start(f32[8,128]{1,0:T(8,128)S(1)} %pad_bitcast_fusion.3), channel_id=1, source_target_pairs={{0,12},{8,20},{16,28},{24,4},{4,8},{12,16},{20,24},{28,0},{1,13},{... | collective-permute-start | bytes 12296 | tf_op jit(solution)/shard_map/ppermute | solution.py:143
  24.0 6.3 %collective-permute-start.7 = (f32[8,128]{1,0:T(8,128)S(1)}, f32[8,128]{1,0:T(8,128)S(1)}, u32[]{:S(2)}, u32[]{:S(2)}) collective-permute-start(f32[8,128]{1,0:T(8,128)S(1)} %pad_bitcast_fusion.2), channel_id=1, source_target_pairs={{0,28},{8,4},{16,12},{24,20},{4,24},{12,0},{20,8},{28,16},{1,29},{... | collective-permute-start | bytes 12296 | tf_op jit(solution)/shard_map/ppermute | solution.py:143
  31.5 3.6 %collective-permute-start.10 = (f32[280,128]{1,0:T(8,128)S(1)}, f32[280,128]{1,0:T(8,128)S(1)}, u32[]{:S(2)}, u32[]{:S(2)}) collective-permute-start(f32[280,128]{1,0:T(8,128)S(1)} %pad_bitcast_fusion.1), channel_id=1, source_target_pairs={{0,1},{1,2},{2,3},{4,5},{5,6},{6,7},{8,9},{9,10},{10,11},{12,13},{... | collective-permute-start | bytes 430088 | tf_op jit(solution)/shard_map/ppermute | solution.py:126
  33.8 6.7 %collective-permute-start.11 = (f32[280,128]{1,0:T(8,128)S(1)}, f32[280,128]{1,0:T(8,128)S(1)}, u32[]{:S(2)}, u32[]{:S(2)}) collective-permute-start(f32[280,128]{1,0:T(8,128)S(1)} %pad_bitcast_fusion), channel_id=1, source_target_pairs={{1,0},{2,1},{3,2},{5,4},{6,5},{7,6},{9,8},{10,9},{11,10},{13,12},{... | collective-permute-start | bytes 430088 | tf_op jit(solution)/shard_map/ppermute | solution.py:126
  42.7 0.9 %copy-start.5 = (f32[4,16,128]{2,1,0:T(8,128)S(1)}, f32[4,16,128]{2,1,0:T(8,128)}, u32[]{:S(2)}) copy-start(f32[4,16,128]{2,1,0:T(8,128)} %param.16) | copy-start | bytes 98308

commit v24 on v19

--- a/solution.py
+++ b/solution.py
@@ -132,7 +132,11 @@
     if lax.axis_size(axis) != 2 or WRAP[axis]:
         return receive(array, low, dims, width), receive(array, high, dims, width)
     me = lax.axis_index(axis)
-    sent = jnp.where(me == 0, take(array, low, dims, width), take(array, high, dims, width))
+    if rel:
+        sent = jnp.where(me == 0, take(array, low, dims, width), take(array, high, dims, width))
+    else:
+        length = array.shape[dims[axis]]
+        sent = lax.dynamic_slice_in_dim(array, (1 - me) * (length - width), width, axis=dims[axis])
     low_nz = {a: r for a, r in low.items() if r}
     axes, pairs = pairs_for({a: -r for a, r in low_nz.items()})
     _, back = pairs_for({a: -r for a, r in dict(low_nz, **{axis: 1}).items()})

time: 58.6 us -> 60.4 us (1.031)
  starting transfers between devices: 20.9 us -> 22.7 us
    ppermute x3, starting transfers between devices: 4.02 us -> 5.87 us  [receive_pair(): got = lax.ppermute(sent, axes, pairs + back)]
    ppermute x2, waiting for transfers between devices: 3.27 us -> 4.94 us  [receive(): lax.ppermute(flat, axes, pairs).reshape(-1)[:size].reshape(slab.shape)]
    ppermute x3, waiting for transfers between devices: 5.01 us -> 3.34 us  [receive_pair(): got = lax.ppermute(sent, axes, pairs + back)]
  transfers between devices with their start and end apart: 12 -> 12, of which waited for: 2 -> 3; matrix products, arithmetic and copies ran while one was open for 6% -> 6% of each run, Pallas kernels for 0% -> 0%
where the time goes in v24:
time: 60.4 us; the launch traced here: 59.9 us
  starting transfers between devices  22.7 us (38%)
  blocking collectives  13.4 us (22%)
  waiting for transfers between devices  8.29 us (14%)
  other arithmetic  7.05 us (12%)
  local copies, waits for them, and re-layouts  6.76 us (11%)
  between operations  1.27 us (2%)
    all_to_all x1, blocking collectives, reduce_panels(): lax.all_to_all(chunks, ORDER[::-1], 0, 0, tiled=False)  13.4 us
    ppermute x6, starting transfers between devices, receive(): return lax.ppermute(slab, axes, pairs)  10.5 us
    ppermute x3, starting transfers between devices, receive_pair(): got = lax.ppermute(sent, axes, pairs + back)  5.87 us
    ppermute x2, waiting for transfers between devices, receive(): lax.ppermute(flat, axes, pairs).reshape(-1)[:size].reshape(slab.shape)  4.94 us
    unnamed x28, local copies, waits for them, and re-layouts  4.02 us
    ppermute x3, waiting for transfers between devices, receive_pair(): got = lax.ppermute(sent, axes, pairs + back)  3.34 us
    ppermute x2, starting transfers between devices, receive(): lax.ppermute(flat, axes, pairs).reshape(-1)[:size].reshape(slab.shape)  3.32 us
    ppermute x1, starting transfers between devices, tile_halos(): got = lax.ppermute(sent, axis, [(0, 1), (1, 0)])  3.03 us
  transfers between devices with their start and end apart: 12, of which 3 were waited for; matrix products, arithmetic and copies ran while one was open for 6% of the time, Pallas kernels for 0%

profile of v24, /device:TPU:0, one launch (start us, length us, event | category | flops | bytes accessed | tf_op | source)
XLA Modules:
  0.0 59.9 jit_solution(13101549543192409130)
XLA Ops:
  0.6 0.8 %fusion.49 = (f32[1,4,16,128]{3,2,1,0:T(8,128)S(1)}, f32[4,16,128]{2,1,0:T(8,128)S(1)}, f32[4,16,128]{2,1,0:T(8,128)S(1)}) fusion(f32[3,4,16,128]{3,2,1,0:T(8,128)} %param.11), kind=kLoop, calls=%fused_computation.150 | loop fusion | bytes 163840 | tf_op jit(solution)/shard_map/slice | solution.py:198
  1.5 0.1 copy-done
  1.6 3.0 %collective-permute-start.2 = (f32[6,4,8,128]{3,2,1,0:T(8,128)S(1)}, f32[6,4,8,128]{3,2,1,0:T(8,128)S(1)}, u32[]{:S(2)}, u32[]{:S(2)}) collective-permute-start(f32[6,4,8,128]{3,2,1,0:T(8,128)S(1)} %pad_maximum_fusion.2), channel_id=1, source_target_pairs={{0,4},{4,0},{1,5},{5,1},{2,6},{6,2},{3,7},{7,3},{8,12},{12,8},{9,1... | collective-permute-start | bytes 294920 | tf_op jit(solution)/shard_map/ppermute | solution.py:153
  4.7 1.5 %collective-permute-start.1 = (f32[6,1,16,128]{3,2,1,0:T(8,128)S(1)}, f32[6,1,16,128]{3,2,1,0:T(8,128)S(1)}, u32[]{:S(2)}, u32[]{:S(2)}) collective-permute-start(f32[6,1,16,128]{3,2,1,0:T(8,128)S(1)} %get-tuple-element.56), channel_id=1, source_target_pairs={{0,1},{1,2},{2,3},{4,5},{5,6},{6,7},{8,9},{9,10},{10,11},{12,13},{... | collective-permute-start | bytes 147464 | tf_op jit(solution)/shard_map/ppermute | solution.py:122
  6.2 1.3 %collective-permute-start = (f32[6,1,16,128]{3,2,1,0:T(8,128)S(1)}, f32[6,1,16,128]{3,2,1,0:T(8,128)S(1)}, u32[]{:S(2)}, u32[]{:S(2)}) collective-permute-start(f32[6,1,16,128]{3,2,1,0:T(8,128)S(1)} %get-tuple-element.57), channel_id=1, source_target_pairs={{1,0},{2,1},{3,2},{5,4},{6,5},{7,6},{9,8},{10,9},{11,10},{13,12},{... | collective-permute-start | bytes 147464 | tf_op jit(solution)/shard_map/ppermute | solution.py:122
  7.6 0.3 copy.113
  7.9 0.3 copy.114
  8.4 1.6 %collective-permute-start.4 = (f32[6,4,16,1]{2,0,3,1:T(8,128)S(1)}, f32[6,4,16,1]{2,0,3,1:T(8,128)S(1)}, u32[]{:S(2)}, u32[]{:S(2)}) collective-permute-start(f32[6,4,16,1]{2,0,3,1:T(8,128)S(1)} %get-tuple-element.67), channel_id=1, source_target_pairs={{0,8},{8,16},{16,24},{24,0},{1,9},{9,17},{17,25},{25,1},{2,10},{10... | collective-permute-start | bytes 4616 | tf_op jit(solution)/shard_map/ppermute | solution.py:122
  10.1 2.2 %collective-permute-start.3 = (f32[6,4,16,1]{2,0,3,1:T(8,128)S(1)}, f32[6,4,16,1]{2,0,3,1:T(8,128)S(1)}, u32[]{:S(2)}, u32[]{:S(2)}) collective-permute-start(f32[6,4,16,1]{2,0,3,1:T(8,128)S(1)} %get-tuple-element.68), channel_id=1, source_target_pairs={{0,24},{8,0},{16,8},{24,16},{1,25},{9,1},{17,9},{25,17},{2,26},{10... | collective-permute-start | bytes 4616 | tf_op jit(solution)/shard_map/ppermute | solution.py:122
  12.3 0.7 %copy-done.7 = f32[3,5,5]{2,0,1:T(4,128)S(1)} copy-done((f32[3,5,5]{2,0,1:T(4,128)S(1)}, f32[3,5,5]{2,0,1:T(4,128)}, u32[]{:S(2)}) %copy-start.7) | copy-done | bytes 324
  13.1 0.1 subtract_multiply_fusion
  13.3 0.7 %copy-done.9 = s32[4,128]{1,0:T(4,128)S(1)} copy-done((s32[4,128]{1,0:T(4,128)S(1)}, s32[4,128]{1,0:T(4,128)}, u32[]{:S(2)}) %copy-start.9) | copy-done | bytes 2072
  14.0 0.5 multiply_reduce_fusion.2
  14.5 0.2 multiply_reduce_fusion
  14.7 0.1 multiply_reduce_fusion.4
  14.9 0.2 slice_reduce_fusion
  15.1 0.6 %copy-done.8 = f32[3,5]{1,0:T(4,128)S(1)} copy-done((f32[3,5]{1,0:T(4,128)S(1)}, f32[3,5]{1,0:T(4,128)}, u32[]{:S(2)}) %copy-start.8) | copy-done | bytes 84
  16.1 0.2 copy.102
  16.3 0.2 copy.100
  16.6 0.1 multiply_reduce_fusion.7
  17.0 0.5 copy-done.4
  17.5 0.2 fusion.15
  17.8 0.7 %copy-done.1 = f32[4,16,128]{2,1,0:T(8,128)S(1)} copy-done((f32[4,16,128]{2,1,0:T(8,128)S(1)}, f32[4,16,128]{2,1,0:T(8,128)}, u32[]{:S(2)}) %copy-start.1) | copy-done | bytes 32792
  18.6 0.1 fusion.26
  18.7 3.8 %collective-permute-start.9 = (f32[4,4,16,3]{3,2,1,0:T(8,128)S(1)}, f32[4,4,16,3]{3,2,1,0:T(8,128)S(1)}, u32[]{:S(2)}, u32[]{:S(2)}) collective-permute-start(f32[4,4,16,3]{3,2,1,0:T(8,128)S(1)} %get-tuple-element.46), channel_id=1, source_target_pairs={{0,24},{8,0},{16,8},{24,16},{1,25},{9,1},{17,9},{25,17},{2,26},{10... | collective-permute-start | bytes 9224 | tf_op jit(solution)/shard_map/ppermute | solution.py:122
  22.5 4.7 %collective-permute-start.7 = (f32[4,4,3,3]{3,2,1,0:T(4,128)S(1)}, f32[4,4,3,3]{3,2,1,0:T(4,128)S(1)}, u32[]{:S(2)}, u32[]{:S(2)}) collective-permute-start(f32[4,4,3,3]{3,2,1,0:T(4,128)S(1)} %get-tuple-element.48), channel_id=1, source_target_pairs={{0,28},{8,4},{16,12},{24,20},{4,24},{12,0},{20,8},{28,16},{1,29},{... | collective-permute-start | bytes 1736 | tf_op jit(solution)/shard_map/ppermute | solution.py:143
  27.3 1.1 %collective-permute-start.6 = (f32[4,4,3,128]{3,2,1,0:T(4,128)S(1)}, f32[4,4,3,128]{3,2,1,0:T(4,128)S(1)}, u32[]{:S(2)}, u32[]{:S(2)}) collective-permute-start(f32[4,4,3,128]{3,2,1,0:T(4,128)S(1)} %fusion.28), channel_id=1, source_target_pairs={{0,4},{4,0},{1,5},{5,1},{2,6},{6,2},{3,7},{7,3},{8,12},{12,8},{9,1... | collective-permute-start | bytes 73736 | tf_op jit(solution)/shard_map/ppermute | solution.py:143
  28.4 1.6 %collective-permute-done.5 = f32[4,4,3,3]{3,2,1,0:T(4,128)S(1)} collective-permute-done((f32[4,4,3,3]{3,2,1,0:T(4,128)S(1)}, f32[4,4,3,3]{3,2,1,0:T(4,128)S(1)}, u32[]{:S(2)}, u32[]{:S(2)}) %collective-permute-start.5) | collective-permute-done | bytes 608 | tf_op jit(solution)/shard_map/ppermute | solution.py:143
  30.0 1.8 %collective-permute-done.6 = f32[4,4,3,128]{3,2,1,0:T(4,128)S(1)} collective-permute-done((f32[4,4,3,128]{3,2,1,0:T(4,128)S(1)}, f32[4,4,3,128]{3,2,1,0:T(4,128)S(1)}, u32[]{:S(2)}, u32[]{:S(2)}) %collective-permute-start.6) | collective-permute-done | bytes 24608 | tf_op jit(solution)/shard_map/ppermute | solution.py:143
  31.9 0.3 maximum_maximum_fusion
  32.2 0.2 reshape.159
  32.5 2.0 %collective-permute-start.10 = (f32[280,128]{1,0:T(8,128)S(1)}, f32[280,128]{1,0:T(8,128)S(1)}, u32[]{:S(2)}, u32[]{:S(2)}) collective-permute-start(f32[280,128]{1,0:T(8,128)S(1)} %pad_bitcast_fusion.1), channel_id=1, source_target_pairs={{0,1},{1,2},{2,3},{4,5},{5,6},{6,7},{8,9},{9,10},{10,11},{12,13},{... | collective-permute-start | bytes 430088 | tf_op jit(solution)/shard_map/ppermute | solution.py:126
  34.5 0.2 reshape.163
  34.7 1.3 %collective-permute-start.11 = (f32[280,128]{1,0:T(8,128)S(1)}, f32[280,128]{1,0:T(8,128)S(1)}, u32[]{:S(2)}, u32[]{:S(2)}) collective-permute-start(f32[280,128]{1,0:T(8,128)S(1)} %pad_bitcast_fusion), channel_id=1, source_target_pairs={{1,0},{2,1},{3,2},{5,4},{6,5},{7,6},{9,8},{10,9},{11,10},{13,12},{... | collective-permute-start | bytes 430088 | tf_op jit(solution)/shard_map/ppermute | solution.py:126
  36.1 0.2 reshape.162
  36.3 4.9 %collective-permute-done.11 = f32[280,128]{1,0:T(8,128)S(1)} collective-permute-done((f32[280,128]{1,0:T(8,128)S(1)}, f32[280,128]{1,0:T(8,128)S(1)}, u32[]{:S(2)}, u32[]{:S(2)}) %collective-permute-start.11) | collective-permute-done | bytes 143392 | tf_op jit(solution)/shard_map/ppermute | solution.py:126
  41.2 0.2 reshape.166
  41.5 0.3 pad_maximum_fusion
  41.9 0.1 multiply_add_fusion
  42.0 0.1 multiply_add_fusion.1
  42.2 0.1 broadcast_multiply_fusion
  42.3 1.2 %broadcast_multiply_fusion.1 = (f32[3,8,20,132]{3,2,1,0:T(8,128)S(1)}, f32[3,8,20,132]{3,2,1,0:T(8,128)S(1)}) fusion(f32[8,20,132]{2,1,0:T(8,128)S(1)} %get-tuple-element.36, f32[3,10,22,134]{3,2,1,0:T(8,128)S(1)} %get-tuple-element.27, f32[8,20,132]{2,1,0:T(8,128)S(1)} %get-tuple-element.35, f32[4,10,22,134]{3,2,1,0:T(8,128)S(1)} %pad_maximum_fusion, ...), kind=kLoop, calls=%fused_computation.41 | loop fusion | flops 760320 | bytes 2703360 | tf_op jit(solution)/shard_map/mul | solution.py:60
  43.5 0.9 %broadcast_multiply_fusion.2 = (f32[3,6,18,130]{3,2,1,0:T(8,128)S(1)}, f32[3,6,18,130]{3,2,1,0:T(8,128)S(1)}) fusion(f32[6,18,130]{2,1,0:T(8,128)S(1)} %get-tuple-element.34, f32[3,8,20,132]{3,2,1,0:T(8,128)S(1)} %get-tuple-element.25, f32[6,18,130]{2,1,0:T(8,128)S(1)} %get-tuple-element.33, f32[4,10,22,134]{3,2,1,0:T(8,128)S(1)} %pad_maximum_fusion, ...), kind=kLoop, calls=%fused_computation.44 | loop fusion | flops 505440 | bytes 1797120 | tf_op jit(solution)/shard_map/mul | solution.py:60
  44.4 0.9 %multiply_reduce_fusion.9 = (f32[3,4,128]{2,1,0:T(4,128)S(1)}, f32[3,4,16,128]{3,2,1,0:T(8,128)}) fusion(f32[4,16,128]{2,1,0:T(8,128)S(1)} %copy-done.5, f32[3,6,18,130]{3,2,1,0:T(8,128)S(1)} %get-tuple-element.23, f32[3,4,16,128]{3,2,1,0:T(8,128)S(1)} %multiply_reduce_fusion.6, f32[4,16,128]{2,1,0:T(8,128)S(1)} %fusion.32, ...), kind=kLoop, calls=%fused_computation.80 | loop fusion | flops 317952 | bytes 956416 | tf_op jit(solution)/shard_map/reduce_sum | solution.py:269
  45.3 0.4 convolution_bitcast_fusion
  45.7 0.2 select_select_fusion
  45.9 13.4 %all_to_all.5 = f32[32,3,128]{2,1,0:T(4,128)S(1)} all-to-all(f32[32,3,128]{2,1,0:T(4,128)S(1)} %select_select_fusion), channel_id=1, replica_groups=mesh['circ'=4,'normal'=2,'span'=4] {'span','normal','circ'}, dimensions={0} | all-to-all | bytes 98304 | tf_op jit(solution)/shard_map/all_to_all | solution.py:234
  59.2 0.6 %reduce_sum.167 = f32[3,128]{1,0:T(4,128)} reduce(f32[32,3,128]{2,1,0:T(4,128)S(1)} %all_to_all.5, f32[]{:T(128)} %constant.19.clone.1), dimensions={0}, to_apply=%region_14.15 | reduce | flops 11904 | bytes 50692 | tf_op jit(solution)/shard_map/reduce_sum | solution.py:234
  (84 shorter events, 1.8 us)
Async XLA Ops:
  0.6 0.9 %copy-start = (f32[5,4,16,128]{3,2,1,0:T(8,128)S(1)}, f32[5,4,16,128]{3,2,1,0:T(8,128)}, u32[]{:S(2)}) copy-start(f32[5,4,16,128]{3,2,1,0:T(8,128)} %param.9) | copy-start | bytes 491524
  1.6 3.1 %copy-start.3 = (f32[3,4,16,128]{3,2,1,0:T(8,128)S(1)}, f32[3,4,16,128]{3,2,1,0:T(8,128)}, u32[]{:S(2)}) copy-start(f32[3,4,16,128]{3,2,1,0:T(8,128)} %param.11) | copy-start | bytes 294916
  1.6 15.1 %collective-permute-start.2 = (f32[6,4,8,128]{3,2,1,0:T(8,128)S(1)}, f32[6,4,8,128]{3,2,1,0:T(8,128)S(1)}, u32[]{:S(2)}, u32[]{:S(2)}) collective-permute-start(f32[6,4,8,128]{3,2,1,0:T(8,128)S(1)} %pad_maximum_fusion.2), channel_id=1, source_target_pairs={{0,4},{4,0},{1,5},{5,1},{2,6},{6,2},{3,7},{7,3},{8,12},{12,8},{9,1... | collective-permute-start | bytes 294920 | tf_op jit(solution)/shard_map/ppermute | solution.py:153
  4.7 11.8 %collective-permute-start.1 = (f32[6,1,16,128]{3,2,1,0:T(8,128)S(1)}, f32[6,1,16,128]{3,2,1,0:T(8,128)S(1)}, u32[]{:S(2)}, u32[]{:S(2)}) collective-permute-start(f32[6,1,16,128]{3,2,1,0:T(8,128)S(1)} %get-tuple-element.56), channel_id=1, source_target_pairs={{0,1},{1,2},{2,3},{4,5},{5,6},{6,7},{8,9},{9,10},{10,11},{12,13},{... | collective-permute-start | bytes 147464 | tf_op jit(solution)/shard_map/ppermute | solution.py:122
  6.2 10.4 %collective-permute-start = (f32[6,1,16,128]{3,2,1,0:T(8,128)S(1)}, f32[6,1,16,128]{3,2,1,0:T(8,128)S(1)}, u32[]{:S(2)}, u32[]{:S(2)}) collective-permute-start(f32[6,1,16,128]{3,2,1,0:T(8,128)S(1)} %get-tuple-element.57), channel_id=1, source_target_pairs={{1,0},{2,1},{3,2},{5,4},{6,5},{7,6},{9,8},{10,9},{11,10},{13,12},{... | collective-permute-start | bytes 147464 | tf_op jit(solution)/shard_map/ppermute | solution.py:122
  8.4 7.4 %collective-permute-start.4 = (f32[6,4,16,1]{2,0,3,1:T(8,128)S(1)}, f32[6,4,16,1]{2,0,3,1:T(8,128)S(1)}, u32[]{:S(2)}, u32[]{:S(2)}) collective-permute-start(f32[6,4,16,1]{2,0,3,1:T(8,128)S(1)} %get-tuple-element.67), channel_id=1, source_target_pairs={{0,8},{8,16},{16,24},{24,0},{1,9},{9,17},{17,25},{25,1},{2,10},{10... | collective-permute-start | bytes 4616 | tf_op jit(solution)/shard_map/ppermute | solution.py:122
  10.0 2.3 %copy-start.6 = (f32[3,5,5]{2,0,1:T(4,128)S(1)}, f32[3,5,5]{2,0,1:T(4,128)}, u32[]{:S(2)}) copy-start(f32[3,5,5]{2,0,1:T(4,128)} %param.12) | copy-start | bytes 904
  10.1 5.9 %collective-permute-start.3 = (f32[6,4,16,1]{2,0,3,1:T(8,128)S(1)}, f32[6,4,16,1]{2,0,3,1:T(8,128)S(1)}, u32[]{:S(2)}, u32[]{:S(2)}) collective-permute-start(f32[6,4,16,1]{2,0,3,1:T(8,128)S(1)} %get-tuple-element.68), channel_id=1, source_target_pairs={{0,24},{8,0},{16,8},{24,16},{1,25},{9,1},{17,9},{25,17},{2,26},{10... | collective-permute-start | bytes 4616 | tf_op jit(solution)/shard_map/ppermute | solution.py:122
  12.3 0.7 %copy-start.7 = (f32[3,5,5]{2,0,1:T(4,128)S(1)}, f32[3,5,5]{2,0,1:T(4,128)}, u32[]{:S(2)}) copy-start(f32[3,5,5]{2,0,1:T(4,128)} %param.13) | copy-start | bytes 904
  13.3 0.7 %copy-start.9 = (s32[4,128]{1,0:T(4,128)S(1)}, s32[4,128]{1,0:T(4,128)}, u32[]{:S(2)}) copy-start(s32[4,128]{1,0:T(4,128)} %param.17) | copy-start | bytes 6148
  15.1 0.7 %copy-start.8 = (f32[3,5]{1,0:T(4,128)S(1)}, f32[3,5]{1,0:T(4,128)}, u32[]{:S(2)}) copy-start(f32[3,5]{1,0:T(4,128)} %param.14) | copy-start | bytes 184
  16.6 0.9 %copy-start.4 = (f32[5,4,16,128]{3,2,1,0:T(8,128)S(1)}, f32[5,4,16,128]{3,2,1,0:T(8,128)}, u32[]{:S(2)}) copy-start(f32[5,4,16,128]{3,2,1,0:T(8,128)} %param.10) | copy-start | bytes 491524
  17.7 0.9 %copy-start.2 = (f32[5,4,16,128]{3,2,1,0:T(8,128)}, f32[5,4,16,128]{3,2,1,0:T(8,128)S(1)}, u32[]{:S(2)}) copy-start(f32[5,4,16,128]{3,2,1,0:T(8,128)S(1)} %fusion.15) | copy-start | bytes 491524
  17.7 0.8 %copy-start.1 = (f32[4,16,128]{2,1,0:T(8,128)S(1)}, f32[4,16,128]{2,1,0:T(8,128)}, u32[]{:S(2)}) copy-start(f32[4,16,128]{2,1,0:T(8,128)} %param.15) | copy-start | bytes 98308
  18.7 13.2 %collective-permute-start.8 = (f32[4,4,16,3]{3,2,1,0:T(8,128)S(1)}, f32[4,4,16,3]{3,2,1,0:T(8,128)S(1)}, u32[]{:S(2)}, u32[]{:S(2)}) collective-permute-start(f32[4,4,16,3]{3,2,1,0:T(8,128)S(1)} %get-tuple-element.45), channel_id=1, source_target_pairs={{0,8},{8,16},{16,24},{24,0},{1,9},{9,17},{17,25},{25,1},{2,10},{10... | collective-permute-start | bytes 9224 | tf_op jit(solution)/shard_map/ppermute | solution.py:122
  18.7 13.1 %collective-permute-start.9 = (f32[4,4,16,3]{3,2,1,0:T(8,128)S(1)}, f32[4,4,16,3]{3,2,1,0:T(8,128)S(1)}, u32[]{:S(2)}, u32[]{:S(2)}) collective-permute-start(f32[4,4,16,3]{3,2,1,0:T(8,128)S(1)} %get-tuple-element.46), channel_id=1, source_target_pairs={{0,24},{8,0},{16,8},{24,16},{1,25},{9,1},{17,9},{25,17},{2,26},{10... | collective-permute-start | bytes 9224 | tf_op jit(solution)/shard_map/ppermute | solution.py:122
  22.5 7.5 %collective-permute-start.5 = (f32[4,4,3,3]{3,2,1,0:T(4,128)S(1)}, f32[4,4,3,3]{3,2,1,0:T(4,128)S(1)}, u32[]{:S(2)}, u32[]{:S(2)}) collective-permute-start(f32[4,4,3,3]{3,2,1,0:T(4,128)S(1)} %get-tuple-element.47), channel_id=1, source_target_pairs={{0,12},{8,20},{16,28},{24,4},{4,8},{12,16},{20,24},{28,0},{1,13},{... | collective-permute-start | bytes 1736 | tf_op jit(solution)/shard_map/ppermute | solution.py:143
  22.5 7.5 %collective-permute-start.7 = (f32[4,4,3,3]{3,2,1,0:T(4,128)S(1)}, f32[4,4,3,3]{3,2,1,0:T(4,128)S(1)}, u32[]{:S(2)}, u32[]{:S(2)}) collective-permute-start(f32[4,4,3,3]{3,2,1,0:T(4,128)S(1)} %get-tuple-element.48), channel_id=1, source_target_pairs={{0,28},{8,4},{16,12},{24,20},{4,24},{12,0},{20,8},{28,16},{1,29},{... | collective-permute-start | bytes 1736 | tf_op jit(solution)/shard_map/ppermute | solution.py:143
  27.3 4.5 %collective-permute-start.6 = (f32[4,4,3,128]{3,2,1,0:T(4,128)S(1)}, f32[4,4,3,128]{3,2,1,0:T(4,128)S(1)}, u32[]{:S(2)}, u32[]{:S(2)}) collective-permute-start(f32[4,4,3,128]{3,2,1,0:T(4,128)S(1)} %fusion.28), channel_id=1, source_target_pairs={{0,4},{4,0},{1,5},{5,1},{2,6},{6,2},{3,7},{7,3},{8,12},{12,8},{9,1... | collective-permute-start | bytes 73736 | tf_op jit(solution)/shard_map/ppermute | solution.py:143
  32.5 3.6 %collective-permute-start.10 = (f32[280,128]{1,0:T(8,128)S(1)}, f32[280,128]{1,0:T(8,128)S(1)}, u32[]{:S(2)}, u32[]{:S(2)}) collective-permute-start(f32[280,128]{1,0:T(8,128)S(1)} %pad_bitcast_fusion.1), channel_id=1, source_target_pairs={{0,1},{1,2},{2,3},{4,5},{5,6},{6,7},{8,9},{9,10},{10,11},{12,13},{... | collective-permute-start | bytes 430088 | tf_op jit(solution)/shard_map/ppermute | solution.py:126
  34.7 6.5 %collective-permute-start.11 = (f32[280,128]{1,0:T(8,128)S(1)}, f32[280,128]{1,0:T(8,128)S(1)}, u32[]{:S(2)}, u32[]{:S(2)}) collective-permute-start(f32[280,128]{1,0:T(8,128)S(1)} %pad_bitcast_fusion), channel_id=1, source_target_pairs={{1,0},{2,1},{3,2},{5,4},{6,5},{7,6},{9,8},{10,9},{11,10},{13,12},{... | collective-permute-start | bytes 430088 | tf_op jit(solution)/shard_map/ppermute | solution.py:126
  43.5 0.9 %copy-start.5 = (f32[4,16,128]{2,1,0:T(8,128)S(1)}, f32[4,16,128]{2,1,0:T(8,128)}, u32[]{:S(2)}) copy-start(f32[4,16,128]{2,1,0:T(8,128)} %param.16) | copy-start | bytes 98308
